TPU v7x, 512 devices: a whole 4x8x8 slice. The times are simulated.
512 devices in a mesh: ctx: 64 (over z, y_lo, core), tp: 8 (over y_hi, x).
Axes of the slice: x: 4, y: 8 (y_hi: 2, y_lo: 4; y = y_hi * 4 + y_lo), z: 8, core: 2. Of those that a mesh axis runs over, the one named last changes fastest.
Arguments:
- qkv: bfloat16 [8192, 3, 8192], P('ctx', None, 'tp'), may hold values from -2048 to 2048
- taps: float32 [7, 3, 8192], P(None, None, 'tp'), may hold values from -2 to 2
- rate: float32 [512, 16], P('tp'), may hold values from 0 to 1
- angle: float32 [512, 16], P('tp'), may hold values from -0.5 to 0.5
- residue: float32 [2, 512, 16], P(None, 'tp'), may hold values from -3 to 3
- skip: float32 [8192], P('tp'), may hold values from 0.5 to 1.5
- gain: float32 [8192], P('tp'), may hold values from 0.25 to 1.75
- lengths: int32 [4], replicated, may hold values from 1 to 4096, 8192 in all
Outputs:
- mixed: bfloat16 [8192, 8192], P('ctx', 'tp')
Inputs may be any that keep to these rules, and one draw needn't show every extreme that they name: `lengths`: they sum to 8192.
All inputs are finite; a program needn't handle non-finite values.
Results may differ from a plain program's by a relative error of at most 0.001.
Values may be sent and summed in bfloat16 or wider, within the bound.
No kernel may reach another device: no remote copies, remote signals or barrier semaphores. Data moves between devices by JAX's collectives and lax.ppermute only.
A program may use at most 128 MiB of HBM per device.

v0:
```python
import jax
import jax.numpy as jnp
from jax import lax
from jax.sharding import PartitionSpec as P

D = 8192
SPAN = 128


HIGHEST = lax.Precision.HIGHEST
EPSILON = 1e-06


def passed_along(block, axis, distance):
    devices = range(lax.axis_size(axis))
    route = [(i - distance, i) for i in devices if i - distance in devices]
    return lax.ppermute(block, axis, route)


def genome_begin(lengths, positions):
    ending = jnp.cumsum(lengths)
    starting = ending - lengths
    reached = starting[None, :] <= positions[:, None]
    return jnp.max(jnp.where(reached, starting[None, :], 0), axis=1)


def toeplitz(response):
    group_count, block = response.shape
    folded = jnp.concatenate(
        [response[:, :1], jnp.zeros((group_count, block), response.dtype), response[:, :0:-1]],
        axis=1,
    )
    tiled = jnp.tile(folded, (1, block))[:, : block * (2 * block - 1)]
    return tiled.reshape(group_count, block, 2 * block - 1)[:, :, :block]


def pole_tables(rate, angle, residue, block):
    counter = jnp.arange(block + 1).astype(jnp.float32)
    magnitude = jnp.exp(-rate[:, :, None] * counter)
    power_re = magnitude * jnp.cos(angle[:, :, None] * counter)
    power_im = magnitude * jnp.sin(angle[:, :, None] * counter)
    resid_re = residue[0][:, :, None]
    resid_im = residue[1][:, :, None]
    response = jnp.sum(
        resid_re * power_re[:, :, :block] - resid_im * power_im[:, :, :block], axis=1
    )
    enter_re = resid_re * power_re[:, :, 1:] - resid_im * power_im[:, :, 1:]
    enter_im = resid_re * power_im[:, :, 1:] + resid_im * power_re[:, :, 1:]
    entering = jnp.stack([enter_re, -enter_im])
    leaving = jnp.stack([power_re[:, :, block - 1 :: -1], power_im[:, :, block - 1 :: -1]])
    stepping = jnp.stack([power_re[:, :, block].T, power_im[:, :, block].T])
    return (toeplitz(response), entering, leaving, stepping)


def complex_times(factor_one, factor_two):
    return jnp.stack(
        [
            factor_one[0] * factor_two[0] - factor_one[1] * factor_two[1],
            factor_one[0] * factor_two[1] + factor_one[1] * factor_two[0],
        ]
    )


def block_terms(tables, columns, block_positions, block_starts):
    matrix_table, entering, leaving, stepping = tables
    same_genome = (block_positions[None, :] >= block_starts[:, None]).astype(jnp.float32)
    inside = jnp.einsum(
        "gts,gis->git", matrix_table * same_genome[None], columns, precision=HIGHEST
    )
    tail_mask = (block_positions >= block_starts[-1]).astype(jnp.float32)
    fresh_state = jnp.einsum("rgns,gis->rngi", leaving * tail_mask, columns, precision=HIGHEST)
    return (inside, fresh_state)


def carried(entering, carry_state):
    return jnp.einsum("rgnt,rngi->git", entering, carry_state, precision=HIGHEST)


def short_filter(padded, taps_part, positions, genome_start):
    lead = taps_part.shape[0] - 1
    row_count = positions.shape[0]
    result = jnp.zeros((row_count,) + padded.shape[1:], jnp.float32)
    for offset in range(taps_part.shape[0]):
        keep_tap = (positions - offset >= genome_start)[:, None, None]
        window = padded[lead - offset : lead - offset + row_count].astype(jnp.float32)
        result = result + jnp.where(keep_tap, taps_part[offset][None] * window, 0.0)
    return result


def on_device(qkv, taps, rate, angle, residue, skip, gain, lengths):
    tok_rows = qkv.shape[0]
    channels = qkv.shape[2]
    group_count = rate.shape[0]
    group_width = channels // group_count
    mode_count = rate.shape[1]
    reach = taps.shape[0]
    span_count = tok_rows // SPAN
    device = lax.axis_index("ctx")
    anchor = device * tok_rows
    positions = anchor + jnp.arange(tok_rows, dtype=jnp.int32)
    genome_start = genome_begin(lengths, positions)
    before = passed_along(qkv[tok_rows - (reach - 1) :], "ctx", 1)
    padded = jnp.concatenate([before, qkv], axis=0)
    filtered = short_filter(padded, taps, positions, genome_start)
    product = filtered[:, 1] * filtered[:, 2]
    tables = pole_tables(rate, angle, residue, SPAN)
    stepping = tables[3]
    values = jnp.transpose(
        product.reshape(span_count, SPAN, group_count, group_width), (0, 2, 3, 1)
    )
    span_pos = positions.reshape(span_count, SPAN)
    span_begin = genome_start.reshape(span_count, SPAN)
    summary = jnp.zeros((2, mode_count, group_count, group_width), jnp.float32)
    freshes = []
    keepers = []
    span_index = 0
    inside, fresh_state = block_terms(
        tables, values[span_index], span_pos[span_index], span_begin[span_index]
    )
    keep_state = span_begin[span_index, -1] < span_pos[span_index, 0]
    summary = jnp.where(keep_state, complex_times(stepping[..., None], summary), 0.0) + fresh_state
    insides = [inside]
    freshes.append(fresh_state)
    keepers.append(keep_state)
    device_count = lax.axis_size("ctx")
    starting = jnp.cumsum(lengths) - lengths

    def unbroken(first_row, last_row):
        hit = (starting >= first_row) & (starting <= last_row)
        return jnp.logical_not(jnp.any(hit))

    def widen(factor):
        return jnp.repeat(factor, group_width, axis=2)

    running = passed_along(summary.reshape(2, mode_count, channels), "ctx", 1)
    power = stepping
    distance = 1
    while distance < device_count:
        earlier = passed_along(running, "ctx", distance)
        alive = unbroken(anchor - distance * tok_rows, anchor - 1)
        factor = widen(power) * alive.astype(jnp.float32)
        running = running + complex_times(factor, earlier)
        power = complex_times(power, power)
        distance = distance * 2
    incoming = running.reshape(2, mode_count, group_count, group_width)
    span_index = 0
    entered = (span_begin[span_index] < span_pos[span_index, 0])[None, None, :]
    outputs = [insides[span_index] + jnp.where(entered, carried(tables[1], incoming), 0.0)]
    stacked = jnp.stack(outputs, axis=0)
    long_part = jnp.transpose(stacked, (0, 3, 1, 2)).reshape(tok_rows, channels)
    gated_rows = filtered[:, 0] * (long_part + skip[None] * product)
    squares = lax.psum(jnp.sum(gated_rows * gated_rows, axis=1), "tp")
    root_mean = jnp.sqrt(squares / D + EPSILON)
    return (gated_rows / root_mean[:, None] * gain[None]).astype(jnp.bfloat16)


def solution(mesh):
    return jax.shard_map(
        on_device,
        mesh=mesh,
        in_specs=(
            P("ctx", None, "tp"),
            P(None, None, "tp"),
            P("tp", None),
            P("tp", None),
            P(None, "tp", None),
            P("tp"),
            P("tp"),
            P(),
        ),
        out_specs=P("ctx", "tp"),
        check_vma=False,
    )
```

profile of v0, /device:TPU:64, one launch (start us, length us, event | category | flops | bytes accessed | tf_op | source)
XLA Modules:
  0.0 183.6 jit_solution(18116560297953018858)
XLA Ops:
  0.0 0.8 slice.277
  0.8 1.9 %collective-permute-start = (bf16[6,3,1024]{2,0,1:T(8,128)(2,1)S(1)}, bf16[6,3,1024]{2,0,1:T(8,128)(2,1)S(1)}, u32[]{:S(2)}, u32[]{:S(2)}) collective-permute-start(bf16[6,3,1024]{2,0,1:T(8,128)(2,1)S(1)} %slice.277), channel_id=1, source_target_pairs={{0,8},{8,16},{16,24},{24,32},{32,40},{40,48},{48,56},{56,64},{64,7... | collective-permute-start | bytes 110600 | tf_op jit(solution)/shard_map/ppermute | solution.py:17
  2.8 0.7 slice_bitcast_fusion.14
  3.7 0.8 copy.95
  4.5 0.7 neg.7
  5.2 3.9 %fusion.5 = (f32[64,16,129]{2,1,0:T(8,128)S(1)}, f32[64,16,129]{2,1,0:T(8,128)S(1)}) fusion(f32[64,16]{1,0:T(8,128)S(1)} %copy.95, f32[129]{0:T(256)S(1)} %iota_convert_fusion, f32[64,16]{1,0:T(8,128)S(1)} %copy.94), kind=kLoop, calls=%fused_computation.21 | loop fusion | flops 528384 | bytes 1065476 | tf_op jit(solution)/shard_map/mul | solution.py:40
  10.0 0.7 and_reduce_fusion
  12.2 0.6 slice.304
  12.8 1.9 %subtract_reduce_fusion = (f32[64,128]{1,0:T(8,128)S(1)}, f32[1,64,16,128]{3,2,0,1:T(8,128)}, f32[1,64,16,128]{3,2,0,1:T(8,128)}, f32[64,16,128]{2,1,0:T(8,128)}, f32[64,16,128]{2,1,0:T(8,128)}) fusion(f32[64,16]{1,0:T(8,128)S(1)} %copy.96, f32[64,16]{1,0:T(8,128)S(1)} %copy.93, f32[64,16,129]{2,1,0:T(8,128)S(1)} %get-tuple-element.44, ...), kind=kLoop, calls=%fused_computation.45 | loop fusion | flops 1433600 | bytes 4235264 | tf_op jit(solution)/shard_map/reduce_sum | solution.py:44
  14.9 0.7 compare_convert_fusion.1
  15.6 1.2 copy.90
  16.7 0.9 copy.99
  17.7 0.6 slice.301
  18.9 1.0 rev.11
  19.9 1.0 rev.10
  20.9 1.3 copy.91
  22.2 10.9 %select_add_fusion = f32[128,3,1024]{0,2,1:T(8,128)S(1)} fusion(bf16[128,3,1024]{0,2,1:T(8,128)(2,1)} %copy.90, bf16[6,3,1024]{0,2,1:T(8,128)(2,1)} %copy.91, f32[3,1024]{1,0:T(4,128)S(1)} %get-tuple-element.74, f32[3,1024]{1,0:T(4,128)S(1)} %get-tuple-element.75, f32[3,1024]{1,0:T(4,128)S(1)} %get-tuple-element.76, f32[3,1024]{1,0:T(4,128)S(1)} %get-tuple-element.77, ...), kind=kLoop, calls=%fused_computation.13 | loop fusion | flops 17694720 | bytes 2483072 | tf_op jit(solution)/shard_map/add | solution.py:86
  33.2 1.0 copy-done
  34.3 8.4 %fusion.2 = f32[2,16,64,16]{1,3,0,2:T(8,128)} fusion(f32[64,16,128,1]{2,1,3,0:T(8,128)S(1)} %bitcast.180, f32[2,16,64,16]{1,3,0,2:T(8,128)S(1)} %copy.99, pred[]{:T(512)S(6)} %lt.15, f32[1,64,16,128]{3,2,1,0:T(8,128)S(1)} %bitcast.182, f32[1,64,16,128]{3,2,1,0:T(8,128)S(1)} %bitcast.183, f32[128]{0:T(128)S(1)} %compare_convert_fusion.1), kind=kOutput, calls=%fused_computation.17 | convolution fusion | flops 50921472 | bytes 1835521 | tf_op jit(solution)/shard_map/rgns,gis->rngi/dot_general | solution.py:71
  42.7 2.1 %copy.101 = f32[2,16,64,16]{3,2,1,0:T(8,128)S(1)} copy(f32[2,16,64,16]{1,3,0,2:T(8,128)} %fusion.2) | data formatting | bytes 262144 | tf_op jit(solution)/shard_map/add | solution.py:121
  44.8 0.6 reshape.224
  45.4 3.6 %collective-permute-start.1 = (f32[2,16,1024]{2,1,0:T(8,128)S(1)}, f32[2,16,1024]{2,1,0:T(8,128)S(1)}, u32[]{:S(2)}, u32[]{:S(2)}) collective-permute-start(f32[2,16,1024]{2,1,0:T(8,128)S(1)} %reshape.224), channel_id=1, source_target_pairs={{0,8},{8,16},{16,24},{24,32},{32,40},{40,48},{48,56},{56,64},{64,7... | collective-permute-start | bytes 393224 | tf_op jit(solution)/shard_map/ppermute | solution.py:17
  49.6 4.8 %collective-permute-done.1 = f32[2,16,1024]{2,1,0:T(8,128)S(1)} collective-permute-done((f32[2,16,1024]{2,1,0:T(8,128)S(1)}, f32[2,16,1024]{2,1,0:T(8,128)S(1)}, u32[]{:S(2)}, u32[]{:S(2)}) %collective-permute-start.1) | collective-permute-done | bytes 131104 | tf_op jit(solution)/shard_map/ppermute | solution.py:17
  54.4 1.9 %collective-permute-start.2 = (f32[2,16,1024]{2,1,0:T(8,128)S(1)}, f32[2,16,1024]{2,1,0:T(8,128)S(1)}, u32[]{:S(2)}, u32[]{:S(2)}) collective-permute-start(f32[2,16,1024]{2,1,0:T(8,128)S(1)} %collective-permute-done.1), channel_id=1, source_target_pairs={{0,8},{8,16},{16,24},{24,32},{32,40},{40,48},{48,56},{56,64},{64,7... | collective-permute-start | bytes 393224 | tf_op jit(solution)/shard_map/ppermute | solution.py:17
  57.8 5.5 %collective-permute-done.2 = f32[2,16,1024]{2,1,0:T(8,128)S(1)} collective-permute-done((f32[2,16,1024]{2,1,0:T(8,128)S(1)}, f32[2,16,1024]{2,1,0:T(8,128)S(1)}, u32[]{:S(2)}, u32[]{:S(2)}) %collective-permute-start.2) | collective-permute-done | bytes 131104 | tf_op jit(solution)/shard_map/ppermute | solution.py:17
  63.4 1.9 %collective-permute-start.3 = (f32[2,16,1024]{2,1,0:T(8,128)S(1)}, f32[2,16,1024]{2,1,0:T(8,128)S(1)}, u32[]{:S(2)}, u32[]{:S(2)}) collective-permute-start(f32[2,16,1024]{2,1,0:T(8,128)S(1)} %maximum_add_fusion), channel_id=1, source_target_pairs={{0,16},{8,24},{16,32},{24,40},{32,48},{40,56},{48,64},{56,72},{64,... | collective-permute-start | bytes 393224 | tf_op jit(solution)/shard_map/ppermute | solution.py:17
  66.9 7.5 %collective-permute-done.3 = f32[2,16,1024]{2,1,0:T(8,128)S(1)} collective-permute-done((f32[2,16,1024]{2,1,0:T(8,128)S(1)}, f32[2,16,1024]{2,1,0:T(8,128)S(1)}, u32[]{:S(2)}, u32[]{:S(2)}) %collective-permute-start.3) | collective-permute-done | bytes 131104 | tf_op jit(solution)/shard_map/ppermute | solution.py:17
  74.4 1.9 %collective-permute-start.4 = (f32[2,16,1024]{2,1,0:T(8,128)S(1)}, f32[2,16,1024]{2,1,0:T(8,128)}, u32[]{:S(2)}, u32[]{:S(2)}) collective-permute-start(f32[2,16,1024]{2,1,0:T(8,128)S(1)} %maximum_add_fusion.1), channel_id=1, source_target_pairs={{0,32},{8,40},{16,48},{24,56},{32,64},{40,72},{48,80},{56,88},{64,... | collective-permute-start | bytes 393224 | tf_op jit(solution)/shard_map/ppermute | solution.py:17
  79.5 0.9 slice.323
  80.4 2.9 %collective-permute-done.4 = f32[2,16,1024]{2,1,0:T(8,128)} collective-permute-done((f32[2,16,1024]{2,1,0:T(8,128)S(1)}, f32[2,16,1024]{2,1,0:T(8,128)}, u32[]{:S(2)}, u32[]{:S(2)}) %collective-permute-start.4) | collective-permute-done | bytes 131104 | tf_op jit(solution)/shard_map/ppermute | solution.py:17
  83.3 0.9 multiply_subtract_fusion.3
  84.2 0.7 maximum_add_fusion.2
  84.9 4.3 %collective-permute-start.5 = (f32[2,16,1024]{2,1,0:T(8,128)}, f32[2,16,1024]{2,1,0:T(8,128)}, u32[]{:S(2)}, u32[]{:S(2)}) collective-permute-start(f32[2,16,1024]{2,1,0:T(8,128)} %maximum_add_fusion.2), channel_id=1, source_target_pairs={{0,64},{8,72},{16,80},{24,88},{32,96},{40,104},{48,112},{56,120},{... | collective-permute-start | bytes 393224 | tf_op jit(solution)/shard_map/ppermute | solution.py:17
  89.9 0.9 slice.331
  91.0 2.4 %collective-permute-done.5 = f32[2,16,1024]{2,1,0:T(8,128)} collective-permute-done((f32[2,16,1024]{2,1,0:T(8,128)}, f32[2,16,1024]{2,1,0:T(8,128)}, u32[]{:S(2)}, u32[]{:S(2)}) %collective-permute-start.5) | collective-permute-done | bytes 131104 | tf_op jit(solution)/shard_map/ppermute | solution.py:17
  93.4 0.9 multiply_subtract_fusion.2
  94.4 11.2 %collective-permute-start.6 = (f32[2,16,1024]{2,1,0:T(8,128)S(1)}, f32[2,16,1024]{2,1,0:T(8,128)S(1)}, u32[]{:S(2)}, u32[]{:S(2)}) collective-permute-start(f32[2,16,1024]{2,1,0:T(8,128)S(1)} %maximum_add_fusion.3), channel_id=1, source_target_pairs={{0,128},{8,136},{16,144},{24,152},{32,160},{40,168},{48,176},{56,1... | collective-permute-start | bytes 393224 | tf_op jit(solution)/shard_map/ppermute | solution.py:17
  105.7 0.7 tile.4
  106.3 4.7 %copy.114 = f32[8,8,128,256]{3,1,2,0:T(8,128)S(1)} copy(f32[8,8,128,256]{3,2,1,0:T(8,128)S(1)} %bitcast.178) | data formatting | bytes 16777216
  111.1 3.8 %slice.372 = f32[64,32640]{1,0:T(8,128)} slice(f32[64,32768]{1,0:T(8,128)S(1)} %bitcast.179), slice={[0:64], [0:32640]} | slice | bytes 16711680 | tf_op jit(solution)/shard_map/slice | solution.py:33
  114.8 15.9 %reshape.222 = f32[64,128,255]{2,1,0:T(8,128)} reshape(f32[64,32640]{1,0:T(8,128)} %slice.372) | data formatting | bytes 16711680 | tf_op jit(solution)/shard_map/reshape | solution.py:34
  130.8 4.5 %collective-permute-start.7 = (f32[2,16,1024]{2,1,0:T(8,128)S(1)}, f32[2,16,1024]{2,1,0:T(8,128)S(1)}, u32[]{:S(2)}, u32[]{:S(2)}) collective-permute-start(f32[2,16,1024]{2,1,0:T(8,128)S(1)} %maximum_add_fusion.4), channel_id=1, source_target_pairs={{0,256},{8,264},{16,272},{24,280},{32,288},{40,296},{48,304},{56,3... | collective-permute-start | bytes 393224 | tf_op jit(solution)/shard_map/ppermute | solution.py:17
  135.5 2.9 %collective-permute-done.7 = f32[2,16,1024]{2,1,0:T(8,128)S(1)} collective-permute-done((f32[2,16,1024]{2,1,0:T(8,128)S(1)}, f32[2,16,1024]{2,1,0:T(8,128)S(1)}, u32[]{:S(2)}, u32[]{:S(2)}) %collective-permute-start.7) | collective-permute-done | bytes 131104 | tf_op jit(solution)/shard_map/ppermute | solution.py:17
  138.4 0.4 reshape.225
  138.8 3.4 %fusion.4 = f32[64,16,128]{2,1,0:T(8,128)S(1)} fusion(f32[1,64,16,128]{3,2,0,1:T(8,128)} %get-tuple-element.21, f32[1,64,16,128]{3,2,0,1:T(8,128)} %get-tuple-element.20, f32[2,16,64,16]{3,2,1,0:T(8,128)S(1)} %reshape.225, pred[128]{0:T(512)(128)(4,1)S(1)} %get-tuple-element.66), kind=kOutput, calls=%fused_computation.20 | convolution fusion | flops 50724864 | bytes 1704064 | tf_op jit(solution)/shard_map/rgnt,rngi->git/dot_general | solution.py:76
  142.2 8.3 %fusion.3 = f32[64,16,128]{2,1,0:T(8,128)S(1)} fusion(f32[64,16,128]{2,1,0:T(8,128)S(1)} %fusion.4, f32[64,16,128]{2,1,0:T(8,128)S(1)} %bitcast.181, f32[64,128,255]{2,1,0:T(8,128)} %reshape.222, f32[128,128]{1,0:T(8,128)S(1)} %compare_convert_fusion), kind=kOutput, calls=%fused_computation.18 | convolution fusion | flops 202506240 | bytes 5832704 | tf_op jit(solution)/shard_map/gts,gis->git/dot_general | solution.py:67
  150.8 31.8 %psum.7 = f32[128]{0:T(128)S(1)} all-reduce(f32[128]{0:T(128)S(1)} %get-tuple-element.11), channel_id=1, replica_groups=mesh['ctx'=64,'tp'=8] {'tp'}, use_global_device_ids=true, to_apply=%region_10.11 | all-reduce | flops 128 | bytes 1024 | tf_op jit(solution)/shard_map/psum | solution.py:152
  182.8 0.9 copy.104
  (99 shorter events, 7.8 us)
Async XLA Ops:
  0.8 20.1 %collective-permute-start = (bf16[6,3,1024]{2,0,1:T(8,128)(2,1)S(1)}, bf16[6,3,1024]{2,0,1:T(8,128)(2,1)S(1)}, u32[]{:S(2)}, u32[]{:S(2)}) collective-permute-start(bf16[6,3,1024]{2,0,1:T(8,128)(2,1)S(1)} %slice.277), channel_id=1, source_target_pairs={{0,8},{8,16},{16,24},{24,32},{32,40},{40,48},{48,56},{56,64},{64,7... | collective-permute-start | bytes 110600 | tf_op jit(solution)/shard_map/ppermute | solution.py:17
  2.8 9.3 %copy-start.8 = (s32[128]{0:T(128)}, s32[128]{0:T(128)S(1)}, u32[]{:S(2)}) copy-start(s32[128]{0:T(128)S(1)} %iota_add_fusion.1) | copy-start | bytes 1540
  9.1 0.7 copy-start.10
  9.1 2.9 %copy-start.5 = (f32[7,3,1024]{2,0,1:T(8,128)S(1)}, f32[7,3,1024]{2,0,1:T(8,128)}, u32[]{:S(2)}) copy-start(f32[7,3,1024]{2,0,1:T(8,128)} %param.9) | copy-start | bytes 258052
  12.8 2.7 %copy-start.4 = (bf16[128,3,1024]{2,0,1:T(8,128)(2,1)S(1)}, bf16[128,3,1024]{2,0,1:T(8,128)(2,1)}, u32[]{:S(2)}) copy-start(bf16[128,3,1024]{2,0,1:T(8,128)(2,1)} %param.8) | copy-start | bytes 2359300
  14.8 4.1 %copy-start.3 = (f32[64,16,128]{2,1,0:T(8,128)S(1)}, f32[64,16,128]{2,1,0:T(8,128)}, u32[]{:S(2)}) copy-start(f32[64,16,128]{2,1,0:T(8,128)} %get-tuple-element.23) | copy-start | bytes 1572868
  16.7 3.2 %copy-start.2 = (f32[64,16,128]{2,1,0:T(8,128)S(1)}, f32[64,16,128]{2,1,0:T(8,128)}, u32[]{:S(2)}) copy-start(f32[64,16,128]{2,1,0:T(8,128)} %get-tuple-element.22) | copy-start | bytes 1572868
  33.1 1.0 copy-start
  33.1 1.2 copy-start.1
  45.4 9.0 %collective-permute-start.1 = (f32[2,16,1024]{2,1,0:T(8,128)S(1)}, f32[2,16,1024]{2,1,0:T(8,128)S(1)}, u32[]{:S(2)}, u32[]{:S(2)}) collective-permute-start(f32[2,16,1024]{2,1,0:T(8,128)S(1)} %reshape.224), channel_id=1, source_target_pairs={{0,8},{8,16},{16,24},{24,32},{32,40},{40,48},{48,56},{56,64},{64,7... | collective-permute-start | bytes 393224 | tf_op jit(solution)/shard_map/ppermute | solution.py:17
  54.4 9.0 %collective-permute-start.2 = (f32[2,16,1024]{2,1,0:T(8,128)S(1)}, f32[2,16,1024]{2,1,0:T(8,128)S(1)}, u32[]{:S(2)}, u32[]{:S(2)}) collective-permute-start(f32[2,16,1024]{2,1,0:T(8,128)S(1)} %collective-permute-done.1), channel_id=1, source_target_pairs={{0,8},{8,16},{16,24},{24,32},{32,40},{40,48},{48,56},{56,64},{64,7... | collective-permute-start | bytes 393224 | tf_op jit(solution)/shard_map/ppermute | solution.py:17
  63.4 11.0 %collective-permute-start.3 = (f32[2,16,1024]{2,1,0:T(8,128)S(1)}, f32[2,16,1024]{2,1,0:T(8,128)S(1)}, u32[]{:S(2)}, u32[]{:S(2)}) collective-permute-start(f32[2,16,1024]{2,1,0:T(8,128)S(1)} %maximum_add_fusion), channel_id=1, source_target_pairs={{0,16},{8,24},{16,32},{24,40},{32,48},{40,56},{48,64},{56,72},{64,... | collective-permute-start | bytes 393224 | tf_op jit(solution)/shard_map/ppermute | solution.py:17
  74.4 8.9 %collective-permute-start.4 = (f32[2,16,1024]{2,1,0:T(8,128)S(1)}, f32[2,16,1024]{2,1,0:T(8,128)}, u32[]{:S(2)}, u32[]{:S(2)}) collective-permute-start(f32[2,16,1024]{2,1,0:T(8,128)S(1)} %maximum_add_fusion.1), channel_id=1, source_target_pairs={{0,32},{8,40},{16,48},{24,56},{32,64},{40,72},{48,80},{56,88},{64,... | collective-permute-start | bytes 393224 | tf_op jit(solution)/shard_map/ppermute | solution.py:17
  84.9 8.5 %collective-permute-start.5 = (f32[2,16,1024]{2,1,0:T(8,128)}, f32[2,16,1024]{2,1,0:T(8,128)}, u32[]{:S(2)}, u32[]{:S(2)}) collective-permute-start(f32[2,16,1024]{2,1,0:T(8,128)} %maximum_add_fusion.2), channel_id=1, source_target_pairs={{0,64},{8,72},{16,80},{24,88},{32,96},{40,104},{48,112},{56,120},{... | collective-permute-start | bytes 393224 | tf_op jit(solution)/shard_map/ppermute | solution.py:17
  94.4 36.4 %collective-permute-start.6 = (f32[2,16,1024]{2,1,0:T(8,128)S(1)}, f32[2,16,1024]{2,1,0:T(8,128)S(1)}, u32[]{:S(2)}, u32[]{:S(2)}) collective-permute-start(f32[2,16,1024]{2,1,0:T(8,128)S(1)} %maximum_add_fusion.3), channel_id=1, source_target_pairs={{0,128},{8,136},{16,144},{24,152},{32,160},{40,168},{48,176},{56,1... | collective-permute-start | bytes 393224 | tf_op jit(solution)/shard_map/ppermute | solution.py:17
  114.8 20.6 %copy-start.9 = (s32[128]{0:T(128)S(1)}, s32[128]{0:T(128)}, u32[]{:S(2)}) copy-start(s32[128]{0:T(128)} %copy-done.8) | copy-start | bytes 1540
  130.8 7.5 %collective-permute-start.7 = (f32[2,16,1024]{2,1,0:T(8,128)S(1)}, f32[2,16,1024]{2,1,0:T(8,128)S(1)}, u32[]{:S(2)}, u32[]{:S(2)}) collective-permute-start(f32[2,16,1024]{2,1,0:T(8,128)S(1)} %maximum_add_fusion.4), channel_id=1, source_target_pairs={{0,256},{8,264},{16,272},{24,280},{32,288},{40,296},{48,304},{56,3... | collective-permute-start | bytes 393224 | tf_op jit(solution)/shard_map/ppermute | solution.py:17
  142.2 8.3 %copy-start.6 = (f32[1024]{0:T(1024)S(1)}, f32[1024]{0:T(1024)}, u32[]{:S(2)}) copy-start(f32[1024]{0:T(1024)} %param.13) | copy-start | bytes 12292
  150.5 32.0 %copy-start.7 = (f32[1024]{0:T(1024)S(1)}, f32[1024]{0:T(1024)}, u32[]{:S(2)}) copy-start(f32[1024]{0:T(1024)} %param.14) | copy-start | bytes 12292
where the time goes:
time: 185 us; the launch traced here: 184 us
  local copies, waits for them, and re-layouts  47.1 us (25%)
  blocking collectives  31.8 us (17%)
  starting transfers between devices  31.3 us (17%)
  waiting for transfers between devices  25.9 us (14%)
  other arithmetic  22.6 us (12%)
  matrix products  20.1 us (11%)
  between operations  4.92 us (3%)
    psum x1, blocking collectives, on_device(): squares = lax.psum(jnp.sum(gated_rows * gated_rows, axis=1), 'tp')  31.8 us
    ppermute x8, starting transfers between devices, passed_along(): return lax.ppermute(block, axis, route)  31.3 us
    ppermute x8, waiting for transfers between devices, passed_along(): return lax.ppermute(block, axis, route)  25.9 us
    reshape x1, local copies, waits for them, and re-layouts, toeplitz(): return tiled.reshape(group_count, block, 2 * block - 1)[:, :, :block]  15.9 us
    add x1, other arithmetic, short_filter(): result = result + jnp.where(keep_tap, taps_part[offset][None] * window, 0.0)  10.9 us
    dot_general x1, matrix products, block_terms(): jnp.einsum('rgns,gis->rngi', leaving * tail_mask, columns, precision=HIGH...  8.39 us
    dot_general x1, matrix products, block_terms(): jnp.einsum('gts,gis->git', matrix_table * same_genome[None], columns, pre...  8.31 us
    unnamed x29, local copies, waits for them, and re-layouts  7.89 us
  transfers between devices with their start and end apart: 8, of which 6 were waited for; matrix products, arithmetic and copies ran while one was open for 26% of the time, Pallas kernels for 0%

commit v1 on v0

--- a/solution.py
+++ b/solution.py
@@ -5,6 +5,7 @@
 
 D = 8192
 SPAN = 128
+GENOME_MAX = 4096
 
 
 HIGHEST = lax.Precision.HIGHEST
@@ -122,26 +123,46 @@
     insides = [inside]
     freshes.append(fresh_state)
     keepers.append(keep_state)
-    device_count = lax.axis_size("ctx")
     starting = jnp.cumsum(lengths) - lengths
+    reach_rows = GENOME_MAX - 1
+    reach = -(-reach_rows // tok_rows)
 
     def unbroken(first_row, last_row):
         hit = (starting >= first_row) & (starting <= last_row)
-        return jnp.logical_not(jnp.any(hit))
+        return jnp.logical_not(jnp.any(hit)).astype(jnp.float32)
 
     def widen(factor):
         return jnp.repeat(factor, group_width, axis=2)
 
-    running = passed_along(summary.reshape(2, mode_count, channels), "ctx", 1)
-    power = stepping
-    distance = 1
-    while distance < device_count:
-        earlier = passed_along(running, "ctx", distance)
-        alive = unbroken(anchor - distance * tok_rows, anchor - 1)
-        factor = widen(power) * alive.astype(jnp.float32)
-        running = running + complex_times(factor, earlier)
-        power = complex_times(power, power)
-        distance = distance * 2
+    powers = {1: stepping}
+
+    def power_of(count):
+        if count not in powers:
+            half = power_of(count // 2)
+            whole = complex_times(half, half)
+            if count % 2:
+                whole = complex_times(whole, stepping)
+            powers[count] = whole
+        return powers[count]
+
+    fresh = summary.reshape(2, mode_count, channels)
+    running = passed_along(fresh, "ctx", 1)
+    for distance in range(2, min(4, reach) + 1):
+        earlier = passed_along(fresh, "ctx", distance)
+        alive = unbroken(anchor - (distance - 1) * tok_rows, anchor - 1)
+        running = running + complex_times(widen(power_of(distance - 1)) * alive, earlier)
+    covered = min(4, reach)
+    while covered < reach:
+        stride = covered
+        width = min(4, -(-reach // stride))
+        total = running
+        for hop in range(1, width):
+            distance = hop * stride
+            earlier = passed_along(running, "ctx", distance)
+            alive = unbroken(anchor - distance * tok_rows, anchor - 1)
+            total = total + complex_times(widen(power_of(distance)) * alive, earlier)
+        running = total
+        covered = stride * width
     incoming = running.reshape(2, mode_count, group_count, group_width)
     span_index = 0
     entered = (span_begin[span_index] < span_pos[span_index, 0])[None, None, :]

time: 185 us -> 194 us (1.049)
  the two profiles are of different devices: /device:TPU:64 before, /device:TPU:128 now
where the time goes in v1:
time: 194 us; the launch traced here: 193 us
  local copies, waits for them, and re-layouts  57.6 us (30%)
  starting transfers between devices  39.2 us (20%)
  blocking collectives  30.1 us (16%)
  other arithmetic  22.7 us (12%)
  matrix products  20.1 us (10%)
  waiting for transfers between devices  16.9 us (9%)
  between operations  6.08 us (3%)
    ppermute x9, starting transfers between devices, passed_along(): return lax.ppermute(block, axis, route)  39.2 us
    psum x1, blocking collectives, on_device(): squares = lax.psum(jnp.sum(gated_rows * gated_rows, axis=1), 'tp')  30.1 us
    ppermute x9, waiting for transfers between devices, passed_along(): return lax.ppermute(block, axis, route)  16.9 us
    reshape x1, local copies, waits for them, and re-layouts, toeplitz(): return tiled.reshape(group_count, block, 2 * block - 1)[:, :, :block]  16 us
    add x1, other arithmetic, short_filter(): result = result + jnp.where(keep_tap, taps_part[offset][None] * window, 0.0)  10.7 us
    unnamed x95, local copies, waits for them, and re-layouts  9.23 us
    dot_general x1, matrix products, block_terms(): jnp.einsum('rgns,gis->rngi', leaving * tail_mask, columns, precision=HIGH...  8.41 us
    dot_general x1, matrix products, block_terms(): jnp.einsum('gts,gis->git', matrix_table * same_genome[None], columns, pre...  8.31 us
  transfers between devices with their start and end apart: 9, of which 4 were waited for; matrix products, arithmetic and copies ran while one was open for 31% of the time, Pallas kernels for 0%

profile of v1, /device:TPU:128, one launch (start us, length us, event | category | flops | bytes accessed | tf_op | source)
XLA Modules:
  0.0 192.6 jit_solution(13566403475053717121)
XLA Ops:
  0.0 1.4 slice.305
  1.4 1.9 collective-permute-start
  3.4 0.7 slice_bitcast_fusion.16
  4.3 0.8 copy.99
  5.1 0.7 neg.7
  5.9 3.9 %fusion.5 = (f32[64,16,129]{2,1,0:T(8,128)S(1)}, f32[64,16,129]{2,1,0:T(8,128)S(1)}) fusion(f32[64,16]{1,0:T(8,128)S(1)} %copy.99, f32[129]{0:T(256)S(1)} %iota_convert_fusion, f32[64,16]{1,0:T(8,128)S(1)} %copy.98), kind=kLoop, calls=%fused_computation.21 | loop fusion | flops 528384 | bytes 1065476 | tf_op jit(solution)/shard_map/mul | solution.py:41
  10.6 0.8 and_reduce_fusion
  20.5 1.9 subtract_reduce_fusion
  23.7 1.2 compare_convert_fusion.1
  24.9 1.2 copy.94
  28.0 0.9 copy.103
  30.2 1.0 rev.11
  31.2 1.0 rev.10
  32.4 0.9 slice.339
  33.5 0.9 slice.335
  34.6 0.9 slice.347
  35.7 0.9 slice.343
  36.8 0.9 slice.355
  37.9 0.9 slice.351
  39.5 0.9 slice.367
  40.4 2.0 %copy.95 = bf16[6,3,1024]{0,2,1:T(8,128)(2,1)} copy(bf16[6,3,1024]{2,0,1:T(8,128)(2,1)} %collective-permute-done) | data formatting | bytes 73728 | tf_op jit(solution)/shard_map/ppermute | solution.py:18
  42.5 10.7 %select_add_fusion = f32[128,3,1024]{0,2,1:T(8,128)S(1)} fusion(bf16[128,3,1024]{0,2,1:T(8,128)(2,1)} %copy.94, bf16[6,3,1024]{0,2,1:T(8,128)(2,1)} %copy.95, f32[3,1024]{1,0:T(4,128)S(1)} %get-tuple-element.81, f32[3,1024]{1,0:T(4,128)S(1)} %get-tuple-element.82, f32[3,1024]{1,0:T(4,128)S(1)} %get-tuple-element.83, f32[3,1024]{1,0:T(4,128)S(1)} %copy-done.14, ...), kind=kLoop, calls=%fused_computation.13 | loop fusion | flops 17694720 | bytes 2483072 | tf_op jit(solution)/shard_map/add | solution.py:87
  53.4 0.9 copy-done
  54.5 8.4 %fusion.2 = f32[2,16,64,16]{1,3,0,2:T(8,128)} fusion(f32[64,16,128,1]{2,1,3,0:T(8,128)S(1)} %bitcast.270, f32[2,16,64,16]{1,3,0,2:T(8,128)S(1)} %copy.103, pred[]{:T(512)S(6)} %lt.15, f32[1,64,16,128]{3,2,1,0:T(8,128)S(1)} %bitcast.272, f32[1,64,16,128]{3,2,1,0:T(8,128)S(1)} %bitcast.273, f32[128]{0:T(128)S(1)} %copy-done.40), kind=kOutput, calls=%fused_computation.17 | convolution fusion | flops 50921472 | bytes 1835521 | tf_op jit(solution)/shard_map/rgns,gis->rngi/dot_general | solution.py:72
  62.9 2.1 %copy.105 = f32[2,16,64,16]{3,2,1,0:T(8,128)S(1)} copy(f32[2,16,64,16]{1,3,0,2:T(8,128)} %fusion.2) | data formatting | bytes 262144 | tf_op jit(solution)/shard_map/add | solution.py:122
  65.0 1.3 reshape.231
  66.3 3.6 %collective-permute-start.2 = (f32[2,16,1024]{2,1,0:T(8,128)}, f32[2,16,1024]{2,1,0:T(8,128)}, u32[]{:S(2)}, u32[]{:S(2)}) collective-permute-start(f32[2,16,1024]{2,1,0:T(8,128)} %reshape.231), channel_id=1, source_target_pairs={{0,16},{8,24},{16,32},{24,40},{32,48},{40,56},{48,64},{56,72},{64,... | collective-permute-start | bytes 393224 | tf_op jit(solution)/shard_map/ppermute | solution.py:18
  71.0 0.7 rev.9
  71.8 3.3 %collective-permute-start.1 = (f32[2,16,1024]{2,1,0:T(8,128)}, f32[2,16,1024]{2,1,0:T(8,128)S(1)}, u32[]{:S(2)}, u32[]{:S(2)}) collective-permute-start(f32[2,16,1024]{2,1,0:T(8,128)} %reshape.231), channel_id=1, source_target_pairs={{0,8},{8,16},{16,24},{24,32},{32,40},{40,48},{48,56},{56,64},{64,7... | collective-permute-start | bytes 393224 | tf_op jit(solution)/shard_map/ppermute | solution.py:18
  75.1 3.4 %collective-permute-start.3 = (f32[2,16,1024]{2,1,0:T(8,128)}, f32[2,16,1024]{2,1,0:T(8,128)S(1)}, u32[]{:S(2)}, u32[]{:S(2)}) collective-permute-start(f32[2,16,1024]{2,1,0:T(8,128)} %reshape.231), channel_id=1, source_target_pairs={{0,24},{8,32},{16,40},{24,48},{32,56},{40,64},{48,72},{56,80},{64,... | collective-permute-start | bytes 393224 | tf_op jit(solution)/shard_map/ppermute | solution.py:18
  78.4 5.0 %collective-permute-start.4 = (f32[2,16,1024]{2,1,0:T(8,128)}, f32[2,16,1024]{2,1,0:T(8,128)S(1)}, u32[]{:S(2)}, u32[]{:S(2)}) collective-permute-start(f32[2,16,1024]{2,1,0:T(8,128)} %reshape.231), channel_id=1, source_target_pairs={{0,32},{8,40},{16,48},{24,56},{32,64},{40,72},{48,80},{56,88},{64,... | collective-permute-start | bytes 393224 | tf_op jit(solution)/shard_map/ppermute | solution.py:18
  83.4 0.9 multiply_subtract_fusion.6
  84.3 2.1 %collective-permute-done.3 = f32[2,16,1024]{2,1,0:T(8,128)S(1)} collective-permute-done((f32[2,16,1024]{2,1,0:T(8,128)}, f32[2,16,1024]{2,1,0:T(8,128)S(1)}, u32[]{:S(2)}, u32[]{:S(2)}) %collective-permute-start.3) | collective-permute-done | bytes 131104 | tf_op jit(solution)/shard_map/ppermute | solution.py:18
  86.4 4.9 %collective-permute-done.4 = f32[2,16,1024]{2,1,0:T(8,128)S(1)} collective-permute-done((f32[2,16,1024]{2,1,0:T(8,128)}, f32[2,16,1024]{2,1,0:T(8,128)S(1)}, u32[]{:S(2)}, u32[]{:S(2)}) %collective-permute-start.4) | collective-permute-done | bytes 131104 | tf_op jit(solution)/shard_map/ppermute | solution.py:18
  91.4 2.1 %collective-permute-start.5 = (f32[2,16,1024]{2,1,0:T(8,128)S(1)}, f32[2,16,1024]{2,1,0:T(8,128)S(1)}, u32[]{:S(2)}, u32[]{:S(2)}) collective-permute-start(f32[2,16,1024]{2,1,0:T(8,128)S(1)} %fusion.19), channel_id=1, source_target_pairs={{0,32},{8,40},{16,48},{24,56},{32,64},{40,72},{48,80},{56,88},{64,... | collective-permute-start | bytes 393224 | tf_op jit(solution)/shard_map/ppermute | solution.py:18
  93.6 0.7 tile.4
  94.3 4.7 %copy.118 = f32[8,8,128,256]{3,1,2,0:T(8,128)S(1)} copy(f32[8,8,128,256]{3,2,1,0:T(8,128)S(1)} %bitcast.268) | data formatting | bytes 16777216
  99.0 3.8 %slice.408 = f32[64,32640]{1,0:T(8,128)} slice(f32[64,32768]{1,0:T(8,128)S(1)} %bitcast.269), slice={[0:64], [0:32640]} | slice | bytes 16711680 | tf_op jit(solution)/shard_map/slice | solution.py:34
  102.8 16.0 %reshape.229 = f32[64,128,255]{2,1,0:T(8,128)} reshape(f32[64,32640]{1,0:T(8,128)} %slice.408) | data formatting | bytes 16711680 | tf_op jit(solution)/shard_map/reshape | solution.py:35
  118.8 6.4 %collective-permute-start.6 = (f32[2,16,1024]{2,1,0:T(8,128)S(1)}, f32[2,16,1024]{2,1,0:T(8,128)S(1)}, u32[]{:S(2)}, u32[]{:S(2)}) collective-permute-start(f32[2,16,1024]{2,1,0:T(8,128)S(1)} %fusion.19), channel_id=1, source_target_pairs={{0,64},{8,72},{16,80},{24,88},{32,96},{40,104},{48,112},{56,120},{... | collective-permute-start | bytes 393224 | tf_op jit(solution)/shard_map/ppermute | solution.py:18
  125.2 7.0 %collective-permute-start.7 = (f32[2,16,1024]{2,1,0:T(8,128)S(1)}, f32[2,16,1024]{2,1,0:T(8,128)S(1)}, u32[]{:S(2)}, u32[]{:S(2)}) collective-permute-start(f32[2,16,1024]{2,1,0:T(8,128)S(1)} %fusion.19), channel_id=1, source_target_pairs={{0,96},{8,104},{16,112},{24,120},{32,128},{40,136},{48,144},{56,15... | collective-permute-start | bytes 393224 | tf_op jit(solution)/shard_map/ppermute | solution.py:18
  132.3 5.6 %collective-permute-done.7 = f32[2,16,1024]{2,1,0:T(8,128)S(1)} collective-permute-done((f32[2,16,1024]{2,1,0:T(8,128)S(1)}, f32[2,16,1024]{2,1,0:T(8,128)S(1)}, u32[]{:S(2)}, u32[]{:S(2)}) %collective-permute-start.7) | collective-permute-done | bytes 131104 | tf_op jit(solution)/shard_map/ppermute | solution.py:18
  138.0 6.5 %collective-permute-start.8 = (f32[2,16,1024]{2,1,0:T(8,128)S(1)}, f32[2,16,1024]{2,1,0:T(8,128)S(1)}, u32[]{:S(2)}, u32[]{:S(2)}) collective-permute-start(f32[2,16,1024]{2,1,0:T(8,128)S(1)} %fusion.21), channel_id=1, source_target_pairs={{0,128},{8,136},{16,144},{24,152},{32,160},{40,168},{48,176},{56,1... | collective-permute-start | bytes 393224 | tf_op jit(solution)/shard_map/ppermute | solution.py:18
  144.7 4.3 %collective-permute-done.8 = f32[2,16,1024]{2,1,0:T(8,128)S(1)} collective-permute-done((f32[2,16,1024]{2,1,0:T(8,128)S(1)}, f32[2,16,1024]{2,1,0:T(8,128)S(1)}, u32[]{:S(2)}, u32[]{:S(2)}) %collective-permute-start.8) | collective-permute-done | bytes 131104 | tf_op jit(solution)/shard_map/ppermute | solution.py:18
  149.5 3.4 %fusion.4 = f32[64,16,128]{2,1,0:T(8,128)S(1)} fusion(f32[1,64,16,128]{3,2,0,1:T(8,128)} %get-tuple-element.20, f32[1,64,16,128]{3,2,0,1:T(8,128)} %get-tuple-element.19, f32[2,16,64,16]{3,2,1,0:T(8,128)S(1)} %reshape.232, pred[128]{0:T(512)(128)(4,1)S(1)} %copy-done.37), kind=kOutput, calls=%fused_computation.20 | convolution fusion | flops 50724864 | bytes 1704064 | tf_op jit(solution)/shard_map/rgnt,rngi->git/dot_general | solution.py:77
  152.9 8.3 %fusion.3 = f32[64,16,128]{2,1,0:T(8,128)S(1)} fusion(f32[64,16,128]{2,1,0:T(8,128)S(1)} %fusion.4, f32[64,16,128]{2,1,0:T(8,128)S(1)} %bitcast.271, f32[64,128,255]{2,1,0:T(8,128)} %reshape.229, f32[128,128]{1,0:T(8,128)S(1)} %compare_convert_fusion), kind=kOutput, calls=%fused_computation.18 | convolution fusion | flops 202506240 | bytes 5832704 | tf_op jit(solution)/shard_map/gts,gis->git/dot_general | solution.py:68
  161.4 30.1 %psum.7 = f32[128]{0:T(128)S(1)} all-reduce(f32[128]{0:T(128)S(1)} %get-tuple-element.12), channel_id=1, replica_groups=mesh['ctx'=64,'tp'=8] {'tp'}, use_global_device_ids=true, to_apply=%region_11.12 | all-reduce | flops 128 | bytes 1024 | tf_op jit(solution)/shard_map/psum | solution.py:173
  191.8 0.9 copy.108
  (169 shorter events, 13.8 us)
Async XLA Ops:
  1.4 39.0 %collective-permute-start = (bf16[6,3,1024]{2,0,1:T(8,128)(2,1)}, bf16[6,3,1024]{2,0,1:T(8,128)(2,1)}, u32[]{:S(2)}, u32[]{:S(2)}) collective-permute-start(bf16[6,3,1024]{2,0,1:T(8,128)(2,1)} %slice.305), channel_id=1, source_target_pairs={{0,8},{8,16},{16,24},{24,32},{32,40},{40,48},{48,56},{56,64},{64,7... | collective-permute-start | bytes 110600 | tf_op jit(solution)/shard_map/ppermute | solution.py:18
  3.4 10.7 %copy-start.38 = (s32[128]{0:T(128)}, s32[128]{0:T(128)S(1)}, u32[]{:S(2)}) copy-start(s32[128]{0:T(128)S(1)} %iota_add_fusion.1) | copy-start | bytes 1540
  3.4 11.4 %copy-start.42 = (s32[1,128]{1,0:T(1,128)}, s32[1,128]{1,0:T(1,128)S(1)}, u32[]{:S(2)}) copy-start(s32[1,128]{1,0:T(1,128)S(1)} %iota_add_fusion) | copy-start | bytes 1540
  9.7 4.3 %copy-start.13 = (f32[7,3,1024]{2,0,1:T(8,128)S(1)}, f32[7,3,1024]{2,0,1:T(8,128)}, u32[]{:S(2)}) copy-start(f32[7,3,1024]{2,0,1:T(8,128)} %param.9) | copy-start | bytes 258052
  14.2 14.8 %copy-start.28 = (s32[128]{0:T(128)}, s32[128]{0:T(128)S(1)}, u32[]{:S(2)}) copy-start(s32[128]{0:T(128)S(1)} %select_reduce_fusion) | copy-start | bytes 1540
  20.5 4.4 %copy-start.4 = (bf16[128,3,1024]{2,0,1:T(8,128)(2,1)S(1)}, bf16[128,3,1024]{2,0,1:T(8,128)(2,1)}, u32[]{:S(2)}) copy-start(bf16[128,3,1024]{2,0,1:T(8,128)(2,1)} %param.8) | copy-start | bytes 2359300
  27.2 2.9 %copy-start.3 = (f32[64,16,128]{2,1,0:T(8,128)S(1)}, f32[64,16,128]{2,1,0:T(8,128)}, u32[]{:S(2)}) copy-start(f32[64,16,128]{2,1,0:T(8,128)} %get-tuple-element.22) | copy-start | bytes 1572868
  27.7 3.5 %copy-start.2 = (f32[64,16,128]{2,1,0:T(8,128)S(1)}, f32[64,16,128]{2,1,0:T(8,128)}, u32[]{:S(2)}) copy-start(f32[64,16,128]{2,1,0:T(8,128)} %get-tuple-element.21) | copy-start | bytes 1572868
  28.0 4.2 %copy-start.19 = (f32[16,64]{1,0:T(8,128)S(1)}, f32[16,64]{1,0:T(8,128)}, u32[]{:S(2)}) copy-start(f32[16,64]{1,0:T(8,128)} %get-tuple-element.70) | copy-start | bytes 12292
  30.2 3.1 %copy-start.18 = (f32[16,64]{1,0:T(8,128)S(1)}, f32[16,64]{1,0:T(8,128)}, u32[]{:S(2)}) copy-start(f32[16,64]{1,0:T(8,128)} %get-tuple-element.69) | copy-start | bytes 12292
  31.2 3.2 %copy-start.24 = (f32[16,64]{1,0:T(8,128)S(1)}, f32[16,64]{1,0:T(8,128)}, u32[]{:S(2)}) copy-start(f32[16,64]{1,0:T(8,128)} %get-tuple-element.68) | copy-start | bytes 12292
  32.2 3.3 %copy-start.22 = (f32[16,64]{1,0:T(8,128)S(1)}, f32[16,64]{1,0:T(8,128)}, u32[]{:S(2)}) copy-start(f32[16,64]{1,0:T(8,128)} %get-tuple-element.67) | copy-start | bytes 12292
  33.3 3.3 %copy-start.21 = (f32[16,64]{1,0:T(8,128)S(1)}, f32[16,64]{1,0:T(8,128)}, u32[]{:S(2)}) copy-start(f32[16,64]{1,0:T(8,128)} %get-tuple-element.66) | copy-start | bytes 12292
  34.4 3.3 %copy-start.20 = (f32[16,64]{1,0:T(8,128)S(1)}, f32[16,64]{1,0:T(8,128)}, u32[]{:S(2)}) copy-start(f32[16,64]{1,0:T(8,128)} %get-tuple-element.65) | copy-start | bytes 12292
  35.5 3.3 %copy-start.25 = (f32[16,64]{1,0:T(8,128)S(1)}, f32[16,64]{1,0:T(8,128)}, u32[]{:S(2)}) copy-start(f32[16,64]{1,0:T(8,128)} %get-tuple-element.56) | copy-start | bytes 12292
  36.6 2.7 %copy-start.23 = (f32[16,64]{1,0:T(8,128)S(1)}, f32[16,64]{1,0:T(8,128)}, u32[]{:S(2)}) copy-start(f32[16,64]{1,0:T(8,128)} %get-tuple-element.55) | copy-start | bytes 12292
  38.8 3.7 %copy-start.14 = (f32[3,1024]{1,0:T(4,128)S(1)}, f32[3,1024]{1,0:T(4,128)}, u32[]{:S(2)}) copy-start(f32[3,1024]{1,0:T(4,128)} %get-tuple-element.84) | copy-start | bytes 36868
  38.8 3.7 %copy-start.15 = (f32[3,1024]{1,0:T(4,128)S(1)}, f32[3,1024]{1,0:T(4,128)}, u32[]{:S(2)}) copy-start(f32[3,1024]{1,0:T(4,128)} %get-tuple-element.85) | copy-start | bytes 36868
  38.8 3.7 %copy-start.16 = (f32[3,1024]{1,0:T(4,128)S(1)}, f32[3,1024]{1,0:T(4,128)}, u32[]{:S(2)}) copy-start(f32[3,1024]{1,0:T(4,128)} %get-tuple-element.86) | copy-start | bytes 36868
  38.8 3.7 %copy-start.30 = (pred[128]{0:T(512)(128)(4,1)S(1)}, pred[128]{0:T(512)(128)(4,1)}, u32[]{:S(2)}) copy-start(pred[128]{0:T(512)(128)(4,1)} %get-tuple-element.74) | copy-start | bytes 388
  38.8 3.7 %copy-start.31 = (pred[128]{0:T(512)(128)(4,1)S(1)}, pred[128]{0:T(512)(128)(4,1)}, u32[]{:S(2)}) copy-start(pred[128]{0:T(512)(128)(4,1)} %get-tuple-element.75) | copy-start | bytes 388
  38.8 3.7 %copy-start.32 = (pred[128]{0:T(512)(128)(4,1)S(1)}, pred[128]{0:T(512)(128)(4,1)}, u32[]{:S(2)}) copy-start(pred[128]{0:T(512)(128)(4,1)} %get-tuple-element.76) | copy-start | bytes 388
  38.8 3.7 %copy-start.33 = (pred[128]{0:T(512)(128)(4,1)S(1)}, pred[128]{0:T(512)(128)(4,1)}, u32[]{:S(2)}) copy-start(pred[128]{0:T(512)(128)(4,1)} %get-tuple-element.77) | copy-start | bytes 388
  38.8 3.7 %copy-start.34 = (pred[128]{0:T(512)(128)(4,1)S(1)}, pred[128]{0:T(512)(128)(4,1)}, u32[]{:S(2)}) copy-start(pred[128]{0:T(512)(128)(4,1)} %get-tuple-element.78) | copy-start | bytes 388
  38.8 3.7 %copy-start.35 = (pred[128]{0:T(512)(128)(4,1)S(1)}, pred[128]{0:T(512)(128)(4,1)}, u32[]{:S(2)}) copy-start(pred[128]{0:T(512)(128)(4,1)} %get-tuple-element.79) | copy-start | bytes 388
  38.8 3.7 %copy-start.36 = (pred[128]{0:T(512)(128)(4,1)S(1)}, pred[128]{0:T(512)(128)(4,1)}, u32[]{:S(2)}) copy-start(pred[128]{0:T(512)(128)(4,1)} %get-tuple-element.80) | copy-start | bytes 388
  62.9 7.0 %copy-start.17 = (f32[2,16,64]{2,1,0:T(8,128)S(1)}, f32[2,16,64]{2,1,0:T(8,128)}, u32[]{:S(2)}) copy-start(f32[2,16,64]{2,1,0:T(8,128)} %get-tuple-element.89) | copy-start | bytes 24580
  66.3 17.1 %copy-start.6 = (f32[1,16,1024]{2,1,0:T(8,128)S(1)}, f32[1,16,1024]{2,1,0:T(8,128)}, u32[]{:S(2)}) copy-start(f32[1,16,1024]{2,1,0:T(8,128)} %slice.339) | copy-start | bytes 196612
  66.3 17.1 %copy-start.9 = (f32[1,16,1024]{2,1,0:T(8,128)S(1)}, f32[1,16,1024]{2,1,0:T(8,128)}, u32[]{:S(2)}) copy-start(f32[1,16,1024]{2,1,0:T(8,128)} %slice.335) | copy-start | bytes 196612
  66.3 20.1 %copy-start.7 = (f32[1,16,1024]{2,1,0:T(8,128)S(1)}, f32[1,16,1024]{2,1,0:T(8,128)}, u32[]{:S(2)}) copy-start(f32[1,16,1024]{2,1,0:T(8,128)} %slice.347) | copy-start | bytes 196612
  66.3 20.1 %copy-start.10 = (f32[1,16,1024]{2,1,0:T(8,128)S(1)}, f32[1,16,1024]{2,1,0:T(8,128)}, u32[]{:S(2)}) copy-start(f32[1,16,1024]{2,1,0:T(8,128)} %slice.343) | copy-start | bytes 196612
  66.3 17.1 %collective-permute-start.2 = (f32[2,16,1024]{2,1,0:T(8,128)}, f32[2,16,1024]{2,1,0:T(8,128)}, u32[]{:S(2)}, u32[]{:S(2)}) collective-permute-start(f32[2,16,1024]{2,1,0:T(8,128)} %reshape.231), channel_id=1, source_target_pairs={{0,16},{8,24},{16,32},{24,40},{32,48},{40,56},{48,64},{56,72},{64,... | collective-permute-start | bytes 393224 | tf_op jit(solution)/shard_map/ppermute | solution.py:18
  70.0 21.4 %copy-start.8 = (f32[1,16,1024]{2,1,0:T(8,128)S(1)}, f32[1,16,1024]{2,1,0:T(8,128)}, u32[]{:S(2)}) copy-start(f32[1,16,1024]{2,1,0:T(8,128)} %slice.355) | copy-start | bytes 196612
  70.0 21.4 %copy-start.11 = (f32[1,16,1024]{2,1,0:T(8,128)S(1)}, f32[1,16,1024]{2,1,0:T(8,128)}, u32[]{:S(2)}) copy-start(f32[1,16,1024]{2,1,0:T(8,128)} %slice.351) | copy-start | bytes 196612
  71.7 21.9 %copy-start.12 = (f32[64,127]{1,0:T(8,128)S(1)}, f32[64,127]{1,0:T(8,128)}, u32[]{:S(2)}) copy-start(f32[64,127]{1,0:T(8,128)} %rev.9) | copy-start | bytes 97540
  71.8 19.6 %collective-permute-start.1 = (f32[2,16,1024]{2,1,0:T(8,128)}, f32[2,16,1024]{2,1,0:T(8,128)S(1)}, u32[]{:S(2)}, u32[]{:S(2)}) collective-permute-start(f32[2,16,1024]{2,1,0:T(8,128)} %reshape.231), channel_id=1, source_target_pairs={{0,8},{8,16},{16,24},{24,32},{32,40},{40,48},{48,56},{56,64},{64,7... | collective-permute-start | bytes 393224 | tf_op jit(solution)/shard_map/ppermute | solution.py:18
  75.1 11.4 %collective-permute-start.3 = (f32[2,16,1024]{2,1,0:T(8,128)}, f32[2,16,1024]{2,1,0:T(8,128)S(1)}, u32[]{:S(2)}, u32[]{:S(2)}) collective-permute-start(f32[2,16,1024]{2,1,0:T(8,128)} %reshape.231), channel_id=1, source_target_pairs={{0,24},{8,32},{16,40},{24,48},{32,56},{40,64},{48,72},{56,80},{64,... | collective-permute-start | bytes 393224 | tf_op jit(solution)/shard_map/ppermute | solution.py:18
  78.4 12.9 %collective-permute-start.4 = (f32[2,16,1024]{2,1,0:T(8,128)}, f32[2,16,1024]{2,1,0:T(8,128)S(1)}, u32[]{:S(2)}, u32[]{:S(2)}) collective-permute-start(f32[2,16,1024]{2,1,0:T(8,128)} %reshape.231), channel_id=1, source_target_pairs={{0,32},{8,40},{16,48},{24,56},{32,64},{40,72},{48,80},{56,88},{64,... | collective-permute-start | bytes 393224 | tf_op jit(solution)/shard_map/ppermute | solution.py:18
  91.4 40.8 %collective-permute-start.5 = (f32[2,16,1024]{2,1,0:T(8,128)S(1)}, f32[2,16,1024]{2,1,0:T(8,128)S(1)}, u32[]{:S(2)}, u32[]{:S(2)}) collective-permute-start(f32[2,16,1024]{2,1,0:T(8,128)S(1)} %fusion.19), channel_id=1, source_target_pairs={{0,32},{8,40},{16,48},{24,56},{32,64},{40,72},{48,80},{56,88},{64,... | collective-permute-start | bytes 393224 | tf_op jit(solution)/shard_map/ppermute | solution.py:18
  102.8 29.5 %copy-start.5 = (f32[1,16,1024]{2,1,0:T(8,128)S(1)}, f32[1,16,1024]{2,1,0:T(8,128)}, u32[]{:S(2)}) copy-start(f32[1,16,1024]{2,1,0:T(8,128)} %slice.367) | copy-start | bytes 196612
  118.8 25.7 %copy-start.29 = (s32[128]{0:T(128)S(1)}, s32[128]{0:T(128)}, u32[]{:S(2)}) copy-start(s32[128]{0:T(128)} %copy-done.28) | copy-start | bytes 1540
  118.8 25.7 %copy-start.39 = (s32[128]{0:T(128)S(1)}, s32[128]{0:T(128)}, u32[]{:S(2)}) copy-start(s32[128]{0:T(128)} %copy-done.38) | copy-start | bytes 1540
  118.8 13.4 %collective-permute-start.6 = (f32[2,16,1024]{2,1,0:T(8,128)S(1)}, f32[2,16,1024]{2,1,0:T(8,128)S(1)}, u32[]{:S(2)}, u32[]{:S(2)}) collective-permute-start(f32[2,16,1024]{2,1,0:T(8,128)S(1)} %fusion.19), channel_id=1, source_target_pairs={{0,64},{8,72},{16,80},{24,88},{32,96},{40,104},{48,112},{56,120},{... | collective-permute-start | bytes 393224 | tf_op jit(solution)/shard_map/ppermute | solution.py:18
  125.2 12.7 %collective-permute-start.7 = (f32[2,16,1024]{2,1,0:T(8,128)S(1)}, f32[2,16,1024]{2,1,0:T(8,128)S(1)}, u32[]{:S(2)}, u32[]{:S(2)}) collective-permute-start(f32[2,16,1024]{2,1,0:T(8,128)S(1)} %fusion.19), channel_id=1, source_target_pairs={{0,96},{8,104},{16,112},{24,120},{32,128},{40,136},{48,144},{56,15... | collective-permute-start | bytes 393224 | tf_op jit(solution)/shard_map/ppermute | solution.py:18
  138.0 11.4 %copy-start.37 = (pred[128]{0:T(512)(128)(4,1)S(1)}, pred[128]{0:T(512)(128)(4,1)}, u32[]{:S(2)}) copy-start(pred[128]{0:T(512)(128)(4,1)} %get-tuple-element.73) | copy-start | bytes 388
  138.0 11.0 %collective-permute-start.8 = (f32[2,16,1024]{2,1,0:T(8,128)S(1)}, f32[2,16,1024]{2,1,0:T(8,128)S(1)}, u32[]{:S(2)}, u32[]{:S(2)}) collective-permute-start(f32[2,16,1024]{2,1,0:T(8,128)S(1)} %fusion.21), channel_id=1, source_target_pairs={{0,128},{8,136},{16,144},{24,152},{32,160},{40,168},{48,176},{56,1... | collective-permute-start | bytes 393224 | tf_op jit(solution)/shard_map/ppermute | solution.py:18
  152.9 8.3 %copy-start.26 = (f32[1024]{0:T(1024)S(1)}, f32[1024]{0:T(1024)}, u32[]{:S(2)}) copy-start(f32[1024]{0:T(1024)} %param.13) | copy-start | bytes 12292
  161.2 30.4 %copy-start.27 = (f32[1024]{0:T(1024)S(1)}, f32[1024]{0:T(1024)}, u32[]{:S(2)}) copy-start(f32[1024]{0:T(1024)} %param.14) | copy-start | bytes 12292
  (5 other events, 6.4 us)

commit v2 on v0

--- a/solution.py
+++ b/solution.py
@@ -5,6 +5,7 @@
 
 D = 8192
 SPAN = 128
+GENOME_MAX = 4096
 
 
 HIGHEST = lax.Precision.HIGHEST
@@ -26,12 +27,9 @@
 
 def toeplitz(response):
     group_count, block = response.shape
-    folded = jnp.concatenate(
-        [response[:, :1], jnp.zeros((group_count, block), response.dtype), response[:, :0:-1]],
-        axis=1,
-    )
-    tiled = jnp.tile(folded, (1, block))[:, : block * (2 * block - 1)]
-    return tiled.reshape(group_count, block, 2 * block - 1)[:, :, :block]
+    lag = jnp.arange(block, dtype=jnp.int32)
+    picks = (lag[:, None, None] == lag[None, :, None] - lag[None, None, :]).astype(jnp.float32)
+    return jnp.einsum("gk,kts->gts", response, picks, precision=HIGHEST)
 
 
 def pole_tables(rate, angle, residue, block):
@@ -123,6 +121,7 @@
     freshes.append(fresh_state)
     keepers.append(keep_state)
     device_count = lax.axis_size("ctx")
+    reach = min(device_count, -(-(GENOME_MAX - 1) // tok_rows))
     starting = jnp.cumsum(lengths) - lengths
 
     def unbroken(first_row, last_row):
@@ -135,7 +134,7 @@
     running = passed_along(summary.reshape(2, mode_count, channels), "ctx", 1)
     power = stepping
     distance = 1
-    while distance < device_count:
+    while distance < reach:
         earlier = passed_along(running, "ctx", distance)
         alive = unbroken(anchor - distance * tok_rows, anchor - 1)
         factor = widen(power) * alive.astype(jnp.float32)

time: 185 us -> 163 us (0.88)
  the two profiles are of different devices: /device:TPU:64 before, /device:TPU:128 now
where the time goes in v2:
time: 163 us; the launch traced here: 162 us
  blocking collectives  31.9 us (20%)
  starting transfers between devices  27.7 us (17%)
  matrix products  27.1 us (17%)
  waiting for transfers between devices  25.6 us (16%)
  other arithmetic  23.7 us (15%)
  local copies, waits for them, and re-layouts  21.6 us (13%)
  between operations  4.08 us (3%)
    psum x1, blocking collectives, on_device(): squares = lax.psum(jnp.sum(gated_rows * gated_rows, axis=1), 'tp')  31.9 us
    ppermute x7, starting transfers between devices, passed_along(): return lax.ppermute(block, axis, route)  27.7 us
    ppermute x7, waiting for transfers between devices, passed_along(): return lax.ppermute(block, axis, route)  25.6 us
    dot_general x1, matrix products, block_terms(): jnp.einsum('gts,gis->git', matrix_table * same_genome[None], columns, pre...  10.6 us
    add x1, other arithmetic, short_filter(): result = result + jnp.where(keep_tap, taps_part[offset][None] * window, 0.0)  10.5 us
    dot_general x1, matrix products, block_terms(): jnp.einsum('rgns,gis->rngi', leaving * tail_mask, columns, precision=HIGH...  8.39 us
    dot_general x1, matrix products, toeplitz(): return jnp.einsum('gk,kts->gts', response, picks, precision=HIGHEST)  4.71 us
    mul x1, other arithmetic, pole_tables(): power_re = magnitude * jnp.cos(angle[:, :, None] * counter)  3.86 us
  transfers between devices with their start and end apart: 7, of which 6 were waited for; matrix products, arithmetic and copies ran while one was open for 19% of the time, Pallas kernels for 0%

profile of v2, /device:TPU:128, one launch (start us, length us, event | category | flops | bytes accessed | tf_op | source)
XLA Modules:
  0.0 161.7 jit_solution(8779578035649616602)
XLA Ops:
  0.0 0.8 slice.237
  0.8 1.9 %collective-permute-start = (bf16[6,3,1024]{2,0,1:T(8,128)(2,1)S(1)}, bf16[6,3,1024]{2,0,1:T(8,128)(2,1)S(1)}, u32[]{:S(2)}, u32[]{:S(2)}) collective-permute-start(bf16[6,3,1024]{2,0,1:T(8,128)(2,1)S(1)} %slice.237), channel_id=1, source_target_pairs={{0,8},{8,16},{16,24},{24,32},{32,40},{40,48},{48,56},{56,64},{64,7... | collective-permute-start | bytes 110600 | tf_op jit(solution)/shard_map/ppermute | solution.py:18
  2.8 0.8 reduce-window.9
  3.6 1.4 and_reduce_fusion
  5.1 0.6 slice.260
  5.8 0.6 broadcast_compare_fusion.1
  6.4 0.7 neg.7
  7.1 0.7 slice_bitcast_fusion.12
  8.1 0.8 copy.93
  8.9 2.1 %fusion.35 = (f32[1,3,1024]{2,0,1:T(1,128)}, f32[1,3,1024]{2,0,1:T(1,128)S(1)}, f32[1,3,1024]{2,0,1:T(1,128)S(1)}, f32[1,3,1024]{2,0,1:T(1,128)S(1)}, f32[1,3,10...) fusion(f32[7,3,1024]{2,0,1:T(8,128)} %param.9), kind=kLoop, calls=%fused_computation.133 | loop fusion | bytes 172032 | tf_op jit(solution)/shard_map/slice | solution.py:84
  10.9 3.9 %fusion.10 = (f32[64,16,129]{2,1,0:T(8,128)S(1)}, f32[64,16,129]{2,1,0:T(8,128)S(1)}) fusion(f32[64,16]{1,0:T(8,128)S(1)} %copy.93, f32[129]{0:T(256)S(1)} %iota_convert_fusion, f32[64,16]{1,0:T(8,128)S(1)} %copy.92), kind=kLoop, calls=%fused_computation.24 | loop fusion | flops 528384 | bytes 1065476 | tf_op jit(solution)/shard_map/mul | solution.py:38
  15.5 1.6 %subtract_reduce_fusion = (f32[64,128]{1,0:T(8,128)S(1)}, f32[1,64,16,128]{3,2,0,1:T(8,128)}, f32[1,64,16,128]{3,2,0,1:T(8,128)}, f32[64,16,128]{2,1,0:T(8,128)S(1)}, f32[64,16,128]{2,1,0:T(8,128)S(1)}) fusion(f32[64,16]{1,0:T(8,128)S(1)} %copy.94, f32[64,16]{1,0:T(8,128)S(1)} %copy.91, f32[64,16,129]{2,1,0:T(8,128)S(1)} %get-tuple-element.39, ...), kind=kLoop, calls=%fused_computation.48 | loop fusion | flops 1433600 | bytes 4235264 | tf_op jit(solution)/shard_map/reduce_sum | solution.py:42
  17.1 0.6 subtract_bitcast_fusion.1
  17.8 4.7 %fusion.4 = f32[64,128,128]{2,0,1:T(8,128)} fusion(s32[128,128]{1,0:T(8,128)S(1)} %iota_subtract_fusion, f32[128,128]{1,0:T(8,128)S(1)} %compare_convert_fusion, f32[64,128]{1,0:T(8,128)S(1)} %get-tuple-element.16), kind=kOutput, calls=%fused_computation.15 | convolution fusion | flops 1613758464 | bytes 4358144 | tf_op jit(solution)/shard_map/gk,kts->gts/dot_general | solution.py:32
  22.5 0.6 compare_convert_fusion.1
  23.1 1.2 copy.88
  24.3 0.6 slice.257
  25.6 1.0 rev.6
  26.6 1.0 rev.7
  27.6 0.9 copy.98
  28.6 1.3 copy.89
  29.9 10.5 %select_add_fusion = f32[128,3,1024]{0,2,1:T(8,128)S(1)} fusion(bf16[128,3,1024]{0,2,1:T(8,128)(2,1)} %copy.88, bf16[6,3,1024]{0,2,1:T(8,128)(2,1)} %copy.89, f32[3,1024]{1,0:T(4,128)S(1)} %get-tuple-element.67, f32[3,1024]{1,0:T(4,128)S(1)} %get-tuple-element.68, f32[3,1024]{1,0:T(4,128)S(1)} %get-tuple-element.69, f32[3,1024]{1,0:T(4,128)S(1)} %get-tuple-element.70, ...), kind=kLoop, calls=%fused_computation.16 | loop fusion | flops 17694720 | bytes 2483072 | tf_op jit(solution)/shard_map/add | solution.py:84
  40.5 1.0 copy-done
  41.6 8.4 %fusion.5 = f32[2,16,64,16]{1,3,0,2:T(8,128)} fusion(f32[64,16,128,1]{2,1,3,0:T(8,128)S(1)} %bitcast.168, f32[2,16,64,16]{1,3,0,2:T(8,128)S(1)} %copy.98, pred[]{:T(512)S(6)} %lt.15, f32[1,64,16,128]{3,2,1,0:T(8,128)S(1)} %bitcast.171, f32[1,64,16,128]{3,2,1,0:T(8,128)S(1)} %bitcast.170, f32[128]{0:T(128)S(1)} %compare_convert_fusion.1), kind=kOutput, calls=%fused_computation.20 | convolution fusion | flops 50921472 | bytes 1835521 | tf_op jit(solution)/shard_map/rgns,gis->rngi/dot_general | solution.py:69
  50.0 2.1 %copy.100 = f32[2,16,64,16]{3,2,1,0:T(8,128)S(1)} copy(f32[2,16,64,16]{1,3,0,2:T(8,128)} %fusion.5) | data formatting | bytes 262144 | tf_op jit(solution)/shard_map/add | solution.py:119
  52.1 0.6 reshape.224
  52.7 3.6 %collective-permute-start.1 = (f32[2,16,1024]{2,1,0:T(8,128)S(1)}, f32[2,16,1024]{2,1,0:T(8,128)S(1)}, u32[]{:S(2)}, u32[]{:S(2)}) collective-permute-start(f32[2,16,1024]{2,1,0:T(8,128)S(1)} %reshape.224), channel_id=1, source_target_pairs={{0,8},{8,16},{16,24},{24,32},{32,40},{40,48},{48,56},{56,64},{64,7... | collective-permute-start | bytes 393224 | tf_op jit(solution)/shard_map/ppermute | solution.py:18
  56.3 0.6 multiply_bitcast_fusion
  57.5 4.2 %collective-permute-done.1 = f32[2,16,1024]{2,1,0:T(8,128)S(1)} collective-permute-done((f32[2,16,1024]{2,1,0:T(8,128)S(1)}, f32[2,16,1024]{2,1,0:T(8,128)S(1)}, u32[]{:S(2)}, u32[]{:S(2)}) %collective-permute-start.1) | collective-permute-done | bytes 131104 | tf_op jit(solution)/shard_map/ppermute | solution.py:18
  61.7 1.9 %collective-permute-start.2 = (f32[2,16,1024]{2,1,0:T(8,128)S(1)}, f32[2,16,1024]{2,1,0:T(8,128)S(1)}, u32[]{:S(2)}, u32[]{:S(2)}) collective-permute-start(f32[2,16,1024]{2,1,0:T(8,128)S(1)} %collective-permute-done.1), channel_id=1, source_target_pairs={{0,8},{8,16},{16,24},{24,32},{32,40},{40,48},{48,56},{56,64},{64,7... | collective-permute-start | bytes 393224 | tf_op jit(solution)/shard_map/ppermute | solution.py:18
  64.4 0.3 slice.263
  65.1 5.5 %collective-permute-done.2 = f32[2,16,1024]{2,1,0:T(8,128)S(1)} collective-permute-done((f32[2,16,1024]{2,1,0:T(8,128)S(1)}, f32[2,16,1024]{2,1,0:T(8,128)S(1)}, u32[]{:S(2)}, u32[]{:S(2)}) %collective-permute-start.2) | collective-permute-done | bytes 131104 | tf_op jit(solution)/shard_map/ppermute | solution.py:18
  70.7 1.9 %collective-permute-start.3 = (f32[2,16,1024]{2,1,0:T(8,128)S(1)}, f32[2,16,1024]{2,1,0:T(8,128)S(1)}, u32[]{:S(2)}, u32[]{:S(2)}) collective-permute-start(f32[2,16,1024]{2,1,0:T(8,128)S(1)} %maximum_add_fusion), channel_id=1, source_target_pairs={{0,16},{8,24},{16,32},{24,40},{32,48},{40,56},{48,64},{56,72},{64,... | collective-permute-start | bytes 393224 | tf_op jit(solution)/shard_map/ppermute | solution.py:18
  74.7 7.0 %collective-permute-done.3 = f32[2,16,1024]{2,1,0:T(8,128)S(1)} collective-permute-done((f32[2,16,1024]{2,1,0:T(8,128)S(1)}, f32[2,16,1024]{2,1,0:T(8,128)S(1)}, u32[]{:S(2)}, u32[]{:S(2)}) %collective-permute-start.3) | collective-permute-done | bytes 131104 | tf_op jit(solution)/shard_map/ppermute | solution.py:18
  81.7 2.1 %collective-permute-start.4 = (f32[2,16,1024]{2,1,0:T(8,128)S(1)}, f32[2,16,1024]{2,1,0:T(8,128)S(1)}, u32[]{:S(2)}, u32[]{:S(2)}) collective-permute-start(f32[2,16,1024]{2,1,0:T(8,128)S(1)} %maximum_add_fusion.1), channel_id=1, source_target_pairs={{0,32},{8,40},{16,48},{24,56},{32,64},{40,72},{48,80},{56,88},{64,... | collective-permute-start | bytes 393224 | tf_op jit(solution)/shard_map/ppermute | solution.py:18
  84.8 5.6 %collective-permute-done.4 = f32[2,16,1024]{2,1,0:T(8,128)S(1)} collective-permute-done((f32[2,16,1024]{2,1,0:T(8,128)S(1)}, f32[2,16,1024]{2,1,0:T(8,128)S(1)}, u32[]{:S(2)}, u32[]{:S(2)}) %collective-permute-start.4) | collective-permute-done | bytes 131104 | tf_op jit(solution)/shard_map/ppermute | solution.py:18
  90.5 4.3 %collective-permute-start.5 = (f32[2,16,1024]{2,1,0:T(8,128)S(1)}, f32[2,16,1024]{2,1,0:T(8,128)S(1)}, u32[]{:S(2)}, u32[]{:S(2)}) collective-permute-start(f32[2,16,1024]{2,1,0:T(8,128)S(1)} %maximum_add_fusion.2), channel_id=1, source_target_pairs={{0,64},{8,72},{16,80},{24,88},{32,96},{40,104},{48,112},{56,120},{... | collective-permute-start | bytes 393224 | tf_op jit(solution)/shard_map/ppermute | solution.py:18
  96.1 0.3 slice.291
  96.3 0.7 maximum_multiply_fusion.5
  97.1 1.5 collective-permute-done.5
  98.6 0.7 maximum_add_fusion.3
  99.3 11.9 %collective-permute-start.6 = (f32[2,16,1024]{2,1,0:T(8,128)}, f32[2,16,1024]{2,1,0:T(8,128)S(1)}, u32[]{:S(2)}, u32[]{:S(2)}) collective-permute-start(f32[2,16,1024]{2,1,0:T(8,128)} %maximum_add_fusion.3), channel_id=1, source_target_pairs={{0,128},{8,136},{16,144},{24,152},{32,160},{40,168},{48,176},{56,1... | collective-permute-start | bytes 393224 | tf_op jit(solution)/shard_map/ppermute | solution.py:18
  112.2 1.9 %collective-permute-done.6 = f32[2,16,1024]{2,1,0:T(8,128)S(1)} collective-permute-done((f32[2,16,1024]{2,1,0:T(8,128)}, f32[2,16,1024]{2,1,0:T(8,128)S(1)}, u32[]{:S(2)}, u32[]{:S(2)}) %collective-permute-start.6) | collective-permute-done | bytes 131104 | tf_op jit(solution)/shard_map/ppermute | solution.py:18
  114.1 0.4 reshape.225
  114.5 3.4 %fusion.9 = f32[64,16,128]{2,1,0:T(8,128)S(1)} fusion(f32[1,64,16,128]{3,2,0,1:T(8,128)} %get-tuple-element.18, f32[1,64,16,128]{3,2,0,1:T(8,128)} %get-tuple-element.17, f32[2,16,64,16]{3,2,1,0:T(8,128)S(1)} %reshape.225, pred[128]{0:T(512)(128)(4,1)S(1)} %copy-done.15), kind=kOutput, calls=%fused_computation.23 | convolution fusion | flops 50724864 | bytes 1704064 | tf_op jit(solution)/shard_map/rgnt,rngi->git/dot_general | solution.py:74
  117.9 10.6 %fusion.6 = f32[64,16,128]{2,1,0:T(8,128)S(1)} fusion(f32[64,16,128]{2,1,0:T(8,128)S(1)} %fusion.9, f32[64,16,128]{2,1,0:T(8,128)S(1)} %bitcast.169, f32[64,128,128]{2,0,1:T(8,128)} %fusion.4), kind=kOutput, calls=%fused_computation.21 | convolution fusion | flops 201457664 | bytes 5767168 | tf_op jit(solution)/shard_map/gts,gis->git/dot_general | solution.py:65
  128.7 31.9 %psum.7 = f32[128]{0:T(128)S(1)} all-reduce(f32[128]{0:T(128)S(1)} %get-tuple-element.10), channel_id=1, replica_groups=mesh['ctx'=64,'tp'=8] {'tp'}, use_global_device_ids=true, to_apply=%region_9.10 | all-reduce | flops 128 | bytes 1024 | tf_op jit(solution)/shard_map/psum | solution.py:151
  160.9 0.8 copy.103
  (95 shorter events, 6.2 us)
Async XLA Ops:
  0.8 27.7 %collective-permute-start = (bf16[6,3,1024]{2,0,1:T(8,128)(2,1)S(1)}, bf16[6,3,1024]{2,0,1:T(8,128)(2,1)S(1)}, u32[]{:S(2)}, u32[]{:S(2)}) collective-permute-start(bf16[6,3,1024]{2,0,1:T(8,128)(2,1)S(1)} %slice.237), channel_id=1, source_target_pairs={{0,8},{8,16},{16,24},{24,32},{32,40},{40,48},{48,56},{56,64},{64,7... | collective-permute-start | bytes 110600 | tf_op jit(solution)/shard_map/ppermute | solution.py:18
  2.8 5.3 %copy-start.16 = (s32[1,128]{1,0:T(1,128)}, s32[1,128]{1,0:T(1,128)S(1)}, u32[]{:S(2)}) copy-start(s32[1,128]{1,0:T(1,128)S(1)} %iota_add_fusion) | copy-start | bytes 1540
  5.1 2.8 %copy-start.13 = (s32[128]{0:T(128)}, s32[128]{0:T(128)S(1)}, u32[]{:S(2)}) copy-start(s32[128]{0:T(128)S(1)} %select_reduce_fusion) | copy-start | bytes 1540
  17.8 5.4 %copy-start.2 = (bf16[128,3,1024]{2,0,1:T(8,128)(2,1)S(1)}, bf16[128,3,1024]{2,0,1:T(8,128)(2,1)}, u32[]{:S(2)}) copy-start(bf16[128,3,1024]{2,0,1:T(8,128)(2,1)} %param.8) | copy-start | bytes 2359300
  22.5 1.8 %copy-start.14 = (s32[128]{0:T(128)S(1)}, s32[128]{0:T(128)}, u32[]{:S(2)}) copy-start(s32[128]{0:T(128)} %copy-done.13) | copy-start | bytes 1540
  22.5 2.4 %copy-start.17 = (s32[1,128]{1,0:T(1,128)S(1)}, s32[1,128]{1,0:T(1,128)}, u32[]{:S(2)}) copy-start(s32[1,128]{1,0:T(1,128)} %copy-done.16) | copy-start | bytes 1540
  22.5 3.1 %copy-start.3 = (f32[1,3,1024]{2,0,1:T(1,128)S(1)}, f32[1,3,1024]{2,0,1:T(1,128)}, u32[]{:S(2)}) copy-start(f32[1,3,1024]{2,0,1:T(1,128)} %get-tuple-element.31) | copy-start | bytes 36868
  26.6 3.2 %copy-start.6 = (pred[128]{0:T(512)(128)(4,1)S(1)}, pred[128]{0:T(512)(128)(4,1)}, u32[]{:S(2)}) copy-start(pred[128]{0:T(512)(128)(4,1)} %get-tuple-element.60) | copy-start | bytes 388
  26.6 3.2 %copy-start.7 = (pred[128]{0:T(512)(128)(4,1)S(1)}, pred[128]{0:T(512)(128)(4,1)}, u32[]{:S(2)}) copy-start(pred[128]{0:T(512)(128)(4,1)} %get-tuple-element.61) | copy-start | bytes 388
  26.6 3.2 %copy-start.8 = (pred[128]{0:T(512)(128)(4,1)S(1)}, pred[128]{0:T(512)(128)(4,1)}, u32[]{:S(2)}) copy-start(pred[128]{0:T(512)(128)(4,1)} %get-tuple-element.62) | copy-start | bytes 388
  26.6 3.2 %copy-start.9 = (pred[128]{0:T(512)(128)(4,1)S(1)}, pred[128]{0:T(512)(128)(4,1)}, u32[]{:S(2)}) copy-start(pred[128]{0:T(512)(128)(4,1)} %get-tuple-element.63) | copy-start | bytes 388
  26.6 3.2 %copy-start.10 = (pred[128]{0:T(512)(128)(4,1)S(1)}, pred[128]{0:T(512)(128)(4,1)}, u32[]{:S(2)}) copy-start(pred[128]{0:T(512)(128)(4,1)} %get-tuple-element.64) | copy-start | bytes 388
  26.6 3.2 %copy-start.11 = (pred[128]{0:T(512)(128)(4,1)S(1)}, pred[128]{0:T(512)(128)(4,1)}, u32[]{:S(2)}) copy-start(pred[128]{0:T(512)(128)(4,1)} %get-tuple-element.65) | copy-start | bytes 388
  26.6 3.2 %copy-start.12 = (pred[128]{0:T(512)(128)(4,1)S(1)}, pred[128]{0:T(512)(128)(4,1)}, u32[]{:S(2)}) copy-start(pred[128]{0:T(512)(128)(4,1)} %get-tuple-element.66) | copy-start | bytes 388
  40.4 1.0 copy-start
  40.4 1.2 copy-start.1
  52.7 9.0 %collective-permute-start.1 = (f32[2,16,1024]{2,1,0:T(8,128)S(1)}, f32[2,16,1024]{2,1,0:T(8,128)S(1)}, u32[]{:S(2)}, u32[]{:S(2)}) collective-permute-start(f32[2,16,1024]{2,1,0:T(8,128)S(1)} %reshape.224), channel_id=1, source_target_pairs={{0,8},{8,16},{16,24},{24,32},{32,40},{40,48},{48,56},{56,64},{64,7... | collective-permute-start | bytes 393224 | tf_op jit(solution)/shard_map/ppermute | solution.py:18
  61.7 9.0 %collective-permute-start.2 = (f32[2,16,1024]{2,1,0:T(8,128)S(1)}, f32[2,16,1024]{2,1,0:T(8,128)S(1)}, u32[]{:S(2)}, u32[]{:S(2)}) collective-permute-start(f32[2,16,1024]{2,1,0:T(8,128)S(1)} %collective-permute-done.1), channel_id=1, source_target_pairs={{0,8},{8,16},{16,24},{24,32},{32,40},{40,48},{48,56},{56,64},{64,7... | collective-permute-start | bytes 393224 | tf_op jit(solution)/shard_map/ppermute | solution.py:18
  70.7 11.0 %collective-permute-start.3 = (f32[2,16,1024]{2,1,0:T(8,128)S(1)}, f32[2,16,1024]{2,1,0:T(8,128)S(1)}, u32[]{:S(2)}, u32[]{:S(2)}) collective-permute-start(f32[2,16,1024]{2,1,0:T(8,128)S(1)} %maximum_add_fusion), channel_id=1, source_target_pairs={{0,16},{8,24},{16,32},{24,40},{32,48},{40,56},{48,64},{56,72},{64,... | collective-permute-start | bytes 393224 | tf_op jit(solution)/shard_map/ppermute | solution.py:18
  81.7 8.7 %collective-permute-start.4 = (f32[2,16,1024]{2,1,0:T(8,128)S(1)}, f32[2,16,1024]{2,1,0:T(8,128)S(1)}, u32[]{:S(2)}, u32[]{:S(2)}) collective-permute-start(f32[2,16,1024]{2,1,0:T(8,128)S(1)} %maximum_add_fusion.1), channel_id=1, source_target_pairs={{0,32},{8,40},{16,48},{24,56},{32,64},{40,72},{48,80},{56,88},{64,... | collective-permute-start | bytes 393224 | tf_op jit(solution)/shard_map/ppermute | solution.py:18
  90.5 8.1 %collective-permute-start.5 = (f32[2,16,1024]{2,1,0:T(8,128)S(1)}, f32[2,16,1024]{2,1,0:T(8,128)S(1)}, u32[]{:S(2)}, u32[]{:S(2)}) collective-permute-start(f32[2,16,1024]{2,1,0:T(8,128)S(1)} %maximum_add_fusion.2), channel_id=1, source_target_pairs={{0,64},{8,72},{16,80},{24,88},{32,96},{40,104},{48,112},{56,120},{... | collective-permute-start | bytes 393224 | tf_op jit(solution)/shard_map/ppermute | solution.py:18
  99.3 14.7 %collective-permute-start.6 = (f32[2,16,1024]{2,1,0:T(8,128)}, f32[2,16,1024]{2,1,0:T(8,128)S(1)}, u32[]{:S(2)}, u32[]{:S(2)}) collective-permute-start(f32[2,16,1024]{2,1,0:T(8,128)} %maximum_add_fusion.3), channel_id=1, source_target_pairs={{0,128},{8,136},{16,144},{24,152},{32,160},{40,168},{48,176},{56,1... | collective-permute-start | bytes 393224 | tf_op jit(solution)/shard_map/ppermute | solution.py:18
  111.9 2.6 %copy-start.15 = (pred[128]{0:T(512)(128)(4,1)S(1)}, pred[128]{0:T(512)(128)(4,1)}, u32[]{:S(2)}) copy-start(pred[128]{0:T(512)(128)(4,1)} %get-tuple-element.59) | copy-start | bytes 388
  117.9 10.6 %copy-start.4 = (f32[1024]{0:T(1024)S(1)}, f32[1024]{0:T(1024)}, u32[]{:S(2)}) copy-start(f32[1024]{0:T(1024)} %param.13) | copy-start | bytes 12292
  128.5 32.1 %copy-start.5 = (f32[1024]{0:T(1024)S(1)}, f32[1024]{0:T(1024)}, u32[]{:S(2)}) copy-start(f32[1024]{0:T(1024)} %param.14) | copy-start | bytes 12292

commit v3 on v2

--- a/solution.py
+++ b/solution.py
@@ -100,7 +100,7 @@
     before = passed_along(qkv[tok_rows - (reach - 1) :], "ctx", 1)
     padded = jnp.concatenate([before, qkv], axis=0)
     filtered = short_filter(padded, taps, positions, genome_start)
-    product = filtered[:, 1] * filtered[:, 2]
+    query, product = lax.optimization_barrier((filtered[:, 0], filtered[:, 1] * filtered[:, 2]))
     tables = pole_tables(rate, angle, residue, SPAN)
     stepping = tables[3]
     values = jnp.transpose(
@@ -117,7 +117,7 @@
     )
     keep_state = span_begin[span_index, -1] < span_pos[span_index, 0]
     summary = jnp.where(keep_state, complex_times(stepping[..., None], summary), 0.0) + fresh_state
-    insides = [inside]
+    insides = [lax.optimization_barrier(inside)]
     freshes.append(fresh_state)
     keepers.append(keep_state)
     device_count = lax.axis_size("ctx")
@@ -147,8 +147,9 @@
     outputs = [insides[span_index] + jnp.where(entered, carried(tables[1], incoming), 0.0)]
     stacked = jnp.stack(outputs, axis=0)
     long_part = jnp.transpose(stacked, (0, 3, 1, 2)).reshape(tok_rows, channels)
-    gated_rows = filtered[:, 0] * (long_part + skip[None] * product)
-    squares = lax.psum(jnp.sum(gated_rows * gated_rows, axis=1), "tp")
+    gated_rows = query * (long_part + skip[None] * product)
+    partial = jnp.sum(gated_rows * gated_rows, axis=1)
+    squares = jnp.sum(lax.all_gather(partial, "tp", axis=0), axis=0)
     root_mean = jnp.sqrt(squares / D + EPSILON)
     return (gated_rows / root_mean[:, None] * gain[None]).astype(jnp.bfloat16)
 

time: 163 us -> 154 us (0.945)
  other arithmetic: 23.7 us -> 17.7 us
  starting transfers between devices: 27.7 us -> 30.3 us
  waiting for transfers between devices: 25.6 us -> 23.3 us
    psum x1 -> x0, blocking collectives: 31.9 us -> none  [on_device(): squares = lax.psum(jnp.sum(gated_rows * gated_rows, axis=1), 'tp')]
    all_gather x0 -> x1, blocking collectives: none -> 30.9 us  [on_device(): squares = jnp.sum(lax.all_gather(partial, 'tp', axis=0), axis=0)]
    add x1, other arithmetic: 10.5 us -> 5.63 us  [short_filter(): result = result + jnp.where(keep_tap, taps_part[offset][None] * window, 0.0)]
    ppermute x7, starting transfers between devices: 27.7 us -> 30.3 us  [passed_along(): return lax.ppermute(block, axis, route)]
    ppermute x7, waiting for transfers between devices: 25.6 us -> 23.3 us  [passed_along(): return lax.ppermute(block, axis, route)]
    another operation x1 -> x2, other arithmetic: 0.83 us -> 2.51 us  [the longest x1 1.68 us: pole_tables(): entering = jnp.stack([enter_re, -enter_im])]
  transfers between devices with their start and end apart: 7 -> 7, of which waited for: 6 -> 5; matrix products, arithmetic and copies ran while one was open for 19% -> 26% of each run, Pallas kernels for 0% -> 0%
where the time goes in v3:
time: 154 us; the launch traced here: 153 us
  blocking collectives  30.9 us (20%)
  starting transfers between devices  30.3 us (20%)
  matrix products  25.9 us (17%)
  waiting for transfers between devices  23.3 us (15%)
  local copies, waits for them, and re-layouts  20.8 us (14%)
  other arithmetic  17.7 us (11%)
  between operations  4.54 us (3%)
    all_gather x1, blocking collectives, on_device(): squares = jnp.sum(lax.all_gather(partial, 'tp', axis=0), axis=0)  30.9 us
    ppermute x7, starting transfers between devices, passed_along(): return lax.ppermute(block, axis, route)  30.3 us
    ppermute x7, waiting for transfers between devices, passed_along(): return lax.ppermute(block, axis, route)  23.3 us
    dot_general x1, matrix products, block_terms(): jnp.einsum('gts,gis->git', matrix_table * same_genome[None], columns, pre...  10.6 us
    dot_general x1, matrix products, block_terms(): jnp.einsum('rgns,gis->rngi', leaving * tail_mask, columns, precision=HIGH...  7.4 us
    add x1, other arithmetic, short_filter(): result = result + jnp.where(keep_tap, taps_part[offset][None] * window, 0.0)  5.63 us
    dot_general x1, matrix products, toeplitz(): return jnp.einsum('gk,kts->gts', response, picks, precision=HIGHEST)  4.69 us
    mul x1, other arithmetic, pole_tables(): power_re = magnitude * jnp.cos(angle[:, :, None] * counter)  3.86 us
  transfers between devices with their start and end apart: 7, of which 5 were waited for; matrix products, arithmetic and copies ran while one was open for 26% of the time, Pallas kernels for 0%

profile of v3, /device:TPU:128, one launch (start us, length us, event | category | flops | bytes accessed | tf_op | source)
XLA Modules:
  0.0 153.4 jit_solution(14606321080109926040)
XLA Ops:
  0.0 1.4 slice.237
  1.4 1.9 %collective-permute-start = (bf16[6,3,1024]{2,0,1:T(8,128)(2,1)}, bf16[6,3,1024]{2,0,1:T(8,128)(2,1)}, u32[]{:S(2)}, u32[]{:S(2)}) collective-permute-start(bf16[6,3,1024]{2,0,1:T(8,128)(2,1)} %slice.237), channel_id=1, source_target_pairs={{0,8},{8,16},{16,24},{24,32},{32,40},{40,48},{48,56},{56,64},{64,7... | collective-permute-start | bytes 110600 | tf_op jit(solution)/shard_map/ppermute | solution.py:18
  3.4 0.8 reduce-window.9
  4.2 1.4 and_reduce_fusion
  5.7 0.6 slice.260
  7.0 0.7 broadcast_compare_fusion.1
  7.7 0.7 neg.7
  8.4 0.7 slice_bitcast_fusion.12
  9.4 0.8 copy.93
  10.2 2.1 %fusion.34 = (f32[1,3,1024]{2,0,1:T(1,128)}, f32[1,3,1024]{2,0,1:T(1,128)S(1)}, f32[1,3,1024]{2,0,1:T(1,128)S(1)}, f32[1,3,1024]{2,0,1:T(1,128)S(1)}, f32[1,3,10...) fusion(f32[7,3,1024]{2,0,1:T(8,128)} %param.9), kind=kLoop, calls=%fused_computation.133 | loop fusion | bytes 172032 | tf_op jit(solution)/shard_map/slice | solution.py:84
  12.3 3.9 %fusion.8 = (f32[64,16,129]{2,1,0:T(8,128)S(1)}, f32[64,16,129]{2,1,0:T(8,128)S(1)}) fusion(f32[64,16]{1,0:T(8,128)S(1)} %copy.93, f32[129]{0:T(256)S(1)} %iota_convert_fusion, f32[64,16]{1,0:T(8,128)S(1)} %copy.92), kind=kLoop, calls=%fused_computation.24 | loop fusion | flops 528384 | bytes 1065476 | tf_op jit(solution)/shard_map/mul | solution.py:38
  16.8 1.7 %subtract_bitcast_fusion = (f32[1,64,16,128]{3,2,0,1:T(8,128)}, f32[64,128]{1,0:T(8,128)S(1)}, f32[1,64,16,128]{3,2,0,1:T(8,128)}, f32[64,16,128]{2,1,0:T(8,128)S(1)}, f32[64,16,128]{2,1,0:T(8,128)S(1)}) fusion(f32[64,16,129]{2,1,0:T(8,128)S(1)} %get-tuple-element.45, f32[64,16,129]{2,1,0:T(8,128)S(1)} %get-tuple-element.44, f32[64,16]{1,0:T(8,128)S(1)} %copy.94, ...), kind=kLoop, calls=%fused_computation.47 | loop fusion | flops 1433600 | bytes 4235264 | tf_op jit(solution)/shard_map/stack | solution.py:47
  18.5 0.6 subtract_bitcast_fusion.1
  19.1 0.6 multiply_bitcast_fusion
  19.8 4.7 %fusion.4 = f32[64,128,128]{2,0,1:T(8,128)} fusion(s32[128,128]{1,0:T(8,128)S(1)} %iota_subtract_fusion, f32[128,128]{1,0:T(8,128)S(1)} %compare_convert_fusion, f32[64,128]{1,0:T(8,128)S(1)} %get-tuple-element.21), kind=kOutput, calls=%fused_computation.15 | convolution fusion | flops 1613758464 | bytes 4358144 | tf_op jit(solution)/shard_map/gk,kts->gts/dot_general | solution.py:32
  24.5 0.6 compare_convert_fusion.1
  25.1 0.4 copy.88
  25.5 0.7 slice.257
  26.9 1.0 rev.6
  27.9 1.0 rev.7
  29.0 0.9 copy.98
  29.9 1.2 copy.89
  31.2 5.6 %select_add_fusion = f32[128,3,1024]{0,2,1:T(8,128)S(1)} fusion(bf16[128,3,1024]{0,2,1:T(8,128)(2,1)S(1)} %copy.88, bf16[6,3,1024]{0,2,1:T(8,128)(2,1)S(1)} %copy.89, f32[3,1024]{1,0:T(4,128)S(1)} %get-tuple-element.73, f32[3,1024]{1,0:T(4,128)S(1)} %get-tuple-element.74, f32[3,1024]{1,0:T(4,128)S(1)} %get-tuple-element.75, ...), kind=kLoop, calls=%fused_computation.16 | loop fusion | flops 17694720 | bytes 2483072 | tf_op jit(solution)/shard_map/add | solution.py:84
  36.9 0.9 copy-done
  38.0 7.4 %fusion.5 = f32[2,16,64,16]{1,3,0,2:T(8,128)S(1)} fusion(f32[64,16,128,1]{2,1,3,0:T(8,128)S(1)} %bitcast.165, f32[2,16,64,16]{1,3,0,2:T(8,128)S(1)} %copy.98, pred[]{:T(512)S(6)} %lt.15, f32[1,64,16,128]{3,2,1,0:T(8,128)S(1)} %bitcast.168, f32[1,64,16,128]{3,2,1,0:T(8,128)S(1)} %bitcast.167, f32[128]{0:T(128)S(1)} %compare_convert_fusion.1), kind=kOutput, calls=%fused_computation.20 | convolution fusion | flops 50921472 | bytes 1835521 | tf_op jit(solution)/shard_map/rgns,gis->rngi/dot_general | solution.py:69
  45.4 0.9 copy.100
  46.3 0.6 reshape.213
  46.9 3.6 %collective-permute-start.1 = (f32[2,16,1024]{2,1,0:T(8,128)S(1)}, f32[2,16,1024]{2,1,0:T(8,128)S(1)}, u32[]{:S(2)}, u32[]{:S(2)}) collective-permute-start(f32[2,16,1024]{2,1,0:T(8,128)S(1)} %reshape.213), channel_id=1, source_target_pairs={{0,8},{8,16},{16,24},{24,32},{32,40},{40,48},{48,56},{56,64},{64,7... | collective-permute-start | bytes 393224 | tf_op jit(solution)/shard_map/ppermute | solution.py:18
  51.2 4.7 %collective-permute-done.1 = f32[2,16,1024]{2,1,0:T(8,128)S(1)} collective-permute-done((f32[2,16,1024]{2,1,0:T(8,128)S(1)}, f32[2,16,1024]{2,1,0:T(8,128)S(1)}, u32[]{:S(2)}, u32[]{:S(2)}) %collective-permute-start.1) | collective-permute-done | bytes 131104 | tf_op jit(solution)/shard_map/ppermute | solution.py:18
  55.9 1.9 %collective-permute-start.2 = (f32[2,16,1024]{2,1,0:T(8,128)S(1)}, f32[2,16,1024]{2,1,0:T(8,128)S(1)}, u32[]{:S(2)}, u32[]{:S(2)}) collective-permute-start(f32[2,16,1024]{2,1,0:T(8,128)S(1)} %collective-permute-done.1), channel_id=1, source_target_pairs={{0,8},{8,16},{16,24},{24,32},{32,40},{40,48},{48,56},{56,64},{64,7... | collective-permute-start | bytes 393224 | tf_op jit(solution)/shard_map/ppermute | solution.py:18
  59.3 0.3 slice.271
  59.9 0.3 slice.263
  60.8 0.3 slice.267
  61.1 3.8 %collective-permute-done.2 = f32[2,16,1024]{2,1,0:T(8,128)S(1)} collective-permute-done((f32[2,16,1024]{2,1,0:T(8,128)S(1)}, f32[2,16,1024]{2,1,0:T(8,128)S(1)}, u32[]{:S(2)}, u32[]{:S(2)}) %collective-permute-start.2) | collective-permute-done | bytes 131104 | tf_op jit(solution)/shard_map/ppermute | solution.py:18
  64.9 1.9 %collective-permute-start.3 = (f32[2,16,1024]{2,1,0:T(8,128)S(1)}, f32[2,16,1024]{2,1,0:T(8,128)S(1)}, u32[]{:S(2)}, u32[]{:S(2)}) collective-permute-start(f32[2,16,1024]{2,1,0:T(8,128)S(1)} %maximum_add_fusion), channel_id=1, source_target_pairs={{0,16},{8,24},{16,32},{24,40},{32,48},{40,56},{48,64},{56,72},{64,... | collective-permute-start | bytes 393224 | tf_op jit(solution)/shard_map/ppermute | solution.py:18
  66.9 7.6 %collective-permute-done.3 = f32[2,16,1024]{2,1,0:T(8,128)S(1)} collective-permute-done((f32[2,16,1024]{2,1,0:T(8,128)S(1)}, f32[2,16,1024]{2,1,0:T(8,128)S(1)}, u32[]{:S(2)}, u32[]{:S(2)}) %collective-permute-start.3) | collective-permute-done | bytes 131104 | tf_op jit(solution)/shard_map/ppermute | solution.py:18
  74.6 1.9 %collective-permute-start.4 = (f32[2,16,1024]{2,1,0:T(8,128)S(1)}, f32[2,16,1024]{2,1,0:T(8,128)S(1)}, u32[]{:S(2)}, u32[]{:S(2)}) collective-permute-start(f32[2,16,1024]{2,1,0:T(8,128)S(1)} %maximum_add_fusion.1), channel_id=1, source_target_pairs={{0,32},{8,40},{16,48},{24,56},{32,64},{40,72},{48,80},{56,88},{64,... | collective-permute-start | bytes 393224 | tf_op jit(solution)/shard_map/ppermute | solution.py:18
  77.3 0.3 slice.287
  78.5 4.8 %collective-permute-done.4 = f32[2,16,1024]{2,1,0:T(8,128)S(1)} collective-permute-done((f32[2,16,1024]{2,1,0:T(8,128)S(1)}, f32[2,16,1024]{2,1,0:T(8,128)S(1)}, u32[]{:S(2)}, u32[]{:S(2)}) %collective-permute-start.4) | collective-permute-done | bytes 131104 | tf_op jit(solution)/shard_map/ppermute | solution.py:18
  83.4 4.5 %collective-permute-start.5 = (f32[2,16,1024]{2,1,0:T(8,128)S(1)}, f32[2,16,1024]{2,1,0:T(8,128)S(1)}, u32[]{:S(2)}, u32[]{:S(2)}) collective-permute-start(f32[2,16,1024]{2,1,0:T(8,128)S(1)} %maximum_add_fusion.2), channel_id=1, source_target_pairs={{0,64},{8,72},{16,80},{24,88},{32,96},{40,104},{48,112},{56,120},{... | collective-permute-start | bytes 393224 | tf_op jit(solution)/shard_map/ppermute | solution.py:18
  89.3 2.3 %collective-permute-done.5 = f32[2,16,1024]{2,1,0:T(8,128)S(1)} collective-permute-done((f32[2,16,1024]{2,1,0:T(8,128)S(1)}, f32[2,16,1024]{2,1,0:T(8,128)S(1)}, u32[]{:S(2)}, u32[]{:S(2)}) %collective-permute-start.5) | collective-permute-done | bytes 131104 | tf_op jit(solution)/shard_map/ppermute | solution.py:18
  91.7 14.5 %collective-permute-start.6 = (f32[2,16,1024]{2,1,0:T(8,128)S(1)}, f32[2,16,1024]{2,1,0:T(8,128)S(1)}, u32[]{:S(2)}, u32[]{:S(2)}) collective-permute-start(f32[2,16,1024]{2,1,0:T(8,128)S(1)} %maximum_add_fusion.3), channel_id=1, source_target_pairs={{0,128},{8,136},{16,144},{24,152},{32,160},{40,168},{48,176},{56,1... | collective-permute-start | bytes 393224 | tf_op jit(solution)/shard_map/ppermute | solution.py:18
  106.3 10.6 %fusion.1 = f32[64,16,128]{2,1,0:T(8,128)S(1)} fusion(f32[64,16,128]{2,1,0:T(8,128)S(1)} %bitcast.166, f32[64,128,128]{2,0,1:T(8,128)} %fusion.4), kind=kOutput, calls=%fused_computation.2 | convolution fusion | flops 201326592 | bytes 5242880 | tf_op jit(solution)/shard_map/gts,gis->git/dot_general | solution.py:65
  117.0 0.4 reshape.214
  117.4 0.6 copy-done.2
  117.9 3.3 %fusion.7 = f32[64,16,128]{2,1,0:T(8,128)S(1)} fusion(f32[64,16,128]{2,1,0:T(8,128)S(1)} %fusion.1, f32[1,64,16,128]{3,2,0,1:T(8,128)} %get-tuple-element.22, f32[1,64,16,128]{3,2,0,1:T(8,128)S(1)} %copy-done.2, f32[2,16,64,16]{3,2,1,0:T(8,128)S(1)} %reshape.214, pred[128]{0:T(512)(128)(4,1)S(1)} %copy-done.22), kind=kOutput, calls=%fused_computation.23 | convolution fusion | flops 50855936 | bytes 2228352 | tf_op jit(solution)/shard_map/rgnt,rngi->git/dot_general | solution.py:74
  121.4 30.9 %all-gather.1 = f32[8,1,128]{2,1,0:T(1,128)S(1)} all-gather(f32[1,1,128]{2,1,0:T(1,128)S(1)} %bitcast.174), channel_id=2, replica_groups=mesh['ctx'=64,'tp'=8] {'tp'}, dimensions={0}, use_global_device_ids=true | all-gather | bytes 4608 | tf_op jit(solution)/shard_map/all_gather | solution.py:152
  152.6 0.8 copy.103
  (110 shorter events, 5.8 us)
Async XLA Ops:
  1.4 28.5 %collective-permute-start = (bf16[6,3,1024]{2,0,1:T(8,128)(2,1)}, bf16[6,3,1024]{2,0,1:T(8,128)(2,1)}, u32[]{:S(2)}, u32[]{:S(2)}) collective-permute-start(bf16[6,3,1024]{2,0,1:T(8,128)(2,1)} %slice.237), channel_id=1, source_target_pairs={{0,8},{8,16},{16,24},{24,32},{32,40},{40,48},{48,56},{56,64},{64,7... | collective-permute-start | bytes 110600 | tf_op jit(solution)/shard_map/ppermute | solution.py:18
  3.4 6.8 %copy-start.23 = (s32[1,128]{1,0:T(1,128)}, s32[1,128]{1,0:T(1,128)S(1)}, u32[]{:S(2)}) copy-start(s32[1,128]{1,0:T(1,128)S(1)} %iota_add_fusion) | copy-start | bytes 1540
  5.7 4.4 %copy-start.20 = (s32[128]{0:T(128)}, s32[128]{0:T(128)S(1)}, u32[]{:S(2)}) copy-start(s32[128]{0:T(128)S(1)} %select_reduce_fusion) | copy-start | bytes 1540
  19.8 5.4 %copy-start.3 = (bf16[128,3,1024]{2,0,1:T(8,128)(2,1)S(1)}, bf16[128,3,1024]{2,0,1:T(8,128)(2,1)}, u32[]{:S(2)}) copy-start(bf16[128,3,1024]{2,0,1:T(8,128)(2,1)} %param.8) | copy-start | bytes 2359300
  24.5 1.0 copy-start.21
  24.5 1.7 %copy-start.24 = (s32[1,128]{1,0:T(1,128)S(1)}, s32[1,128]{1,0:T(1,128)}, u32[]{:S(2)}) copy-start(s32[1,128]{1,0:T(1,128)} %copy-done.23) | copy-start | bytes 1540
  24.5 2.4 %copy-start.4 = (f32[1,3,1024]{2,0,1:T(1,128)S(1)}, f32[1,3,1024]{2,0,1:T(1,128)}, u32[]{:S(2)}) copy-start(f32[1,3,1024]{2,0,1:T(1,128)} %get-tuple-element.37) | copy-start | bytes 36868
  27.9 3.2 %copy-start.13 = (pred[128]{0:T(512)(128)(4,1)S(1)}, pred[128]{0:T(512)(128)(4,1)}, u32[]{:S(2)}) copy-start(pred[128]{0:T(512)(128)(4,1)} %get-tuple-element.66) | copy-start | bytes 388
  27.9 3.2 %copy-start.14 = (pred[128]{0:T(512)(128)(4,1)S(1)}, pred[128]{0:T(512)(128)(4,1)}, u32[]{:S(2)}) copy-start(pred[128]{0:T(512)(128)(4,1)} %get-tuple-element.67) | copy-start | bytes 388
  27.9 3.2 %copy-start.15 = (pred[128]{0:T(512)(128)(4,1)S(1)}, pred[128]{0:T(512)(128)(4,1)}, u32[]{:S(2)}) copy-start(pred[128]{0:T(512)(128)(4,1)} %get-tuple-element.68) | copy-start | bytes 388
  27.9 3.2 %copy-start.16 = (pred[128]{0:T(512)(128)(4,1)S(1)}, pred[128]{0:T(512)(128)(4,1)}, u32[]{:S(2)}) copy-start(pred[128]{0:T(512)(128)(4,1)} %get-tuple-element.69) | copy-start | bytes 388
  27.9 3.2 %copy-start.17 = (pred[128]{0:T(512)(128)(4,1)S(1)}, pred[128]{0:T(512)(128)(4,1)}, u32[]{:S(2)}) copy-start(pred[128]{0:T(512)(128)(4,1)} %get-tuple-element.70) | copy-start | bytes 388
  27.9 3.2 %copy-start.18 = (pred[128]{0:T(512)(128)(4,1)S(1)}, pred[128]{0:T(512)(128)(4,1)}, u32[]{:S(2)}) copy-start(pred[128]{0:T(512)(128)(4,1)} %get-tuple-element.71) | copy-start | bytes 388
  27.9 3.2 %copy-start.19 = (pred[128]{0:T(512)(128)(4,1)S(1)}, pred[128]{0:T(512)(128)(4,1)}, u32[]{:S(2)}) copy-start(pred[128]{0:T(512)(128)(4,1)} %get-tuple-element.72) | copy-start | bytes 388
  36.8 1.0 copy-start
  36.8 1.2 copy-start.1
  46.9 9.0 %collective-permute-start.1 = (f32[2,16,1024]{2,1,0:T(8,128)S(1)}, f32[2,16,1024]{2,1,0:T(8,128)S(1)}, u32[]{:S(2)}, u32[]{:S(2)}) collective-permute-start(f32[2,16,1024]{2,1,0:T(8,128)S(1)} %reshape.213), channel_id=1, source_target_pairs={{0,8},{8,16},{16,24},{24,32},{32,40},{40,48},{48,56},{56,64},{64,7... | collective-permute-start | bytes 393224 | tf_op jit(solution)/shard_map/ppermute | solution.py:18
  55.9 9.0 %collective-permute-start.2 = (f32[2,16,1024]{2,1,0:T(8,128)S(1)}, f32[2,16,1024]{2,1,0:T(8,128)S(1)}, u32[]{:S(2)}, u32[]{:S(2)}) collective-permute-start(f32[2,16,1024]{2,1,0:T(8,128)S(1)} %collective-permute-done.1), channel_id=1, source_target_pairs={{0,8},{8,16},{16,24},{24,32},{32,40},{40,48},{48,56},{56,64},{64,7... | collective-permute-start | bytes 393224 | tf_op jit(solution)/shard_map/ppermute | solution.py:18
  59.6 1.5 copy-start.7
  59.6 1.5 copy-start.8
  59.6 1.5 copy-start.9
  59.6 1.5 copy-start.10
  64.9 9.6 %collective-permute-start.3 = (f32[2,16,1024]{2,1,0:T(8,128)S(1)}, f32[2,16,1024]{2,1,0:T(8,128)S(1)}, u32[]{:S(2)}, u32[]{:S(2)}) collective-permute-start(f32[2,16,1024]{2,1,0:T(8,128)S(1)} %maximum_add_fusion), channel_id=1, source_target_pairs={{0,16},{8,24},{16,32},{24,40},{32,48},{40,56},{48,64},{56,72},{64,... | collective-permute-start | bytes 393224 | tf_op jit(solution)/shard_map/ppermute | solution.py:18
  74.6 8.8 %collective-permute-start.4 = (f32[2,16,1024]{2,1,0:T(8,128)S(1)}, f32[2,16,1024]{2,1,0:T(8,128)S(1)}, u32[]{:S(2)}, u32[]{:S(2)}) collective-permute-start(f32[2,16,1024]{2,1,0:T(8,128)S(1)} %maximum_add_fusion.1), channel_id=1, source_target_pairs={{0,32},{8,40},{16,48},{24,56},{32,64},{40,72},{48,80},{56,88},{64,... | collective-permute-start | bytes 393224 | tf_op jit(solution)/shard_map/ppermute | solution.py:18
  77.1 1.4 copy-start.5
  77.1 1.4 copy-start.6
  83.4 8.3 %collective-permute-start.5 = (f32[2,16,1024]{2,1,0:T(8,128)S(1)}, f32[2,16,1024]{2,1,0:T(8,128)S(1)}, u32[]{:S(2)}, u32[]{:S(2)}) collective-permute-start(f32[2,16,1024]{2,1,0:T(8,128)S(1)} %maximum_add_fusion.2), channel_id=1, source_target_pairs={{0,64},{8,72},{16,80},{24,88},{32,96},{40,104},{48,112},{56,120},{... | collective-permute-start | bytes 393224 | tf_op jit(solution)/shard_map/ppermute | solution.py:18
  91.7 25.2 %collective-permute-start.6 = (f32[2,16,1024]{2,1,0:T(8,128)S(1)}, f32[2,16,1024]{2,1,0:T(8,128)S(1)}, u32[]{:S(2)}, u32[]{:S(2)}) collective-permute-start(f32[2,16,1024]{2,1,0:T(8,128)S(1)} %maximum_add_fusion.3), channel_id=1, source_target_pairs={{0,128},{8,136},{16,144},{24,152},{32,160},{40,168},{48,176},{56,1... | collective-permute-start | bytes 393224 | tf_op jit(solution)/shard_map/ppermute | solution.py:18
  116.9 1.0 copy-start.2
  116.9 1.0 copy-start.22
  117.9 3.3 %copy-start.11 = (f32[1024]{0:T(1024)S(1)}, f32[1024]{0:T(1024)}, u32[]{:S(2)}) copy-start(f32[1024]{0:T(1024)} %param.13) | copy-start | bytes 12292
  121.2 31.2 %copy-start.12 = (f32[1024]{0:T(1024)S(1)}, f32[1024]{0:T(1024)}, u32[]{:S(2)}) copy-start(f32[1024]{0:T(1024)} %param.14) | copy-start | bytes 12292

commit v4 on v3

--- a/solution.py
+++ b/solution.py
@@ -149,7 +149,12 @@
     long_part = jnp.transpose(stacked, (0, 3, 1, 2)).reshape(tok_rows, channels)
     gated_rows = query * (long_part + skip[None] * product)
     partial = jnp.sum(gated_rows * gated_rows, axis=1)
-    squares = jnp.sum(lax.all_gather(partial, "tp", axis=0), axis=0)
+    squares = partial
+    span = 1
+    while span < lax.axis_size("tp"):
+        pairs = [(i, i ^ span) for i in range(lax.axis_size("tp"))]
+        squares = squares + lax.ppermute(squares, "tp", pairs)
+        span = span * 2
     root_mean = jnp.sqrt(squares / D + EPSILON)
     return (gated_rows / root_mean[:, None] * gain[None]).astype(jnp.bfloat16)
 

time: 154 us -> 149 us (0.968)
  blocking collectives: 30.9 us -> 0 us
  starting transfers between devices: 30.3 us -> 46.3 us
  waiting for transfers between devices: 23.3 us -> 29 us
  local copies, waits for them, and re-layouts: 20.8 us -> 23.4 us
    all_gather x1 -> x0, blocking collectives: 30.9 us -> none  [on_device(): squares = jnp.sum(lax.all_gather(partial, 'tp', axis=0), axis=0)]
    ppermute x0 -> x3, starting transfers between devices: none -> 16 us  [on_device(): squares = squares + lax.ppermute(squares, 'tp', pairs)]
    ppermute x0 -> x3, waiting for transfers between devices: none -> 5.71 us  [on_device(): squares = squares + lax.ppermute(squares, 'tp', pairs)]
    unnamed x56 -> x76, local copies, waits for them, and re-layouts: 2.94 us -> 4.35 us
  transfers between devices with their start and end apart: 7 -> 10, of which waited for: 5 -> 8; matrix products, arithmetic and copies ran while one was open for 26% -> 30% of each run, Pallas kernels for 0% -> 0%
where the time goes in v4:
time: 149 us; the launch traced here: 148 us
  starting transfers between devices  46.3 us (31%)
  waiting for transfers between devices  29 us (19%)
  matrix products  25.9 us (17%)
  local copies, waits for them, and re-layouts  23.4 us (16%)
  other arithmetic  19 us (13%)
  between operations  4.68 us (3%)
    ppermute x7, starting transfers between devices, passed_along(): return lax.ppermute(block, axis, route)  30.2 us
    ppermute x7, waiting for transfers between devices, passed_along(): return lax.ppermute(block, axis, route)  23.3 us
    ppermute x3, starting transfers between devices, on_device(): squares = squares + lax.ppermute(squares, 'tp', pairs)  16 us
    dot_general x1, matrix products, block_terms(): jnp.einsum('gts,gis->git', matrix_table * same_genome[None], columns, pre...  10.6 us
    dot_general x1, matrix products, block_terms(): jnp.einsum('rgns,gis->rngi', leaving * tail_mask, columns, precision=HIGH...  7.4 us
    ppermute x3, waiting for transfers between devices, on_device(): squares = squares + lax.ppermute(squares, 'tp', pairs)  5.71 us
    add x1, other arithmetic, short_filter(): result = result + jnp.where(keep_tap, taps_part[offset][None] * window, 0.0)  5.63 us
    dot_general x1, matrix products, toeplitz(): return jnp.einsum('gk,kts->gts', response, picks, precision=HIGHEST)  4.53 us
  transfers between devices with their start and end apart: 10, of which 8 were waited for; matrix products, arithmetic and copies ran while one was open for 30% of the time, Pallas kernels for 0%

profile of v4, /device:TPU:128, one launch (start us, length us, event | category | flops | bytes accessed | tf_op | source)
XLA Modules:
  0.0 148.2 jit_solution(14711210890283254249)
XLA Ops:
  0.0 1.4 slice.237
  1.4 1.9 %collective-permute-start = (bf16[6,3,1024]{2,0,1:T(8,128)(2,1)}, bf16[6,3,1024]{2,0,1:T(8,128)(2,1)}, u32[]{:S(2)}, u32[]{:S(2)}) collective-permute-start(bf16[6,3,1024]{2,0,1:T(8,128)(2,1)} %slice.237), channel_id=1, source_target_pairs={{0,8},{8,16},{16,24},{24,32},{32,40},{40,48},{48,56},{56,64},{64,7... | collective-permute-start | bytes 110600 | tf_op jit(solution)/shard_map/ppermute | solution.py:18
  3.4 0.8 reduce-window.9
  4.2 1.4 and_reduce_fusion
  7.0 0.6 broadcast_compare_fusion.1
  7.7 0.7 neg.7
  8.4 0.7 slice_bitcast_fusion.12
  9.1 0.7 copy.91
  9.9 0.7 copy.94
  10.6 0.8 copy.93
  11.4 2.1 %fusion.34 = (f32[1,3,1024]{2,0,1:T(1,128)}, f32[1,3,1024]{2,0,1:T(1,128)S(1)}, f32[1,3,1024]{2,0,1:T(1,128)S(1)}, f32[1,3,1024]{2,0,1:T(1,128)S(1)}, f32[1,3,10...) fusion(f32[7,3,1024]{2,0,1:T(8,128)} %param.9), kind=kLoop, calls=%fused_computation.133 | loop fusion | bytes 172032 | tf_op jit(solution)/shard_map/slice | solution.py:84
  13.5 3.9 %fusion.8 = (f32[64,16,129]{2,1,0:T(8,128)S(1)}, f32[64,16,129]{2,1,0:T(8,128)S(1)}) fusion(f32[64,16]{1,0:T(8,128)S(1)} %copy.93, f32[129]{0:T(256)S(1)} %iota_convert_fusion, f32[64,16]{1,0:T(8,128)S(1)} %copy.92), kind=kLoop, calls=%fused_computation.24 | loop fusion | flops 528384 | bytes 1065476 | tf_op jit(solution)/shard_map/mul | solution.py:38
  17.9 0.6 copy_bitcast_fusion.2
  18.6 0.6 copy_bitcast_fusion.4
  19.2 0.6 copy_bitcast_fusion
  19.8 2.5 %subtract_bitcast_fusion = (f32[1,64,16,128]{3,2,0,1:T(8,128)}, f32[64,128]{1,0:T(8,128)S(1)}, f32[1,64,16,128]{3,2,0,1:T(8,128)}, f32[64,16,128]{2,1,0:T(8,128)S(1)}, f32[64,16,128]{2,1,0:T(8,128)S(1)}) fusion(f32[64,16,129]{2,1,0:T(8,128)S(1)} %get-tuple-element.45, f32[64,16,129]{2,1,0:T(8,128)S(1)} %get-tuple-element.44, f32[64,16]{1,0:T(8,128)} %copy.94, ...), kind=kLoop, calls=%fused_computation.47 | loop fusion | flops 1433600 | bytes 4235264 | tf_op jit(solution)/shard_map/stack | solution.py:47
  22.8 0.6 multiply_bitcast_fusion
  24.1 4.5 %fusion.4 = f32[64,128,128]{2,0,1:T(8,128)} fusion(s32[128,128]{1,0:T(8,128)S(1)} %iota_subtract_fusion, f32[128,128]{1,0:T(8,128)S(1)} %compare_convert_fusion, f32[64,128]{1,0:T(8,128)S(1)} %get-tuple-element.21), kind=kOutput, calls=%fused_computation.15 | convolution fusion | flops 1613758464 | bytes 4358144 | tf_op jit(solution)/shard_map/gk,kts->gts/dot_general | solution.py:32
  29.7 0.6 slice.257
  30.9 1.0 rev.6
  32.1 1.0 rev.7
  33.1 0.9 copy.98
  34.0 1.2 copy.89
  35.4 5.6 %select_add_fusion = f32[128,3,1024]{0,2,1:T(8,128)S(1)} fusion(bf16[128,3,1024]{0,2,1:T(8,128)(2,1)S(1)} %copy.88, bf16[6,3,1024]{0,2,1:T(8,128)(2,1)S(1)} %copy.89, f32[3,1024]{1,0:T(4,128)S(1)} %copy-done.11, f32[3,1024]{1,0:T(4,128)S(1)} %copy-done.12, f32[3,1024]{1,0:T(4,128)S(1)} %copy-done.7, f32[3,1024]{1,0:T(4,128)S(1)} %copy-done.8, ...), kind=kLoop, calls=%fused_computation.16 | loop fusion | flops 17694720 | bytes 2483072 | tf_op jit(solution)/shard_map/add | solution.py:84
  41.1 0.9 copy-done
  42.2 7.4 %fusion.5 = f32[2,16,64,16]{1,3,0,2:T(8,128)S(1)} fusion(f32[64,16,128,1]{2,1,3,0:T(8,128)S(1)} %bitcast.164, f32[2,16,64,16]{1,3,0,2:T(8,128)S(1)} %copy.98, pred[]{:T(512)S(6)} %lt.15, f32[1,64,16,128]{3,2,1,0:T(8,128)S(1)} %bitcast.167, f32[1,64,16,128]{3,2,1,0:T(8,128)S(1)} %bitcast.166, f32[128]{0:T(128)S(1)} %compare_convert_fusion.1), kind=kOutput, calls=%fused_computation.20 | convolution fusion | flops 50921472 | bytes 1835521 | tf_op jit(solution)/shard_map/rgns,gis->rngi/dot_general | solution.py:69
  49.6 0.9 copy.100
  50.5 0.6 reshape.209
  51.1 3.6 %collective-permute-start.1 = (f32[2,16,1024]{2,1,0:T(8,128)S(1)}, f32[2,16,1024]{2,1,0:T(8,128)S(1)}, u32[]{:S(2)}, u32[]{:S(2)}) collective-permute-start(f32[2,16,1024]{2,1,0:T(8,128)S(1)} %reshape.209), channel_id=1, source_target_pairs={{0,8},{8,16},{16,24},{24,32},{32,40},{40,48},{48,56},{56,64},{64,7... | collective-permute-start | bytes 393224 | tf_op jit(solution)/shard_map/ppermute | solution.py:18
  55.5 4.6 %collective-permute-done.1 = f32[2,16,1024]{2,1,0:T(8,128)S(1)} collective-permute-done((f32[2,16,1024]{2,1,0:T(8,128)S(1)}, f32[2,16,1024]{2,1,0:T(8,128)S(1)}, u32[]{:S(2)}, u32[]{:S(2)}) %collective-permute-start.1) | collective-permute-done | bytes 131104 | tf_op jit(solution)/shard_map/ppermute | solution.py:18
  60.1 1.9 %collective-permute-start.2 = (f32[2,16,1024]{2,1,0:T(8,128)S(1)}, f32[2,16,1024]{2,1,0:T(8,128)S(1)}, u32[]{:S(2)}, u32[]{:S(2)}) collective-permute-start(f32[2,16,1024]{2,1,0:T(8,128)S(1)} %collective-permute-done.1), channel_id=1, source_target_pairs={{0,8},{8,16},{16,24},{24,32},{32,40},{40,48},{48,56},{56,64},{64,7... | collective-permute-start | bytes 393224 | tf_op jit(solution)/shard_map/ppermute | solution.py:18
  65.2 3.9 %collective-permute-done.2 = f32[2,16,1024]{2,1,0:T(8,128)S(1)} collective-permute-done((f32[2,16,1024]{2,1,0:T(8,128)S(1)}, f32[2,16,1024]{2,1,0:T(8,128)S(1)}, u32[]{:S(2)}, u32[]{:S(2)}) %collective-permute-start.2) | collective-permute-done | bytes 131104 | tf_op jit(solution)/shard_map/ppermute | solution.py:18
  69.1 1.9 %collective-permute-start.3 = (f32[2,16,1024]{2,1,0:T(8,128)S(1)}, f32[2,16,1024]{2,1,0:T(8,128)S(1)}, u32[]{:S(2)}, u32[]{:S(2)}) collective-permute-start(f32[2,16,1024]{2,1,0:T(8,128)S(1)} %maximum_add_fusion), channel_id=1, source_target_pairs={{0,16},{8,24},{16,32},{24,40},{32,48},{40,56},{48,64},{56,72},{64,... | collective-permute-start | bytes 393224 | tf_op jit(solution)/shard_map/ppermute | solution.py:18
  71.1 7.7 %collective-permute-done.3 = f32[2,16,1024]{2,1,0:T(8,128)S(1)} collective-permute-done((f32[2,16,1024]{2,1,0:T(8,128)S(1)}, f32[2,16,1024]{2,1,0:T(8,128)S(1)}, u32[]{:S(2)}, u32[]{:S(2)}) %collective-permute-start.3) | collective-permute-done | bytes 131104 | tf_op jit(solution)/shard_map/ppermute | solution.py:18
  78.8 1.9 %collective-permute-start.4 = (f32[2,16,1024]{2,1,0:T(8,128)S(1)}, f32[2,16,1024]{2,1,0:T(8,128)S(1)}, u32[]{:S(2)}, u32[]{:S(2)}) collective-permute-start(f32[2,16,1024]{2,1,0:T(8,128)S(1)} %maximum_add_fusion.1), channel_id=1, source_target_pairs={{0,32},{8,40},{16,48},{24,56},{32,64},{40,72},{48,80},{56,88},{64,... | collective-permute-start | bytes 393224 | tf_op jit(solution)/shard_map/ppermute | solution.py:18
  82.9 4.7 %collective-permute-done.4 = f32[2,16,1024]{2,1,0:T(8,128)S(1)} collective-permute-done((f32[2,16,1024]{2,1,0:T(8,128)S(1)}, f32[2,16,1024]{2,1,0:T(8,128)S(1)}, u32[]{:S(2)}, u32[]{:S(2)}) %collective-permute-start.4) | collective-permute-done | bytes 131104 | tf_op jit(solution)/shard_map/ppermute | solution.py:18
  87.7 4.5 %collective-permute-start.5 = (f32[2,16,1024]{2,1,0:T(8,128)S(1)}, f32[2,16,1024]{2,1,0:T(8,128)S(1)}, u32[]{:S(2)}, u32[]{:S(2)}) collective-permute-start(f32[2,16,1024]{2,1,0:T(8,128)S(1)} %maximum_add_fusion.2), channel_id=1, source_target_pairs={{0,64},{8,72},{16,80},{24,88},{32,96},{40,104},{48,112},{56,120},{... | collective-permute-start | bytes 393224 | tf_op jit(solution)/shard_map/ppermute | solution.py:18
  93.6 2.3 %collective-permute-done.5 = f32[2,16,1024]{2,1,0:T(8,128)S(1)} collective-permute-done((f32[2,16,1024]{2,1,0:T(8,128)S(1)}, f32[2,16,1024]{2,1,0:T(8,128)S(1)}, u32[]{:S(2)}, u32[]{:S(2)}) %collective-permute-start.5) | collective-permute-done | bytes 131104 | tf_op jit(solution)/shard_map/ppermute | solution.py:18
  96.0 14.5 %collective-permute-start.6 = (f32[2,16,1024]{2,1,0:T(8,128)S(1)}, f32[2,16,1024]{2,1,0:T(8,128)S(1)}, u32[]{:S(2)}, u32[]{:S(2)}) collective-permute-start(f32[2,16,1024]{2,1,0:T(8,128)S(1)} %maximum_add_fusion.3), channel_id=1, source_target_pairs={{0,128},{8,136},{16,144},{24,152},{32,160},{40,168},{48,176},{56,1... | collective-permute-start | bytes 393224 | tf_op jit(solution)/shard_map/ppermute | solution.py:18
  110.5 10.6 %fusion.1 = f32[64,16,128]{2,1,0:T(8,128)S(1)} fusion(f32[64,16,128]{2,1,0:T(8,128)S(1)} %bitcast.165, f32[64,128,128]{2,0,1:T(8,128)} %fusion.4), kind=kOutput, calls=%fused_computation.2 | convolution fusion | flops 201326592 | bytes 5242880 | tf_op jit(solution)/shard_map/gts,gis->git/dot_general | solution.py:65
  121.7 3.4 %fusion.7 = f32[64,16,128]{2,1,0:T(8,128)S(1)} fusion(f32[64,16,128]{2,1,0:T(8,128)S(1)} %fusion.1, f32[1,64,16,128]{3,2,0,1:T(8,128)} %get-tuple-element.22, f32[1,64,16,128]{3,2,0,1:T(8,128)} %get-tuple-element.20, f32[2,16,64,16]{3,2,1,0:T(8,128)S(1)} %reshape.210, pred[128]{0:T(512)(128)(4,1)S(1)} %copy-done.32), kind=kOutput, calls=%fused_computation.23 | convolution fusion | flops 50855936 | bytes 2228352 | tf_op jit(solution)/shard_map/rgnt,rngi->git/dot_general | solution.py:74
  125.4 3.4 %collective-permute-start.7 = (f32[128]{0:T(128)S(1)}, f32[128]{0:T(128)S(1)}, u32[]{:S(2)}, u32[]{:S(2)}) collective-permute-start(f32[128]{0:T(128)S(1)} %get-tuple-element.14), channel_id=1, source_target_pairs={{0,1},{1,0},{2,3},{3,2},{4,5},{5,4},{6,7},{7,6},{8,9},{9,8},{10,11... | collective-permute-start | bytes 1544 | tf_op jit(solution)/shard_map/ppermute | solution.py:156
  128.8 2.1 %collective-permute-done.7 = f32[128]{0:T(128)S(1)} collective-permute-done((f32[128]{0:T(128)S(1)}, f32[128]{0:T(128)S(1)}, u32[]{:S(2)}, u32[]{:S(2)}) %collective-permute-start.7) | collective-permute-done | bytes 544 | tf_op jit(solution)/shard_map/ppermute | solution.py:156
  130.8 4.9 %collective-permute-start.8 = (f32[128]{0:T(128)S(1)}, f32[128]{0:T(128)S(1)}, u32[]{:S(2)}, u32[]{:S(2)}) collective-permute-start(f32[128]{0:T(128)S(1)} %add.209), channel_id=1, source_target_pairs={{0,2},{1,3},{2,0},{3,1},{4,6},{5,7},{6,4},{7,5},{8,10},{9,11},{10,... | collective-permute-start | bytes 1544 | tf_op jit(solution)/shard_map/ppermute | solution.py:156
  135.8 2.0 %collective-permute-done.8 = f32[128]{0:T(128)S(1)} collective-permute-done((f32[128]{0:T(128)S(1)}, f32[128]{0:T(128)S(1)}, u32[]{:S(2)}, u32[]{:S(2)}) %collective-permute-start.8) | collective-permute-done | bytes 544 | tf_op jit(solution)/shard_map/ppermute | solution.py:156
  137.8 7.7 %collective-permute-start.9 = (f32[128]{0:T(128)S(1)}, f32[128]{0:T(128)S(1)}, u32[]{:S(2)}, u32[]{:S(2)}) collective-permute-start(f32[128]{0:T(128)S(1)} %add.210), channel_id=1, source_target_pairs={{0,4},{1,5},{2,6},{3,7},{4,0},{5,1},{6,2},{7,3},{8,12},{9,13},{10,... | collective-permute-start | bytes 1544 | tf_op jit(solution)/shard_map/ppermute | solution.py:156
  145.5 1.6 %collective-permute-done.9 = f32[128]{0:T(128)S(1)} collective-permute-done((f32[128]{0:T(128)S(1)}, f32[128]{0:T(128)S(1)}, u32[]{:S(2)}, u32[]{:S(2)}) %collective-permute-start.9) | collective-permute-done | bytes 544 | tf_op jit(solution)/shard_map/ppermute | solution.py:156
  147.4 0.9 copy.103
  (136 shorter events, 9.9 us)
Async XLA Ops:
  1.4 32.6 %collective-permute-start = (bf16[6,3,1024]{2,0,1:T(8,128)(2,1)}, bf16[6,3,1024]{2,0,1:T(8,128)(2,1)}, u32[]{:S(2)}, u32[]{:S(2)}) collective-permute-start(bf16[6,3,1024]{2,0,1:T(8,128)(2,1)} %slice.237), channel_id=1, source_target_pairs={{0,8},{8,16},{16,24},{24,32},{32,40},{40,48},{48,56},{56,64},{64,7... | collective-permute-start | bytes 110600 | tf_op jit(solution)/shard_map/ppermute | solution.py:18
  3.4 13.9 %copy-start.33 = (s32[1,128]{1,0:T(1,128)}, s32[1,128]{1,0:T(1,128)S(1)}, u32[]{:S(2)}) copy-start(s32[1,128]{1,0:T(1,128)S(1)} %iota_add_fusion) | copy-start | bytes 1540
  5.7 5.6 %copy-start.30 = (s32[128]{0:T(128)}, s32[128]{0:T(128)S(1)}, u32[]{:S(2)}) copy-start(s32[128]{0:T(128)S(1)} %select_reduce_fusion) | copy-start | bytes 1540
  22.8 5.8 %copy-start.3 = (f32[16,64]{1,0:T(8,128)}, f32[16,64]{1,0:T(8,128)S(1)}, u32[]{:S(2)}) copy-start(f32[16,64]{1,0:T(8,128)S(1)} %get-tuple-element.17) | copy-start | bytes 12292
  22.8 5.8 %copy-start.5 = (f32[16,64]{1,0:T(8,128)}, f32[16,64]{1,0:T(8,128)S(1)}, u32[]{:S(2)}) copy-start(f32[16,64]{1,0:T(8,128)S(1)} %get-tuple-element.18) | copy-start | bytes 12292
  24.1 5.1 %copy-start.2 = (bf16[128,3,1024]{2,0,1:T(8,128)(2,1)S(1)}, bf16[128,3,1024]{2,0,1:T(8,128)(2,1)}, u32[]{:S(2)}) copy-start(bf16[128,3,1024]{2,0,1:T(8,128)(2,1)} %param.8) | copy-start | bytes 2359300
  28.7 1.0 copy-start.31
  28.7 1.6 %copy-start.34 = (s32[1,128]{1,0:T(1,128)S(1)}, s32[1,128]{1,0:T(1,128)}, u32[]{:S(2)}) copy-start(s32[1,128]{1,0:T(1,128)} %copy-done.33) | copy-start | bytes 1540
  28.7 2.2 %copy-start.14 = (f32[1,3,1024]{2,0,1:T(1,128)S(1)}, f32[1,3,1024]{2,0,1:T(1,128)}, u32[]{:S(2)}) copy-start(f32[1,3,1024]{2,0,1:T(1,128)} %get-tuple-element.37) | copy-start | bytes 36868
  32.0 3.3 %copy-start.7 = (f32[3,1024]{1,0:T(4,128)S(1)}, f32[3,1024]{1,0:T(4,128)}, u32[]{:S(2)}) copy-start(f32[3,1024]{1,0:T(4,128)} %get-tuple-element.75) | copy-start | bytes 36868
  32.0 3.3 %copy-start.8 = (f32[3,1024]{1,0:T(4,128)S(1)}, f32[3,1024]{1,0:T(4,128)}, u32[]{:S(2)}) copy-start(f32[3,1024]{1,0:T(4,128)} %get-tuple-element.76) | copy-start | bytes 36868
  32.0 3.3 %copy-start.9 = (f32[3,1024]{1,0:T(4,128)S(1)}, f32[3,1024]{1,0:T(4,128)}, u32[]{:S(2)}) copy-start(f32[3,1024]{1,0:T(4,128)} %get-tuple-element.77) | copy-start | bytes 36868
  32.0 3.3 %copy-start.10 = (f32[3,1024]{1,0:T(4,128)S(1)}, f32[3,1024]{1,0:T(4,128)}, u32[]{:S(2)}) copy-start(f32[3,1024]{1,0:T(4,128)} %get-tuple-element.78) | copy-start | bytes 36868
  32.0 3.3 %copy-start.11 = (f32[3,1024]{1,0:T(4,128)S(1)}, f32[3,1024]{1,0:T(4,128)}, u32[]{:S(2)}) copy-start(f32[3,1024]{1,0:T(4,128)} %get-tuple-element.73) | copy-start | bytes 36868
  32.0 3.3 %copy-start.12 = (f32[3,1024]{1,0:T(4,128)S(1)}, f32[3,1024]{1,0:T(4,128)}, u32[]{:S(2)}) copy-start(f32[3,1024]{1,0:T(4,128)} %get-tuple-element.74) | copy-start | bytes 36868
  32.0 3.3 %copy-start.23 = (pred[128]{0:T(512)(128)(4,1)S(1)}, pred[128]{0:T(512)(128)(4,1)}, u32[]{:S(2)}) copy-start(pred[128]{0:T(512)(128)(4,1)} %get-tuple-element.66) | copy-start | bytes 388
  32.0 3.3 %copy-start.24 = (pred[128]{0:T(512)(128)(4,1)S(1)}, pred[128]{0:T(512)(128)(4,1)}, u32[]{:S(2)}) copy-start(pred[128]{0:T(512)(128)(4,1)} %get-tuple-element.67) | copy-start | bytes 388
  32.0 3.3 %copy-start.25 = (pred[128]{0:T(512)(128)(4,1)S(1)}, pred[128]{0:T(512)(128)(4,1)}, u32[]{:S(2)}) copy-start(pred[128]{0:T(512)(128)(4,1)} %get-tuple-element.68) | copy-start | bytes 388
  32.0 3.3 %copy-start.26 = (pred[128]{0:T(512)(128)(4,1)S(1)}, pred[128]{0:T(512)(128)(4,1)}, u32[]{:S(2)}) copy-start(pred[128]{0:T(512)(128)(4,1)} %get-tuple-element.69) | copy-start | bytes 388
  32.0 3.3 %copy-start.27 = (pred[128]{0:T(512)(128)(4,1)S(1)}, pred[128]{0:T(512)(128)(4,1)}, u32[]{:S(2)}) copy-start(pred[128]{0:T(512)(128)(4,1)} %get-tuple-element.70) | copy-start | bytes 388
  32.0 3.3 %copy-start.28 = (pred[128]{0:T(512)(128)(4,1)S(1)}, pred[128]{0:T(512)(128)(4,1)}, u32[]{:S(2)}) copy-start(pred[128]{0:T(512)(128)(4,1)} %get-tuple-element.71) | copy-start | bytes 388
  32.0 3.3 %copy-start.29 = (pred[128]{0:T(512)(128)(4,1)S(1)}, pred[128]{0:T(512)(128)(4,1)}, u32[]{:S(2)}) copy-start(pred[128]{0:T(512)(128)(4,1)} %get-tuple-element.72) | copy-start | bytes 388
  41.0 1.0 copy-start
  41.0 1.2 copy-start.1
  49.6 5.1 %copy-start.13 = (f32[2,16,64]{2,1,0:T(8,128)S(1)}, f32[2,16,64]{2,1,0:T(8,128)}, u32[]{:S(2)}) copy-start(f32[2,16,64]{2,1,0:T(8,128)} %maximum_multiply_fusion.1) | copy-start | bytes 24580
  49.6 5.8 %copy-start.4 = (f32[16,64]{1,0:T(8,128)S(1)}, f32[16,64]{1,0:T(8,128)}, u32[]{:S(2)}) copy-start(f32[16,64]{1,0:T(8,128)} %copy-done.3) | copy-start | bytes 12292
  49.6 5.8 %copy-start.6 = (f32[16,64]{1,0:T(8,128)S(1)}, f32[16,64]{1,0:T(8,128)}, u32[]{:S(2)}) copy-start(f32[16,64]{1,0:T(8,128)} %copy-done.5) | copy-start | bytes 12292
  51.1 9.0 %collective-permute-start.1 = (f32[2,16,1024]{2,1,0:T(8,128)S(1)}, f32[2,16,1024]{2,1,0:T(8,128)S(1)}, u32[]{:S(2)}, u32[]{:S(2)}) collective-permute-start(f32[2,16,1024]{2,1,0:T(8,128)S(1)} %reshape.209), channel_id=1, source_target_pairs={{0,8},{8,16},{16,24},{24,32},{32,40},{40,48},{48,56},{56,64},{64,7... | collective-permute-start | bytes 393224 | tf_op jit(solution)/shard_map/ppermute | solution.py:18
  60.1 9.0 %collective-permute-start.2 = (f32[2,16,1024]{2,1,0:T(8,128)S(1)}, f32[2,16,1024]{2,1,0:T(8,128)S(1)}, u32[]{:S(2)}, u32[]{:S(2)}) collective-permute-start(f32[2,16,1024]{2,1,0:T(8,128)S(1)} %collective-permute-done.1), channel_id=1, source_target_pairs={{0,8},{8,16},{16,24},{24,32},{32,40},{40,48},{48,56},{56,64},{64,7... | collective-permute-start | bytes 393224 | tf_op jit(solution)/shard_map/ppermute | solution.py:18
  63.7 1.5 copy-start.17
  63.7 1.5 copy-start.18
  63.7 1.5 copy-start.19
  63.7 1.5 copy-start.20
  69.1 9.7 %collective-permute-start.3 = (f32[2,16,1024]{2,1,0:T(8,128)S(1)}, f32[2,16,1024]{2,1,0:T(8,128)S(1)}, u32[]{:S(2)}, u32[]{:S(2)}) collective-permute-start(f32[2,16,1024]{2,1,0:T(8,128)S(1)} %maximum_add_fusion), channel_id=1, source_target_pairs={{0,16},{8,24},{16,32},{24,40},{32,48},{40,56},{48,64},{56,72},{64,... | collective-permute-start | bytes 393224 | tf_op jit(solution)/shard_map/ppermute | solution.py:18
  78.8 8.8 %collective-permute-start.4 = (f32[2,16,1024]{2,1,0:T(8,128)S(1)}, f32[2,16,1024]{2,1,0:T(8,128)S(1)}, u32[]{:S(2)}, u32[]{:S(2)}) collective-permute-start(f32[2,16,1024]{2,1,0:T(8,128)S(1)} %maximum_add_fusion.1), channel_id=1, source_target_pairs={{0,32},{8,40},{16,48},{24,56},{32,64},{40,72},{48,80},{56,88},{64,... | collective-permute-start | bytes 393224 | tf_op jit(solution)/shard_map/ppermute | solution.py:18
  81.5 1.4 copy-start.15
  81.5 1.4 copy-start.16
  87.7 8.3 %collective-permute-start.5 = (f32[2,16,1024]{2,1,0:T(8,128)S(1)}, f32[2,16,1024]{2,1,0:T(8,128)S(1)}, u32[]{:S(2)}, u32[]{:S(2)}) collective-permute-start(f32[2,16,1024]{2,1,0:T(8,128)S(1)} %maximum_add_fusion.2), channel_id=1, source_target_pairs={{0,64},{8,72},{16,80},{24,88},{32,96},{40,104},{48,112},{56,120},{... | collective-permute-start | bytes 393224 | tf_op jit(solution)/shard_map/ppermute | solution.py:18
  96.0 25.1 %collective-permute-start.6 = (f32[2,16,1024]{2,1,0:T(8,128)S(1)}, f32[2,16,1024]{2,1,0:T(8,128)S(1)}, u32[]{:S(2)}, u32[]{:S(2)}) collective-permute-start(f32[2,16,1024]{2,1,0:T(8,128)S(1)} %maximum_add_fusion.3), channel_id=1, source_target_pairs={{0,128},{8,136},{16,144},{24,152},{32,160},{40,168},{48,176},{56,1... | collective-permute-start | bytes 393224 | tf_op jit(solution)/shard_map/ppermute | solution.py:18
  121.1 0.6 copy-start.32
  121.7 3.4 %copy-start.21 = (f32[1024]{0:T(1024)S(1)}, f32[1024]{0:T(1024)}, u32[]{:S(2)}) copy-start(f32[1024]{0:T(1024)} %param.13) | copy-start | bytes 12292
  125.2 22.0 %copy-start.22 = (f32[1024]{0:T(1024)S(1)}, f32[1024]{0:T(1024)}, u32[]{:S(2)}) copy-start(f32[1024]{0:T(1024)} %param.14) | copy-start | bytes 12292
  125.4 5.5 %collective-permute-start.7 = (f32[128]{0:T(128)S(1)}, f32[128]{0:T(128)S(1)}, u32[]{:S(2)}, u32[]{:S(2)}) collective-permute-start(f32[128]{0:T(128)S(1)} %get-tuple-element.14), channel_id=1, source_target_pairs={{0,1},{1,0},{2,3},{3,2},{4,5},{5,4},{6,7},{7,6},{8,9},{9,8},{10,11... | collective-permute-start | bytes 1544 | tf_op jit(solution)/shard_map/ppermute | solution.py:156
  130.8 7.0 %collective-permute-start.8 = (f32[128]{0:T(128)S(1)}, f32[128]{0:T(128)S(1)}, u32[]{:S(2)}, u32[]{:S(2)}) collective-permute-start(f32[128]{0:T(128)S(1)} %add.209), channel_id=1, source_target_pairs={{0,2},{1,3},{2,0},{3,1},{4,6},{5,7},{6,4},{7,5},{8,10},{9,11},{10,... | collective-permute-start | bytes 1544 | tf_op jit(solution)/shard_map/ppermute | solution.py:156
  137.8 9.4 %collective-permute-start.9 = (f32[128]{0:T(128)S(1)}, f32[128]{0:T(128)S(1)}, u32[]{:S(2)}, u32[]{:S(2)}) collective-permute-start(f32[128]{0:T(128)S(1)} %add.210), channel_id=1, source_target_pairs={{0,4},{1,5},{2,6},{3,7},{4,0},{5,1},{6,2},{7,3},{8,12},{9,13},{10,... | collective-permute-start | bytes 1544 | tf_op jit(solution)/shard_map/ppermute | solution.py:156

commit v5 on v4

--- a/solution.py
+++ b/solution.py
@@ -9,6 +9,7 @@
 
 
 HIGHEST = lax.Precision.HIGHEST
+HIGH = lax.Precision.HIGH
 EPSILON = 1e-06
 
 
@@ -47,7 +48,7 @@
     entering = jnp.stack([enter_re, -enter_im])
     leaving = jnp.stack([power_re[:, :, block - 1 :: -1], power_im[:, :, block - 1 :: -1]])
     stepping = jnp.stack([power_re[:, :, block].T, power_im[:, :, block].T])
-    return (toeplitz(response), entering, leaving, stepping)
+    return (response, entering, leaving, stepping)
 
 
 def complex_times(factor_one, factor_two):
@@ -59,19 +60,18 @@
     )
 
 
-def block_terms(tables, columns, block_positions, block_starts):
-    matrix_table, entering, leaving, stepping = tables
+def inside_terms(matrix_table, columns, block_positions, block_starts):
     same_genome = (block_positions[None, :] >= block_starts[:, None]).astype(jnp.float32)
-    inside = jnp.einsum(
-        "gts,gis->git", matrix_table * same_genome[None], columns, precision=HIGHEST
-    )
+    return jnp.einsum("gts,gis->git", matrix_table * same_genome[None], columns, precision=HIGH)
+
+
+def fresh_terms(leaving, columns, block_positions, block_starts):
     tail_mask = (block_positions >= block_starts[-1]).astype(jnp.float32)
-    fresh_state = jnp.einsum("rgns,gis->rngi", leaving * tail_mask, columns, precision=HIGHEST)
-    return (inside, fresh_state)
+    return jnp.einsum("rgns,gis->rngi", leaving * tail_mask, columns, precision=HIGH)
 
 
 def carried(entering, carry_state):
-    return jnp.einsum("rgnt,rngi->git", entering, carry_state, precision=HIGHEST)
+    return jnp.einsum("rgnt,rngi->git", entering, carry_state, precision=HIGH)
 
 
 def short_filter(padded, taps_part, positions, genome_start):
@@ -112,12 +112,11 @@
     freshes = []
     keepers = []
     span_index = 0
-    inside, fresh_state = block_terms(
-        tables, values[span_index], span_pos[span_index], span_begin[span_index]
+    fresh_state = fresh_terms(
+        tables[2], values[span_index], span_pos[span_index], span_begin[span_index]
     )
     keep_state = span_begin[span_index, -1] < span_pos[span_index, 0]
     summary = jnp.where(keep_state, complex_times(stepping[..., None], summary), 0.0) + fresh_state
-    insides = [lax.optimization_barrier(inside)]
     freshes.append(fresh_state)
     keepers.append(keep_state)
     device_count = lax.axis_size("ctx")
@@ -132,6 +131,11 @@
         return jnp.repeat(factor, group_width, axis=2)
 
     running = passed_along(summary.reshape(2, mode_count, channels), "ctx", 1)
+    response, running = lax.optimization_barrier((tables[0], running))
+    inside = inside_terms(
+        toeplitz(response), values[span_index], span_pos[span_index], span_begin[span_index]
+    )
+    insides = [lax.optimization_barrier(inside)]
     power = stepping
     distance = 1
     while distance < reach:

time: 149 us -> 131 us (0.88)
  the two profiles are of different devices: /device:TPU:128 before, /device:TPU:162 now
where the time goes in v5:
time: 131 us
  starting transfers between devices  38.5 us (29%)
  waiting for transfers between devices  34 us (26%)
  local copies, waits for them, and re-layouts  20.7 us (16%)
  other arithmetic  18.2 us (14%)
  matrix products  14.4 us (11%)
  between operations  4.74 us (4%)
    ppermute x7, starting transfers between devices, passed_along(): return lax.ppermute(block, axis, route)  30.1 us
    ppermute x7, waiting for transfers between devices, passed_along(): return lax.ppermute(block, axis, route)  20.7 us
    ppermute x3, waiting for transfers between devices, on_device(): squares = squares + lax.ppermute(squares, 'tp', pairs)  13.3 us
    ppermute x3, starting transfers between devices, on_device(): squares = squares + lax.ppermute(squares, 'tp', pairs)  8.47 us
    add x1, other arithmetic, short_filter(): result = result + jnp.where(keep_tap, taps_part[offset][None] * window, 0.0)  5.63 us
    dot_general x1, matrix products, inside_terms(): jnp.einsum('gts,gis->git', matrix_table * same_genome[None], columns, pre...  4.91 us
    mul x1, other arithmetic, pole_tables(): power_re = magnitude * jnp.cos(angle[:, :, None] * counter)  3.86 us
    dot_general x1, matrix products, fresh_terms(): jnp.einsum('rgns,gis->rngi', leaving * tail_mask, columns, precision=HIGH)  3.76 us
  transfers between devices with their start and end apart: 10, of which 7 were waited for; matrix products, arithmetic and copies ran while one was open for 26% of the time, Pallas kernels for 0%

profile of v5, /device:TPU:162, one launch (start us, length us, event | category | flops | bytes accessed | tf_op | source)
XLA Modules:
  0.0 130.6 jit_solution(5431031949029932945)
XLA Ops:
  0.0 0.8 slice.237
  0.8 1.9 %collective-permute-start = (bf16[6,3,1024]{2,0,1:T(8,128)(2,1)S(1)}, bf16[6,3,1024]{2,0,1:T(8,128)(2,1)S(1)}, u32[]{:S(2)}, u32[]{:S(2)}) collective-permute-start(bf16[6,3,1024]{2,0,1:T(8,128)(2,1)S(1)} %slice.237), channel_id=1, source_target_pairs={{0,8},{8,16},{16,24},{24,32},{32,40},{40,48},{48,56},{56,64},{64,7... | collective-permute-start | bytes 110600 | tf_op jit(solution)/shard_map/ppermute | solution.py:19
  2.8 0.8 reduce-window.9
  3.6 1.4 %and_reduce_fusion = (pred[]{:T(512)}, pred[]{:T(512)}, pred[]{:T(512)}, pred[]{:T(512)}, pred[]{:T(512)}, /*index=5*/s32[4]{0:T(128)S(1)}) fusion(s32[]{:T(128)S(6)} %sub.135, s32[]{:T(128)S(6)} %sub.123, s32[]{:T(128)S(6)} %sub.132, s32[]{:T(128)S(6)} %sub.129, s32[]{:T(128)S(6)} %sub.126, s32[]{:T(128)S(6)} %sub.122, s32[4]{0:T(128)} %param.15, ...), kind=kLoop, calls=%fused_computation.108 | loop fusion | flops 63 | bytes 77 | tf_op jit(solution)/shard_map/reduce_or | solution.py:128
  5.2 0.6 slice.260
  5.8 1.5 %fusion.34 = (f32[1,3,1024]{2,0,1:T(1,128)S(1)}, f32[1,3,1024]{2,0,1:T(1,128)S(1)}, f32[1,3,1024]{2,0,1:T(1,128)S(1)}, f32[1,3,1024]{2,0,1:T(1,128)S(1)}, f32[1,...) fusion(f32[7,3,1024]{2,0,1:T(8,128)} %param.9), kind=kLoop, calls=%fused_computation.133 | loop fusion | bytes 172032 | tf_op jit(solution)/shard_map/slice | solution.py:84
  7.2 0.6 broadcast_compare_fusion.1
  7.9 0.8 copy.93
  8.7 0.7 neg.7
  9.4 0.7 slice_bitcast_fusion.12
  10.3 3.9 %fusion.8 = (f32[64,16,129]{2,1,0:T(8,128)S(1)}, f32[64,16,129]{2,1,0:T(8,128)S(1)}) fusion(f32[64,16]{1,0:T(8,128)S(1)} %copy.93, f32[129]{0:T(256)S(1)} %iota_convert_fusion, f32[64,16]{1,0:T(8,128)S(1)} %copy.92), kind=kLoop, calls=%fused_computation.24 | loop fusion | flops 528384 | bytes 1065476 | tf_op jit(solution)/shard_map/mul | solution.py:39
  15.5 0.6 subtract_bitcast_fusion.1
  16.1 0.6 multiply_bitcast_fusion
  16.7 0.6 slice_bitcast_fusion.2
  18.0 1.7 %subtract_bitcast_fusion = (f32[1,64,16,128]{3,2,0,1:T(8,128)}, f32[64,128]{1,0:T(8,128)S(1)}, f32[1,64,16,128]{3,2,0,1:T(8,128)}, f32[64,16,128]{2,1,0:T(8,128)S(1)}, f32[64,16,128]{2,1,0:T(8,128)S(1)}) fusion(f32[64,16,129]{2,1,0:T(8,128)S(1)} %get-tuple-element.49, f32[64,16,129]{2,1,0:T(8,128)S(1)} %get-tuple-element.48, f32[64,16]{1,0:T(8,128)S(1)} %copy.94, ...), kind=kLoop, calls=%fused_computation.47 | loop fusion | flops 1433600 | bytes 4235264 | tf_op jit(solution)/shard_map/stack | solution.py:48
  19.8 0.5 compare_convert_fusion.1
  20.4 1.5 %copy.88 = bf16[128,3,1024]{0,2,1:T(8,128)(2,1)S(1)} copy(bf16[128,3,1024]{2,0,1:T(8,128)(2,1)} %param.8) | data formatting | bytes 1572864 | tf_op args[0]
  21.9 0.9 copy.97
  22.9 0.6 slice.256
  24.1 1.0 rev.7
  25.2 1.0 rev.6
  26.6 5.6 %select_add_fusion = f32[128,3,1024]{0,2,1:T(8,128)S(1)} fusion(bf16[128,3,1024]{0,2,1:T(8,128)(2,1)S(1)} %copy.88, bf16[6,3,1024]{0,2,1:T(8,128)(2,1)S(1)} %copy.89, f32[3,1024]{1,0:T(4,128)S(1)} %get-tuple-element.77, f32[3,1024]{1,0:T(4,128)S(1)} %get-tuple-element.78, f32[3,1024]{1,0:T(4,128)S(1)} %get-tuple-element.79, ...), kind=kLoop, calls=%fused_computation.16 | loop fusion | flops 17694720 | bytes 2483072 | tf_op jit(solution)/shard_map/add | solution.py:84
  32.4 0.9 copy-done
  33.5 3.8 %fusion.5 = f32[2,16,64,16]{1,3,0,2:T(8,128)S(1)} fusion(f32[64,16,128,1]{2,1,3,0:T(8,128)S(1)} %bitcast.164, f32[2,16,64,16]{1,3,0,2:T(8,128)S(1)} %copy.97, pred[]{:T(512)S(6)} %lt.13, f32[1,64,16,128]{3,2,1,0:T(8,128)S(1)} %bitcast.166, f32[1,64,16,128]{3,2,1,0:T(8,128)S(1)} %bitcast.167, f32[128]{0:T(128)S(1)} %compare_convert_fusion.1), kind=kOutput, calls=%fused_computation.20 | convolution fusion | flops 25755648 | bytes 1835521 | tf_op jit(solution)/shard_map/rgns,gis->rngi/dot_general | solution.py:70
  37.2 0.9 copy.99
  38.1 0.6 reshape.209
  38.8 2.7 %collective-permute-start.1 = (f32[2,16,1024]{2,1,0:T(8,128)S(1)}, f32[2,16,1024]{2,1,0:T(8,128)S(1)}, u32[]{:S(2)}, u32[]{:S(2)}) collective-permute-start(f32[2,16,1024]{2,1,0:T(8,128)S(1)} %reshape.209), channel_id=1, source_target_pairs={{0,8},{8,16},{16,24},{24,32},{32,40},{40,48},{48,56},{56,64},{64,7... | collective-permute-start | bytes 393224 | tf_op jit(solution)/shard_map/ppermute | solution.py:19
  42.1 5.6 %collective-permute-done.1 = f32[2,16,1024]{2,1,0:T(8,128)S(1)} collective-permute-done((f32[2,16,1024]{2,1,0:T(8,128)S(1)}, f32[2,16,1024]{2,1,0:T(8,128)S(1)}, u32[]{:S(2)}, u32[]{:S(2)}) %collective-permute-start.1) | collective-permute-done | bytes 131104 | tf_op jit(solution)/shard_map/ppermute | solution.py:19
  47.7 2.1 %collective-permute-start.2 = (f32[2,16,1024]{2,1,0:T(8,128)S(1)}, f32[2,16,1024]{2,1,0:T(8,128)S(1)}, u32[]{:S(2)}, u32[]{:S(2)}) collective-permute-start(f32[2,16,1024]{2,1,0:T(8,128)S(1)} %collective-permute-done.1), channel_id=1, source_target_pairs={{0,8},{8,16},{16,24},{24,32},{32,40},{40,48},{48,56},{56,64},{64,7... | collective-permute-start | bytes 393224 | tf_op jit(solution)/shard_map/ppermute | solution.py:19
  53.2 3.5 %collective-permute-done.2 = f32[2,16,1024]{2,1,0:T(8,128)S(1)} collective-permute-done((f32[2,16,1024]{2,1,0:T(8,128)S(1)}, f32[2,16,1024]{2,1,0:T(8,128)S(1)}, u32[]{:S(2)}, u32[]{:S(2)}) %collective-permute-start.2) | collective-permute-done | bytes 131104 | tf_op jit(solution)/shard_map/ppermute | solution.py:19
  56.8 1.9 %collective-permute-start.3 = (f32[2,16,1024]{2,1,0:T(8,128)S(1)}, f32[2,16,1024]{2,1,0:T(8,128)S(1)}, u32[]{:S(2)}, u32[]{:S(2)}) collective-permute-start(f32[2,16,1024]{2,1,0:T(8,128)S(1)} %maximum_add_fusion), channel_id=1, source_target_pairs={{0,16},{8,24},{16,32},{24,40},{32,48},{40,56},{48,64},{56,72},{64,... | collective-permute-start | bytes 393224 | tf_op jit(solution)/shard_map/ppermute | solution.py:19
  58.7 7.6 %collective-permute-done.3 = f32[2,16,1024]{2,1,0:T(8,128)S(1)} collective-permute-done((f32[2,16,1024]{2,1,0:T(8,128)S(1)}, f32[2,16,1024]{2,1,0:T(8,128)S(1)}, u32[]{:S(2)}, u32[]{:S(2)}) %collective-permute-start.3) | collective-permute-done | bytes 131104 | tf_op jit(solution)/shard_map/ppermute | solution.py:19
  66.4 1.9 %collective-permute-start.4 = (f32[2,16,1024]{2,1,0:T(8,128)S(1)}, f32[2,16,1024]{2,1,0:T(8,128)S(1)}, u32[]{:S(2)}, u32[]{:S(2)}) collective-permute-start(f32[2,16,1024]{2,1,0:T(8,128)S(1)} %maximum_add_fusion.1), channel_id=1, source_target_pairs={{0,32},{8,40},{16,48},{24,56},{32,64},{40,72},{48,80},{56,88},{64,... | collective-permute-start | bytes 393224 | tf_op jit(solution)/shard_map/ppermute | solution.py:19
  71.2 4.0 %collective-permute-done.4 = f32[2,16,1024]{2,1,0:T(8,128)S(1)} collective-permute-done((f32[2,16,1024]{2,1,0:T(8,128)S(1)}, f32[2,16,1024]{2,1,0:T(8,128)S(1)}, u32[]{:S(2)}, u32[]{:S(2)}) %collective-permute-start.4) | collective-permute-done | bytes 131104 | tf_op jit(solution)/shard_map/ppermute | solution.py:19
  75.2 4.2 %collective-permute-start.5 = (f32[2,16,1024]{2,1,0:T(8,128)S(1)}, f32[2,16,1024]{2,1,0:T(8,128)S(1)}, u32[]{:S(2)}, u32[]{:S(2)}) collective-permute-start(f32[2,16,1024]{2,1,0:T(8,128)S(1)} %maximum_add_fusion.2), channel_id=1, source_target_pairs={{0,64},{8,72},{16,80},{24,88},{32,96},{40,104},{48,112},{56,120},{... | collective-permute-start | bytes 393224 | tf_op jit(solution)/shard_map/ppermute | solution.py:19
  79.4 3.2 %fusion.4 = f32[64,128,128]{2,0,1:T(8,128)S(1)} fusion(s32[128,128]{1,0:T(8,128)S(1)} %iota_subtract_fusion, f32[128,128]{1,0:T(8,128)S(1)} %compare_convert_fusion, f32[64,128]{1,0:T(8,128)S(1)} %get-tuple-element.11), kind=kOutput, calls=%fused_computation.15 | convolution fusion | flops 1613758464 | bytes 4358144 | tf_op jit(solution)/shard_map/gk,kts->gts/dot_general | solution.py:33
  82.8 15.3 %collective-permute-start.6 = (f32[2,16,1024]{2,1,0:T(8,128)S(1)}, f32[2,16,1024]{2,1,0:T(8,128)S(1)}, u32[]{:S(2)}, u32[]{:S(2)}) collective-permute-start(f32[2,16,1024]{2,1,0:T(8,128)S(1)} %maximum_add_fusion.3), channel_id=1, source_target_pairs={{0,128},{8,136},{16,144},{24,152},{32,160},{40,168},{48,176},{56,1... | collective-permute-start | bytes 393224 | tf_op jit(solution)/shard_map/ppermute | solution.py:19
  98.1 4.9 %fusion.1 = f32[64,16,128]{2,1,0:T(8,128)S(1)} fusion(f32[64,16,128]{2,1,0:T(8,128)S(1)} %bitcast.165, f32[64,128,128]{2,0,1:T(8,128)S(1)} %fusion.4), kind=kOutput, calls=%fused_computation.2 | convolution fusion | flops 100663296 | bytes 5242880 | tf_op jit(solution)/shard_map/gts,gis->git/dot_general | solution.py:65
  103.0 0.7 maximum_add_fusion.4
  103.7 1.3 reshape.210
  105.0 2.4 %fusion.7 = f32[64,16,128]{2,1,0:T(8,128)S(1)} fusion(f32[64,16,128]{2,1,0:T(8,128)S(1)} %fusion.1, f32[1,64,16,128]{3,2,0,1:T(8,128)} %get-tuple-element.26, f32[1,64,16,128]{3,2,0,1:T(8,128)S(1)} %copy-done.2, f32[2,16,64,16]{3,2,1,0:T(8,128)S(1)} %reshape.210, pred[128]{0:T(512)(128)(4,1)S(1)} %copy-done.21), kind=kOutput, calls=%fused_computation.23 | convolution fusion | flops 25690112 | bytes 2228352 | tf_op jit(solution)/shard_map/rgnt,rngi->git/dot_general | solution.py:74
  107.7 2.4 %collective-permute-start.7 = (f32[128]{0:T(128)S(1)}, f32[128]{0:T(128)S(1)}, u32[]{:S(2)}, u32[]{:S(2)}) collective-permute-start(f32[128]{0:T(128)S(1)} %get-tuple-element.18), channel_id=1, source_target_pairs={{0,1},{1,0},{2,3},{3,2},{4,5},{5,4},{6,7},{7,6},{8,9},{9,8},{10,11... | collective-permute-start | bytes 1544 | tf_op jit(solution)/shard_map/ppermute | solution.py:160
  110.2 3.0 %collective-permute-done.7 = f32[128]{0:T(128)S(1)} collective-permute-done((f32[128]{0:T(128)S(1)}, f32[128]{0:T(128)S(1)}, u32[]{:S(2)}, u32[]{:S(2)}) %collective-permute-start.7) | collective-permute-done | bytes 544 | tf_op jit(solution)/shard_map/ppermute | solution.py:160
  113.2 4.0 %collective-permute-start.8 = (f32[128]{0:T(128)S(1)}, f32[128]{0:T(128)S(1)}, u32[]{:S(2)}, u32[]{:S(2)}) collective-permute-start(f32[128]{0:T(128)S(1)} %add.209), channel_id=1, source_target_pairs={{0,2},{1,3},{2,0},{3,1},{4,6},{5,7},{6,4},{7,5},{8,10},{9,11},{10,... | collective-permute-start | bytes 1544 | tf_op jit(solution)/shard_map/ppermute | solution.py:160
  117.2 2.9 %collective-permute-done.8 = f32[128]{0:T(128)S(1)} collective-permute-done((f32[128]{0:T(128)S(1)}, f32[128]{0:T(128)S(1)}, u32[]{:S(2)}, u32[]{:S(2)}) %collective-permute-start.8) | collective-permute-done | bytes 544 | tf_op jit(solution)/shard_map/ppermute | solution.py:160
  120.2 2.0 %collective-permute-start.9 = (f32[128]{0:T(128)S(1)}, f32[128]{0:T(128)S(1)}, u32[]{:S(2)}, u32[]{:S(2)}) collective-permute-start(f32[128]{0:T(128)S(1)} %add.210), channel_id=1, source_target_pairs={{0,4},{1,5},{2,6},{3,7},{4,0},{5,1},{6,2},{7,3},{8,12},{9,13},{10,... | collective-permute-start | bytes 1544 | tf_op jit(solution)/shard_map/ppermute | solution.py:160
  122.2 7.3 %collective-permute-done.9 = f32[128]{0:T(128)S(1)} collective-permute-done((f32[128]{0:T(128)S(1)}, f32[128]{0:T(128)S(1)}, u32[]{:S(2)}, u32[]{:S(2)}) %collective-permute-start.9) | collective-permute-done | bytes 544 | tf_op jit(solution)/shard_map/ppermute | solution.py:160
  129.7 0.9 copy.103
  (114 shorter events, 7.2 us)
Async XLA Ops:
  0.8 25.3 %collective-permute-start = (bf16[6,3,1024]{2,0,1:T(8,128)(2,1)S(1)}, bf16[6,3,1024]{2,0,1:T(8,128)(2,1)S(1)}, u32[]{:S(2)}, u32[]{:S(2)}) collective-permute-start(bf16[6,3,1024]{2,0,1:T(8,128)(2,1)S(1)} %slice.237), channel_id=1, source_target_pairs={{0,8},{8,16},{16,24},{24,32},{32,40},{40,48},{48,56},{56,64},{64,7... | collective-permute-start | bytes 110600 | tf_op jit(solution)/shard_map/ppermute | solution.py:19
  2.8 6.6 %copy-start.22 = (s32[1,128]{1,0:T(1,128)}, s32[1,128]{1,0:T(1,128)S(1)}, u32[]{:S(2)}) copy-start(s32[1,128]{1,0:T(1,128)S(1)} %iota_add_fusion) | copy-start | bytes 1540
  5.1 2.7 %copy-start.19 = (s32[128]{0:T(128)}, s32[128]{0:T(128)S(1)}, u32[]{:S(2)}) copy-start(s32[128]{0:T(128)S(1)} %select_reduce_fusion) | copy-start | bytes 1540
  18.0 1.7 %copy-start.6 = (f32[16,64]{1,0:T(8,128)S(1)}, f32[16,64]{1,0:T(8,128)}, u32[]{:S(2)}) copy-start(f32[16,64]{1,0:T(8,128)} %get-tuple-element.63) | copy-start | bytes 12292
  18.0 1.7 %copy-start.5 = (f32[16,64]{1,0:T(8,128)S(1)}, f32[16,64]{1,0:T(8,128)}, u32[]{:S(2)}) copy-start(f32[16,64]{1,0:T(8,128)} %get-tuple-element.64) | copy-start | bytes 12292
  19.8 3.1 %copy-start.20 = (s32[128]{0:T(128)S(1)}, s32[128]{0:T(128)}, u32[]{:S(2)}) copy-start(s32[128]{0:T(128)} %copy-done.19) | copy-start | bytes 1540
  19.8 3.7 %copy-start.23 = (s32[1,128]{1,0:T(1,128)S(1)}, s32[1,128]{1,0:T(1,128)}, u32[]{:S(2)}) copy-start(s32[1,128]{1,0:T(1,128)} %copy-done.22) | copy-start | bytes 1540
  22.8 3.8 %copy-start.13 = (pred[128]{0:T(512)(128)(4,1)S(1)}, pred[128]{0:T(512)(128)(4,1)}, u32[]{:S(2)}) copy-start(pred[128]{0:T(512)(128)(4,1)} %get-tuple-element.71) | copy-start | bytes 388
  22.8 3.7 %copy-start.14 = (pred[128]{0:T(512)(128)(4,1)S(1)}, pred[128]{0:T(512)(128)(4,1)}, u32[]{:S(2)}) copy-start(pred[128]{0:T(512)(128)(4,1)} %get-tuple-element.72) | copy-start | bytes 388
  22.9 3.7 %copy-start.15 = (pred[128]{0:T(512)(128)(4,1)S(1)}, pred[128]{0:T(512)(128)(4,1)}, u32[]{:S(2)}) copy-start(pred[128]{0:T(512)(128)(4,1)} %get-tuple-element.73) | copy-start | bytes 388
  22.9 3.7 %copy-start.16 = (pred[128]{0:T(512)(128)(4,1)S(1)}, pred[128]{0:T(512)(128)(4,1)}, u32[]{:S(2)}) copy-start(pred[128]{0:T(512)(128)(4,1)} %get-tuple-element.74) | copy-start | bytes 388
  22.9 3.7 %copy-start.17 = (pred[128]{0:T(512)(128)(4,1)S(1)}, pred[128]{0:T(512)(128)(4,1)}, u32[]{:S(2)}) copy-start(pred[128]{0:T(512)(128)(4,1)} %get-tuple-element.75) | copy-start | bytes 388
  22.9 3.7 %copy-start.18 = (pred[128]{0:T(512)(128)(4,1)S(1)}, pred[128]{0:T(512)(128)(4,1)}, u32[]{:S(2)}) copy-start(pred[128]{0:T(512)(128)(4,1)} %get-tuple-element.76) | copy-start | bytes 388
  32.3 1.0 copy-start
  32.3 1.2 copy-start.1
  38.8 9.0 %collective-permute-start.1 = (f32[2,16,1024]{2,1,0:T(8,128)S(1)}, f32[2,16,1024]{2,1,0:T(8,128)S(1)}, u32[]{:S(2)}, u32[]{:S(2)}) collective-permute-start(f32[2,16,1024]{2,1,0:T(8,128)S(1)} %reshape.209), channel_id=1, source_target_pairs={{0,8},{8,16},{16,24},{24,32},{32,40},{40,48},{48,56},{56,64},{64,7... | collective-permute-start | bytes 393224 | tf_op jit(solution)/shard_map/ppermute | solution.py:19
  47.7 9.0 %collective-permute-start.2 = (f32[2,16,1024]{2,1,0:T(8,128)S(1)}, f32[2,16,1024]{2,1,0:T(8,128)S(1)}, u32[]{:S(2)}, u32[]{:S(2)}) collective-permute-start(f32[2,16,1024]{2,1,0:T(8,128)S(1)} %collective-permute-done.1), channel_id=1, source_target_pairs={{0,8},{8,16},{16,24},{24,32},{32,40},{40,48},{48,56},{56,64},{64,7... | collective-permute-start | bytes 393224 | tf_op jit(solution)/shard_map/ppermute | solution.py:19
  51.6 1.5 %copy-start.7 = (f32[1,16,64]{2,1,0:T(8,128)S(1)}, f32[1,16,64]{2,1,0:T(8,128)}, u32[]{:S(2)}) copy-start(f32[1,16,64]{2,1,0:T(8,128)} %get-tuple-element.53) | copy-start | bytes 12292
  51.6 1.5 %copy-start.8 = (f32[1,16,64]{2,1,0:T(8,128)S(1)}, f32[1,16,64]{2,1,0:T(8,128)}, u32[]{:S(2)}) copy-start(f32[1,16,64]{2,1,0:T(8,128)} %get-tuple-element.54) | copy-start | bytes 12292
  51.7 1.5 %copy-start.9 = (f32[1,16,64]{2,1,0:T(8,128)S(1)}, f32[1,16,64]{2,1,0:T(8,128)}, u32[]{:S(2)}) copy-start(f32[1,16,64]{2,1,0:T(8,128)} %get-tuple-element.55) | copy-start | bytes 12292
  51.7 1.5 %copy-start.10 = (f32[1,16,64]{2,1,0:T(8,128)S(1)}, f32[1,16,64]{2,1,0:T(8,128)}, u32[]{:S(2)}) copy-start(f32[1,16,64]{2,1,0:T(8,128)} %get-tuple-element.56) | copy-start | bytes 12292
  52.6 15.7 %copy-start.4 = (f32[16,64]{1,0:T(8,128)S(1)}, f32[16,64]{1,0:T(8,128)}, u32[]{:S(2)}) copy-start(f32[16,64]{1,0:T(8,128)} %get-tuple-element.51) | copy-start | bytes 12292
  53.1 15.7 %copy-start.3 = (f32[16,64]{1,0:T(8,128)S(1)}, f32[16,64]{1,0:T(8,128)}, u32[]{:S(2)}) copy-start(f32[16,64]{1,0:T(8,128)} %get-tuple-element.50) | copy-start | bytes 12292
  56.8 9.6 %collective-permute-start.3 = (f32[2,16,1024]{2,1,0:T(8,128)S(1)}, f32[2,16,1024]{2,1,0:T(8,128)S(1)}, u32[]{:S(2)}, u32[]{:S(2)}) collective-permute-start(f32[2,16,1024]{2,1,0:T(8,128)S(1)} %maximum_add_fusion), channel_id=1, source_target_pairs={{0,16},{8,24},{16,32},{24,40},{32,48},{40,56},{48,64},{56,72},{64,... | collective-permute-start | bytes 393224 | tf_op jit(solution)/shard_map/ppermute | solution.py:19
  66.4 8.8 %collective-permute-start.4 = (f32[2,16,1024]{2,1,0:T(8,128)S(1)}, f32[2,16,1024]{2,1,0:T(8,128)S(1)}, u32[]{:S(2)}, u32[]{:S(2)}) collective-permute-start(f32[2,16,1024]{2,1,0:T(8,128)S(1)} %maximum_add_fusion.1), channel_id=1, source_target_pairs={{0,32},{8,40},{16,48},{24,56},{32,64},{40,72},{48,80},{56,88},{64,... | collective-permute-start | bytes 393224 | tf_op jit(solution)/shard_map/ppermute | solution.py:19
  75.2 7.5 %collective-permute-start.5 = (f32[2,16,1024]{2,1,0:T(8,128)S(1)}, f32[2,16,1024]{2,1,0:T(8,128)S(1)}, u32[]{:S(2)}, u32[]{:S(2)}) collective-permute-start(f32[2,16,1024]{2,1,0:T(8,128)S(1)} %maximum_add_fusion.2), channel_id=1, source_target_pairs={{0,64},{8,72},{16,80},{24,88},{32,96},{40,104},{48,112},{56,120},{... | collective-permute-start | bytes 393224 | tf_op jit(solution)/shard_map/ppermute | solution.py:19
  82.8 20.2 %collective-permute-start.6 = (f32[2,16,1024]{2,1,0:T(8,128)S(1)}, f32[2,16,1024]{2,1,0:T(8,128)S(1)}, u32[]{:S(2)}, u32[]{:S(2)}) collective-permute-start(f32[2,16,1024]{2,1,0:T(8,128)S(1)} %maximum_add_fusion.3), channel_id=1, source_target_pairs={{0,128},{8,136},{16,144},{24,152},{32,160},{40,168},{48,176},{56,1... | collective-permute-start | bytes 393224 | tf_op jit(solution)/shard_map/ppermute | solution.py:19
  103.0 2.0 %copy-start.2 = (f32[1,64,16,128]{3,2,0,1:T(8,128)S(1)}, f32[1,64,16,128]{3,2,0,1:T(8,128)}, u32[]{:S(2)}) copy-start(f32[1,64,16,128]{3,2,0,1:T(8,128)} %get-tuple-element.24) | copy-start | bytes 1572868
  103.0 2.0 %copy-start.21 = (pred[128]{0:T(512)(128)(4,1)S(1)}, pred[128]{0:T(512)(128)(4,1)}, u32[]{:S(2)}) copy-start(pred[128]{0:T(512)(128)(4,1)} %get-tuple-element.69) | copy-start | bytes 388
  105.0 2.5 %copy-start.11 = (f32[1024]{0:T(1024)S(1)}, f32[1024]{0:T(1024)}, u32[]{:S(2)}) copy-start(f32[1024]{0:T(1024)} %param.13) | copy-start | bytes 12292
  107.5 22.0 %copy-start.12 = (f32[1024]{0:T(1024)S(1)}, f32[1024]{0:T(1024)}, u32[]{:S(2)}) copy-start(f32[1024]{0:T(1024)} %param.14) | copy-start | bytes 12292
  107.7 5.5 %collective-permute-start.7 = (f32[128]{0:T(128)S(1)}, f32[128]{0:T(128)S(1)}, u32[]{:S(2)}, u32[]{:S(2)}) collective-permute-start(f32[128]{0:T(128)S(1)} %get-tuple-element.18), channel_id=1, source_target_pairs={{0,1},{1,0},{2,3},{3,2},{4,5},{5,4},{6,7},{7,6},{8,9},{9,8},{10,11... | collective-permute-start | bytes 1544 | tf_op jit(solution)/shard_map/ppermute | solution.py:160
  113.2 7.0 %collective-permute-start.8 = (f32[128]{0:T(128)S(1)}, f32[128]{0:T(128)S(1)}, u32[]{:S(2)}, u32[]{:S(2)}) collective-permute-start(f32[128]{0:T(128)S(1)} %add.209), channel_id=1, source_target_pairs={{0,2},{1,3},{2,0},{3,1},{4,6},{5,7},{6,4},{7,5},{8,10},{9,11},{10,... | collective-permute-start | bytes 1544 | tf_op jit(solution)/shard_map/ppermute | solution.py:160
  120.2 9.4 %collective-permute-start.9 = (f32[128]{0:T(128)S(1)}, f32[128]{0:T(128)S(1)}, u32[]{:S(2)}, u32[]{:S(2)}) collective-permute-start(f32[128]{0:T(128)S(1)} %add.210), channel_id=1, source_target_pairs={{0,4},{1,5},{2,6},{3,7},{4,0},{5,1},{6,2},{7,3},{8,12},{9,13},{10,... | collective-permute-start | bytes 1544 | tf_op jit(solution)/shard_map/ppermute | solution.py:160

commit v6 on v5

--- a/solution.py
+++ b/solution.py
@@ -51,6 +51,18 @@
     return (response, entering, leaving, stepping)
 
 
+def pole_exits(rate, angle, block):
+    counter = (block - 1 - jnp.arange(block)).astype(jnp.float32)
+    magnitude = jnp.exp(-rate[:, :, None] * counter)
+    leaving = jnp.stack(
+        [magnitude * jnp.cos(angle[:, :, None] * counter), magnitude * jnp.sin(angle[:, :, None] * counter)]
+    )
+    last = jnp.float32(block)
+    step_size = jnp.exp(-rate * last)
+    stepping = jnp.stack([(step_size * jnp.cos(angle * last)).T, (step_size * jnp.sin(angle * last)).T])
+    return (leaving, stepping)
+
+
 def complex_times(factor_one, factor_two):
     return jnp.stack(
         [
@@ -101,8 +113,7 @@
     padded = jnp.concatenate([before, qkv], axis=0)
     filtered = short_filter(padded, taps, positions, genome_start)
     query, product = lax.optimization_barrier((filtered[:, 0], filtered[:, 1] * filtered[:, 2]))
-    tables = pole_tables(rate, angle, residue, SPAN)
-    stepping = tables[3]
+    leaving, stepping = pole_exits(rate, angle, SPAN)
     values = jnp.transpose(
         product.reshape(span_count, SPAN, group_count, group_width), (0, 2, 3, 1)
     )
@@ -113,7 +124,7 @@
     keepers = []
     span_index = 0
     fresh_state = fresh_terms(
-        tables[2], values[span_index], span_pos[span_index], span_begin[span_index]
+        leaving, values[span_index], span_pos[span_index], span_begin[span_index]
     )
     keep_state = span_begin[span_index, -1] < span_pos[span_index, 0]
     summary = jnp.where(keep_state, complex_times(stepping[..., None], summary), 0.0) + fresh_state
@@ -131,7 +142,9 @@
         return jnp.repeat(factor, group_width, axis=2)
 
     running = passed_along(summary.reshape(2, mode_count, channels), "ctx", 1)
-    response, running = lax.optimization_barrier((tables[0], running))
+    pole_inputs, running = lax.optimization_barrier(((rate, angle, residue), running))
+    tables = pole_tables(*pole_inputs, SPAN)
+    response = tables[0]
     inside = inside_terms(
         toeplitz(response), values[span_index], span_pos[span_index], span_begin[span_index]
     )

time: 131 us -> 130 us (level)
  the two profiles are of different devices: /device:TPU:162 before, /device:TPU:166 now
where the time goes in v6:
time: 130 us
  starting transfers between devices  35.7 us (27%)
  waiting for transfers between devices  26.9 us (21%)
  local copies, waits for them, and re-layouts  24 us (18%)
  other arithmetic  23.4 us (18%)
  matrix products  15.2 us (12%)
  between operations  4.35 us (3%)
    ppermute x7, starting transfers between devices, passed_along(): return lax.ppermute(block, axis, route)  27.7 us
    ppermute x3, waiting for transfers between devices, on_device(): squares = squares + lax.ppermute(squares, 'tp', pairs)  13.8 us
    ppermute x7, waiting for transfers between devices, passed_along(): return lax.ppermute(block, axis, route)  13.1 us
    ppermute x3, starting transfers between devices, on_device(): squares = squares + lax.ppermute(squares, 'tp', pairs)  7.95 us
    dot_general x1, matrix products, inside_terms(): jnp.einsum('gts,gis->git', matrix_table * same_genome[None], columns, pre...  5.75 us
    add x1, other arithmetic, short_filter(): result = result + jnp.where(keep_tap, taps_part[offset][None] * window, 0.0)  5.62 us
    slice x5, local copies, waits for them, and re-layouts, complex_times(): factor_one[1] * factor_two[1]  4.52 us
    slice x10, local copies, waits for them, and re-layouts, complex_times(): factor_one[0] * factor_two[0] - factor_one[1] * factor_two[1]  4.5 us
  transfers between devices with their start and end apart: 10, of which 6 were waited for; matrix products, arithmetic and copies ran while one was open for 32% of the time, Pallas kernels for 0%

profile of v6, /device:TPU:166, one launch (start us, length us, event | category | flops | bytes accessed | tf_op | source)
XLA Modules:
  0.0 129.6 jit_solution(5468484833464131088)
XLA Ops:
  0.0 0.9 slice.229
  0.9 1.9 %collective-permute-start = (bf16[6,3,1024]{2,0,1:T(8,128)(2,1)S(1)}, bf16[6,3,1024]{2,0,1:T(8,128)(2,1)S(1)}, u32[]{:S(2)}, u32[]{:S(2)}) collective-permute-start(bf16[6,3,1024]{2,0,1:T(8,128)(2,1)S(1)} %slice.229), channel_id=1, source_target_pairs={{0,8},{8,16},{16,24},{24,32},{32,40},{40,48},{48,56},{56,64},{64,7... | collective-permute-start | bytes 110600 | tf_op jit(solution)/shard_map/ppermute | solution.py:19
  2.9 0.8 copy.55
  3.6 0.7 neg.12
  4.3 0.8 subtract_bitcast_fusion.1
  5.1 0.8 reduce-window.9
  5.9 1.4 %and_reduce_fusion = (pred[]{:T(512)}, pred[]{:T(512)}, pred[]{:T(512)}, pred[]{:T(512)}, pred[]{:T(512)}, /*index=5*/s32[4]{0:T(128)S(1)}) fusion(s32[]{:T(128)S(6)} %sub.149, s32[]{:T(128)S(6)} %sub.137, s32[]{:T(128)S(6)} %sub.146, s32[]{:T(128)S(6)} %sub.143, s32[]{:T(128)S(6)} %sub.140, s32[]{:T(128)S(6)} %sub.136, s32[4]{0:T(128)} %param.15, ...), kind=kLoop, calls=%fused_computation.121 | loop fusion | flops 63 | bytes 77 | tf_op jit(solution)/shard_map/reduce_or | solution.py:139
  8.1 1.5 %fusion.41 = (f32[1,3,1024]{2,0,1:T(1,128)S(1)}, f32[1,3,1024]{2,0,1:T(1,128)S(1)}, f32[1,3,1024]{2,0,1:T(1,128)S(1)}, f32[1,3,1024]{2,0,1:T(1,128)S(1)}, f32[1,...) fusion(f32[7,3,1024]{2,0,1:T(8,128)} %param.9), kind=kLoop, calls=%fused_computation.148 | loop fusion | bytes 172032 | tf_op jit(solution)/shard_map/slice | solution.py:96
  13.5 3.1 %fusion.21 = (f32[1,64,16,128]{3,2,0,1:T(8,128)}, f32[1,64,16,128]{3,2,0,1:T(8,128)}) fusion(f32[64,16]{1,0:T(8,128)S(1)} %copy.55, f32[128]{0:T(128)S(1)} %subtract_convert_fusion, f32[64,16]{1,0:T(8,128)S(1)} %copy.54), kind=kLoop, calls=%fused_computation.42 | loop fusion | flops 524288 | bytes 1057280 | tf_op jit(solution)/shard_map/mul | solution.py:58
  17.7 0.9 copy.53
  20.3 5.6 %select_add_fusion = f32[128,3,1024]{0,2,1:T(8,128)S(1)} fusion(bf16[128,3,1024]{0,2,1:T(8,128)(2,1)S(1)} %copy.50, bf16[6,3,1024]{0,2,1:T(8,128)(2,1)S(1)} %copy.51, f32[3,1024]{1,0:T(4,128)S(1)} %get-tuple-element.83, f32[3,1024]{1,0:T(4,128)S(1)} %get-tuple-element.84, f32[3,1024]{1,0:T(4,128)S(1)} %get-tuple-element.85, ...), kind=kLoop, calls=%fused_computation.16 | loop fusion | flops 17694720 | bytes 2483072 | tf_op jit(solution)/shard_map/add | solution.py:96
  26.1 0.9 copy-done.2
  27.2 3.8 %fusion.5 = f32[2,16,64,16]{1,3,0,2:T(8,128)S(1)} fusion(f32[64,16,128,1]{2,1,3,0:T(8,128)S(1)} %bitcast.158, f32[1,64,16,128]{3,2,0,1:T(8,128)S(1)} %copy-done.3, f32[1,64,16,128]{3,2,0,1:T(8,128)S(1)} %copy-done.2, f32[2,16,64,16]{1,3,0,2:T(8,128)S(1)} %copy.53, f32[128]{0:T(128)S(1)} %compare_convert_fusion.1, pred[]{:T(512)S(6)} %lt.13), kind=kOutput, calls=%fused_computation.20 | convolution fusion | flops 25755648 | bytes 1835521 | tf_op jit(solution)/shard_map/rgns,gis->rngi/dot_general | solution.py:82
  30.9 0.9 copy.56
  32.4 2.7 %collective-permute-start.1 = (f32[2,16,1024]{2,1,0:T(8,128)S(1)}, f32[2,16,1024]{2,1,0:T(8,128)S(1)}, u32[]{:S(2)}, u32[]{:S(2)}) collective-permute-start(f32[2,16,1024]{2,1,0:T(8,128)S(1)} %reshape.238), channel_id=1, source_target_pairs={{0,8},{8,16},{16,24},{24,32},{32,40},{40,48},{48,56},{56,64},{64,7... | collective-permute-start | bytes 393224 | tf_op jit(solution)/shard_map/ppermute | solution.py:19
  35.3 0.9 slice.289
  36.4 0.9 slice.285
  37.5 0.9 slice.281
  38.6 0.9 slice.277
  39.7 0.9 slice.273
  40.8 0.9 slice.269
  41.9 0.9 slice.265
  43.0 0.9 slice.261
  44.1 0.9 slice.257
  45.2 0.9 slice.253
  46.3 2.2 %collective-permute-start.2 = (f32[2,16,1024]{2,1,0:T(8,128)S(1)}, f32[2,16,1024]{2,1,0:T(8,128)S(1)}, u32[]{:S(2)}, u32[]{:S(2)}) collective-permute-start(f32[2,16,1024]{2,1,0:T(8,128)S(1)} %collective-permute-done.1), channel_id=1, source_target_pairs={{0,8},{8,16},{16,24},{24,32},{32,40},{40,48},{48,56},{56,64},{64,7... | collective-permute-start | bytes 393224 | tf_op jit(solution)/shard_map/ppermute | solution.py:19
  48.6 3.9 %fusion.8 = (f32[64,16,129]{2,1,0:T(8,128)S(1)}, f32[64,16,129]{2,1,0:T(8,128)S(1)}) fusion(f32[64,16]{1,0:T(8,128)S(1)} %copy.59, f32[129]{0:T(256)S(1)} %iota_convert_fusion, f32[64,16]{1,0:T(8,128)S(1)} %copy.58), kind=kLoop, calls=%fused_computation.24 | loop fusion | flops 528384 | bytes 1065476 | tf_op jit(solution)/shard_map/mul | solution.py:39
  52.4 3.0 %collective-permute-done.2 = f32[2,16,1024]{2,1,0:T(8,128)S(1)} collective-permute-done((f32[2,16,1024]{2,1,0:T(8,128)S(1)}, f32[2,16,1024]{2,1,0:T(8,128)S(1)}, u32[]{:S(2)}, u32[]{:S(2)}) %collective-permute-start.2) | collective-permute-done | bytes 131104 | tf_op jit(solution)/shard_map/ppermute | solution.py:19
  55.5 0.9 multiply_subtract_fusion.4
  57.0 1.9 %collective-permute-start.3 = (f32[2,16,1024]{2,1,0:T(8,128)}, f32[2,16,1024]{2,1,0:T(8,128)}, u32[]{:S(2)}, u32[]{:S(2)}) collective-permute-start(f32[2,16,1024]{2,1,0:T(8,128)} %maximum_add_fusion), channel_id=1, source_target_pairs={{0,16},{8,24},{16,32},{24,40},{32,48},{40,56},{48,64},{56,72},{64,... | collective-permute-start | bytes 393224 | tf_op jit(solution)/shard_map/ppermute | solution.py:19
  58.9 0.7 slice_bitcast_fusion.12
  61.0 5.8 %collective-permute-done.3 = f32[2,16,1024]{2,1,0:T(8,128)} collective-permute-done((f32[2,16,1024]{2,1,0:T(8,128)}, f32[2,16,1024]{2,1,0:T(8,128)}, u32[]{:S(2)}, u32[]{:S(2)}) %collective-permute-start.3) | collective-permute-done | bytes 131104 | tf_op jit(solution)/shard_map/ppermute | solution.py:19
  66.9 1.0 multiply_subtract_fusion.3
  67.8 1.9 %collective-permute-start.4 = (f32[2,16,1024]{2,1,0:T(8,128)S(1)}, f32[2,16,1024]{2,1,0:T(8,128)S(1)}, u32[]{:S(2)}, u32[]{:S(2)}) collective-permute-start(f32[2,16,1024]{2,1,0:T(8,128)S(1)} %maximum_add_fusion.1), channel_id=1, source_target_pairs={{0,32},{8,40},{16,48},{24,56},{32,64},{40,72},{48,80},{56,88},{64,... | collective-permute-start | bytes 393224 | tf_op jit(solution)/shard_map/ppermute | solution.py:19
  69.8 2.4 %subtract_bitcast_fusion = (f32[1,64,16,128]{3,2,0,1:T(8,128)}, f32[1,64,16,128]{3,2,0,1:T(8,128)}, f32[64,128]{1,0:T(8,128)S(1)}) fusion(f32[64,16,129]{2,1,0:T(8,128)S(1)} %get-tuple-element.53, f32[64,16,129]{2,1,0:T(8,128)S(1)} %get-tuple-element.52, f32[64,16]{1,0:T(8,128)} %copy.60, f32[64,16]{1,0:T(8,128)} %copy.57), kind=kLoop, calls=%fused_computation.56 | loop fusion | flops 1433600 | bytes 3186688 | tf_op jit(solution)/shard_map/stack | solution.py:48
  72.2 4.3 %collective-permute-done.4 = f32[2,16,1024]{2,1,0:T(8,128)S(1)} collective-permute-done((f32[2,16,1024]{2,1,0:T(8,128)S(1)}, f32[2,16,1024]{2,1,0:T(8,128)S(1)}, u32[]{:S(2)}, u32[]{:S(2)}) %collective-permute-start.4) | collective-permute-done | bytes 131104 | tf_op jit(solution)/shard_map/ppermute | solution.py:19
  76.6 4.3 %collective-permute-start.5 = (f32[2,16,1024]{2,1,0:T(8,128)S(1)}, f32[2,16,1024]{2,1,0:T(8,128)S(1)}, u32[]{:S(2)}, u32[]{:S(2)}) collective-permute-start(f32[2,16,1024]{2,1,0:T(8,128)S(1)} %maximum_add_fusion.2), channel_id=1, source_target_pairs={{0,64},{8,72},{16,80},{24,88},{32,96},{40,104},{48,112},{56,120},{... | collective-permute-start | bytes 393224 | tf_op jit(solution)/shard_map/ppermute | solution.py:19
  80.9 3.3 %fusion.4 = f32[64,128,128]{2,0,1:T(8,128)S(1)} fusion(s32[128,128]{1,0:T(8,128)S(1)} %iota_subtract_fusion, f32[128,128]{1,0:T(8,128)S(1)} %compare_convert_fusion, f32[64,128]{1,0:T(8,128)S(1)} %get-tuple-element.32), kind=kOutput, calls=%fused_computation.15 | convolution fusion | flops 1613758464 | bytes 4358144 | tf_op jit(solution)/shard_map/gk,kts->gts/dot_general | solution.py:33
  84.3 12.8 %collective-permute-start.6 = (f32[2,16,1024]{2,1,0:T(8,128)S(1)}, f32[2,16,1024]{2,1,0:T(8,128)S(1)}, u32[]{:S(2)}, u32[]{:S(2)}) collective-permute-start(f32[2,16,1024]{2,1,0:T(8,128)S(1)} %maximum_add_fusion.3), channel_id=1, source_target_pairs={{0,128},{8,136},{16,144},{24,152},{32,160},{40,168},{48,176},{56,1... | collective-permute-start | bytes 393224 | tf_op jit(solution)/shard_map/ppermute | solution.py:19
  97.1 5.7 %fusion.1 = f32[64,16,128]{2,1,0:T(8,128)} fusion(f32[64,16,128]{2,1,0:T(8,128)S(1)} %bitcast.159, f32[64,128,128]{2,0,1:T(8,128)S(1)} %fusion.4), kind=kOutput, calls=%fused_computation.2 | convolution fusion | flops 100663296 | bytes 5242880 | tf_op jit(solution)/shard_map/gts,gis->git/dot_general | solution.py:77
  104.0 2.4 %fusion.7 = f32[64,16,128]{2,1,0:T(8,128)S(1)} fusion(f32[64,16,128]{2,1,0:T(8,128)} %fusion.1, f32[1,64,16,128]{3,2,0,1:T(8,128)S(1)} %copy-done.1, f32[1,64,16,128]{3,2,0,1:T(8,128)S(1)} %copy-done, f32[2,16,64,16]{3,2,1,0:T(8,128)S(1)} %reshape.239, pred[128]{0:T(512)(128)(4,1)S(1)} %copy-done.16), kind=kOutput, calls=%fused_computation.23 | convolution fusion | flops 25690112 | bytes 2228352 | tf_op jit(solution)/shard_map/rgnt,rngi->git/dot_general | solution.py:86
  106.7 2.7 %collective-permute-start.7 = (f32[128]{0:T(128)S(1)}, f32[128]{0:T(128)S(1)}, u32[]{:S(2)}, u32[]{:S(2)}) collective-permute-start(f32[128]{0:T(128)S(1)} %get-tuple-element.22), channel_id=1, source_target_pairs={{0,1},{1,0},{2,3},{3,2},{4,5},{5,4},{6,7},{7,6},{8,9},{9,8},{10,11... | collective-permute-start | bytes 1544 | tf_op jit(solution)/shard_map/ppermute | solution.py:173
  109.4 2.7 %collective-permute-done.7 = f32[128]{0:T(128)S(1)} collective-permute-done((f32[128]{0:T(128)S(1)}, f32[128]{0:T(128)S(1)}, u32[]{:S(2)}, u32[]{:S(2)}) %collective-permute-start.7) | collective-permute-done | bytes 544 | tf_op jit(solution)/shard_map/ppermute | solution.py:173
  112.2 3.3 %collective-permute-start.8 = (f32[128]{0:T(128)S(1)}, f32[128]{0:T(128)S(1)}, u32[]{:S(2)}, u32[]{:S(2)}) collective-permute-start(f32[128]{0:T(128)S(1)} %add.209), channel_id=1, source_target_pairs={{0,2},{1,3},{2,0},{3,1},{4,6},{5,7},{6,4},{7,5},{8,10},{9,11},{10,... | collective-permute-start | bytes 1544 | tf_op jit(solution)/shard_map/ppermute | solution.py:173
  115.5 3.6 %collective-permute-done.8 = f32[128]{0:T(128)S(1)} collective-permute-done((f32[128]{0:T(128)S(1)}, f32[128]{0:T(128)S(1)}, u32[]{:S(2)}, u32[]{:S(2)}) %collective-permute-start.8) | collective-permute-done | bytes 544 | tf_op jit(solution)/shard_map/ppermute | solution.py:173
  119.1 1.9 %collective-permute-start.9 = (f32[128]{0:T(128)S(1)}, f32[128]{0:T(128)S(1)}, u32[]{:S(2)}, u32[]{:S(2)}) collective-permute-start(f32[128]{0:T(128)S(1)} %add.210), channel_id=1, source_target_pairs={{0,4},{1,5},{2,6},{3,7},{4,0},{5,1},{6,2},{7,3},{8,12},{9,13},{10,... | collective-permute-start | bytes 1544 | tf_op jit(solution)/shard_map/ppermute | solution.py:173
  121.0 7.4 %collective-permute-done.9 = f32[128]{0:T(128)S(1)} collective-permute-done((f32[128]{0:T(128)S(1)}, f32[128]{0:T(128)S(1)}, u32[]{:S(2)}, u32[]{:S(2)}) %collective-permute-start.9) | collective-permute-done | bytes 544 | tf_op jit(solution)/shard_map/ppermute | solution.py:173
  128.7 0.9 copy.64
  (100 shorter events, 10.4 us)
Async XLA Ops:
  0.0 17.3 %copy-start.4 = (bf16[128,3,1024]{2,0,1:T(8,128)(2,1)S(1)}, bf16[128,3,1024]{2,0,1:T(8,128)(2,1)}, u32[]{:S(2)}) copy-start(bf16[128,3,1024]{2,0,1:T(8,128)(2,1)} %param.8) | copy-start | bytes 2359300
  0.9 19.0 %collective-permute-start = (bf16[6,3,1024]{2,0,1:T(8,128)(2,1)S(1)}, bf16[6,3,1024]{2,0,1:T(8,128)(2,1)S(1)}, u32[]{:S(2)}, u32[]{:S(2)}) collective-permute-start(bf16[6,3,1024]{2,0,1:T(8,128)(2,1)S(1)} %slice.229), channel_id=1, source_target_pairs={{0,8},{8,16},{16,24},{24,32},{32,40},{40,48},{48,56},{56,64},{64,7... | collective-permute-start | bytes 110600 | tf_op jit(solution)/shard_map/ppermute | solution.py:19
  26.0 1.0 copy-start.2
  26.0 1.2 copy-start.3
  32.4 13.7 %collective-permute-start.1 = (f32[2,16,1024]{2,1,0:T(8,128)S(1)}, f32[2,16,1024]{2,1,0:T(8,128)S(1)}, u32[]{:S(2)}, u32[]{:S(2)}) collective-permute-start(f32[2,16,1024]{2,1,0:T(8,128)S(1)} %reshape.238), channel_id=1, source_target_pairs={{0,8},{8,16},{16,24},{24,32},{32,40},{40,48},{48,56},{56,64},{64,7... | collective-permute-start | bytes 393224 | tf_op jit(solution)/shard_map/ppermute | solution.py:19
  43.0 3.1 %copy-start.12 = (f32[64,16]{0,1:T(8,128)S(1)}, f32[64,16]{0,1:T(8,128)}, u32[]{:S(2)}) copy-start(f32[64,16]{0,1:T(8,128)} %param.11) | copy-start | bytes 12292
  43.0 3.2 %copy-start.13 = (f32[64,16]{0,1:T(8,128)S(1)}, f32[64,16]{0,1:T(8,128)}, u32[]{:S(2)}) copy-start(f32[64,16]{0,1:T(8,128)} %param.10) | copy-start | bytes 12292
  46.3 9.1 %copy-start.11 = (f32[1,16,1024]{2,1,0:T(8,128)S(1)}, f32[1,16,1024]{2,1,0:T(8,128)}, u32[]{:S(2)}) copy-start(f32[1,16,1024]{2,1,0:T(8,128)} %slice.253) | copy-start | bytes 196612
  46.3 9.1 %collective-permute-start.2 = (f32[2,16,1024]{2,1,0:T(8,128)S(1)}, f32[2,16,1024]{2,1,0:T(8,128)S(1)}, u32[]{:S(2)}, u32[]{:S(2)}) collective-permute-start(f32[2,16,1024]{2,1,0:T(8,128)S(1)} %collective-permute-done.1), channel_id=1, source_target_pairs={{0,8},{8,16},{16,24},{24,32},{32,40},{40,48},{48,56},{56,64},{64,7... | collective-permute-start | bytes 393224 | tf_op jit(solution)/shard_map/ppermute | solution.py:19
  57.0 9.9 %collective-permute-start.3 = (f32[2,16,1024]{2,1,0:T(8,128)}, f32[2,16,1024]{2,1,0:T(8,128)}, u32[]{:S(2)}, u32[]{:S(2)}) collective-permute-start(f32[2,16,1024]{2,1,0:T(8,128)} %maximum_add_fusion), channel_id=1, source_target_pairs={{0,16},{8,24},{16,32},{24,40},{32,48},{40,56},{48,64},{56,72},{64,... | collective-permute-start | bytes 393224 | tf_op jit(solution)/shard_map/ppermute | solution.py:19
  67.8 8.7 %collective-permute-start.4 = (f32[2,16,1024]{2,1,0:T(8,128)S(1)}, f32[2,16,1024]{2,1,0:T(8,128)S(1)}, u32[]{:S(2)}, u32[]{:S(2)}) collective-permute-start(f32[2,16,1024]{2,1,0:T(8,128)S(1)} %maximum_add_fusion.1), channel_id=1, source_target_pairs={{0,32},{8,40},{16,48},{24,56},{32,64},{40,72},{48,80},{56,88},{64,... | collective-permute-start | bytes 393224 | tf_op jit(solution)/shard_map/ppermute | solution.py:19
  69.8 6.7 %copy-start.9 = (f32[1,16,1024]{2,1,0:T(8,128)S(1)}, f32[1,16,1024]{2,1,0:T(8,128)}, u32[]{:S(2)}) copy-start(f32[1,16,1024]{2,1,0:T(8,128)} %slice.273) | copy-start | bytes 196612
  69.8 6.7 %copy-start.10 = (f32[1,16,1024]{2,1,0:T(8,128)S(1)}, f32[1,16,1024]{2,1,0:T(8,128)}, u32[]{:S(2)}) copy-start(f32[1,16,1024]{2,1,0:T(8,128)} %slice.269) | copy-start | bytes 196612
  76.6 7.6 %collective-permute-start.5 = (f32[2,16,1024]{2,1,0:T(8,128)S(1)}, f32[2,16,1024]{2,1,0:T(8,128)S(1)}, u32[]{:S(2)}, u32[]{:S(2)}) collective-permute-start(f32[2,16,1024]{2,1,0:T(8,128)S(1)} %maximum_add_fusion.2), channel_id=1, source_target_pairs={{0,64},{8,72},{16,80},{24,88},{32,96},{40,104},{48,112},{56,120},{... | collective-permute-start | bytes 393224 | tf_op jit(solution)/shard_map/ppermute | solution.py:19
  80.9 3.3 %copy-start.7 = (f32[1,16,1024]{2,1,0:T(8,128)S(1)}, f32[1,16,1024]{2,1,0:T(8,128)}, u32[]{:S(2)}) copy-start(f32[1,16,1024]{2,1,0:T(8,128)} %slice.281) | copy-start | bytes 196612
  80.9 3.3 %copy-start.8 = (f32[1,16,1024]{2,1,0:T(8,128)S(1)}, f32[1,16,1024]{2,1,0:T(8,128)}, u32[]{:S(2)}) copy-start(f32[1,16,1024]{2,1,0:T(8,128)} %slice.277) | copy-start | bytes 196612
  84.3 18.6 %collective-permute-start.6 = (f32[2,16,1024]{2,1,0:T(8,128)S(1)}, f32[2,16,1024]{2,1,0:T(8,128)S(1)}, u32[]{:S(2)}, u32[]{:S(2)}) collective-permute-start(f32[2,16,1024]{2,1,0:T(8,128)S(1)} %maximum_add_fusion.3), channel_id=1, source_target_pairs={{0,128},{8,136},{16,144},{24,152},{32,160},{40,168},{48,176},{56,1... | collective-permute-start | bytes 393224 | tf_op jit(solution)/shard_map/ppermute | solution.py:19
  97.0 5.8 %copy-start.5 = (f32[1,16,1024]{2,1,0:T(8,128)S(1)}, f32[1,16,1024]{2,1,0:T(8,128)}, u32[]{:S(2)}) copy-start(f32[1,16,1024]{2,1,0:T(8,128)} %slice.289) | copy-start | bytes 196612
  97.1 5.8 %copy-start.6 = (f32[1,16,1024]{2,1,0:T(8,128)S(1)}, f32[1,16,1024]{2,1,0:T(8,128)}, u32[]{:S(2)}) copy-start(f32[1,16,1024]{2,1,0:T(8,128)} %slice.285) | copy-start | bytes 196612
  102.8 1.0 copy-start
  102.8 1.2 copy-start.1
  102.8 1.2 copy-start.16
  104.0 2.5 %copy-start.14 = (f32[1024]{0:T(1024)S(1)}, f32[1024]{0:T(1024)}, u32[]{:S(2)}) copy-start(f32[1024]{0:T(1024)} %param.13) | copy-start | bytes 12292
  106.5 22.0 %copy-start.15 = (f32[1024]{0:T(1024)S(1)}, f32[1024]{0:T(1024)}, u32[]{:S(2)}) copy-start(f32[1024]{0:T(1024)} %param.14) | copy-start | bytes 12292
  106.7 5.5 %collective-permute-start.7 = (f32[128]{0:T(128)S(1)}, f32[128]{0:T(128)S(1)}, u32[]{:S(2)}, u32[]{:S(2)}) collective-permute-start(f32[128]{0:T(128)S(1)} %get-tuple-element.22), channel_id=1, source_target_pairs={{0,1},{1,0},{2,3},{3,2},{4,5},{5,4},{6,7},{7,6},{8,9},{9,8},{10,11... | collective-permute-start | bytes 1544 | tf_op jit(solution)/shard_map/ppermute | solution.py:173
  112.2 7.0 %collective-permute-start.8 = (f32[128]{0:T(128)S(1)}, f32[128]{0:T(128)S(1)}, u32[]{:S(2)}, u32[]{:S(2)}) collective-permute-start(f32[128]{0:T(128)S(1)} %add.209), channel_id=1, source_target_pairs={{0,2},{1,3},{2,0},{3,1},{4,6},{5,7},{6,4},{7,5},{8,10},{9,11},{10,... | collective-permute-start | bytes 1544 | tf_op jit(solution)/shard_map/ppermute | solution.py:173
  119.1 9.4 %collective-permute-start.9 = (f32[128]{0:T(128)S(1)}, f32[128]{0:T(128)S(1)}, u32[]{:S(2)}, u32[]{:S(2)}) collective-permute-start(f32[128]{0:T(128)S(1)} %add.210), channel_id=1, source_target_pairs={{0,4},{1,5},{2,6},{3,7},{4,0},{5,1},{6,2},{7,3},{8,12},{9,13},{10,... | collective-permute-start | bytes 1544 | tf_op jit(solution)/shard_map/ppermute | solution.py:173

commit v7 on v6

--- a/solution.py
+++ b/solution.py
@@ -149,15 +149,17 @@
         toeplitz(response), values[span_index], span_pos[span_index], span_begin[span_index]
     )
     insides = [lax.optimization_barrier(inside)]
-    power = stepping
-    distance = 1
-    while distance < reach:
+    distances = []
+    ladder = [stepping]
+    while 2 ** len(distances) < reach:
+        distances.append(2 ** len(distances))
+        ladder.append(complex_times(ladder[-1], ladder[-1]))
+    alive = jnp.stack([unbroken(anchor - step * tok_rows, anchor - 1) for step in distances])
+    factors = jnp.repeat(jnp.stack(ladder[: len(distances)]), group_width, axis=3)
+    factors = factors * alive.astype(jnp.float32)[:, None, None, None]
+    for index, distance in enumerate(distances):
         earlier = passed_along(running, "ctx", distance)
-        alive = unbroken(anchor - distance * tok_rows, anchor - 1)
-        factor = widen(power) * alive.astype(jnp.float32)
-        running = running + complex_times(factor, earlier)
-        power = complex_times(power, power)
-        distance = distance * 2
+        running = running + complex_times(factors[index], earlier)
     incoming = running.reshape(2, mode_count, group_count, group_width)
     span_index = 0
     entered = (span_begin[span_index] < span_pos[span_index, 0])[None, None, :]

time: 130 us -> 137 us (1.054)
  waiting for transfers between devices: 26.9 us -> 32.5 us
  other arithmetic: 23.4 us -> 26.9 us
  local copies, waits for them, and re-layouts: 24 us -> 21.1 us
    slice x15 -> x0, local copies, waits for them, and re-layouts: 9.02 us -> none  [the longest x5 4.52 us: complex_times(): factor_one[1] * factor_two[1]]
    ppermute x7, waiting for transfers between devices: 13.1 us -> 18.8 us  [passed_along(): return lax.ppermute(block, axis, route)]
    reshape x0 -> x1, local copies, waits for them, and re-layouts: none -> 5.34 us  [on_device(): jnp.repeat(jnp.stack(ladder[:len(distances)]), group_width, axis=3)]
    broadcast_in_dim x10 -> x1, local copies, waits for them, and re-layouts: 1.88 us -> 3.06 us  [on_device(): jnp.repeat(jnp.stack(ladder[:len(distances)]), group_width, axis=3)]
    unnamed x40 -> x38, local copies, waits for them, and re-layouts: 3.05 us -> 2.6 us
  transfers between devices with their start and end apart: 10 -> 10, of which waited for: 6 -> 7; matrix products, arithmetic and copies ran while one was open for 32% -> 31% of each run, Pallas kernels for 0% -> 0%
where the time goes in v7:
time: 137 us; the launch traced here: 136 us
  starting transfers between devices  36.8 us (27%)
  waiting for transfers between devices  32.5 us (24%)
  other arithmetic  26.9 us (20%)
  local copies, waits for them, and re-layouts  21.1 us (15%)
  matrix products  14.1 us (10%)
  between operations  4.32 us (3%)
    ppermute x7, starting transfers between devices, passed_along(): return lax.ppermute(block, axis, route)  28.8 us
    ppermute x7, waiting for transfers between devices, passed_along(): return lax.ppermute(block, axis, route)  18.8 us
    ppermute x3, waiting for transfers between devices, on_device(): squares = squares + lax.ppermute(squares, 'tp', pairs)  13.7 us
    ppermute x3, starting transfers between devices, on_device(): squares = squares + lax.ppermute(squares, 'tp', pairs)  8.02 us
    dot_general x1, matrix products, inside_terms(): jnp.einsum('gts,gis->git', matrix_table * same_genome[None], columns, pre...  5.72 us
    add x1, other arithmetic, short_filter(): result = result + jnp.where(keep_tap, taps_part[offset][None] * window, 0.0)  5.62 us
    reshape x1, local copies, waits for them, and re-layouts, on_device(): jnp.repeat(jnp.stack(ladder[:len(distances)]), group_width, axis=3)  5.34 us
    mul x1, other arithmetic, pole_tables(): power_re = magnitude * jnp.cos(angle[:, :, None] * counter)  3.86 us
  transfers between devices with their start and end apart: 10, of which 7 were waited for; matrix products, arithmetic and copies ran while one was open for 31% of the time, Pallas kernels for 0%

profile of v7, /device:TPU:166, one launch (start us, length us, event | category | flops | bytes accessed | tf_op | source)
XLA Modules:
  0.0 135.7 jit_solution(6324485856036508468)
XLA Ops:
  0.0 0.8 slice.194
  0.8 1.9 %collective-permute-start = (bf16[6,3,1024]{2,0,1:T(8,128)(2,1)S(1)}, bf16[6,3,1024]{2,0,1:T(8,128)(2,1)S(1)}, u32[]{:S(2)}, u32[]{:S(2)}) collective-permute-start(bf16[6,3,1024]{2,0,1:T(8,128)(2,1)S(1)} %slice.194), channel_id=1, source_target_pairs={{0,8},{8,16},{16,24},{24,32},{32,40},{40,48},{48,56},{56,64},{64,7... | collective-permute-start | bytes 110600 | tf_op jit(solution)/shard_map/ppermute | solution.py:19
  2.8 0.7 neg.12
  3.5 0.8 subtract_bitcast_fusion.1
  4.2 0.8 copy.55
  5.0 0.8 reduce-window.9
  5.9 1.4 %and_reduce_fusion = (pred[]{:T(512)}, pred[]{:T(512)}, pred[]{:T(512)}, pred[]{:T(512)}, pred[]{:T(512)}, /*index=5*/s32[4]{0:T(128)S(1)}) fusion(s32[]{:T(128)S(6)} %sub.145, s32[]{:T(128)S(6)} %sub.141, s32[]{:T(128)S(6)} %sub.144, s32[]{:T(128)S(6)} %sub.143, s32[]{:T(128)S(6)} %sub.142, s32[]{:T(128)S(6)} %sub.140, s32[4]{0:T(128)} %param.15, ...), kind=kLoop, calls=%fused_computation.127 | loop fusion | flops 63 | bytes 77 | tf_op jit(solution)/shard_map/reduce_or | solution.py:139
  7.9 0.7 compare_convert_fusion
  9.3 1.5 %fusion.46 = (f32[1,3,1024]{2,0,1:T(1,128)S(1)}, f32[1,3,1024]{2,0,1:T(1,128)S(1)}, f32[1,3,1024]{2,0,1:T(1,128)S(1)}, f32[1,3,1024]{2,0,1:T(1,128)S(1)}, f32[1,...) fusion(f32[7,3,1024]{2,0,1:T(8,128)} %param.9), kind=kLoop, calls=%fused_computation.154 | loop fusion | bytes 172032 | tf_op jit(solution)/shard_map/slice | solution.py:96
  14.2 3.1 %broadcast_in_dim.121 = f32[5,2,16,64,16]{4,3,2,1,0:T(8,128)} broadcast(f32[5,2,16,64]{3,2,1,0:T(8,128)S(1)} %fusion.33), dimensions={0,1,2,3} | broadcast | bytes 696320 | tf_op jit(solution)/shard_map/broadcast_in_dim | solution.py:158
  17.3 5.3 %reshape.288 = f32[5,2,16,1024]{3,2,1,0:T(8,128)S(1)} reshape(f32[5,2,16,64,16]{4,3,2,1,0:T(8,128)} %broadcast_in_dim.121) | data formatting | bytes 1310720 | tf_op jit(solution)/shard_map/reshape | solution.py:158
  22.7 1.0 broadcast_multiply_fusion
  23.7 3.1 %fusion.21 = (f32[1,64,16,128]{3,2,0,1:T(8,128)}, f32[1,64,16,128]{3,2,0,1:T(8,128)}) fusion(f32[64,16]{1,0:T(8,128)S(1)} %copy.55, f32[128]{0:T(128)S(1)} %subtract_convert_fusion, f32[64,16]{1,0:T(8,128)S(1)} %copy.54), kind=kLoop, calls=%fused_computation.42 | loop fusion | flops 524288 | bytes 1057280 | tf_op jit(solution)/shard_map/mul | solution.py:58
  26.8 1.1 compare_convert_fusion.1
  28.3 0.6 slice.209
  29.6 0.9 copy.53
  31.0 5.6 %select_add_fusion = f32[128,3,1024]{0,2,1:T(8,128)S(1)} fusion(bf16[128,3,1024]{0,2,1:T(8,128)(2,1)S(1)} %copy.50, bf16[6,3,1024]{0,2,1:T(8,128)(2,1)S(1)} %copy.51, f32[3,1024]{1,0:T(4,128)S(1)} %get-tuple-element.73, f32[3,1024]{1,0:T(4,128)S(1)} %get-tuple-element.74, f32[3,1024]{1,0:T(4,128)S(1)} %get-tuple-element.75, ...), kind=kLoop, calls=%fused_computation.16 | loop fusion | flops 17694720 | bytes 2483072 | tf_op jit(solution)/shard_map/add | solution.py:96
  36.6 0.9 fusion.25
  38.0 3.8 %fusion.5 = f32[2,16,64,16]{1,3,0,2:T(8,128)S(1)} fusion(f32[64,16,128,1]{2,1,3,0:T(8,128)S(1)} %bitcast.205, f32[1,64,16,128]{3,2,0,1:T(8,128)S(1)} %copy-done.6, f32[1,64,16,128]{3,2,0,1:T(8,128)S(1)} %copy-done.5, f32[2,16,64,16]{1,3,0,2:T(8,128)S(1)} %copy.53, f32[128]{0:T(128)S(1)} %copy-done.15, pred[]{:T(512)S(6)} %lt.13), kind=kOutput, calls=%fused_computation.20 | convolution fusion | flops 25755648 | bytes 1835521 | tf_op jit(solution)/shard_map/rgns,gis->rngi/dot_general | solution.py:82
  41.8 0.9 copy.56
  43.3 2.7 %collective-permute-start.1 = (f32[2,16,1024]{2,1,0:T(8,128)S(1)}, f32[2,16,1024]{2,1,0:T(8,128)S(1)}, u32[]{:S(2)}, u32[]{:S(2)}) collective-permute-start(f32[2,16,1024]{2,1,0:T(8,128)S(1)} %reshape.287), channel_id=1, source_target_pairs={{0,8},{8,16},{16,24},{24,32},{32,40},{40,48},{48,56},{56,64},{64,7... | collective-permute-start | bytes 393224 | tf_op jit(solution)/shard_map/ppermute | solution.py:19
  46.6 5.6 %collective-permute-done.1 = f32[2,16,1024]{2,1,0:T(8,128)S(1)} collective-permute-done((f32[2,16,1024]{2,1,0:T(8,128)S(1)}, f32[2,16,1024]{2,1,0:T(8,128)S(1)}, u32[]{:S(2)}, u32[]{:S(2)}) %collective-permute-start.1) | collective-permute-done | bytes 131104 | tf_op jit(solution)/shard_map/ppermute | solution.py:19
  52.3 2.1 %collective-permute-start.2 = (f32[2,16,1024]{2,1,0:T(8,128)S(1)}, f32[2,16,1024]{2,1,0:T(8,128)}, u32[]{:S(2)}, u32[]{:S(2)}) collective-permute-start(f32[2,16,1024]{2,1,0:T(8,128)S(1)} %collective-permute-done.1), channel_id=1, source_target_pairs={{0,8},{8,16},{16,24},{24,32},{32,40},{40,48},{48,56},{56,64},{64,7... | collective-permute-start | bytes 393224 | tf_op jit(solution)/shard_map/ppermute | solution.py:19
  54.6 3.9 %fusion.8 = (f32[64,16,129]{2,1,0:T(8,128)S(1)}, f32[64,16,129]{2,1,0:T(8,128)S(1)}) fusion(f32[64,16]{1,0:T(8,128)S(1)} %copy.59, f32[129]{0:T(256)S(1)} %iota_convert_fusion, f32[64,16]{1,0:T(8,128)S(1)} %copy.58), kind=kLoop, calls=%fused_computation.24 | loop fusion | flops 528384 | bytes 1065476 | tf_op jit(solution)/shard_map/mul | solution.py:39
  58.4 2.9 %collective-permute-done.2 = f32[2,16,1024]{2,1,0:T(8,128)} collective-permute-done((f32[2,16,1024]{2,1,0:T(8,128)S(1)}, f32[2,16,1024]{2,1,0:T(8,128)}, u32[]{:S(2)}, u32[]{:S(2)}) %collective-permute-start.2) | collective-permute-done | bytes 131104 | tf_op jit(solution)/shard_map/ppermute | solution.py:19
  61.4 0.9 multiply_subtract_fusion.4
  62.3 0.7 maximum_add_fusion
  62.9 1.9 %collective-permute-start.3 = (f32[2,16,1024]{2,1,0:T(8,128)}, f32[2,16,1024]{2,1,0:T(8,128)}, u32[]{:S(2)}, u32[]{:S(2)}) collective-permute-start(f32[2,16,1024]{2,1,0:T(8,128)} %maximum_add_fusion), channel_id=1, source_target_pairs={{0,16},{8,24},{16,32},{24,40},{32,48},{40,56},{48,64},{56,72},{64,... | collective-permute-start | bytes 393224 | tf_op jit(solution)/shard_map/ppermute | solution.py:19
  64.8 0.7 slice_bitcast_fusion.12
  65.6 0.7 copy.57
  66.3 0.7 copy.60
  66.9 5.9 %collective-permute-done.3 = f32[2,16,1024]{2,1,0:T(8,128)} collective-permute-done((f32[2,16,1024]{2,1,0:T(8,128)}, f32[2,16,1024]{2,1,0:T(8,128)}, u32[]{:S(2)}, u32[]{:S(2)}) %collective-permute-start.3) | collective-permute-done | bytes 131104 | tf_op jit(solution)/shard_map/ppermute | solution.py:19
  72.8 0.9 multiply_subtract_fusion.3
  73.7 1.9 %collective-permute-start.4 = (f32[2,16,1024]{2,1,0:T(8,128)S(1)}, f32[2,16,1024]{2,1,0:T(8,128)S(1)}, u32[]{:S(2)}, u32[]{:S(2)}) collective-permute-start(f32[2,16,1024]{2,1,0:T(8,128)S(1)} %maximum_add_fusion.1), channel_id=1, source_target_pairs={{0,32},{8,40},{16,48},{24,56},{32,64},{40,72},{48,80},{56,88},{64,... | collective-permute-start | bytes 393224 | tf_op jit(solution)/shard_map/ppermute | solution.py:19
  75.7 2.4 %subtract_bitcast_fusion = (f32[1,64,16,128]{3,2,0,1:T(8,128)}, f32[1,64,16,128]{3,2,0,1:T(8,128)}, f32[64,128]{1,0:T(8,128)S(1)}) fusion(f32[64,16,129]{2,1,0:T(8,128)S(1)} %get-tuple-element.53, f32[64,16,129]{2,1,0:T(8,128)S(1)} %get-tuple-element.52, f32[64,16]{1,0:T(8,128)} %copy.60, f32[64,16]{1,0:T(8,128)} %copy.57), kind=kLoop, calls=%fused_computation.56 | loop fusion | flops 1433600 | bytes 3186688 | tf_op jit(solution)/shard_map/stack | solution.py:48
  78.0 4.3 %collective-permute-done.4 = f32[2,16,1024]{2,1,0:T(8,128)S(1)} collective-permute-done((f32[2,16,1024]{2,1,0:T(8,128)S(1)}, f32[2,16,1024]{2,1,0:T(8,128)S(1)}, u32[]{:S(2)}, u32[]{:S(2)}) %collective-permute-start.4) | collective-permute-done | bytes 131104 | tf_op jit(solution)/shard_map/ppermute | solution.py:19
  82.5 4.3 %collective-permute-start.5 = (f32[2,16,1024]{2,1,0:T(8,128)S(1)}, f32[2,16,1024]{2,1,0:T(8,128)S(1)}, u32[]{:S(2)}, u32[]{:S(2)}) collective-permute-start(f32[2,16,1024]{2,1,0:T(8,128)S(1)} %maximum_add_fusion.2), channel_id=1, source_target_pairs={{0,64},{8,72},{16,80},{24,88},{32,96},{40,104},{48,112},{56,120},{... | collective-permute-start | bytes 393224 | tf_op jit(solution)/shard_map/ppermute | solution.py:19
  86.8 3.3 %fusion.4 = f32[64,128,128]{2,0,1:T(8,128)S(1)} fusion(s32[128,128]{1,0:T(8,128)S(1)} %copy-done.9, f32[128,128]{1,0:T(8,128)S(1)} %copy-done.8, f32[64,128]{1,0:T(8,128)S(1)} %get-tuple-element.32), kind=kOutput, calls=%fused_computation.15 | convolution fusion | flops 1613758464 | bytes 4358144 | tf_op jit(solution)/shard_map/gk,kts->gts/dot_general | solution.py:33
  90.1 14.0 %collective-permute-start.6 = (f32[2,16,1024]{2,1,0:T(8,128)S(1)}, f32[2,16,1024]{2,1,0:T(8,128)S(1)}, u32[]{:S(2)}, u32[]{:S(2)}) collective-permute-start(f32[2,16,1024]{2,1,0:T(8,128)S(1)} %maximum_add_fusion.3), channel_id=1, source_target_pairs={{0,128},{8,136},{16,144},{24,152},{32,160},{40,168},{48,176},{56,1... | collective-permute-start | bytes 393224 | tf_op jit(solution)/shard_map/ppermute | solution.py:19
  104.1 5.7 %fusion.1 = f32[64,16,128]{2,1,0:T(8,128)} fusion(f32[64,16,128]{2,1,0:T(8,128)S(1)} %bitcast.206, f32[64,128,128]{2,0,1:T(8,128)S(1)} %fusion.4), kind=kOutput, calls=%fused_computation.2 | convolution fusion | flops 100663296 | bytes 5242880 | tf_op jit(solution)/shard_map/gts,gis->git/dot_general | solution.py:77
  111.2 1.4 %fusion.7 = f32[64,16,128]{2,1,0:T(8,128)S(1)} fusion(f32[64,16,128]{2,1,0:T(8,128)S(1)} %copy-done.4, f32[1,64,16,128]{3,2,0,1:T(8,128)S(1)} %copy-done.3, f32[1,64,16,128]{3,2,0,1:T(8,128)S(1)} %copy-done.2, f32[2,16,64,16]{3,2,1,0:T(8,128)S(1)} %reshape.289, pred[128]{0:T(512)(128)(4,1)S(1)} %copy-done.14), kind=kOutput, calls=%fused_computation.23 | convolution fusion | flops 25690112 | bytes 2228352 | tf_op jit(solution)/shard_map/rgnt,rngi->git/dot_general | solution.py:86
  112.8 2.7 %collective-permute-start.7 = (f32[128]{0:T(128)S(1)}, f32[128]{0:T(128)S(1)}, u32[]{:S(2)}, u32[]{:S(2)}) collective-permute-start(f32[128]{0:T(128)S(1)} %get-tuple-element.22), channel_id=1, source_target_pairs={{0,1},{1,0},{2,3},{3,2},{4,5},{5,4},{6,7},{7,6},{8,9},{9,8},{10,11... | collective-permute-start | bytes 1544 | tf_op jit(solution)/shard_map/ppermute | solution.py:175
  115.6 2.7 %collective-permute-done.7 = f32[128]{0:T(128)S(1)} collective-permute-done((f32[128]{0:T(128)S(1)}, f32[128]{0:T(128)S(1)}, u32[]{:S(2)}, u32[]{:S(2)}) %collective-permute-start.7) | collective-permute-done | bytes 544 | tf_op jit(solution)/shard_map/ppermute | solution.py:175
  118.3 3.3 %collective-permute-start.8 = (f32[128]{0:T(128)S(1)}, f32[128]{0:T(128)S(1)}, u32[]{:S(2)}, u32[]{:S(2)}) collective-permute-start(f32[128]{0:T(128)S(1)} %add.209), channel_id=1, source_target_pairs={{0,2},{1,3},{2,0},{3,1},{4,6},{5,7},{6,4},{7,5},{8,10},{9,11},{10,... | collective-permute-start | bytes 1544 | tf_op jit(solution)/shard_map/ppermute | solution.py:175
  121.6 3.7 %collective-permute-done.8 = f32[128]{0:T(128)S(1)} collective-permute-done((f32[128]{0:T(128)S(1)}, f32[128]{0:T(128)S(1)}, u32[]{:S(2)}, u32[]{:S(2)}) %collective-permute-start.8) | collective-permute-done | bytes 544 | tf_op jit(solution)/shard_map/ppermute | solution.py:175
  125.2 2.0 %collective-permute-start.9 = (f32[128]{0:T(128)S(1)}, f32[128]{0:T(128)S(1)}, u32[]{:S(2)}, u32[]{:S(2)}) collective-permute-start(f32[128]{0:T(128)S(1)} %add.210), channel_id=1, source_target_pairs={{0,4},{1,5},{2,6},{3,7},{4,0},{5,1},{6,2},{7,3},{8,12},{9,13},{10,... | collective-permute-start | bytes 1544 | tf_op jit(solution)/shard_map/ppermute | solution.py:175
  127.3 7.4 %collective-permute-done.9 = f32[128]{0:T(128)S(1)} collective-permute-done((f32[128]{0:T(128)S(1)}, f32[128]{0:T(128)S(1)}, u32[]{:S(2)}, u32[]{:S(2)}) %collective-permute-start.9) | collective-permute-done | bytes 544 | tf_op jit(solution)/shard_map/ppermute | solution.py:175
  134.8 0.9 copy.64
  (79 shorter events, 6.3 us)
Async XLA Ops:
  0.8 29.7 %collective-permute-start = (bf16[6,3,1024]{2,0,1:T(8,128)(2,1)S(1)}, bf16[6,3,1024]{2,0,1:T(8,128)(2,1)S(1)}, u32[]{:S(2)}, u32[]{:S(2)}) collective-permute-start(bf16[6,3,1024]{2,0,1:T(8,128)(2,1)S(1)} %slice.194), channel_id=1, source_target_pairs={{0,8},{8,16},{16,24},{24,32},{32,40},{40,48},{48,56},{56,64},{64,7... | collective-permute-start | bytes 110600 | tf_op jit(solution)/shard_map/ppermute | solution.py:19
  22.7 5.2 %copy-start.7 = (bf16[128,3,1024]{2,0,1:T(8,128)(2,1)S(1)}, bf16[128,3,1024]{2,0,1:T(8,128)(2,1)}, u32[]{:S(2)}) copy-start(bf16[128,3,1024]{2,0,1:T(8,128)(2,1)} %param.8) | copy-start | bytes 2359300
  36.6 1.1 copy-start.5
  36.6 1.4 %copy-start.6 = (f32[1,64,16,128]{3,2,0,1:T(8,128)S(1)}, f32[1,64,16,128]{3,2,0,1:T(8,128)}, u32[]{:S(2)}) copy-start(f32[1,64,16,128]{3,2,0,1:T(8,128)} %get-tuple-element.55) | copy-start | bytes 1572868
  36.6 1.4 %copy-start.15 = (f32[128]{0:T(128)S(1)}, f32[128]{0:T(128)}, u32[]{:S(2)}) copy-start(f32[128]{0:T(128)} %compare_convert_fusion.1) | copy-start | bytes 1540
  41.8 12.6 %copy-start.11 = (f32[64,16]{0,1:T(8,128)S(1)}, f32[64,16]{0,1:T(8,128)}, u32[]{:S(2)}) copy-start(f32[64,16]{0,1:T(8,128)} %param.10) | copy-start | bytes 12292
  41.8 12.7 %copy-start.10 = (f32[64,16]{0,1:T(8,128)S(1)}, f32[64,16]{0,1:T(8,128)}, u32[]{:S(2)}) copy-start(f32[64,16]{0,1:T(8,128)} %param.11) | copy-start | bytes 12292
  42.7 18.7 %copy-start = (f32[5,2,16,1024]{3,2,1,0:T(8,128)S(1)}, f32[5,2,16,1024]{3,2,1,0:T(8,128)}, u32[]{:S(2)}) copy-start(f32[5,2,16,1024]{3,2,1,0:T(8,128)} %broadcast_multiply_fusion) | copy-start | bytes 1966084
  43.3 9.0 %collective-permute-start.1 = (f32[2,16,1024]{2,1,0:T(8,128)S(1)}, f32[2,16,1024]{2,1,0:T(8,128)S(1)}, u32[]{:S(2)}, u32[]{:S(2)}) collective-permute-start(f32[2,16,1024]{2,1,0:T(8,128)S(1)} %reshape.287), channel_id=1, source_target_pairs={{0,8},{8,16},{16,24},{24,32},{32,40},{40,48},{48,56},{56,64},{64,7... | collective-permute-start | bytes 393224 | tf_op jit(solution)/shard_map/ppermute | solution.py:19
  52.3 9.1 %collective-permute-start.2 = (f32[2,16,1024]{2,1,0:T(8,128)S(1)}, f32[2,16,1024]{2,1,0:T(8,128)}, u32[]{:S(2)}, u32[]{:S(2)}) collective-permute-start(f32[2,16,1024]{2,1,0:T(8,128)S(1)} %collective-permute-done.1), channel_id=1, source_target_pairs={{0,8},{8,16},{16,24},{24,32},{32,40},{40,48},{48,56},{56,64},{64,7... | collective-permute-start | bytes 393224 | tf_op jit(solution)/shard_map/ppermute | solution.py:19
  62.9 9.9 %collective-permute-start.3 = (f32[2,16,1024]{2,1,0:T(8,128)}, f32[2,16,1024]{2,1,0:T(8,128)}, u32[]{:S(2)}, u32[]{:S(2)}) collective-permute-start(f32[2,16,1024]{2,1,0:T(8,128)} %maximum_add_fusion), channel_id=1, source_target_pairs={{0,16},{8,24},{16,32},{24,40},{32,48},{40,56},{48,64},{56,72},{64,... | collective-permute-start | bytes 393224 | tf_op jit(solution)/shard_map/ppermute | solution.py:19
  73.7 8.7 %collective-permute-start.4 = (f32[2,16,1024]{2,1,0:T(8,128)S(1)}, f32[2,16,1024]{2,1,0:T(8,128)S(1)}, u32[]{:S(2)}, u32[]{:S(2)}) collective-permute-start(f32[2,16,1024]{2,1,0:T(8,128)S(1)} %maximum_add_fusion.1), channel_id=1, source_target_pairs={{0,32},{8,40},{16,48},{24,56},{32,64},{40,72},{48,80},{56,88},{64,... | collective-permute-start | bytes 393224 | tf_op jit(solution)/shard_map/ppermute | solution.py:19
  75.6 11.1 %copy-start.8 = (f32[128,128]{1,0:T(8,128)S(1)}, f32[128,128]{1,0:T(8,128)}, u32[]{:S(2)}) copy-start(f32[128,128]{1,0:T(8,128)} %compare_convert_fusion) | copy-start | bytes 196612
  75.7 11.1 %copy-start.9 = (s32[128,128]{1,0:T(8,128)S(1)}, s32[128,128]{1,0:T(8,128)}, u32[]{:S(2)}) copy-start(s32[128,128]{1,0:T(8,128)} %iota_subtract_fusion) | copy-start | bytes 196612
  82.5 7.6 %collective-permute-start.5 = (f32[2,16,1024]{2,1,0:T(8,128)S(1)}, f32[2,16,1024]{2,1,0:T(8,128)S(1)}, u32[]{:S(2)}, u32[]{:S(2)}) collective-permute-start(f32[2,16,1024]{2,1,0:T(8,128)S(1)} %maximum_add_fusion.2), channel_id=1, source_target_pairs={{0,64},{8,72},{16,80},{24,88},{32,96},{40,104},{48,112},{56,120},{... | collective-permute-start | bytes 393224 | tf_op jit(solution)/shard_map/ppermute | solution.py:19
  90.1 19.7 %collective-permute-start.6 = (f32[2,16,1024]{2,1,0:T(8,128)S(1)}, f32[2,16,1024]{2,1,0:T(8,128)S(1)}, u32[]{:S(2)}, u32[]{:S(2)}) collective-permute-start(f32[2,16,1024]{2,1,0:T(8,128)S(1)} %maximum_add_fusion.3), channel_id=1, source_target_pairs={{0,128},{8,136},{16,144},{24,152},{32,160},{40,168},{48,176},{56,1... | collective-permute-start | bytes 393224 | tf_op jit(solution)/shard_map/ppermute | solution.py:19
  109.8 1.0 copy-start.2
  109.8 1.2 copy-start.3
  109.8 1.2 copy-start.14
  109.8 1.3 copy-start.4
  111.2 1.4 %copy-start.1 = (f32[128,1024]{0,1:T(8,128)S(1)}, f32[128,1024]{0,1:T(8,128)}, u32[]{:S(2)}) copy-start(f32[128,1024]{0,1:T(8,128)} %get-tuple-element.11) | copy-start | bytes 1572868
  111.2 1.4 %copy-start.12 = (f32[1024]{0:T(1024)S(1)}, f32[1024]{0:T(1024)}, u32[]{:S(2)}) copy-start(f32[1024]{0:T(1024)} %param.13) | copy-start | bytes 12292
  112.6 22.0 %copy-start.13 = (f32[1024]{0:T(1024)S(1)}, f32[1024]{0:T(1024)}, u32[]{:S(2)}) copy-start(f32[1024]{0:T(1024)} %param.14) | copy-start | bytes 12292
  112.8 5.5 %collective-permute-start.7 = (f32[128]{0:T(128)S(1)}, f32[128]{0:T(128)S(1)}, u32[]{:S(2)}, u32[]{:S(2)}) collective-permute-start(f32[128]{0:T(128)S(1)} %get-tuple-element.22), channel_id=1, source_target_pairs={{0,1},{1,0},{2,3},{3,2},{4,5},{5,4},{6,7},{7,6},{8,9},{9,8},{10,11... | collective-permute-start | bytes 1544 | tf_op jit(solution)/shard_map/ppermute | solution.py:175
  118.3 7.0 %collective-permute-start.8 = (f32[128]{0:T(128)S(1)}, f32[128]{0:T(128)S(1)}, u32[]{:S(2)}, u32[]{:S(2)}) collective-permute-start(f32[128]{0:T(128)S(1)} %add.209), channel_id=1, source_target_pairs={{0,2},{1,3},{2,0},{3,1},{4,6},{5,7},{6,4},{7,5},{8,10},{9,11},{10,... | collective-permute-start | bytes 1544 | tf_op jit(solution)/shard_map/ppermute | solution.py:175
  125.2 9.4 %collective-permute-start.9 = (f32[128]{0:T(128)S(1)}, f32[128]{0:T(128)S(1)}, u32[]{:S(2)}, u32[]{:S(2)}) collective-permute-start(f32[128]{0:T(128)S(1)} %add.210), channel_id=1, source_target_pairs={{0,4},{1,5},{2,6},{3,7},{4,0},{5,1},{6,2},{7,3},{8,12},{9,13},{10,... | collective-permute-start | bytes 1544 | tf_op jit(solution)/shard_map/ppermute | solution.py:175

commit v8 on v6

--- a/solution.py
+++ b/solution.py
@@ -141,7 +141,7 @@
     def widen(factor):
         return jnp.repeat(factor, group_width, axis=2)
 
-    running = passed_along(summary.reshape(2, mode_count, channels), "ctx", 1)
+    running = passed_along(summary, "ctx", 1)
     pole_inputs, running = lax.optimization_barrier(((rate, angle, residue), running))
     tables = pole_tables(*pole_inputs, SPAN)
     response = tables[0]
@@ -154,11 +154,11 @@
     while distance < reach:
         earlier = passed_along(running, "ctx", distance)
         alive = unbroken(anchor - distance * tok_rows, anchor - 1)
-        factor = widen(power) * alive.astype(jnp.float32)
+        factor = power[..., None] * alive.astype(jnp.float32)
         running = running + complex_times(factor, earlier)
         power = complex_times(power, power)
         distance = distance * 2
-    incoming = running.reshape(2, mode_count, group_count, group_width)
+    incoming = running
     span_index = 0
     entered = (span_begin[span_index] < span_pos[span_index, 0])[None, None, :]
     outputs = [insides[span_index] + jnp.where(entered, carried(tables[1], incoming), 0.0)]

time: 130 us -> 134 us (1.031)
  the two profiles are of different devices: /device:TPU:166 before, /device:TPU:164 now
where the time goes in v8:
time: 134 us; the launch traced here: 133 us
  waiting for transfers between devices  39.6 us (30%)
  starting transfers between devices  38.7 us (29%)
  other arithmetic  22.4 us (17%)
  local copies, waits for them, and re-layouts  15.1 us (11%)
  matrix products  12.6 us (9%)
  between operations  4.46 us (3%)
    ppermute x7, starting transfers between devices, passed_along(): return lax.ppermute(block, axis, route)  31.3 us
    ppermute x7, waiting for transfers between devices, passed_along(): return lax.ppermute(block, axis, route)  25.3 us
    ppermute x3, waiting for transfers between devices, on_device(): squares = squares + lax.ppermute(squares, 'tp', pairs)  14.3 us
    ppermute x3, starting transfers between devices, on_device(): squares = squares + lax.ppermute(squares, 'tp', pairs)  7.42 us
    add x1, other arithmetic, short_filter(): result = result + jnp.where(keep_tap, taps_part[offset][None] * window, 0.0)  5.62 us
    dot_general x1, matrix products, inside_terms(): jnp.einsum('gts,gis->git', matrix_table * same_genome[None], columns, pre...  4.91 us
    mul x1, other arithmetic, pole_tables(): power_re = magnitude * jnp.cos(angle[:, :, None] * counter)  3.86 us
    dot_general x1, matrix products, fresh_terms(): jnp.einsum('rgns,gis->rngi', leaving * tail_mask, columns, precision=HIGH)  3.76 us
  transfers between devices with their start and end apart: 10, of which 8 were waited for; matrix products, arithmetic and copies ran while one was open for 24% of the time, Pallas kernels for 0%

profile of v8, /device:TPU:164, one launch (start us, length us, event | category | flops | bytes accessed | tf_op | source)
XLA Modules:
  0.0 132.9 jit_solution(915778312472118406)
XLA Ops:
  0.0 0.9 slice.169
  0.9 1.9 %collective-permute-start = (bf16[6,3,1024]{2,0,1:T(8,128)(2,1)S(1)}, bf16[6,3,1024]{2,0,1:T(8,128)(2,1)S(1)}, u32[]{:S(2)}, u32[]{:S(2)}) collective-permute-start(bf16[6,3,1024]{2,0,1:T(8,128)(2,1)S(1)} %slice.169), channel_id=1, source_target_pairs={{0,8},{8,16},{16,24},{24,32},{32,40},{40,48},{48,56},{56,64},{64,7... | collective-permute-start | bytes 110600 | tf_op jit(solution)/shard_map/ppermute | solution.py:19
  2.9 0.8 copy.73
  3.6 0.7 neg.12
  4.3 0.8 subtract_bitcast_fusion.1
  5.1 0.8 reduce-window.9
  5.9 1.5 %and_reduce_fusion = (pred[]{:T(512)}, pred[]{:T(512)}, pred[]{:T(512)}, pred[]{:T(512)}, pred[]{:T(512)}, /*index=5*/s32[4]{0:T(128)S(1)}) fusion(s32[]{:T(128)S(6)} %sub.149, s32[]{:T(128)S(6)} %sub.137, s32[]{:T(128)S(6)} %sub.146, s32[]{:T(128)S(6)} %sub.143, s32[]{:T(128)S(6)} %sub.140, s32[]{:T(128)S(6)} %sub.136, s32[4]{0:T(128)} %param.15, ...), kind=kLoop, calls=%fused_computation.120 | loop fusion | flops 63 | bytes 77 | tf_op jit(solution)/shard_map/reduce_or | solution.py:139
  7.6 0.6 slice.186
  8.2 1.5 %fusion.40 = (f32[1,3,1024]{2,0,1:T(1,128)S(1)}, f32[1,3,1024]{2,0,1:T(1,128)S(1)}, f32[1,3,1024]{2,0,1:T(1,128)S(1)}, f32[1,3,1024]{2,0,1:T(1,128)S(1)}, f32[1,...) fusion(f32[7,3,1024]{2,0,1:T(8,128)} %param.9), kind=kLoop, calls=%fused_computation.147 | loop fusion | bytes 172032 | tf_op jit(solution)/shard_map/slice | solution.py:96
  9.7 0.6 broadcast_compare_fusion.1
  11.7 0.6 slice_bitcast_fusion.8
  13.7 0.6 slice_bitcast_fusion.6
  14.3 0.6 slice_bitcast_fusion.4
  15.7 3.1 %fusion.20 = (f32[1,64,16,128]{3,2,0,1:T(8,128)}, f32[1,64,16,128]{3,2,0,1:T(8,128)}) fusion(f32[64,16]{1,0:T(8,128)S(1)} %copy.73, f32[128]{0:T(128)S(1)} %subtract_convert_fusion, f32[64,16]{1,0:T(8,128)S(1)} %copy.72), kind=kLoop, calls=%fused_computation.41 | loop fusion | flops 524288 | bytes 1057280 | tf_op jit(solution)/shard_map/mul | solution.py:58
  18.8 0.7 compare_convert_fusion.1
  19.9 0.9 copy.71
  20.8 0.6 slice.184
  22.5 5.6 %select_add_fusion = f32[128,3,1024]{0,2,1:T(8,128)S(1)} fusion(bf16[128,3,1024]{0,2,1:T(8,128)(2,1)S(1)} %copy.68, bf16[6,3,1024]{0,2,1:T(8,128)(2,1)S(1)} %copy.69, f32[3,1024]{1,0:T(4,128)S(1)} %get-tuple-element.83, f32[3,1024]{1,0:T(4,128)S(1)} %get-tuple-element.84, f32[3,1024]{1,0:T(4,128)S(1)} %get-tuple-element.85, ...), kind=kLoop, calls=%fused_computation.16 | loop fusion | flops 17694720 | bytes 2483072 | tf_op jit(solution)/shard_map/add | solution.py:96
  28.2 0.9 fusion.24
  29.5 3.8 %fusion.5 = f32[2,16,64,16]{1,3,0,2:T(8,128)S(1)} fusion(f32[64,16,128,1]{2,1,3,0:T(8,128)S(1)} %bitcast.137, f32[1,64,16,128]{3,2,0,1:T(8,128)S(1)} %copy-done.4, f32[1,64,16,128]{3,2,0,1:T(8,128)S(1)} %copy-done.3, f32[2,16,64,16]{1,3,0,2:T(8,128)S(1)} %copy.71, f32[128]{0:T(128)S(1)} %compare_convert_fusion.1, pred[]{:T(512)S(6)} %lt.13), kind=kOutput, calls=%fused_computation.20 | convolution fusion | flops 25755648 | bytes 1835521 | tf_op jit(solution)/shard_map/rgns,gis->rngi/dot_general | solution.py:82
  33.3 0.7 copy.74
  34.0 2.7 %collective-permute-start.1 = (f32[2,16,64,16]{2,3,1,0:T(8,128)S(1)}, f32[2,16,64,16]{2,3,1,0:T(8,128)S(1)}, u32[]{:S(2)}, u32[]{:S(2)}) collective-permute-start(f32[2,16,64,16]{2,3,1,0:T(8,128)S(1)} %copy.74), channel_id=1, source_target_pairs={{0,8},{8,16},{16,24},{24,32},{32,40},{40,48},{48,56},{56,64},{64,7... | collective-permute-start | bytes 393224 | tf_op jit(solution)/shard_map/ppermute | solution.py:19
  36.7 7.7 %collective-permute-done.1 = f32[2,16,64,16]{2,3,1,0:T(8,128)S(1)} collective-permute-done((f32[2,16,64,16]{2,3,1,0:T(8,128)S(1)}, f32[2,16,64,16]{2,3,1,0:T(8,128)S(1)}, u32[]{:S(2)}, u32[]{:S(2)}) %collective-permute-start.1) | collective-permute-done | bytes 131104 | tf_op jit(solution)/shard_map/ppermute | solution.py:19
  44.5 2.0 %collective-permute-start.2 = (f32[2,16,64,16]{2,3,1,0:T(8,128)S(1)}, f32[2,16,64,16]{2,3,1,0:T(8,128)S(1)}, u32[]{:S(2)}, u32[]{:S(2)}) collective-permute-start(f32[2,16,64,16]{2,3,1,0:T(8,128)S(1)} %collective-permute-done.1), channel_id=1, source_target_pairs={{0,8},{8,16},{16,24},{24,32},{32,40},{40,48},{48,56},{56,64},{64,7... | collective-permute-start | bytes 393224 | tf_op jit(solution)/shard_map/ppermute | solution.py:19
  46.6 3.9 %fusion.8 = (f32[64,16,129]{2,1,0:T(8,128)S(1)}, f32[64,16,129]{2,1,0:T(8,128)S(1)}) fusion(f32[64,16]{1,0:T(8,128)S(1)} %copy.77, f32[129]{0:T(256)S(1)} %iota_convert_fusion, f32[64,16]{1,0:T(8,128)S(1)} %copy.76), kind=kLoop, calls=%fused_computation.24 | loop fusion | flops 528384 | bytes 1065476 | tf_op jit(solution)/shard_map/mul | solution.py:39
  50.5 4.6 %collective-permute-done.2 = f32[2,16,64,16]{2,3,1,0:T(8,128)S(1)} collective-permute-done((f32[2,16,64,16]{2,3,1,0:T(8,128)S(1)}, f32[2,16,64,16]{2,3,1,0:T(8,128)S(1)}, u32[]{:S(2)}, u32[]{:S(2)}) %collective-permute-start.2) | collective-permute-done | bytes 131104 | tf_op jit(solution)/shard_map/ppermute | solution.py:19
  55.1 1.9 %collective-permute-start.3 = (f32[2,16,64,16]{2,3,1,0:T(8,128)S(1)}, f32[2,16,64,16]{2,3,1,0:T(8,128)}, u32[]{:S(2)}, u32[]{:S(2)}) collective-permute-start(f32[2,16,64,16]{2,3,1,0:T(8,128)S(1)} %maximum_add_fusion), channel_id=1, source_target_pairs={{0,16},{8,24},{16,32},{24,40},{32,48},{40,56},{48,64},{56,72},{64,... | collective-permute-start | bytes 393224 | tf_op jit(solution)/shard_map/ppermute | solution.py:19
  57.1 0.6 slice_bitcast_fusion.12
  57.7 1.4 %copy.78 = f32[64,16]{1,0:T(8,128)} copy(f32[64,16]{0,1:T(8,128)} %get-tuple-element.72) | data formatting | bytes 8192 | tf_op jit(solution)/shard_map/mul | solution.py:44
  59.1 1.4 %copy.75 = f32[64,16]{1,0:T(8,128)} copy(f32[64,16]{0,1:T(8,128)} %get-tuple-element.71) | data formatting | bytes 8192 | tf_op jit(solution)/shard_map/mul | solution.py:44
  60.5 5.7 %collective-permute-done.3 = f32[2,16,64,16]{2,3,1,0:T(8,128)} collective-permute-done((f32[2,16,64,16]{2,3,1,0:T(8,128)S(1)}, f32[2,16,64,16]{2,3,1,0:T(8,128)}, u32[]{:S(2)}, u32[]{:S(2)}) %collective-permute-start.3) | collective-permute-done | bytes 131104 | tf_op jit(solution)/shard_map/ppermute | solution.py:19
  66.2 1.0 multiply_subtract_fusion.3
  67.3 1.9 %collective-permute-start.4 = (f32[2,16,64,16]{2,3,1,0:T(8,128)S(1)}, f32[2,16,64,16]{2,3,1,0:T(8,128)S(1)}, u32[]{:S(2)}, u32[]{:S(2)}) collective-permute-start(f32[2,16,64,16]{2,3,1,0:T(8,128)S(1)} %maximum_add_fusion.1), channel_id=1, source_target_pairs={{0,32},{8,40},{16,48},{24,56},{32,64},{40,72},{48,80},{56,88},{64,... | collective-permute-start | bytes 393224 | tf_op jit(solution)/shard_map/ppermute | solution.py:19
  69.2 1.7 %subtract_bitcast_fusion = (f32[1,64,16,128]{3,2,0,1:T(8,128)}, f32[1,64,16,128]{3,2,0,1:T(8,128)}, f32[64,128]{1,0:T(8,128)S(1)}) fusion(f32[64,16,129]{2,1,0:T(8,128)S(1)} %get-tuple-element.53, f32[64,16,129]{2,1,0:T(8,128)S(1)} %get-tuple-element.52, f32[64,16]{1,0:T(8,128)S(1)} %copy-done.6, f32[64,16]{1,0:T(8,128)S(1)} %copy-done.7), kind=kLoop, calls=%fused_computation.55 | loop fusion | flops 1433600 | bytes 3186688 | tf_op jit(solution)/shard_map/stack | solution.py:48
  70.9 6.8 %collective-permute-done.4 = f32[2,16,64,16]{2,3,1,0:T(8,128)S(1)} collective-permute-done((f32[2,16,64,16]{2,3,1,0:T(8,128)S(1)}, f32[2,16,64,16]{2,3,1,0:T(8,128)S(1)}, u32[]{:S(2)}, u32[]{:S(2)}) %collective-permute-start.4) | collective-permute-done | bytes 131104 | tf_op jit(solution)/shard_map/ppermute | solution.py:19
  77.8 4.5 %collective-permute-start.5 = (f32[2,16,64,16]{2,3,1,0:T(8,128)S(1)}, f32[2,16,64,16]{2,3,1,0:T(8,128)S(1)}, u32[]{:S(2)}, u32[]{:S(2)}) collective-permute-start(f32[2,16,64,16]{2,3,1,0:T(8,128)S(1)} %maximum_add_fusion.2), channel_id=1, source_target_pairs={{0,64},{8,72},{16,80},{24,88},{32,96},{40,104},{48,112},{56,120},{... | collective-permute-start | bytes 393224 | tf_op jit(solution)/shard_map/ppermute | solution.py:19
  82.3 3.3 %fusion.4 = f32[64,128,128]{2,0,1:T(8,128)S(1)} fusion(s32[128,128]{1,0:T(8,128)S(1)} %iota_subtract_fusion, f32[128,128]{1,0:T(8,128)S(1)} %compare_convert_fusion, f32[64,128]{1,0:T(8,128)S(1)} %get-tuple-element.32), kind=kOutput, calls=%fused_computation.15 | convolution fusion | flops 1613758464 | bytes 4358144 | tf_op jit(solution)/shard_map/gk,kts->gts/dot_general | solution.py:33
  86.2 16.3 %collective-permute-start.6 = (f32[2,16,64,16]{2,3,1,0:T(8,128)S(1)}, f32[2,16,64,16]{2,3,1,0:T(8,128)S(1)}, u32[]{:S(2)}, u32[]{:S(2)}) collective-permute-start(f32[2,16,64,16]{2,3,1,0:T(8,128)S(1)} %maximum_add_fusion.3), channel_id=1, source_target_pairs={{0,128},{8,136},{16,144},{24,152},{32,160},{40,168},{48,176},{56,1... | collective-permute-start | bytes 393224 | tf_op jit(solution)/shard_map/ppermute | solution.py:19
  102.6 4.9 %fusion.1 = f32[64,16,128]{2,1,0:T(8,128)S(1)} fusion(f32[64,16,128]{2,1,0:T(8,128)S(1)} %bitcast.138, f32[64,128,128]{2,0,1:T(8,128)S(1)} %fusion.4), kind=kOutput, calls=%fused_computation.2 | convolution fusion | flops 100663296 | bytes 5242880 | tf_op jit(solution)/shard_map/gts,gis->git/dot_general | solution.py:77
  107.7 0.9 copy.81
  108.7 0.6 fusion.7
  110.0 3.1 %collective-permute-start.7 = (f32[128]{0:T(128)S(1)}, f32[128]{0:T(128)S(1)}, u32[]{:S(2)}, u32[]{:S(2)}) collective-permute-start(f32[128]{0:T(128)S(1)} %get-tuple-element.22), channel_id=1, source_target_pairs={{0,1},{1,0},{2,3},{3,2},{4,5},{5,4},{6,7},{7,6},{8,9},{9,8},{10,11... | collective-permute-start | bytes 1544 | tf_op jit(solution)/shard_map/ppermute | solution.py:173
  113.1 2.3 %collective-permute-done.7 = f32[128]{0:T(128)S(1)} collective-permute-done((f32[128]{0:T(128)S(1)}, f32[128]{0:T(128)S(1)}, u32[]{:S(2)}, u32[]{:S(2)}) %collective-permute-start.7) | collective-permute-done | bytes 544 | tf_op jit(solution)/shard_map/ppermute | solution.py:173
  115.5 2.4 %collective-permute-start.8 = (f32[128]{0:T(128)S(1)}, f32[128]{0:T(128)S(1)}, u32[]{:S(2)}, u32[]{:S(2)}) collective-permute-start(f32[128]{0:T(128)S(1)} %add.209), channel_id=1, source_target_pairs={{0,2},{1,3},{2,0},{3,1},{4,6},{5,7},{6,4},{7,5},{8,10},{9,11},{10,... | collective-permute-start | bytes 1544 | tf_op jit(solution)/shard_map/ppermute | solution.py:173
  117.9 4.5 %collective-permute-done.8 = f32[128]{0:T(128)S(1)} collective-permute-done((f32[128]{0:T(128)S(1)}, f32[128]{0:T(128)S(1)}, u32[]{:S(2)}, u32[]{:S(2)}) %collective-permute-start.8) | collective-permute-done | bytes 544 | tf_op jit(solution)/shard_map/ppermute | solution.py:173
  122.4 1.9 %collective-permute-start.9 = (f32[128]{0:T(128)S(1)}, f32[128]{0:T(128)S(1)}, u32[]{:S(2)}, u32[]{:S(2)}) collective-permute-start(f32[128]{0:T(128)S(1)} %add.210), channel_id=1, source_target_pairs={{0,4},{1,5},{2,6},{3,7},{4,0},{5,1},{6,2},{7,3},{8,12},{9,13},{10,... | collective-permute-start | bytes 1544 | tf_op jit(solution)/shard_map/ppermute | solution.py:173
  124.3 7.4 %collective-permute-done.9 = f32[128]{0:T(128)S(1)} collective-permute-done((f32[128]{0:T(128)S(1)}, f32[128]{0:T(128)S(1)}, u32[]{:S(2)}, u32[]{:S(2)}) %collective-permute-start.9) | collective-permute-done | bytes 544 | tf_op jit(solution)/shard_map/ppermute | solution.py:173
  132.0 0.9 copy.82
  (81 shorter events, 3.9 us)
Async XLA Ops:
  0.0 19.5 %copy-start.5 = (bf16[128,3,1024]{2,0,1:T(8,128)(2,1)S(1)}, bf16[128,3,1024]{2,0,1:T(8,128)(2,1)}, u32[]{:S(2)}) copy-start(bf16[128,3,1024]{2,0,1:T(8,128)(2,1)} %param.8) | copy-start | bytes 2359300
  0.9 21.2 %collective-permute-start = (bf16[6,3,1024]{2,0,1:T(8,128)(2,1)S(1)}, bf16[6,3,1024]{2,0,1:T(8,128)(2,1)S(1)}, u32[]{:S(2)}, u32[]{:S(2)}) collective-permute-start(bf16[6,3,1024]{2,0,1:T(8,128)(2,1)S(1)} %slice.169), channel_id=1, source_target_pairs={{0,8},{8,16},{16,24},{24,32},{32,40},{40,48},{48,56},{56,64},{64,7... | collective-permute-start | bytes 110600 | tf_op jit(solution)/shard_map/ppermute | solution.py:19
  28.1 1.1 copy-start.3
  28.1 1.4 %copy-start.4 = (f32[1,64,16,128]{3,2,0,1:T(8,128)S(1)}, f32[1,64,16,128]{3,2,0,1:T(8,128)}, u32[]{:S(2)}) copy-start(f32[1,64,16,128]{3,2,0,1:T(8,128)} %get-tuple-element.55) | copy-start | bytes 1572868
  29.5 14.8 %copy-start.8 = (f32[64,16]{0,1:T(8,128)S(1)}, f32[64,16]{0,1:T(8,128)}, u32[]{:S(2)}) copy-start(f32[64,16]{0,1:T(8,128)} %param.11) | copy-start | bytes 12292
  29.5 14.9 %copy-start.9 = (f32[64,16]{0,1:T(8,128)S(1)}, f32[64,16]{0,1:T(8,128)}, u32[]{:S(2)}) copy-start(f32[64,16]{0,1:T(8,128)} %param.10) | copy-start | bytes 12292
  34.0 10.4 %collective-permute-start.1 = (f32[2,16,64,16]{2,3,1,0:T(8,128)S(1)}, f32[2,16,64,16]{2,3,1,0:T(8,128)S(1)}, u32[]{:S(2)}, u32[]{:S(2)}) collective-permute-start(f32[2,16,64,16]{2,3,1,0:T(8,128)S(1)} %copy.74), channel_id=1, source_target_pairs={{0,8},{8,16},{16,24},{24,32},{32,40},{40,48},{48,56},{56,64},{64,7... | collective-permute-start | bytes 393224 | tf_op jit(solution)/shard_map/ppermute | solution.py:19
  44.5 12.5 %copy-start.14 = (f32[2,64,16]{1,2,0:T(8,128)S(1)}, f32[2,64,16]{1,2,0:T(8,128)}, u32[]{:S(2)}) copy-start(f32[2,64,16]{1,2,0:T(8,128)} %param.12) | copy-start | bytes 24580
  44.5 10.5 %collective-permute-start.2 = (f32[2,16,64,16]{2,3,1,0:T(8,128)S(1)}, f32[2,16,64,16]{2,3,1,0:T(8,128)S(1)}, u32[]{:S(2)}, u32[]{:S(2)}) collective-permute-start(f32[2,16,64,16]{2,3,1,0:T(8,128)S(1)} %collective-permute-done.1), channel_id=1, source_target_pairs={{0,8},{8,16},{16,24},{24,32},{32,40},{40,48},{48,56},{56,64},{64,7... | collective-permute-start | bytes 393224 | tf_op jit(solution)/shard_map/ppermute | solution.py:19
  55.1 11.1 %collective-permute-start.3 = (f32[2,16,64,16]{2,3,1,0:T(8,128)S(1)}, f32[2,16,64,16]{2,3,1,0:T(8,128)}, u32[]{:S(2)}, u32[]{:S(2)}) collective-permute-start(f32[2,16,64,16]{2,3,1,0:T(8,128)S(1)} %maximum_add_fusion), channel_id=1, source_target_pairs={{0,16},{8,24},{16,32},{24,40},{32,48},{40,56},{48,64},{56,72},{64,... | collective-permute-start | bytes 393224 | tf_op jit(solution)/shard_map/ppermute | solution.py:19
  60.5 8.8 %copy-start.6 = (f32[64,16]{1,0:T(8,128)S(1)}, f32[64,16]{1,0:T(8,128)}, u32[]{:S(2)}) copy-start(f32[64,16]{1,0:T(8,128)} %copy.78) | copy-start | bytes 12292
  60.5 8.8 %copy-start.7 = (f32[64,16]{1,0:T(8,128)S(1)}, f32[64,16]{1,0:T(8,128)}, u32[]{:S(2)}) copy-start(f32[64,16]{1,0:T(8,128)} %copy.75) | copy-start | bytes 12292
  67.3 10.4 %collective-permute-start.4 = (f32[2,16,64,16]{2,3,1,0:T(8,128)S(1)}, f32[2,16,64,16]{2,3,1,0:T(8,128)S(1)}, u32[]{:S(2)}, u32[]{:S(2)}) collective-permute-start(f32[2,16,64,16]{2,3,1,0:T(8,128)S(1)} %maximum_add_fusion.1), channel_id=1, source_target_pairs={{0,32},{8,40},{16,48},{24,56},{32,64},{40,72},{48,80},{56,88},{64,... | collective-permute-start | bytes 393224 | tf_op jit(solution)/shard_map/ppermute | solution.py:19
  69.2 8.4 %copy-start.12 = (f32[16,64]{1,0:T(8,128)S(1)}, f32[16,64]{1,0:T(8,128)}, u32[]{:S(2)}) copy-start(f32[16,64]{1,0:T(8,128)} %get-tuple-element.65) | copy-start | bytes 12292
  69.2 8.4 %copy-start.13 = (f32[16,64]{1,0:T(8,128)S(1)}, f32[16,64]{1,0:T(8,128)}, u32[]{:S(2)}) copy-start(f32[16,64]{1,0:T(8,128)} %get-tuple-element.66) | copy-start | bytes 12292
  77.8 8.3 %collective-permute-start.5 = (f32[2,16,64,16]{2,3,1,0:T(8,128)S(1)}, f32[2,16,64,16]{2,3,1,0:T(8,128)S(1)}, u32[]{:S(2)}, u32[]{:S(2)}) collective-permute-start(f32[2,16,64,16]{2,3,1,0:T(8,128)S(1)} %maximum_add_fusion.2), channel_id=1, source_target_pairs={{0,64},{8,72},{16,80},{24,88},{32,96},{40,104},{48,112},{56,120},{... | collective-permute-start | bytes 393224 | tf_op jit(solution)/shard_map/ppermute | solution.py:19
  82.3 3.8 %copy-start.10 = (f32[16,64]{1,0:T(8,128)S(1)}, f32[16,64]{1,0:T(8,128)}, u32[]{:S(2)}) copy-start(f32[16,64]{1,0:T(8,128)} %get-tuple-element.63) | copy-start | bytes 12292
  82.3 3.8 %copy-start.11 = (f32[16,64]{1,0:T(8,128)S(1)}, f32[16,64]{1,0:T(8,128)}, u32[]{:S(2)}) copy-start(f32[16,64]{1,0:T(8,128)} %get-tuple-element.64) | copy-start | bytes 12292
  86.2 21.3 %collective-permute-start.6 = (f32[2,16,64,16]{2,3,1,0:T(8,128)S(1)}, f32[2,16,64,16]{2,3,1,0:T(8,128)S(1)}, u32[]{:S(2)}, u32[]{:S(2)}) collective-permute-start(f32[2,16,64,16]{2,3,1,0:T(8,128)S(1)} %maximum_add_fusion.3), channel_id=1, source_target_pairs={{0,128},{8,136},{16,144},{24,152},{32,160},{40,168},{48,176},{56,1... | collective-permute-start | bytes 393224 | tf_op jit(solution)/shard_map/ppermute | solution.py:19
  107.5 1.1 copy-start.1
  107.5 1.2 copy-start.2
  107.6 1.2 copy-start.17
  108.7 1.0 copy-start
  108.7 1.0 copy-start.15
  109.8 22.0 %copy-start.16 = (f32[1024]{0:T(1024)S(1)}, f32[1024]{0:T(1024)}, u32[]{:S(2)}) copy-start(f32[1024]{0:T(1024)} %param.14) | copy-start | bytes 12292
  110.0 5.5 %collective-permute-start.7 = (f32[128]{0:T(128)S(1)}, f32[128]{0:T(128)S(1)}, u32[]{:S(2)}, u32[]{:S(2)}) collective-permute-start(f32[128]{0:T(128)S(1)} %get-tuple-element.22), channel_id=1, source_target_pairs={{0,1},{1,0},{2,3},{3,2},{4,5},{5,4},{6,7},{7,6},{8,9},{9,8},{10,11... | collective-permute-start | bytes 1544 | tf_op jit(solution)/shard_map/ppermute | solution.py:173
  115.5 7.0 %collective-permute-start.8 = (f32[128]{0:T(128)S(1)}, f32[128]{0:T(128)S(1)}, u32[]{:S(2)}, u32[]{:S(2)}) collective-permute-start(f32[128]{0:T(128)S(1)} %add.209), channel_id=1, source_target_pairs={{0,2},{1,3},{2,0},{3,1},{4,6},{5,7},{6,4},{7,5},{8,10},{9,11},{10,... | collective-permute-start | bytes 1544 | tf_op jit(solution)/shard_map/ppermute | solution.py:173
  122.4 9.4 %collective-permute-start.9 = (f32[128]{0:T(128)S(1)}, f32[128]{0:T(128)S(1)}, u32[]{:S(2)}, u32[]{:S(2)}) collective-permute-start(f32[128]{0:T(128)S(1)} %add.210), channel_id=1, source_target_pairs={{0,4},{1,5},{2,6},{3,7},{4,0},{5,1},{6,2},{7,3},{8,12},{9,13},{10,... | collective-permute-start | bytes 1544 | tf_op jit(solution)/shard_map/ppermute | solution.py:173

commit v9 on v6

--- a/solution.py
+++ b/solution.py
@@ -6,6 +6,7 @@
 D = 8192
 SPAN = 128
 GENOME_MAX = 4096
+X_RING = 4
 
 
 HIGHEST = lax.Precision.HIGHEST
@@ -127,7 +128,7 @@
         leaving, values[span_index], span_pos[span_index], span_begin[span_index]
     )
     keep_state = span_begin[span_index, -1] < span_pos[span_index, 0]
-    summary = jnp.where(keep_state, complex_times(stepping[..., None], summary), 0.0) + fresh_state
+    summary = fresh_state
     freshes.append(fresh_state)
     keepers.append(keep_state)
     device_count = lax.axis_size("ctx")
@@ -166,10 +167,20 @@
     long_part = jnp.transpose(stacked, (0, 3, 1, 2)).reshape(tok_rows, channels)
     gated_rows = query * (long_part + skip[None] * product)
     partial = jnp.sum(gated_rows * gated_rows, axis=1)
-    squares = partial
-    span = 1
-    while span < lax.axis_size("tp"):
-        pairs = [(i, i ^ span) for i in range(lax.axis_size("tp"))]
+    tp_count = lax.axis_size("tp")
+    ring = X_RING if tp_count % X_RING == 0 else 1
+    column = lax.axis_index("tp") % ring
+    gathered = [partial]
+    for offset in range(1, ring):
+        pairs = [(i, i - i % ring + (i + offset) % ring) for i in range(tp_count)]
+        gathered.append(lax.ppermute(partial, "tp", pairs))
+    gathered = jnp.stack(gathered)
+    squares = gathered[(column - 0) % ring]
+    for source in range(1, ring):
+        squares = squares + gathered[(column - source) % ring]
+    span = ring
+    while span < tp_count:
+        pairs = [(i, i ^ span) for i in range(tp_count)]
         squares = squares + lax.ppermute(squares, "tp", pairs)
         span = span * 2
     root_mean = jnp.sqrt(squares / D + EPSILON)

time: 130 us -> 128 us (0.985)
  the two profiles are of different devices: /device:TPU:166 before, /device:TPU:128 now
where the time goes in v9:
time: 128 us; the launch traced here: 127 us
  starting transfers between devices  45.5 us (36%)
  other arithmetic  22.4 us (18%)
  local copies, waits for them, and re-layouts  21.2 us (17%)
  waiting for transfers between devices  18.6 us (15%)
  matrix products  15.2 us (12%)
  between operations  4.04 us (3%)
    ppermute x7, starting transfers between devices, passed_along(): return lax.ppermute(block, axis, route)  27.4 us
    ppermute x7, waiting for transfers between devices, passed_along(): return lax.ppermute(block, axis, route)  13.2 us
    ppermute x3, starting transfers between devices, on_device(): gathered.append(lax.ppermute(partial, 'tp', pairs))  10.2 us
    ppermute x1, starting transfers between devices, on_device(): squares = squares + lax.ppermute(squares, 'tp', pairs)  7.99 us
    dot_general x1, matrix products, inside_terms(): jnp.einsum('gts,gis->git', matrix_table * same_genome[None], columns, pre...  5.73 us
    add x1, other arithmetic, short_filter(): result = result + jnp.where(keep_tap, taps_part[offset][None] * window, 0.0)  5.62 us
    slice x10, local copies, waits for them, and re-layouts, complex_times(): factor_one[0] * factor_two[0] - factor_one[1] * factor_two[1]  4.48 us
    slice x5, local copies, waits for them, and re-layouts, complex_times(): factor_one[1] * factor_two[1]  4.47 us
  transfers between devices with their start and end apart: 11, of which 6 were waited for; matrix products, arithmetic and copies ran while one was open for 31% of the time, Pallas kernels for 0%

profile of v9, /device:TPU:128, one launch (start us, length us, event | category | flops | bytes accessed | tf_op | source)
XLA Modules:
  0.0 127.0 jit_solution(3286217856570392377)
XLA Ops:
  0.0 0.9 slice.219
  0.9 1.9 %collective-permute-start = (bf16[6,3,1024]{2,0,1:T(8,128)(2,1)S(1)}, bf16[6,3,1024]{2,0,1:T(8,128)(2,1)S(1)}, u32[]{:S(2)}, u32[]{:S(2)}) collective-permute-start(bf16[6,3,1024]{2,0,1:T(8,128)(2,1)S(1)} %slice.219), channel_id=1, source_target_pairs={{0,8},{8,16},{16,24},{24,32},{32,40},{40,48},{48,56},{56,64},{64,7... | collective-permute-start | bytes 110600 | tf_op jit(solution)/shard_map/ppermute | solution.py:20
  2.9 0.8 reduce-window.9
  3.7 1.4 %and_reduce_fusion = (pred[]{:T(512)}, pred[]{:T(512)}, pred[]{:T(512)}, pred[]{:T(512)}, pred[]{:T(512)}, /*index=5*/s32[4]{0:T(128)S(1)}) fusion(s32[]{:T(128)S(6)} %sub.153, s32[]{:T(128)S(6)} %sub.141, s32[]{:T(128)S(6)} %sub.150, s32[]{:T(128)S(6)} %sub.147, s32[]{:T(128)S(6)} %sub.144, s32[]{:T(128)S(6)} %sub.140, s32[4]{0:T(128)} %param.15, ...), kind=kLoop, calls=%fused_computation.116 | loop fusion | flops 63 | bytes 77 | tf_op jit(solution)/shard_map/reduce_or | solution.py:140
  5.9 0.8 copy.49
  6.7 0.8 fusion.38
  7.5 0.8 subtract_bitcast_fusion.1
  8.2 1.5 %fusion.44 = (f32[1,3,1024]{2,0,1:T(1,128)S(1)}, f32[1,3,1024]{2,0,1:T(1,128)S(1)}, f32[1,3,1024]{2,0,1:T(1,128)S(1)}, f32[1,3,1024]{2,0,1:T(1,128)S(1)}, f32[1,...) fusion(f32[7,3,1024]{2,0,1:T(8,128)} %param.9), kind=kLoop, calls=%fused_computation.153 | loop fusion | bytes 172032 | tf_op jit(solution)/shard_map/slice | solution.py:97
  13.9 2.0 %fusion.20 = (f32[1,64,16,128]{3,2,0,1:T(8,128)S(1)}, f32[1,64,16,128]{3,2,0,1:T(8,128)S(1)}) fusion(f32[64,16]{1,0:T(8,128)S(1)} %copy.49, f32[128]{0:T(128)S(1)} %subtract_convert_fusion, f32[64,16]{1,0:T(8,128)S(1)} %copy.48), kind=kLoop, calls=%fused_computation.41 | loop fusion | flops 524288 | bytes 1057280 | tf_op jit(solution)/shard_map/mul | solution.py:59
  17.3 5.6 %select_add_fusion = f32[128,3,1024]{0,2,1:T(8,128)S(1)} fusion(bf16[128,3,1024]{0,2,1:T(8,128)(2,1)S(1)} %copy.45, bf16[6,3,1024]{0,2,1:T(8,128)(2,1)S(1)} %copy.46, f32[3,1024]{1,0:T(4,128)S(1)} %get-tuple-element.82, f32[3,1024]{1,0:T(4,128)S(1)} %get-tuple-element.83, f32[3,1024]{1,0:T(4,128)S(1)} %get-tuple-element.84, ...), kind=kLoop, calls=%fused_computation.16 | loop fusion | flops 17694720 | bytes 2483072 | tf_op jit(solution)/shard_map/add | solution.py:97
  23.0 3.8 %convolution_bitcast_fusion = f32[2,16,64,16]{1,3,0,2:T(8,128)S(1)} fusion(f32[64,16,128,1]{2,1,3,0:T(8,128)S(1)} %bitcast.154, f32[1,64,16,128]{3,2,0,1:T(8,128)S(1)} %get-tuple-element.53, f32[1,64,16,128]{3,2,0,1:T(8,128)S(1)} %get-tuple-element.52, f32[128]{0:T(128)S(1)} %compare_convert_fusion.1), kind=kOutput, calls=%fused_computation.19 | convolution fusion | flops 25690112 | bytes 1704448 | tf_op jit(solution)/shard_map/rgns,gis->rngi/dot_general | solution.py:83
  26.8 0.9 copy.50
  28.3 3.6 %collective-permute-start.1 = (f32[2,16,1024]{2,1,0:T(8,128)S(1)}, f32[2,16,1024]{2,1,0:T(8,128)S(1)}, u32[]{:S(2)}, u32[]{:S(2)}) collective-permute-start(f32[2,16,1024]{2,1,0:T(8,128)S(1)} %reshape.229), channel_id=1, source_target_pairs={{0,8},{8,16},{16,24},{24,32},{32,40},{40,48},{48,56},{56,64},{64,7... | collective-permute-start | bytes 393224 | tf_op jit(solution)/shard_map/ppermute | solution.py:20
  32.2 0.9 slice.278
  33.3 0.9 slice.274
  34.4 0.9 slice.270
  35.5 0.9 slice.266
  36.5 0.9 slice.262
  37.6 0.9 slice.258
  38.7 0.9 slice.254
  39.8 0.9 slice.250
  40.9 0.9 slice.246
  42.0 0.9 slice.242
  43.1 2.2 %collective-permute-start.2 = (f32[2,16,1024]{2,1,0:T(8,128)S(1)}, f32[2,16,1024]{2,1,0:T(8,128)S(1)}, u32[]{:S(2)}, u32[]{:S(2)}) collective-permute-start(f32[2,16,1024]{2,1,0:T(8,128)S(1)} %collective-permute-done.1), channel_id=1, source_target_pairs={{0,8},{8,16},{16,24},{24,32},{32,40},{40,48},{48,56},{56,64},{64,7... | collective-permute-start | bytes 393224 | tf_op jit(solution)/shard_map/ppermute | solution.py:20
  45.4 3.9 %fusion.7 = (f32[64,16,129]{2,1,0:T(8,128)S(1)}, f32[64,16,129]{2,1,0:T(8,128)S(1)}) fusion(f32[64,16]{1,0:T(8,128)S(1)} %copy.53, f32[129]{0:T(256)S(1)} %iota_convert_fusion, f32[64,16]{1,0:T(8,128)S(1)} %copy.52), kind=kLoop, calls=%fused_computation.23 | loop fusion | flops 528384 | bytes 1065476 | tf_op jit(solution)/shard_map/mul | solution.py:40
  49.2 3.0 %collective-permute-done.2 = f32[2,16,1024]{2,1,0:T(8,128)S(1)} collective-permute-done((f32[2,16,1024]{2,1,0:T(8,128)S(1)}, f32[2,16,1024]{2,1,0:T(8,128)S(1)}, u32[]{:S(2)}, u32[]{:S(2)}) %collective-permute-start.2) | collective-permute-done | bytes 131104 | tf_op jit(solution)/shard_map/ppermute | solution.py:20
  52.2 0.9 multiply_subtract_fusion.4
  53.8 1.9 %collective-permute-start.3 = (f32[2,16,1024]{2,1,0:T(8,128)}, f32[2,16,1024]{2,1,0:T(8,128)}, u32[]{:S(2)}, u32[]{:S(2)}) collective-permute-start(f32[2,16,1024]{2,1,0:T(8,128)} %maximum_add_fusion), channel_id=1, source_target_pairs={{0,16},{8,24},{16,32},{24,40},{32,48},{40,56},{48,64},{56,72},{64,... | collective-permute-start | bytes 393224 | tf_op jit(solution)/shard_map/ppermute | solution.py:20
  55.7 0.7 slice_bitcast_fusion.12
  56.4 0.7 copy.54
  57.8 5.9 %collective-permute-done.3 = f32[2,16,1024]{2,1,0:T(8,128)} collective-permute-done((f32[2,16,1024]{2,1,0:T(8,128)}, f32[2,16,1024]{2,1,0:T(8,128)}, u32[]{:S(2)}, u32[]{:S(2)}) %collective-permute-start.3) | collective-permute-done | bytes 131104 | tf_op jit(solution)/shard_map/ppermute | solution.py:20
  63.6 1.0 multiply_subtract_fusion.3
  64.6 1.9 %collective-permute-start.4 = (f32[2,16,1024]{2,1,0:T(8,128)S(1)}, f32[2,16,1024]{2,1,0:T(8,128)S(1)}, u32[]{:S(2)}, u32[]{:S(2)}) collective-permute-start(f32[2,16,1024]{2,1,0:T(8,128)S(1)} %maximum_add_fusion.1), channel_id=1, source_target_pairs={{0,32},{8,40},{16,48},{24,56},{32,64},{40,72},{48,80},{56,88},{64,... | collective-permute-start | bytes 393224 | tf_op jit(solution)/shard_map/ppermute | solution.py:20
  66.6 2.4 %subtract_bitcast_fusion = (f32[1,64,16,128]{3,2,0,1:T(8,128)}, f32[1,64,16,128]{3,2,0,1:T(8,128)}, f32[64,128]{1,0:T(8,128)S(1)}) fusion(f32[64,16,129]{2,1,0:T(8,128)S(1)} %get-tuple-element.51, f32[64,16,129]{2,1,0:T(8,128)S(1)} %get-tuple-element.50, f32[64,16]{1,0:T(8,128)} %copy.54, f32[64,16]{1,0:T(8,128)} %copy.51), kind=kLoop, calls=%fused_computation.55 | loop fusion | flops 1433600 | bytes 3186688 | tf_op jit(solution)/shard_map/stack | solution.py:49
  69.0 4.4 %collective-permute-done.4 = f32[2,16,1024]{2,1,0:T(8,128)S(1)} collective-permute-done((f32[2,16,1024]{2,1,0:T(8,128)S(1)}, f32[2,16,1024]{2,1,0:T(8,128)S(1)}, u32[]{:S(2)}, u32[]{:S(2)}) %collective-permute-start.4) | collective-permute-done | bytes 131104 | tf_op jit(solution)/shard_map/ppermute | solution.py:20
  73.4 4.4 %collective-permute-start.5 = (f32[2,16,1024]{2,1,0:T(8,128)S(1)}, f32[2,16,1024]{2,1,0:T(8,128)S(1)}, u32[]{:S(2)}, u32[]{:S(2)}) collective-permute-start(f32[2,16,1024]{2,1,0:T(8,128)S(1)} %maximum_add_fusion.2), channel_id=1, source_target_pairs={{0,64},{8,72},{16,80},{24,88},{32,96},{40,104},{48,112},{56,120},{... | collective-permute-start | bytes 393224 | tf_op jit(solution)/shard_map/ppermute | solution.py:20
  77.9 3.2 %fusion.4 = f32[64,128,128]{2,0,1:T(8,128)S(1)} fusion(s32[128,128]{1,0:T(8,128)S(1)} %iota_subtract_fusion, f32[128,128]{1,0:T(8,128)S(1)} %compare_convert_fusion, f32[64,128]{1,0:T(8,128)S(1)} %get-tuple-element.30), kind=kOutput, calls=%fused_computation.15 | convolution fusion | flops 1613758464 | bytes 4358144 | tf_op jit(solution)/shard_map/gk,kts->gts/dot_general | solution.py:34
  81.2 11.4 %collective-permute-start.6 = (f32[2,16,1024]{2,1,0:T(8,128)S(1)}, f32[2,16,1024]{2,1,0:T(8,128)S(1)}, u32[]{:S(2)}, u32[]{:S(2)}) collective-permute-start(f32[2,16,1024]{2,1,0:T(8,128)S(1)} %maximum_add_fusion.3), channel_id=1, source_target_pairs={{0,128},{8,136},{16,144},{24,152},{32,160},{40,168},{48,176},{56,1... | collective-permute-start | bytes 393224 | tf_op jit(solution)/shard_map/ppermute | solution.py:20
  92.7 5.7 %fusion.1 = f32[64,16,128]{2,1,0:T(8,128)} fusion(f32[64,16,128]{2,1,0:T(8,128)S(1)} %bitcast.155, f32[64,128,128]{2,0,1:T(8,128)S(1)} %fusion.4), kind=kOutput, calls=%fused_computation.2 | convolution fusion | flops 100663296 | bytes 5242880 | tf_op jit(solution)/shard_map/gts,gis->git/dot_general | solution.py:78
  99.6 2.4 %fusion.6 = f32[64,16,128]{2,1,0:T(8,128)S(1)} fusion(f32[64,16,128]{2,1,0:T(8,128)} %fusion.1, f32[1,64,16,128]{3,2,0,1:T(8,128)S(1)} %copy-done.1, f32[1,64,16,128]{3,2,0,1:T(8,128)S(1)} %copy-done, f32[2,16,64,16]{3,2,1,0:T(8,128)S(1)} %reshape.230, pred[128]{0:T(512)(128)(4,1)S(1)} %copy-done.14), kind=kOutput, calls=%fused_computation.22 | convolution fusion | flops 25690112 | bytes 2228352 | tf_op jit(solution)/shard_map/rgnt,rngi->git/dot_general | solution.py:87
  102.3 4.7 %collective-permute-start.9 = (f32[128]{0:T(128)S(1)}, f32[128]{0:T(128)S(1)}, u32[]{:S(2)}, u32[]{:S(2)}) collective-permute-start(f32[128]{0:T(128)S(1)} %get-tuple-element.22), channel_id=1, source_target_pairs={{0,3},{1,0},{2,1},{3,2},{4,7},{5,4},{6,5},{7,6},{8,11},{9,8},{10,9... | collective-permute-start | bytes 1544 | tf_op jit(solution)/shard_map/ppermute | solution.py:176
  107.0 2.7 %collective-permute-start.8 = (f32[128]{0:T(128)S(1)}, f32[128]{0:T(128)S(1)}, u32[]{:S(2)}, u32[]{:S(2)}) collective-permute-start(f32[128]{0:T(128)S(1)} %get-tuple-element.22), channel_id=1, source_target_pairs={{0,2},{1,3},{2,0},{3,1},{4,6},{5,7},{6,4},{7,5},{8,10},{9,11},{10,... | collective-permute-start | bytes 1544 | tf_op jit(solution)/shard_map/ppermute | solution.py:176
  109.7 2.8 %collective-permute-start.7 = (f32[128]{0:T(128)S(1)}, f32[128]{0:T(128)S(1)}, u32[]{:S(2)}, u32[]{:S(2)}) collective-permute-start(f32[128]{0:T(128)S(1)} %get-tuple-element.22), channel_id=1, source_target_pairs={{0,1},{1,2},{2,3},{3,0},{4,5},{5,6},{6,7},{7,4},{8,9},{9,10},{10,1... | collective-permute-start | bytes 1544 | tf_op jit(solution)/shard_map/ppermute | solution.py:176
  112.5 1.4 %collective-permute-done.8 = f32[128]{0:T(128)S(1)} collective-permute-done((f32[128]{0:T(128)S(1)}, f32[128]{0:T(128)S(1)}, u32[]{:S(2)}, u32[]{:S(2)}) %collective-permute-start.8) | collective-permute-done | bytes 544 | tf_op jit(solution)/shard_map/ppermute | solution.py:176
  114.0 2.4 %collective-permute-done.7 = f32[128]{0:T(128)S(1)} collective-permute-done((f32[128]{0:T(128)S(1)}, f32[128]{0:T(128)S(1)}, u32[]{:S(2)}, u32[]{:S(2)}) %collective-permute-start.7) | collective-permute-done | bytes 544 | tf_op jit(solution)/shard_map/ppermute | solution.py:176
  116.4 8.0 %collective-permute-start.10 = (f32[128]{0:T(128)S(1)}, f32[128]{0:T(128)S(1)}, u32[]{:S(2)}, u32[]{:S(2)}) collective-permute-start(f32[128]{0:T(128)S(1)} %fusion.32), channel_id=1, source_target_pairs={{0,4},{1,5},{2,6},{3,7},{4,0},{5,1},{6,2},{7,3},{8,12},{9,13},{10,... | collective-permute-start | bytes 1544 | tf_op jit(solution)/shard_map/ppermute | solution.py:184
  124.4 1.5 %collective-permute-done.10 = f32[128]{0:T(128)S(1)} collective-permute-done((f32[128]{0:T(128)S(1)}, f32[128]{0:T(128)S(1)}, u32[]{:S(2)}, u32[]{:S(2)}) %collective-permute-start.10) | collective-permute-done | bytes 544 | tf_op jit(solution)/shard_map/ppermute | solution.py:184
  126.2 0.8 copy.58
  (92 shorter events, 8.9 us)
Async XLA Ops:
  0.0 16.5 %copy-start.2 = (bf16[128,3,1024]{2,0,1:T(8,128)(2,1)S(1)}, bf16[128,3,1024]{2,0,1:T(8,128)(2,1)}, u32[]{:S(2)}) copy-start(bf16[128,3,1024]{2,0,1:T(8,128)(2,1)} %param.8) | copy-start | bytes 2359300
  0.9 16.0 %collective-permute-start = (bf16[6,3,1024]{2,0,1:T(8,128)(2,1)S(1)}, bf16[6,3,1024]{2,0,1:T(8,128)(2,1)S(1)}, u32[]{:S(2)}, u32[]{:S(2)}) collective-permute-start(bf16[6,3,1024]{2,0,1:T(8,128)(2,1)S(1)} %slice.219), channel_id=1, source_target_pairs={{0,8},{8,16},{16,24},{24,32},{32,40},{40,48},{48,56},{56,64},{64,7... | collective-permute-start | bytes 110600 | tf_op jit(solution)/shard_map/ppermute | solution.py:20
  28.3 14.6 %collective-permute-start.1 = (f32[2,16,1024]{2,1,0:T(8,128)S(1)}, f32[2,16,1024]{2,1,0:T(8,128)S(1)}, u32[]{:S(2)}, u32[]{:S(2)}) collective-permute-start(f32[2,16,1024]{2,1,0:T(8,128)S(1)} %reshape.229), channel_id=1, source_target_pairs={{0,8},{8,16},{16,24},{24,32},{32,40},{40,48},{48,56},{56,64},{64,7... | collective-permute-start | bytes 393224 | tf_op jit(solution)/shard_map/ppermute | solution.py:20
  39.8 3.1 %copy-start.10 = (f32[64,16]{0,1:T(8,128)S(1)}, f32[64,16]{0,1:T(8,128)}, u32[]{:S(2)}) copy-start(f32[64,16]{0,1:T(8,128)} %param.11) | copy-start | bytes 12292
  39.8 3.2 %copy-start.11 = (f32[64,16]{0,1:T(8,128)S(1)}, f32[64,16]{0,1:T(8,128)}, u32[]{:S(2)}) copy-start(f32[64,16]{0,1:T(8,128)} %param.10) | copy-start | bytes 12292
  43.1 9.1 %copy-start.9 = (f32[1,16,1024]{2,1,0:T(8,128)S(1)}, f32[1,16,1024]{2,1,0:T(8,128)}, u32[]{:S(2)}) copy-start(f32[1,16,1024]{2,1,0:T(8,128)} %slice.242) | copy-start | bytes 196612
  43.1 9.1 %collective-permute-start.2 = (f32[2,16,1024]{2,1,0:T(8,128)S(1)}, f32[2,16,1024]{2,1,0:T(8,128)S(1)}, u32[]{:S(2)}, u32[]{:S(2)}) collective-permute-start(f32[2,16,1024]{2,1,0:T(8,128)S(1)} %collective-permute-done.1), channel_id=1, source_target_pairs={{0,8},{8,16},{16,24},{24,32},{32,40},{40,48},{48,56},{56,64},{64,7... | collective-permute-start | bytes 393224 | tf_op jit(solution)/shard_map/ppermute | solution.py:20
  53.8 9.9 %collective-permute-start.3 = (f32[2,16,1024]{2,1,0:T(8,128)}, f32[2,16,1024]{2,1,0:T(8,128)}, u32[]{:S(2)}, u32[]{:S(2)}) collective-permute-start(f32[2,16,1024]{2,1,0:T(8,128)} %maximum_add_fusion), channel_id=1, source_target_pairs={{0,16},{8,24},{16,32},{24,40},{32,48},{40,56},{48,64},{56,72},{64,... | collective-permute-start | bytes 393224 | tf_op jit(solution)/shard_map/ppermute | solution.py:20
  64.6 8.7 %collective-permute-start.4 = (f32[2,16,1024]{2,1,0:T(8,128)S(1)}, f32[2,16,1024]{2,1,0:T(8,128)S(1)}, u32[]{:S(2)}, u32[]{:S(2)}) collective-permute-start(f32[2,16,1024]{2,1,0:T(8,128)S(1)} %maximum_add_fusion.1), channel_id=1, source_target_pairs={{0,32},{8,40},{16,48},{24,56},{32,64},{40,72},{48,80},{56,88},{64,... | collective-permute-start | bytes 393224 | tf_op jit(solution)/shard_map/ppermute | solution.py:20
  66.6 6.8 %copy-start.7 = (f32[1,16,1024]{2,1,0:T(8,128)S(1)}, f32[1,16,1024]{2,1,0:T(8,128)}, u32[]{:S(2)}) copy-start(f32[1,16,1024]{2,1,0:T(8,128)} %slice.262) | copy-start | bytes 196612
  66.6 6.8 %copy-start.8 = (f32[1,16,1024]{2,1,0:T(8,128)S(1)}, f32[1,16,1024]{2,1,0:T(8,128)}, u32[]{:S(2)}) copy-start(f32[1,16,1024]{2,1,0:T(8,128)} %slice.258) | copy-start | bytes 196612
  73.4 7.7 %collective-permute-start.5 = (f32[2,16,1024]{2,1,0:T(8,128)S(1)}, f32[2,16,1024]{2,1,0:T(8,128)S(1)}, u32[]{:S(2)}, u32[]{:S(2)}) collective-permute-start(f32[2,16,1024]{2,1,0:T(8,128)S(1)} %maximum_add_fusion.2), channel_id=1, source_target_pairs={{0,64},{8,72},{16,80},{24,88},{32,96},{40,104},{48,112},{56,120},{... | collective-permute-start | bytes 393224 | tf_op jit(solution)/shard_map/ppermute | solution.py:20
  77.8 3.3 %copy-start.5 = (f32[1,16,1024]{2,1,0:T(8,128)S(1)}, f32[1,16,1024]{2,1,0:T(8,128)}, u32[]{:S(2)}) copy-start(f32[1,16,1024]{2,1,0:T(8,128)} %slice.270) | copy-start | bytes 196612
  77.8 3.3 %copy-start.6 = (f32[1,16,1024]{2,1,0:T(8,128)S(1)}, f32[1,16,1024]{2,1,0:T(8,128)}, u32[]{:S(2)}) copy-start(f32[1,16,1024]{2,1,0:T(8,128)} %slice.266) | copy-start | bytes 196612
  81.2 17.2 %collective-permute-start.6 = (f32[2,16,1024]{2,1,0:T(8,128)S(1)}, f32[2,16,1024]{2,1,0:T(8,128)S(1)}, u32[]{:S(2)}, u32[]{:S(2)}) collective-permute-start(f32[2,16,1024]{2,1,0:T(8,128)S(1)} %maximum_add_fusion.3), channel_id=1, source_target_pairs={{0,128},{8,136},{16,144},{24,152},{32,160},{40,168},{48,176},{56,1... | collective-permute-start | bytes 393224 | tf_op jit(solution)/shard_map/ppermute | solution.py:20
  92.7 5.8 %copy-start.3 = (f32[1,16,1024]{2,1,0:T(8,128)S(1)}, f32[1,16,1024]{2,1,0:T(8,128)}, u32[]{:S(2)}) copy-start(f32[1,16,1024]{2,1,0:T(8,128)} %slice.278) | copy-start | bytes 196612
  92.7 5.8 %copy-start.4 = (f32[1,16,1024]{2,1,0:T(8,128)S(1)}, f32[1,16,1024]{2,1,0:T(8,128)}, u32[]{:S(2)}) copy-start(f32[1,16,1024]{2,1,0:T(8,128)} %slice.274) | copy-start | bytes 196612
  98.4 1.0 copy-start
  98.4 1.2 copy-start.1
  98.4 1.2 copy-start.14
  99.6 2.5 %copy-start.12 = (f32[1024]{0:T(1024)S(1)}, f32[1024]{0:T(1024)}, u32[]{:S(2)}) copy-start(f32[1024]{0:T(1024)} %param.13) | copy-start | bytes 12292
  102.1 23.9 %copy-start.13 = (f32[1024]{0:T(1024)S(1)}, f32[1024]{0:T(1024)}, u32[]{:S(2)}) copy-start(f32[1024]{0:T(1024)} %param.14) | copy-start | bytes 12292
  102.3 10.2 %collective-permute-start.9 = (f32[128]{0:T(128)S(1)}, f32[128]{0:T(128)S(1)}, u32[]{:S(2)}, u32[]{:S(2)}) collective-permute-start(f32[128]{0:T(128)S(1)} %get-tuple-element.22), channel_id=1, source_target_pairs={{0,3},{1,0},{2,1},{3,2},{4,7},{5,4},{6,5},{7,6},{8,11},{9,8},{10,9... | collective-permute-start | bytes 1544 | tf_op jit(solution)/shard_map/ppermute | solution.py:176
  107.0 7.0 %collective-permute-start.8 = (f32[128]{0:T(128)S(1)}, f32[128]{0:T(128)S(1)}, u32[]{:S(2)}, u32[]{:S(2)}) collective-permute-start(f32[128]{0:T(128)S(1)} %get-tuple-element.22), channel_id=1, source_target_pairs={{0,2},{1,3},{2,0},{3,1},{4,6},{5,7},{6,4},{7,5},{8,10},{9,11},{10,... | collective-permute-start | bytes 1544 | tf_op jit(solution)/shard_map/ppermute | solution.py:176
  109.7 6.7 %collective-permute-start.7 = (f32[128]{0:T(128)S(1)}, f32[128]{0:T(128)S(1)}, u32[]{:S(2)}, u32[]{:S(2)}) collective-permute-start(f32[128]{0:T(128)S(1)} %get-tuple-element.22), channel_id=1, source_target_pairs={{0,1},{1,2},{2,3},{3,0},{4,5},{5,6},{6,7},{7,4},{8,9},{9,10},{10,1... | collective-permute-start | bytes 1544 | tf_op jit(solution)/shard_map/ppermute | solution.py:176
  116.4 9.5 %collective-permute-start.10 = (f32[128]{0:T(128)S(1)}, f32[128]{0:T(128)S(1)}, u32[]{:S(2)}, u32[]{:S(2)}) collective-permute-start(f32[128]{0:T(128)S(1)} %fusion.32), channel_id=1, source_target_pairs={{0,4},{1,5},{2,6},{3,7},{4,0},{5,1},{6,2},{7,3},{8,12},{9,13},{10,... | collective-permute-start | bytes 1544 | tf_op jit(solution)/shard_map/ppermute | solution.py:184

commit v10 on v9

--- a/solution.py
+++ b/solution.py
@@ -142,7 +142,7 @@
     def widen(factor):
         return jnp.repeat(factor, group_width, axis=2)
 
-    running = passed_along(summary.reshape(2, mode_count, channels), "ctx", 1)
+    running = passed_along(summary, "ctx", 1)
     pole_inputs, running = lax.optimization_barrier(((rate, angle, residue), running))
     tables = pole_tables(*pole_inputs, SPAN)
     response = tables[0]
@@ -155,11 +155,11 @@
     while distance < reach:
         earlier = passed_along(running, "ctx", distance)
         alive = unbroken(anchor - distance * tok_rows, anchor - 1)
-        factor = widen(power) * alive.astype(jnp.float32)
+        factor = power[..., None] * alive.astype(jnp.float32)
         running = running + complex_times(factor, earlier)
         power = complex_times(power, power)
         distance = distance * 2
-    incoming = running.reshape(2, mode_count, group_count, group_width)
+    incoming = running
     span_index = 0
     entered = (span_begin[span_index] < span_pos[span_index, 0])[None, None, :]
     outputs = [insides[span_index] + jnp.where(entered, carried(tables[1], incoming), 0.0)]

time: 128 us -> 131 us (1.023)
  the two profiles are of different devices: /device:TPU:128 before, /device:TPU:160 now
where the time goes in v10:
time: 131 us
  starting transfers between devices  43.4 us (33%)
  waiting for transfers between devices  36.5 us (28%)
  other arithmetic  21.3 us (16%)
  local copies, waits for them, and re-layouts  13.1 us (10%)
  matrix products  12.6 us (10%)
  between operations  3.79 us (3%)
    ppermute x7, starting transfers between devices, passed_along(): return lax.ppermute(block, axis, route)  31.3 us
    ppermute x7, waiting for transfers between devices, passed_along(): return lax.ppermute(block, axis, route)  25.2 us
    ppermute x3, starting transfers between devices, on_device(): gathered.append(lax.ppermute(partial, 'tp', pairs))  10.2 us
    ppermute x1, waiting for transfers between devices, on_device(): squares = squares + lax.ppermute(squares, 'tp', pairs)  7.44 us
    add x1, other arithmetic, short_filter(): result = result + jnp.where(keep_tap, taps_part[offset][None] * window, 0.0)  5.62 us
    dot_general x1, matrix products, inside_terms(): jnp.einsum('gts,gis->git', matrix_table * same_genome[None], columns, pre...  4.91 us
    mul x1, other arithmetic, pole_tables(): power_re = magnitude * jnp.cos(angle[:, :, None] * counter)  3.86 us
    ppermute x3, waiting for transfers between devices, on_device(): gathered.append(lax.ppermute(partial, 'tp', pairs))  3.83 us
  transfers between devices with their start and end apart: 11, of which 8 were waited for; matrix products, arithmetic and copies ran while one was open for 23% of the time, Pallas kernels for 0%

profile of v10, /device:TPU:160, one launch (start us, length us, event | category | flops | bytes accessed | tf_op | source)
XLA Modules:
  0.0 130.6 jit_solution(3376721445330069719)
XLA Ops:
  0.0 0.9 slice.159
  0.9 1.9 %collective-permute-start = (bf16[6,3,1024]{2,0,1:T(8,128)(2,1)S(1)}, bf16[6,3,1024]{2,0,1:T(8,128)(2,1)S(1)}, u32[]{:S(2)}, u32[]{:S(2)}) collective-permute-start(bf16[6,3,1024]{2,0,1:T(8,128)(2,1)S(1)} %slice.159), channel_id=1, source_target_pairs={{0,8},{8,16},{16,24},{24,32},{32,40},{40,48},{48,56},{56,64},{64,7... | collective-permute-start | bytes 110600 | tf_op jit(solution)/shard_map/ppermute | solution.py:20
  2.9 0.8 reduce-window.9
  3.7 1.4 %and_reduce_fusion = (pred[]{:T(512)}, pred[]{:T(512)}, pred[]{:T(512)}, pred[]{:T(512)}, pred[]{:T(512)}, /*index=5*/s32[4]{0:T(128)S(1)}) fusion(s32[]{:T(128)S(6)} %sub.153, s32[]{:T(128)S(6)} %sub.141, s32[]{:T(128)S(6)} %sub.150, s32[]{:T(128)S(6)} %sub.147, s32[]{:T(128)S(6)} %sub.144, s32[]{:T(128)S(6)} %sub.140, s32[4]{0:T(128)} %param.15, ...), kind=kLoop, calls=%fused_computation.115 | loop fusion | flops 63 | bytes 77 | tf_op jit(solution)/shard_map/reduce_or | solution.py:140
  5.3 0.7 slice.174
  5.9 0.8 copy.67
  6.7 0.8 fusion.37
  7.5 0.8 subtract_bitcast_fusion.1
  8.3 1.5 %fusion.43 = (f32[1,3,1024]{2,0,1:T(1,128)S(1)}, f32[1,3,1024]{2,0,1:T(1,128)S(1)}, f32[1,3,1024]{2,0,1:T(1,128)S(1)}, f32[1,3,1024]{2,0,1:T(1,128)S(1)}, f32[1,...) fusion(f32[7,3,1024]{2,0,1:T(8,128)} %param.9), kind=kLoop, calls=%fused_computation.152 | loop fusion | bytes 172032 | tf_op jit(solution)/shard_map/slice | solution.py:97
  9.8 0.5 broadcast_compare_fusion.1
  11.7 0.6 slice_bitcast_fusion.8
  13.6 0.6 slice_bitcast_fusion.6
  14.2 0.6 slice_bitcast_fusion.4
  15.6 2.0 %fusion.19 = (f32[1,64,16,128]{3,2,0,1:T(8,128)S(1)}, f32[1,64,16,128]{3,2,0,1:T(8,128)S(1)}) fusion(f32[64,16]{1,0:T(8,128)S(1)} %copy.67, f32[128]{0:T(128)S(1)} %subtract_convert_fusion, f32[64,16]{1,0:T(8,128)S(1)} %copy.66), kind=kLoop, calls=%fused_computation.40 | loop fusion | flops 524288 | bytes 1057280 | tf_op jit(solution)/shard_map/mul | solution.py:59
  17.5 0.7 compare_convert_fusion.1
  19.1 5.6 %select_add_fusion = f32[128,3,1024]{0,2,1:T(8,128)S(1)} fusion(bf16[128,3,1024]{0,2,1:T(8,128)(2,1)S(1)} %copy.63, bf16[6,3,1024]{0,2,1:T(8,128)(2,1)S(1)} %copy.64, f32[3,1024]{1,0:T(4,128)S(1)} %get-tuple-element.82, f32[3,1024]{1,0:T(4,128)S(1)} %get-tuple-element.83, f32[3,1024]{1,0:T(4,128)S(1)} %get-tuple-element.84, ...), kind=kLoop, calls=%fused_computation.16 | loop fusion | flops 17694720 | bytes 2483072 | tf_op jit(solution)/shard_map/add | solution.py:97
  24.7 0.9 fusion.23
  25.6 3.8 %convolution_bitcast_fusion = f32[2,16,64,16]{1,3,0,2:T(8,128)S(1)} fusion(f32[64,16,128,1]{2,1,3,0:T(8,128)S(1)} %bitcast.133, f32[1,64,16,128]{3,2,0,1:T(8,128)S(1)} %get-tuple-element.53, f32[1,64,16,128]{3,2,0,1:T(8,128)S(1)} %get-tuple-element.52, f32[128]{0:T(128)S(1)} %compare_convert_fusion.1), kind=kOutput, calls=%fused_computation.19 | convolution fusion | flops 25690112 | bytes 1704448 | tf_op jit(solution)/shard_map/rgns,gis->rngi/dot_general | solution.py:83
  29.3 0.7 copy.68
  30.0 2.7 %collective-permute-start.1 = (f32[2,16,64,16]{2,3,1,0:T(8,128)S(1)}, f32[2,16,64,16]{2,3,1,0:T(8,128)S(1)}, u32[]{:S(2)}, u32[]{:S(2)}) collective-permute-start(f32[2,16,64,16]{2,3,1,0:T(8,128)S(1)} %copy.68), channel_id=1, source_target_pairs={{0,8},{8,16},{16,24},{24,32},{32,40},{40,48},{48,56},{56,64},{64,7... | collective-permute-start | bytes 393224 | tf_op jit(solution)/shard_map/ppermute | solution.py:20
  32.8 7.6 %collective-permute-done.1 = f32[2,16,64,16]{2,3,1,0:T(8,128)S(1)} collective-permute-done((f32[2,16,64,16]{2,3,1,0:T(8,128)S(1)}, f32[2,16,64,16]{2,3,1,0:T(8,128)S(1)}, u32[]{:S(2)}, u32[]{:S(2)}) %collective-permute-start.1) | collective-permute-done | bytes 131104 | tf_op jit(solution)/shard_map/ppermute | solution.py:20
  40.6 2.0 %collective-permute-start.2 = (f32[2,16,64,16]{2,3,1,0:T(8,128)S(1)}, f32[2,16,64,16]{2,3,1,0:T(8,128)S(1)}, u32[]{:S(2)}, u32[]{:S(2)}) collective-permute-start(f32[2,16,64,16]{2,3,1,0:T(8,128)S(1)} %collective-permute-done.1), channel_id=1, source_target_pairs={{0,8},{8,16},{16,24},{24,32},{32,40},{40,48},{48,56},{56,64},{64,7... | collective-permute-start | bytes 393224 | tf_op jit(solution)/shard_map/ppermute | solution.py:20
  42.6 3.9 %fusion.7 = (f32[64,16,129]{2,1,0:T(8,128)S(1)}, f32[64,16,129]{2,1,0:T(8,128)S(1)}) fusion(f32[64,16]{1,0:T(8,128)S(1)} %copy.71, f32[129]{0:T(256)S(1)} %iota_convert_fusion, f32[64,16]{1,0:T(8,128)S(1)} %copy.70), kind=kLoop, calls=%fused_computation.23 | loop fusion | flops 528384 | bytes 1065476 | tf_op jit(solution)/shard_map/mul | solution.py:40
  46.5 4.6 %collective-permute-done.2 = f32[2,16,64,16]{2,3,1,0:T(8,128)S(1)} collective-permute-done((f32[2,16,64,16]{2,3,1,0:T(8,128)S(1)}, f32[2,16,64,16]{2,3,1,0:T(8,128)S(1)}, u32[]{:S(2)}, u32[]{:S(2)}) %collective-permute-start.2) | collective-permute-done | bytes 131104 | tf_op jit(solution)/shard_map/ppermute | solution.py:20
  51.2 1.9 %collective-permute-start.3 = (f32[2,16,64,16]{2,3,1,0:T(8,128)S(1)}, f32[2,16,64,16]{2,3,1,0:T(8,128)}, u32[]{:S(2)}, u32[]{:S(2)}) collective-permute-start(f32[2,16,64,16]{2,3,1,0:T(8,128)S(1)} %maximum_add_fusion), channel_id=1, source_target_pairs={{0,16},{8,24},{16,32},{24,40},{32,48},{40,56},{48,64},{56,72},{64,... | collective-permute-start | bytes 393224 | tf_op jit(solution)/shard_map/ppermute | solution.py:20
  53.1 0.6 slice_bitcast_fusion.12
  53.7 1.4 %copy.72 = f32[64,16]{1,0:T(8,128)} copy(f32[64,16]{0,1:T(8,128)} %get-tuple-element.72) | data formatting | bytes 8192 | tf_op jit(solution)/shard_map/mul | solution.py:45
  55.1 1.4 %copy.69 = f32[64,16]{1,0:T(8,128)} copy(f32[64,16]{0,1:T(8,128)} %get-tuple-element.71) | data formatting | bytes 8192 | tf_op jit(solution)/shard_map/mul | solution.py:45
  56.5 5.7 %collective-permute-done.3 = f32[2,16,64,16]{2,3,1,0:T(8,128)} collective-permute-done((f32[2,16,64,16]{2,3,1,0:T(8,128)S(1)}, f32[2,16,64,16]{2,3,1,0:T(8,128)}, u32[]{:S(2)}, u32[]{:S(2)}) %collective-permute-start.3) | collective-permute-done | bytes 131104 | tf_op jit(solution)/shard_map/ppermute | solution.py:20
  62.3 1.0 multiply_subtract_fusion.3
  63.3 2.1 %collective-permute-start.4 = (f32[2,16,64,16]{2,3,1,0:T(8,128)S(1)}, f32[2,16,64,16]{2,3,1,0:T(8,128)S(1)}, u32[]{:S(2)}, u32[]{:S(2)}) collective-permute-start(f32[2,16,64,16]{2,3,1,0:T(8,128)S(1)} %maximum_add_fusion.1), channel_id=1, source_target_pairs={{0,32},{8,40},{16,48},{24,56},{32,64},{40,72},{48,80},{56,88},{64,... | collective-permute-start | bytes 393224 | tf_op jit(solution)/shard_map/ppermute | solution.py:20
  65.5 1.7 %subtract_bitcast_fusion = (f32[1,64,16,128]{3,2,0,1:T(8,128)}, f32[1,64,16,128]{3,2,0,1:T(8,128)}, f32[64,128]{1,0:T(8,128)S(1)}) fusion(f32[64,16,129]{2,1,0:T(8,128)S(1)} %get-tuple-element.51, f32[64,16,129]{2,1,0:T(8,128)S(1)} %get-tuple-element.50, f32[64,16]{1,0:T(8,128)S(1)} %copy-done.4, f32[64,16]{1,0:T(8,128)S(1)} %copy-done.5), kind=kLoop, calls=%fused_computation.54 | loop fusion | flops 1433600 | bytes 3186688 | tf_op jit(solution)/shard_map/stack | solution.py:49
  67.1 6.6 %collective-permute-done.4 = f32[2,16,64,16]{2,3,1,0:T(8,128)S(1)} collective-permute-done((f32[2,16,64,16]{2,3,1,0:T(8,128)S(1)}, f32[2,16,64,16]{2,3,1,0:T(8,128)S(1)}, u32[]{:S(2)}, u32[]{:S(2)}) %collective-permute-start.4) | collective-permute-done | bytes 131104 | tf_op jit(solution)/shard_map/ppermute | solution.py:20
  73.8 4.3 %collective-permute-start.5 = (f32[2,16,64,16]{2,3,1,0:T(8,128)S(1)}, f32[2,16,64,16]{2,3,1,0:T(8,128)S(1)}, u32[]{:S(2)}, u32[]{:S(2)}) collective-permute-start(f32[2,16,64,16]{2,3,1,0:T(8,128)S(1)} %maximum_add_fusion.2), channel_id=1, source_target_pairs={{0,64},{8,72},{16,80},{24,88},{32,96},{40,104},{48,112},{56,120},{... | collective-permute-start | bytes 393224 | tf_op jit(solution)/shard_map/ppermute | solution.py:20
  78.2 3.3 %fusion.4 = f32[64,128,128]{2,0,1:T(8,128)S(1)} fusion(s32[128,128]{1,0:T(8,128)S(1)} %iota_subtract_fusion, f32[128,128]{1,0:T(8,128)S(1)} %compare_convert_fusion, f32[64,128]{1,0:T(8,128)S(1)} %get-tuple-element.30), kind=kOutput, calls=%fused_computation.15 | convolution fusion | flops 1613758464 | bytes 4358144 | tf_op jit(solution)/shard_map/gk,kts->gts/dot_general | solution.py:34
  81.4 0.7 collective-permute-done.5
  82.3 16.3 %collective-permute-start.6 = (f32[2,16,64,16]{2,3,1,0:T(8,128)S(1)}, f32[2,16,64,16]{2,3,1,0:T(8,128)S(1)}, u32[]{:S(2)}, u32[]{:S(2)}) collective-permute-start(f32[2,16,64,16]{2,3,1,0:T(8,128)S(1)} %maximum_add_fusion.3), channel_id=1, source_target_pairs={{0,128},{8,136},{16,144},{24,152},{32,160},{40,168},{48,176},{56,1... | collective-permute-start | bytes 393224 | tf_op jit(solution)/shard_map/ppermute | solution.py:20
  98.6 4.9 %fusion.1 = f32[64,16,128]{2,1,0:T(8,128)S(1)} fusion(f32[64,16,128]{2,1,0:T(8,128)S(1)} %bitcast.134, f32[64,128,128]{2,0,1:T(8,128)S(1)} %fusion.4), kind=kOutput, calls=%fused_computation.2 | convolution fusion | flops 100663296 | bytes 5242880 | tf_op jit(solution)/shard_map/gts,gis->git/dot_general | solution.py:78
  103.8 0.9 copy.75
  104.8 0.6 fusion.6
  106.1 4.7 %collective-permute-start.9 = (f32[128]{0:T(128)S(1)}, f32[128]{0:T(128)S(1)}, u32[]{:S(2)}, u32[]{:S(2)}) collective-permute-start(f32[128]{0:T(128)S(1)} %get-tuple-element.22), channel_id=1, source_target_pairs={{0,3},{1,0},{2,1},{3,2},{4,7},{5,4},{6,5},{7,6},{8,11},{9,8},{10,9... | collective-permute-start | bytes 1544 | tf_op jit(solution)/shard_map/ppermute | solution.py:176
  110.7 2.7 %collective-permute-start.8 = (f32[128]{0:T(128)S(1)}, f32[128]{0:T(128)S(1)}, u32[]{:S(2)}, u32[]{:S(2)}) collective-permute-start(f32[128]{0:T(128)S(1)} %get-tuple-element.22), channel_id=1, source_target_pairs={{0,2},{1,3},{2,0},{3,1},{4,6},{5,7},{6,4},{7,5},{8,10},{9,11},{10,... | collective-permute-start | bytes 1544 | tf_op jit(solution)/shard_map/ppermute | solution.py:176
  113.4 2.8 %collective-permute-start.7 = (f32[128]{0:T(128)S(1)}, f32[128]{0:T(128)S(1)}, u32[]{:S(2)}, u32[]{:S(2)}) collective-permute-start(f32[128]{0:T(128)S(1)} %get-tuple-element.22), channel_id=1, source_target_pairs={{0,1},{1,2},{2,3},{3,0},{4,5},{5,6},{6,7},{7,4},{8,9},{9,10},{10,1... | collective-permute-start | bytes 1544 | tf_op jit(solution)/shard_map/ppermute | solution.py:176
  116.3 1.4 %collective-permute-done.8 = f32[128]{0:T(128)S(1)} collective-permute-done((f32[128]{0:T(128)S(1)}, f32[128]{0:T(128)S(1)}, u32[]{:S(2)}, u32[]{:S(2)}) %collective-permute-start.8) | collective-permute-done | bytes 544 | tf_op jit(solution)/shard_map/ppermute | solution.py:176
  117.7 2.4 %collective-permute-done.7 = f32[128]{0:T(128)S(1)} collective-permute-done((f32[128]{0:T(128)S(1)}, f32[128]{0:T(128)S(1)}, u32[]{:S(2)}, u32[]{:S(2)}) %collective-permute-start.7) | collective-permute-done | bytes 544 | tf_op jit(solution)/shard_map/ppermute | solution.py:176
  120.2 1.9 %collective-permute-start.10 = (f32[128]{0:T(128)S(1)}, f32[128]{0:T(128)S(1)}, u32[]{:S(2)}, u32[]{:S(2)}) collective-permute-start(f32[128]{0:T(128)S(1)} %fusion.31), channel_id=1, source_target_pairs={{0,4},{1,5},{2,6},{3,7},{4,0},{5,1},{6,2},{7,3},{8,12},{9,13},{10,... | collective-permute-start | bytes 1544 | tf_op jit(solution)/shard_map/ppermute | solution.py:184
  122.1 7.4 %collective-permute-done.10 = f32[128]{0:T(128)S(1)} collective-permute-done((f32[128]{0:T(128)S(1)}, f32[128]{0:T(128)S(1)}, u32[]{:S(2)}, u32[]{:S(2)}) %collective-permute-start.10) | collective-permute-done | bytes 544 | tf_op jit(solution)/shard_map/ppermute | solution.py:184
  129.8 0.9 copy.76
  (73 shorter events, 2.9 us)
Async XLA Ops:
  0.0 18.2 %copy-start.3 = (bf16[128,3,1024]{2,0,1:T(8,128)(2,1)S(1)}, bf16[128,3,1024]{2,0,1:T(8,128)(2,1)}, u32[]{:S(2)}) copy-start(bf16[128,3,1024]{2,0,1:T(8,128)(2,1)} %param.8) | copy-start | bytes 2359300
  0.9 17.7 %collective-permute-start = (bf16[6,3,1024]{2,0,1:T(8,128)(2,1)S(1)}, bf16[6,3,1024]{2,0,1:T(8,128)(2,1)S(1)}, u32[]{:S(2)}, u32[]{:S(2)}) collective-permute-start(bf16[6,3,1024]{2,0,1:T(8,128)(2,1)S(1)} %slice.159), channel_id=1, source_target_pairs={{0,8},{8,16},{16,24},{24,32},{32,40},{40,48},{48,56},{56,64},{64,7... | collective-permute-start | bytes 110600 | tf_op jit(solution)/shard_map/ppermute | solution.py:20
  25.6 14.8 %copy-start.6 = (f32[64,16]{0,1:T(8,128)S(1)}, f32[64,16]{0,1:T(8,128)}, u32[]{:S(2)}) copy-start(f32[64,16]{0,1:T(8,128)} %param.11) | copy-start | bytes 12292
  25.6 14.9 %copy-start.7 = (f32[64,16]{0,1:T(8,128)S(1)}, f32[64,16]{0,1:T(8,128)}, u32[]{:S(2)}) copy-start(f32[64,16]{0,1:T(8,128)} %param.10) | copy-start | bytes 12292
  30.0 10.4 %collective-permute-start.1 = (f32[2,16,64,16]{2,3,1,0:T(8,128)S(1)}, f32[2,16,64,16]{2,3,1,0:T(8,128)S(1)}, u32[]{:S(2)}, u32[]{:S(2)}) collective-permute-start(f32[2,16,64,16]{2,3,1,0:T(8,128)S(1)} %copy.68), channel_id=1, source_target_pairs={{0,8},{8,16},{16,24},{24,32},{32,40},{40,48},{48,56},{56,64},{64,7... | collective-permute-start | bytes 393224 | tf_op jit(solution)/shard_map/ppermute | solution.py:20
  40.6 12.5 %copy-start.12 = (f32[2,64,16]{1,2,0:T(8,128)S(1)}, f32[2,64,16]{1,2,0:T(8,128)}, u32[]{:S(2)}) copy-start(f32[2,64,16]{1,2,0:T(8,128)} %param.12) | copy-start | bytes 24580
  40.6 10.5 %collective-permute-start.2 = (f32[2,16,64,16]{2,3,1,0:T(8,128)S(1)}, f32[2,16,64,16]{2,3,1,0:T(8,128)S(1)}, u32[]{:S(2)}, u32[]{:S(2)}) collective-permute-start(f32[2,16,64,16]{2,3,1,0:T(8,128)S(1)} %collective-permute-done.1), channel_id=1, source_target_pairs={{0,8},{8,16},{16,24},{24,32},{32,40},{40,48},{48,56},{56,64},{64,7... | collective-permute-start | bytes 393224 | tf_op jit(solution)/shard_map/ppermute | solution.py:20
  51.2 11.1 %collective-permute-start.3 = (f32[2,16,64,16]{2,3,1,0:T(8,128)S(1)}, f32[2,16,64,16]{2,3,1,0:T(8,128)}, u32[]{:S(2)}, u32[]{:S(2)}) collective-permute-start(f32[2,16,64,16]{2,3,1,0:T(8,128)S(1)} %maximum_add_fusion), channel_id=1, source_target_pairs={{0,16},{8,24},{16,32},{24,40},{32,48},{40,56},{48,64},{56,72},{64,... | collective-permute-start | bytes 393224 | tf_op jit(solution)/shard_map/ppermute | solution.py:20
  56.5 8.9 %copy-start.4 = (f32[64,16]{1,0:T(8,128)S(1)}, f32[64,16]{1,0:T(8,128)}, u32[]{:S(2)}) copy-start(f32[64,16]{1,0:T(8,128)} %copy.72) | copy-start | bytes 12292
  56.5 8.9 %copy-start.5 = (f32[64,16]{1,0:T(8,128)S(1)}, f32[64,16]{1,0:T(8,128)}, u32[]{:S(2)}) copy-start(f32[64,16]{1,0:T(8,128)} %copy.69) | copy-start | bytes 12292
  63.3 10.4 %collective-permute-start.4 = (f32[2,16,64,16]{2,3,1,0:T(8,128)S(1)}, f32[2,16,64,16]{2,3,1,0:T(8,128)S(1)}, u32[]{:S(2)}, u32[]{:S(2)}) collective-permute-start(f32[2,16,64,16]{2,3,1,0:T(8,128)S(1)} %maximum_add_fusion.1), channel_id=1, source_target_pairs={{0,32},{8,40},{16,48},{24,56},{32,64},{40,72},{48,80},{56,88},{64,... | collective-permute-start | bytes 393224 | tf_op jit(solution)/shard_map/ppermute | solution.py:20
  65.5 8.3 %copy-start.10 = (f32[16,64]{1,0:T(8,128)S(1)}, f32[16,64]{1,0:T(8,128)}, u32[]{:S(2)}) copy-start(f32[16,64]{1,0:T(8,128)} %get-tuple-element.63) | copy-start | bytes 12292
  65.5 8.3 %copy-start.11 = (f32[16,64]{1,0:T(8,128)S(1)}, f32[16,64]{1,0:T(8,128)}, u32[]{:S(2)}) copy-start(f32[16,64]{1,0:T(8,128)} %get-tuple-element.64) | copy-start | bytes 12292
  73.8 8.3 %collective-permute-start.5 = (f32[2,16,64,16]{2,3,1,0:T(8,128)S(1)}, f32[2,16,64,16]{2,3,1,0:T(8,128)S(1)}, u32[]{:S(2)}, u32[]{:S(2)}) collective-permute-start(f32[2,16,64,16]{2,3,1,0:T(8,128)S(1)} %maximum_add_fusion.2), channel_id=1, source_target_pairs={{0,64},{8,72},{16,80},{24,88},{32,96},{40,104},{48,112},{56,120},{... | collective-permute-start | bytes 393224 | tf_op jit(solution)/shard_map/ppermute | solution.py:20
  78.1 4.0 %copy-start.8 = (f32[16,64]{1,0:T(8,128)S(1)}, f32[16,64]{1,0:T(8,128)}, u32[]{:S(2)}) copy-start(f32[16,64]{1,0:T(8,128)} %get-tuple-element.61) | copy-start | bytes 12292
  78.1 4.0 %copy-start.9 = (f32[16,64]{1,0:T(8,128)S(1)}, f32[16,64]{1,0:T(8,128)}, u32[]{:S(2)}) copy-start(f32[16,64]{1,0:T(8,128)} %get-tuple-element.62) | copy-start | bytes 12292
  82.3 21.3 %collective-permute-start.6 = (f32[2,16,64,16]{2,3,1,0:T(8,128)S(1)}, f32[2,16,64,16]{2,3,1,0:T(8,128)S(1)}, u32[]{:S(2)}, u32[]{:S(2)}) collective-permute-start(f32[2,16,64,16]{2,3,1,0:T(8,128)S(1)} %maximum_add_fusion.3), channel_id=1, source_target_pairs={{0,128},{8,136},{16,144},{24,152},{32,160},{40,168},{48,176},{56,1... | collective-permute-start | bytes 393224 | tf_op jit(solution)/shard_map/ppermute | solution.py:20
  103.6 1.1 copy-start.1
  103.6 1.2 copy-start.2
  103.6 1.2 copy-start.15
  104.8 1.0 copy-start
  104.8 1.0 copy-start.13
  105.8 23.7 %copy-start.14 = (f32[1024]{0:T(1024)S(1)}, f32[1024]{0:T(1024)}, u32[]{:S(2)}) copy-start(f32[1024]{0:T(1024)} %param.14) | copy-start | bytes 12292
  106.1 10.2 %collective-permute-start.9 = (f32[128]{0:T(128)S(1)}, f32[128]{0:T(128)S(1)}, u32[]{:S(2)}, u32[]{:S(2)}) collective-permute-start(f32[128]{0:T(128)S(1)} %get-tuple-element.22), channel_id=1, source_target_pairs={{0,3},{1,0},{2,1},{3,2},{4,7},{5,4},{6,5},{7,6},{8,11},{9,8},{10,9... | collective-permute-start | bytes 1544 | tf_op jit(solution)/shard_map/ppermute | solution.py:176
  110.7 7.0 %collective-permute-start.8 = (f32[128]{0:T(128)S(1)}, f32[128]{0:T(128)S(1)}, u32[]{:S(2)}, u32[]{:S(2)}) collective-permute-start(f32[128]{0:T(128)S(1)} %get-tuple-element.22), channel_id=1, source_target_pairs={{0,2},{1,3},{2,0},{3,1},{4,6},{5,7},{6,4},{7,5},{8,10},{9,11},{10,... | collective-permute-start | bytes 1544 | tf_op jit(solution)/shard_map/ppermute | solution.py:176
  113.4 6.7 %collective-permute-start.7 = (f32[128]{0:T(128)S(1)}, f32[128]{0:T(128)S(1)}, u32[]{:S(2)}, u32[]{:S(2)}) collective-permute-start(f32[128]{0:T(128)S(1)} %get-tuple-element.22), channel_id=1, source_target_pairs={{0,1},{1,2},{2,3},{3,0},{4,5},{5,6},{6,7},{7,4},{8,9},{9,10},{10,1... | collective-permute-start | bytes 1544 | tf_op jit(solution)/shard_map/ppermute | solution.py:176
  120.2 9.4 %collective-permute-start.10 = (f32[128]{0:T(128)S(1)}, f32[128]{0:T(128)S(1)}, u32[]{:S(2)}, u32[]{:S(2)}) collective-permute-start(f32[128]{0:T(128)S(1)} %fusion.31), channel_id=1, source_target_pairs={{0,4},{1,5},{2,6},{3,7},{4,0},{5,1},{6,2},{7,3},{8,12},{9,13},{10,... | collective-permute-start | bytes 1544 | tf_op jit(solution)/shard_map/ppermute | solution.py:184

commit v11 on v9

--- a/solution.py
+++ b/solution.py
@@ -142,7 +142,12 @@
     def widen(factor):
         return jnp.repeat(factor, group_width, axis=2)
 
-    running = passed_along(summary.reshape(2, mode_count, channels), "ctx", 1)
+    fresh = summary.reshape(2, mode_count, channels)
+    running = passed_along(fresh, "ctx", 1)
+    if reach > 1:
+        older = passed_along(fresh, "ctx", 2)
+        alive = unbroken(anchor - tok_rows, anchor - 1)
+        running = running + complex_times(widen(stepping) * alive.astype(jnp.float32), older)
     pole_inputs, running = lax.optimization_barrier(((rate, angle, residue), running))
     tables = pole_tables(*pole_inputs, SPAN)
     response = tables[0]
@@ -150,8 +155,8 @@
         toeplitz(response), values[span_index], span_pos[span_index], span_begin[span_index]
     )
     insides = [lax.optimization_barrier(inside)]
-    power = stepping
-    distance = 1
+    power = complex_times(stepping, stepping)
+    distance = 2
     while distance < reach:
         earlier = passed_along(running, "ctx", distance)
         alive = unbroken(anchor - distance * tok_rows, anchor - 1)

time: 128 us -> 127 us (level)
  starting transfers between devices: 45.5 us -> 47 us
    ppermute x7, starting transfers between devices: 27.4 us -> 31.1 us  [passed_along(): return lax.ppermute(block, axis, route)]
    ppermute x1, starting transfers between devices: 7.99 us -> 5.73 us  [on_device(): squares = squares + lax.ppermute(squares, 'tp', pairs)]
    ppermute x7, waiting for transfers between devices: 13.2 us -> 11.1 us  [passed_along(): return lax.ppermute(block, axis, route)]
    ppermute x1, waiting for transfers between devices: 1.53 us -> 3.63 us  [on_device(): squares = squares + lax.ppermute(squares, 'tp', pairs)]
  transfers between devices with their start and end apart: 11 -> 11, of which waited for: 6 -> 6; matrix products, arithmetic and copies ran while one was open for 31% -> 29% of each run, Pallas kernels for 0% -> 0%
where the time goes in v11:
time: 127 us; the launch traced here: 126 us
  starting transfers between devices  47 us (37%)
  other arithmetic  21.6 us (17%)
  local copies, waits for them, and re-layouts  20.1 us (16%)
  waiting for transfers between devices  18.6 us (15%)
  matrix products  15.2 us (12%)
  between operations  3.94 us (3%)
    ppermute x7, starting transfers between devices, passed_along(): return lax.ppermute(block, axis, route)  31.1 us
    ppermute x7, waiting for transfers between devices, passed_along(): return lax.ppermute(block, axis, route)  11.1 us
    ppermute x3, starting transfers between devices, on_device(): gathered.append(lax.ppermute(partial, 'tp', pairs))  10.2 us
    ppermute x1, starting transfers between devices, on_device(): squares = squares + lax.ppermute(squares, 'tp', pairs)  5.73 us
    dot_general x1, matrix products, inside_terms(): jnp.einsum('gts,gis->git', matrix_table * same_genome[None], columns, pre...  5.72 us
    add x1, other arithmetic, short_filter(): result = result + jnp.where(keep_tap, taps_part[offset][None] * window, 0.0)  5.62 us
    mul x1, other arithmetic, pole_tables(): power_re = magnitude * jnp.cos(angle[:, :, None] * counter)  4.63 us
    ppermute x3, waiting for transfers between devices, on_device(): gathered.append(lax.ppermute(partial, 'tp', pairs))  3.83 us
  transfers between devices with their start and end apart: 11, of which 6 were waited for; matrix products, arithmetic and copies ran while one was open for 29% of the time, Pallas kernels for 0%

profile of v11, /device:TPU:128, one launch (start us, length us, event | category | flops | bytes accessed | tf_op | source)
XLA Modules:
  0.0 126.4 jit_solution(12711640718678107862)
XLA Ops:
  0.0 0.9 slice.219
  0.9 1.9 %collective-permute-start = (bf16[6,3,1024]{2,0,1:T(8,128)(2,1)S(1)}, bf16[6,3,1024]{2,0,1:T(8,128)(2,1)S(1)}, u32[]{:S(2)}, u32[]{:S(2)}) collective-permute-start(bf16[6,3,1024]{2,0,1:T(8,128)(2,1)S(1)} %slice.219), channel_id=1, source_target_pairs={{0,8},{8,16},{16,24},{24,32},{32,40},{40,48},{48,56},{56,64},{64,7... | collective-permute-start | bytes 110600 | tf_op jit(solution)/shard_map/ppermute | solution.py:20
  2.9 0.8 reduce-window.9
  3.7 1.4 %and_reduce_fusion = (pred[]{:T(512)}, pred[]{:T(512)}, pred[]{:T(512)}, pred[]{:T(512)}, pred[]{:T(512)}, /*index=5*/s32[4]{0:T(128)S(1)}) fusion(s32[]{:T(128)S(6)} %sub.153, s32[]{:T(128)S(6)} %sub.137, s32[]{:T(128)S(6)} %sub.150, s32[]{:T(128)S(6)} %sub.147, s32[]{:T(128)S(6)} %sub.144, s32[]{:T(128)S(6)} %sub.136, s32[4]{0:T(128)} %param.15, ...), kind=kLoop, calls=%fused_computation.116 | loop fusion | flops 63 | bytes 77 | tf_op jit(solution)/shard_map/reduce_or | solution.py:140
  5.9 0.8 copy.49
  6.7 0.8 fusion.38
  7.4 0.8 subtract_bitcast_fusion.1
  8.2 1.5 %fusion.44 = (f32[1,3,1024]{2,0,1:T(1,128)S(1)}, f32[1,3,1024]{2,0,1:T(1,128)S(1)}, f32[1,3,1024]{2,0,1:T(1,128)S(1)}, f32[1,3,1024]{2,0,1:T(1,128)S(1)}, f32[1,...) fusion(f32[7,3,1024]{2,0,1:T(8,128)} %param.9), kind=kLoop, calls=%fused_computation.153 | loop fusion | bytes 172032 | tf_op jit(solution)/shard_map/slice | solution.py:97
  9.7 0.6 broadcast_compare_fusion
  13.8 2.0 %fusion.20 = (f32[1,64,16,128]{3,2,0,1:T(8,128)S(1)}, f32[1,64,16,128]{3,2,0,1:T(8,128)S(1)}) fusion(f32[64,16]{1,0:T(8,128)S(1)} %copy.49, f32[128]{0:T(128)S(1)} %subtract_convert_fusion, f32[64,16]{1,0:T(8,128)S(1)} %copy.48), kind=kLoop, calls=%fused_computation.41 | loop fusion | flops 524288 | bytes 1057280 | tf_op jit(solution)/shard_map/mul | solution.py:59
  17.2 5.6 %select_add_fusion = f32[128,3,1024]{0,2,1:T(8,128)S(1)} fusion(bf16[128,3,1024]{0,2,1:T(8,128)(2,1)S(1)} %copy.45, bf16[6,3,1024]{0,2,1:T(8,128)(2,1)S(1)} %copy.46, f32[3,1024]{1,0:T(4,128)S(1)} %get-tuple-element.82, f32[3,1024]{1,0:T(4,128)S(1)} %get-tuple-element.83, f32[3,1024]{1,0:T(4,128)S(1)} %get-tuple-element.84, ...), kind=kLoop, calls=%fused_computation.16 | loop fusion | flops 17694720 | bytes 2483072 | tf_op jit(solution)/shard_map/add | solution.py:97
  23.0 3.8 %convolution_bitcast_fusion = f32[2,16,64,16]{1,3,0,2:T(8,128)S(1)} fusion(f32[64,16,128,1]{2,1,3,0:T(8,128)S(1)} %bitcast.154, f32[1,64,16,128]{3,2,0,1:T(8,128)S(1)} %get-tuple-element.53, f32[1,64,16,128]{3,2,0,1:T(8,128)S(1)} %get-tuple-element.52, f32[128]{0:T(128)S(1)} %compare_convert_fusion.1), kind=kOutput, calls=%fused_computation.19 | convolution fusion | flops 25690112 | bytes 1704448 | tf_op jit(solution)/shard_map/rgns,gis->rngi/dot_general | solution.py:83
  26.7 0.9 copy.50
  27.6 0.6 reshape.229
  28.2 3.5 %collective-permute-start.2 = (f32[2,16,1024]{2,1,0:T(8,128)S(1)}, f32[2,16,1024]{2,1,0:T(8,128)S(1)}, u32[]{:S(2)}, u32[]{:S(2)}) collective-permute-start(f32[2,16,1024]{2,1,0:T(8,128)S(1)} %reshape.229), channel_id=1, source_target_pairs={{0,16},{8,24},{16,32},{24,40},{32,48},{40,56},{48,64},{56,72},{64,... | collective-permute-start | bytes 393224 | tf_op jit(solution)/shard_map/ppermute | solution.py:20
  33.9 0.9 slice.270
  35.0 0.9 slice.266
  36.1 0.9 slice.262
  37.2 0.9 slice.258
  38.3 0.9 slice.254
  39.4 0.9 slice.250
  40.3 3.3 %collective-permute-start.1 = (f32[2,16,1024]{2,1,0:T(8,128)S(1)}, f32[2,16,1024]{2,1,0:T(8,128)S(1)}, u32[]{:S(2)}, u32[]{:S(2)}) collective-permute-start(f32[2,16,1024]{2,1,0:T(8,128)S(1)} %reshape.229), channel_id=1, source_target_pairs={{0,8},{8,16},{16,24},{24,32},{32,40},{40,48},{48,56},{56,64},{64,7... | collective-permute-start | bytes 393224 | tf_op jit(solution)/shard_map/ppermute | solution.py:20
  43.7 5.6 %collective-permute-done.1 = f32[2,16,1024]{2,1,0:T(8,128)S(1)} collective-permute-done((f32[2,16,1024]{2,1,0:T(8,128)S(1)}, f32[2,16,1024]{2,1,0:T(8,128)S(1)}, u32[]{:S(2)}, u32[]{:S(2)}) %collective-permute-start.1) | collective-permute-done | bytes 131104 | tf_op jit(solution)/shard_map/ppermute | solution.py:20
  49.3 0.7 copy.53
  50.0 0.7 copy.52
  50.7 2.1 %collective-permute-start.3 = (f32[2,16,1024]{2,1,0:T(8,128)S(1)}, f32[2,16,1024]{2,1,0:T(8,128)}, u32[]{:S(2)}, u32[]{:S(2)}) collective-permute-start(f32[2,16,1024]{2,1,0:T(8,128)S(1)} %maximum_add_fusion), channel_id=1, source_target_pairs={{0,16},{8,24},{16,32},{24,40},{32,48},{40,56},{48,64},{56,72},{64,... | collective-permute-start | bytes 393224 | tf_op jit(solution)/shard_map/ppermute | solution.py:20
  52.8 4.6 %fusion.7 = (f32[64,16,129]{2,1,0:T(8,128)S(1)}, f32[64,16,129]{2,1,0:T(8,128)S(1)}) fusion(f32[64,16]{1,0:T(8,128)} %copy.53, f32[129]{0:T(256)S(1)} %iota_convert_fusion, f32[64,16]{1,0:T(8,128)} %copy.52), kind=kLoop, calls=%fused_computation.23 | loop fusion | flops 528384 | bytes 1065476 | tf_op jit(solution)/shard_map/mul | solution.py:40
  57.4 0.7 slice_bitcast_fusion.12
  58.2 0.7 copy.54
  58.9 0.7 copy.51
  59.6 0.8 collective-permute-done.3
  60.4 1.0 multiply_subtract_fusion.3
  61.3 3.0 %collective-permute-start.4 = (f32[2,16,1024]{2,1,0:T(8,128)S(1)}, f32[2,16,1024]{2,1,0:T(8,128)S(1)}, u32[]{:S(2)}, u32[]{:S(2)}) collective-permute-start(f32[2,16,1024]{2,1,0:T(8,128)S(1)} %maximum_add_fusion.1), channel_id=1, source_target_pairs={{0,32},{8,40},{16,48},{24,56},{32,64},{40,72},{48,80},{56,88},{64,... | collective-permute-start | bytes 393224 | tf_op jit(solution)/shard_map/ppermute | solution.py:20
  64.4 2.4 %subtract_bitcast_fusion = (f32[1,64,16,128]{3,2,0,1:T(8,128)}, f32[1,64,16,128]{3,2,0,1:T(8,128)}, f32[64,128]{1,0:T(8,128)S(1)}) fusion(f32[64,16,129]{2,1,0:T(8,128)S(1)} %get-tuple-element.51, f32[64,16,129]{2,1,0:T(8,128)S(1)} %get-tuple-element.50, f32[64,16]{1,0:T(8,128)} %copy.54, f32[64,16]{1,0:T(8,128)} %copy.51), kind=kLoop, calls=%fused_computation.55 | loop fusion | flops 1433600 | bytes 3186688 | tf_op jit(solution)/shard_map/stack | solution.py:49
  66.8 4.7 %collective-permute-done.4 = f32[2,16,1024]{2,1,0:T(8,128)S(1)} collective-permute-done((f32[2,16,1024]{2,1,0:T(8,128)S(1)}, f32[2,16,1024]{2,1,0:T(8,128)S(1)}, u32[]{:S(2)}, u32[]{:S(2)}) %collective-permute-start.4) | collective-permute-done | bytes 131104 | tf_op jit(solution)/shard_map/ppermute | solution.py:20
  71.6 4.3 %collective-permute-start.5 = (f32[2,16,1024]{2,1,0:T(8,128)S(1)}, f32[2,16,1024]{2,1,0:T(8,128)S(1)}, u32[]{:S(2)}, u32[]{:S(2)}) collective-permute-start(f32[2,16,1024]{2,1,0:T(8,128)S(1)} %maximum_add_fusion.2), channel_id=1, source_target_pairs={{0,64},{8,72},{16,80},{24,88},{32,96},{40,104},{48,112},{56,120},{... | collective-permute-start | bytes 393224 | tf_op jit(solution)/shard_map/ppermute | solution.py:20
  75.9 3.2 %fusion.4 = f32[64,128,128]{2,0,1:T(8,128)S(1)} fusion(s32[128,128]{1,0:T(8,128)S(1)} %iota_subtract_fusion, f32[128,128]{1,0:T(8,128)S(1)} %compare_convert_fusion, f32[64,128]{1,0:T(8,128)S(1)} %get-tuple-element.30), kind=kOutput, calls=%fused_computation.15 | convolution fusion | flops 1613758464 | bytes 4358144 | tf_op jit(solution)/shard_map/gk,kts->gts/dot_general | solution.py:34
  79.3 12.9 %collective-permute-start.6 = (f32[2,16,1024]{2,1,0:T(8,128)S(1)}, f32[2,16,1024]{2,1,0:T(8,128)S(1)}, u32[]{:S(2)}, u32[]{:S(2)}) collective-permute-start(f32[2,16,1024]{2,1,0:T(8,128)S(1)} %maximum_add_fusion.3), channel_id=1, source_target_pairs={{0,128},{8,136},{16,144},{24,152},{32,160},{40,168},{48,176},{56,1... | collective-permute-start | bytes 393224 | tf_op jit(solution)/shard_map/ppermute | solution.py:20
  92.3 5.7 %fusion.1 = f32[64,16,128]{2,1,0:T(8,128)} fusion(f32[64,16,128]{2,1,0:T(8,128)S(1)} %bitcast.155, f32[64,128,128]{2,0,1:T(8,128)S(1)} %fusion.4), kind=kOutput, calls=%fused_computation.2 | convolution fusion | flops 100663296 | bytes 5242880 | tf_op jit(solution)/shard_map/gts,gis->git/dot_general | solution.py:78
  99.2 2.4 %fusion.6 = f32[64,16,128]{2,1,0:T(8,128)S(1)} fusion(f32[64,16,128]{2,1,0:T(8,128)} %fusion.1, f32[1,64,16,128]{3,2,0,1:T(8,128)S(1)} %copy-done.1, f32[1,64,16,128]{3,2,0,1:T(8,128)S(1)} %copy-done, f32[2,16,64,16]{3,2,1,0:T(8,128)S(1)} %reshape.230, pred[128]{0:T(512)(128)(4,1)S(1)} %copy-done.11), kind=kOutput, calls=%fused_computation.22 | convolution fusion | flops 25690112 | bytes 2228352 | tf_op jit(solution)/shard_map/rgnt,rngi->git/dot_general | solution.py:87
  101.9 4.7 %collective-permute-start.9 = (f32[128]{0:T(128)S(1)}, f32[128]{0:T(128)S(1)}, u32[]{:S(2)}, u32[]{:S(2)}) collective-permute-start(f32[128]{0:T(128)S(1)} %get-tuple-element.22), channel_id=1, source_target_pairs={{0,3},{1,0},{2,1},{3,2},{4,7},{5,4},{6,5},{7,6},{8,11},{9,8},{10,9... | collective-permute-start | bytes 1544 | tf_op jit(solution)/shard_map/ppermute | solution.py:181
  106.5 2.7 %collective-permute-start.8 = (f32[128]{0:T(128)S(1)}, f32[128]{0:T(128)S(1)}, u32[]{:S(2)}, u32[]{:S(2)}) collective-permute-start(f32[128]{0:T(128)S(1)} %get-tuple-element.22), channel_id=1, source_target_pairs={{0,2},{1,3},{2,0},{3,1},{4,6},{5,7},{6,4},{7,5},{8,10},{9,11},{10,... | collective-permute-start | bytes 1544 | tf_op jit(solution)/shard_map/ppermute | solution.py:181
  109.3 2.8 %collective-permute-start.7 = (f32[128]{0:T(128)S(1)}, f32[128]{0:T(128)S(1)}, u32[]{:S(2)}, u32[]{:S(2)}) collective-permute-start(f32[128]{0:T(128)S(1)} %get-tuple-element.22), channel_id=1, source_target_pairs={{0,1},{1,2},{2,3},{3,0},{4,5},{5,6},{6,7},{7,4},{8,9},{9,10},{10,1... | collective-permute-start | bytes 1544 | tf_op jit(solution)/shard_map/ppermute | solution.py:181
  112.1 1.4 %collective-permute-done.8 = f32[128]{0:T(128)S(1)} collective-permute-done((f32[128]{0:T(128)S(1)}, f32[128]{0:T(128)S(1)}, u32[]{:S(2)}, u32[]{:S(2)}) %collective-permute-start.8) | collective-permute-done | bytes 544 | tf_op jit(solution)/shard_map/ppermute | solution.py:181
  113.5 2.4 %collective-permute-done.7 = f32[128]{0:T(128)S(1)} collective-permute-done((f32[128]{0:T(128)S(1)}, f32[128]{0:T(128)S(1)}, u32[]{:S(2)}, u32[]{:S(2)}) %collective-permute-start.7) | collective-permute-done | bytes 544 | tf_op jit(solution)/shard_map/ppermute | solution.py:181
  116.0 5.7 %collective-permute-start.10 = (f32[128]{0:T(128)S(1)}, f32[128]{0:T(128)S(1)}, u32[]{:S(2)}, u32[]{:S(2)}) collective-permute-start(f32[128]{0:T(128)S(1)} %fusion.32), channel_id=1, source_target_pairs={{0,4},{1,5},{2,6},{3,7},{4,0},{5,1},{6,2},{7,3},{8,12},{9,13},{10,... | collective-permute-start | bytes 1544 | tf_op jit(solution)/shard_map/ppermute | solution.py:189
  121.7 3.6 %collective-permute-done.10 = f32[128]{0:T(128)S(1)} collective-permute-done((f32[128]{0:T(128)S(1)}, f32[128]{0:T(128)S(1)}, u32[]{:S(2)}, u32[]{:S(2)}) %collective-permute-start.10) | collective-permute-done | bytes 544 | tf_op jit(solution)/shard_map/ppermute | solution.py:189
  125.6 0.8 copy.58
  (86 shorter events, 7.3 us)
Async XLA Ops:
  0.0 16.4 %copy-start.2 = (bf16[128,3,1024]{2,0,1:T(8,128)(2,1)S(1)}, bf16[128,3,1024]{2,0,1:T(8,128)(2,1)}, u32[]{:S(2)}) copy-start(bf16[128,3,1024]{2,0,1:T(8,128)(2,1)} %param.8) | copy-start | bytes 2359300
  0.9 15.9 %collective-permute-start = (bf16[6,3,1024]{2,0,1:T(8,128)(2,1)S(1)}, bf16[6,3,1024]{2,0,1:T(8,128)(2,1)S(1)}, u32[]{:S(2)}, u32[]{:S(2)}) collective-permute-start(bf16[6,3,1024]{2,0,1:T(8,128)(2,1)S(1)} %slice.219), channel_id=1, source_target_pairs={{0,8},{8,16},{16,24},{24,32},{32,40},{40,48},{48,56},{56,64},{64,7... | collective-permute-start | bytes 110600 | tf_op jit(solution)/shard_map/ppermute | solution.py:20
  28.2 15.4 %collective-permute-start.2 = (f32[2,16,1024]{2,1,0:T(8,128)S(1)}, f32[2,16,1024]{2,1,0:T(8,128)S(1)}, u32[]{:S(2)}, u32[]{:S(2)}) collective-permute-start(f32[2,16,1024]{2,1,0:T(8,128)S(1)} %reshape.229), channel_id=1, source_target_pairs={{0,16},{8,24},{16,32},{24,40},{32,48},{40,56},{48,64},{56,72},{64,... | collective-permute-start | bytes 393224 | tf_op jit(solution)/shard_map/ppermute | solution.py:20
  38.1 11.2 %copy-start.7 = (f32[64,16]{0,1:T(8,128)S(1)}, f32[64,16]{0,1:T(8,128)}, u32[]{:S(2)}) copy-start(f32[64,16]{0,1:T(8,128)} %param.11) | copy-start | bytes 12292
  38.1 11.9 %copy-start.8 = (f32[64,16]{0,1:T(8,128)S(1)}, f32[64,16]{0,1:T(8,128)}, u32[]{:S(2)}) copy-start(f32[64,16]{0,1:T(8,128)} %param.10) | copy-start | bytes 12292
  40.3 9.0 %collective-permute-start.1 = (f32[2,16,1024]{2,1,0:T(8,128)S(1)}, f32[2,16,1024]{2,1,0:T(8,128)S(1)}, u32[]{:S(2)}, u32[]{:S(2)}) collective-permute-start(f32[2,16,1024]{2,1,0:T(8,128)S(1)} %reshape.229), channel_id=1, source_target_pairs={{0,8},{8,16},{16,24},{24,32},{32,40},{40,48},{48,56},{56,64},{64,7... | collective-permute-start | bytes 393224 | tf_op jit(solution)/shard_map/ppermute | solution.py:20
  50.7 9.7 %collective-permute-start.3 = (f32[2,16,1024]{2,1,0:T(8,128)S(1)}, f32[2,16,1024]{2,1,0:T(8,128)}, u32[]{:S(2)}, u32[]{:S(2)}) collective-permute-start(f32[2,16,1024]{2,1,0:T(8,128)S(1)} %maximum_add_fusion), channel_id=1, source_target_pairs={{0,16},{8,24},{16,32},{24,40},{32,48},{40,56},{48,64},{56,72},{64,... | collective-permute-start | bytes 393224 | tf_op jit(solution)/shard_map/ppermute | solution.py:20
  61.3 10.2 %collective-permute-start.4 = (f32[2,16,1024]{2,1,0:T(8,128)S(1)}, f32[2,16,1024]{2,1,0:T(8,128)S(1)}, u32[]{:S(2)}, u32[]{:S(2)}) collective-permute-start(f32[2,16,1024]{2,1,0:T(8,128)S(1)} %maximum_add_fusion.1), channel_id=1, source_target_pairs={{0,32},{8,40},{16,48},{24,56},{32,64},{40,72},{48,80},{56,88},{64,... | collective-permute-start | bytes 393224 | tf_op jit(solution)/shard_map/ppermute | solution.py:20
  64.4 7.1 %copy-start.5 = (f32[1,16,1024]{2,1,0:T(8,128)S(1)}, f32[1,16,1024]{2,1,0:T(8,128)}, u32[]{:S(2)}) copy-start(f32[1,16,1024]{2,1,0:T(8,128)} %slice.262) | copy-start | bytes 196612
  64.4 7.1 %copy-start.6 = (f32[1,16,1024]{2,1,0:T(8,128)S(1)}, f32[1,16,1024]{2,1,0:T(8,128)}, u32[]{:S(2)}) copy-start(f32[1,16,1024]{2,1,0:T(8,128)} %slice.258) | copy-start | bytes 196612
  71.6 7.6 %collective-permute-start.5 = (f32[2,16,1024]{2,1,0:T(8,128)S(1)}, f32[2,16,1024]{2,1,0:T(8,128)S(1)}, u32[]{:S(2)}, u32[]{:S(2)}) collective-permute-start(f32[2,16,1024]{2,1,0:T(8,128)S(1)} %maximum_add_fusion.2), channel_id=1, source_target_pairs={{0,64},{8,72},{16,80},{24,88},{32,96},{40,104},{48,112},{56,120},{... | collective-permute-start | bytes 393224 | tf_op jit(solution)/shard_map/ppermute | solution.py:20
  75.9 3.3 %copy-start.3 = (f32[1,16,1024]{2,1,0:T(8,128)S(1)}, f32[1,16,1024]{2,1,0:T(8,128)}, u32[]{:S(2)}) copy-start(f32[1,16,1024]{2,1,0:T(8,128)} %slice.270) | copy-start | bytes 196612
  75.9 3.3 %copy-start.4 = (f32[1,16,1024]{2,1,0:T(8,128)S(1)}, f32[1,16,1024]{2,1,0:T(8,128)}, u32[]{:S(2)}) copy-start(f32[1,16,1024]{2,1,0:T(8,128)} %slice.266) | copy-start | bytes 196612
  79.3 18.7 %collective-permute-start.6 = (f32[2,16,1024]{2,1,0:T(8,128)S(1)}, f32[2,16,1024]{2,1,0:T(8,128)S(1)}, u32[]{:S(2)}, u32[]{:S(2)}) collective-permute-start(f32[2,16,1024]{2,1,0:T(8,128)S(1)} %maximum_add_fusion.3), channel_id=1, source_target_pairs={{0,128},{8,136},{16,144},{24,152},{32,160},{40,168},{48,176},{56,1... | collective-permute-start | bytes 393224 | tf_op jit(solution)/shard_map/ppermute | solution.py:20
  98.0 1.0 copy-start
  98.0 1.2 copy-start.1
  98.0 1.2 copy-start.11
  99.2 2.5 %copy-start.9 = (f32[1024]{0:T(1024)S(1)}, f32[1024]{0:T(1024)}, u32[]{:S(2)}) copy-start(f32[1024]{0:T(1024)} %param.13) | copy-start | bytes 12292
  101.6 23.7 %copy-start.10 = (f32[1024]{0:T(1024)S(1)}, f32[1024]{0:T(1024)}, u32[]{:S(2)}) copy-start(f32[1024]{0:T(1024)} %param.14) | copy-start | bytes 12292
  101.9 10.2 %collective-permute-start.9 = (f32[128]{0:T(128)S(1)}, f32[128]{0:T(128)S(1)}, u32[]{:S(2)}, u32[]{:S(2)}) collective-permute-start(f32[128]{0:T(128)S(1)} %get-tuple-element.22), channel_id=1, source_target_pairs={{0,3},{1,0},{2,1},{3,2},{4,7},{5,4},{6,5},{7,6},{8,11},{9,8},{10,9... | collective-permute-start | bytes 1544 | tf_op jit(solution)/shard_map/ppermute | solution.py:181
  106.5 7.0 %collective-permute-start.8 = (f32[128]{0:T(128)S(1)}, f32[128]{0:T(128)S(1)}, u32[]{:S(2)}, u32[]{:S(2)}) collective-permute-start(f32[128]{0:T(128)S(1)} %get-tuple-element.22), channel_id=1, source_target_pairs={{0,2},{1,3},{2,0},{3,1},{4,6},{5,7},{6,4},{7,5},{8,10},{9,11},{10,... | collective-permute-start | bytes 1544 | tf_op jit(solution)/shard_map/ppermute | solution.py:181
  109.3 6.7 %collective-permute-start.7 = (f32[128]{0:T(128)S(1)}, f32[128]{0:T(128)S(1)}, u32[]{:S(2)}, u32[]{:S(2)}) collective-permute-start(f32[128]{0:T(128)S(1)} %get-tuple-element.22), channel_id=1, source_target_pairs={{0,1},{1,2},{2,3},{3,0},{4,5},{5,6},{6,7},{7,4},{8,9},{9,10},{10,1... | collective-permute-start | bytes 1544 | tf_op jit(solution)/shard_map/ppermute | solution.py:181
  116.0 9.4 %collective-permute-start.10 = (f32[128]{0:T(128)S(1)}, f32[128]{0:T(128)S(1)}, u32[]{:S(2)}, u32[]{:S(2)}) collective-permute-start(f32[128]{0:T(128)S(1)} %fusion.32), channel_id=1, source_target_pairs={{0,4},{1,5},{2,6},{3,7},{4,0},{5,1},{6,2},{7,3},{8,12},{9,13},{10,... | collective-permute-start | bytes 1544 | tf_op jit(solution)/shard_map/ppermute | solution.py:189

commit v12 on v9

--- a/solution.py
+++ b/solution.py
@@ -142,7 +142,15 @@
     def widen(factor):
         return jnp.repeat(factor, group_width, axis=2)
 
-    running = passed_along(summary.reshape(2, mode_count, channels), "ctx", 1)
+    fresh = summary.reshape(2, mode_count, channels)
+    running = passed_along(fresh, "ctx", 1)
+    first_width = min(4, reach)
+    power = stepping
+    for distance in range(2, first_width + 1):
+        older = passed_along(fresh, "ctx", distance)
+        alive = unbroken(anchor - (distance - 1) * tok_rows, anchor - 1)
+        running = running + complex_times(widen(power) * alive.astype(jnp.float32), older)
+        power = complex_times(power, stepping)
     pole_inputs, running = lax.optimization_barrier(((rate, angle, residue), running))
     tables = pole_tables(*pole_inputs, SPAN)
     response = tables[0]
@@ -150,8 +158,7 @@
         toeplitz(response), values[span_index], span_pos[span_index], span_begin[span_index]
     )
     insides = [lax.optimization_barrier(inside)]
-    power = stepping
-    distance = 1
+    distance = first_width
     while distance < reach:
         earlier = passed_along(running, "ctx", distance)
         alive = unbroken(anchor - distance * tok_rows, anchor - 1)

time: 128 us -> 120 us (0.938)
  local copies, waits for them, and re-layouts: 21.2 us -> 13.4 us
  other arithmetic: 22.4 us -> 17.6 us
  waiting for transfers between devices: 18.6 us -> 20.8 us
  starting transfers between devices: 45.5 us -> 47.4 us
    slice x5 -> x6, local copies, waits for them, and re-layouts: 4.47 us -> 1.62 us  [complex_times(): factor_one[1] * factor_two[1]]
    slice x10 -> x12, local copies, waits for them, and re-layouts: 4.48 us -> 1.65 us  [complex_times(): factor_one[0] * factor_two[0] - factor_one[1] * factor_two[1]]
    ppermute x7 -> x8, starting transfers between devices: 27.4 us -> 29.9 us  [passed_along(): return lax.ppermute(block, axis, route)]
    another operation x1, other arithmetic: 2.43 us -> 0.63 us  [pole_tables(): entering = jnp.stack([enter_re, -enter_im])]
    sub x5 -> x6, other arithmetic: 1.87 us -> 0.11 us  [complex_times(): factor_one[0] * factor_two[0] - factor_one[1] * factor_two[1]]
    ppermute x7 -> x8, waiting for transfers between devices: 13.2 us -> 14.9 us  [passed_along(): return lax.ppermute(block, axis, route)]
    mul x2, local copies, waits for them, and re-layouts: 1.4 us -> 0.08 us  [pole_tables(): resid_re * power_re[:, :, :block] - resid_im * power_im[:, :, :block]]
  transfers between devices with their start and end apart: 11 -> 12, of which waited for: 6 -> 7; matrix products, arithmetic and copies ran while one was open for 31% -> 25% of each run, Pallas kernels for 0% -> 0%
where the time goes in v12:
time: 120 us; the launch traced here: 119 us
  starting transfers between devices  47.4 us (40%)
  waiting for transfers between devices  20.8 us (17%)
  other arithmetic  17.6 us (15%)
  matrix products  15.2 us (13%)
  local copies, waits for them, and re-layouts  13.4 us (11%)
  between operations  4.54 us (4%)
    ppermute x8, starting transfers between devices, passed_along(): return lax.ppermute(block, axis, route)  29.9 us
    ppermute x8, waiting for transfers between devices, passed_along(): return lax.ppermute(block, axis, route)  14.9 us
    ppermute x3, starting transfers between devices, on_device(): gathered.append(lax.ppermute(partial, 'tp', pairs))  10.2 us
    ppermute x1, starting transfers between devices, on_device(): squares = squares + lax.ppermute(squares, 'tp', pairs)  7.31 us
    dot_general x1, matrix products, inside_terms(): jnp.einsum('gts,gis->git', matrix_table * same_genome[None], columns, pre...  5.72 us
    add x1, other arithmetic, short_filter(): result = result + jnp.where(keep_tap, taps_part[offset][None] * window, 0.0)  5.62 us
    mul x1, other arithmetic, pole_tables(): power_re = magnitude * jnp.cos(angle[:, :, None] * counter)  3.86 us
    ppermute x3, waiting for transfers between devices, on_device(): gathered.append(lax.ppermute(partial, 'tp', pairs))  3.83 us
  transfers between devices with their start and end apart: 12, of which 7 were waited for; matrix products, arithmetic and copies ran while one was open for 25% of the time, Pallas kernels for 0%

profile of v12, /device:TPU:128, one launch (start us, length us, event | category | flops | bytes accessed | tf_op | source)
XLA Modules:
  0.0 118.9 jit_solution(14712354860001448824)
XLA Ops:
  0.0 0.9 slice.247
  0.9 1.9 %collective-permute-start = (bf16[6,3,1024]{2,0,1:T(8,128)(2,1)S(1)}, bf16[6,3,1024]{2,0,1:T(8,128)(2,1)S(1)}, u32[]{:S(2)}, u32[]{:S(2)}) collective-permute-start(bf16[6,3,1024]{2,0,1:T(8,128)(2,1)S(1)} %slice.247), channel_id=1, source_target_pairs={{0,8},{8,16},{16,24},{24,32},{32,40},{40,48},{48,56},{56,64},{64,7... | collective-permute-start | bytes 110600 | tf_op jit(solution)/shard_map/ppermute | solution.py:20
  2.9 0.8 reduce-window.9
  3.7 1.4 %and_reduce_fusion = (pred[]{:T(512)}, pred[]{:T(512)}, pred[]{:T(512)}, pred[]{:T(512)}, pred[]{:T(512)}, /*index=5*/pred[]{:T(512)}, s32[4]{0:T(128)S(1)}) fusion(s32[]{:T(128)S(6)} %sub.167, s32[]{:T(128)S(6)} %sub.148, s32[]{:T(128)S(6)} %sub.164, s32[]{:T(128)S(6)} %sub.161, s32[]{:T(128)S(6)} %sub.154, s32[]{:T(128)S(6)} %sub.151, s32[]{:T(128)S(6)} %sub.147, ...), kind=kLoop, calls=%fused_computation.133 | loop fusion | flops 74 | bytes 82 | tf_op jit(solution)/shard_map/reduce_or | solution.py:140
  5.3 0.7 slice.262
  6.0 0.8 copy.49
  6.8 0.7 neg.12
  7.5 0.8 subtract_bitcast_fusion.2
  8.2 1.5 %fusion.49 = (f32[1,3,1024]{2,0,1:T(1,128)S(1)}, f32[1,3,1024]{2,0,1:T(1,128)S(1)}, f32[1,3,1024]{2,0,1:T(1,128)S(1)}, f32[1,3,1024]{2,0,1:T(1,128)S(1)}, f32[1,...) fusion(f32[7,3,1024]{2,0,1:T(8,128)} %param.9), kind=kLoop, calls=%fused_computation.167 | loop fusion | bytes 172032 | tf_op jit(solution)/shard_map/slice | solution.py:97
  13.9 2.0 %fusion.20 = (f32[1,64,16,128]{3,2,0,1:T(8,128)S(1)}, f32[1,64,16,128]{3,2,0,1:T(8,128)S(1)}) fusion(f32[64,16]{1,0:T(8,128)S(1)} %copy.49, f32[128]{0:T(128)S(1)} %subtract_convert_fusion, f32[64,16]{1,0:T(8,128)S(1)} %copy.48), kind=kLoop, calls=%fused_computation.41 | loop fusion | flops 524288 | bytes 1057280 | tf_op jit(solution)/shard_map/mul | solution.py:59
  15.8 0.7 compare_convert_fusion.1
  16.6 0.4 copy.45
  17.0 0.4 copy.46
  17.4 5.6 %select_add_fusion = f32[128,3,1024]{0,2,1:T(8,128)S(1)} fusion(bf16[128,3,1024]{0,2,1:T(8,128)(2,1)S(1)} %copy.45, bf16[6,3,1024]{0,2,1:T(8,128)(2,1)S(1)} %copy.46, f32[3,1024]{1,0:T(4,128)S(1)} %get-tuple-element.88, f32[3,1024]{1,0:T(4,128)S(1)} %get-tuple-element.89, f32[3,1024]{1,0:T(4,128)S(1)} %get-tuple-element.90, ...), kind=kLoop, calls=%fused_computation.16 | loop fusion | flops 17694720 | bytes 2483072 | tf_op jit(solution)/shard_map/add | solution.py:97
  23.1 3.8 %convolution_bitcast_fusion = f32[2,16,64,16]{1,3,0,2:T(8,128)S(1)} fusion(f32[64,16,128,1]{2,1,3,0:T(8,128)S(1)} %bitcast.218, f32[1,64,16,128]{3,2,0,1:T(8,128)S(1)} %get-tuple-element.58, f32[1,64,16,128]{3,2,0,1:T(8,128)S(1)} %get-tuple-element.57, f32[128]{0:T(128)S(1)} %compare_convert_fusion.1), kind=kOutput, calls=%fused_computation.19 | convolution fusion | flops 25690112 | bytes 1704448 | tf_op jit(solution)/shard_map/rgns,gis->rngi/dot_general | solution.py:83
  26.9 0.9 copy.50
  27.8 0.6 reshape.236
  28.4 3.5 %collective-permute-start.2 = (f32[2,16,1024]{2,1,0:T(8,128)S(1)}, f32[2,16,1024]{2,1,0:T(8,128)S(1)}, u32[]{:S(2)}, u32[]{:S(2)}) collective-permute-start(f32[2,16,1024]{2,1,0:T(8,128)S(1)} %reshape.236), channel_id=1, source_target_pairs={{0,16},{8,24},{16,32},{24,40},{32,48},{40,56},{48,64},{56,72},{64,... | collective-permute-start | bytes 393224 | tf_op jit(solution)/shard_map/ppermute | solution.py:20
  32.2 0.3 slice.269
  32.6 0.3 slice.265
  33.1 0.3 slice.277
  33.6 0.3 slice.273
  35.0 0.3 slice.314
  36.4 0.3 slice.302
  37.7 3.3 %collective-permute-start.1 = (f32[2,16,1024]{2,1,0:T(8,128)S(1)}, f32[2,16,1024]{2,1,0:T(8,128)S(1)}, u32[]{:S(2)}, u32[]{:S(2)}) collective-permute-start(f32[2,16,1024]{2,1,0:T(8,128)S(1)} %reshape.236), channel_id=1, source_target_pairs={{0,8},{8,16},{16,24},{24,32},{32,40},{40,48},{48,56},{56,64},{64,7... | collective-permute-start | bytes 393224 | tf_op jit(solution)/shard_map/ppermute | solution.py:20
  41.0 3.4 %collective-permute-start.3 = (f32[2,16,1024]{2,1,0:T(8,128)S(1)}, f32[2,16,1024]{2,1,0:T(8,128)S(1)}, u32[]{:S(2)}, u32[]{:S(2)}) collective-permute-start(f32[2,16,1024]{2,1,0:T(8,128)S(1)} %reshape.236), channel_id=1, source_target_pairs={{0,24},{8,32},{16,40},{24,48},{32,56},{40,64},{48,72},{56,80},{64,... | collective-permute-start | bytes 393224 | tf_op jit(solution)/shard_map/ppermute | solution.py:20
  44.4 5.1 %collective-permute-start.4 = (f32[2,16,1024]{2,1,0:T(8,128)S(1)}, f32[2,16,1024]{2,1,0:T(8,128)S(1)}, u32[]{:S(2)}, u32[]{:S(2)}) collective-permute-start(f32[2,16,1024]{2,1,0:T(8,128)S(1)} %reshape.236), channel_id=1, source_target_pairs={{0,32},{8,40},{16,48},{24,56},{32,64},{40,72},{48,80},{56,88},{64,... | collective-permute-start | bytes 393224 | tf_op jit(solution)/shard_map/ppermute | solution.py:20
  49.5 2.6 %collective-permute-done.3 = f32[2,16,1024]{2,1,0:T(8,128)S(1)} collective-permute-done((f32[2,16,1024]{2,1,0:T(8,128)S(1)}, f32[2,16,1024]{2,1,0:T(8,128)S(1)}, u32[]{:S(2)}, u32[]{:S(2)}) %collective-permute-start.3) | collective-permute-done | bytes 131104 | tf_op jit(solution)/shard_map/ppermute | solution.py:20
  52.1 4.9 %collective-permute-done.4 = f32[2,16,1024]{2,1,0:T(8,128)S(1)} collective-permute-done((f32[2,16,1024]{2,1,0:T(8,128)S(1)}, f32[2,16,1024]{2,1,0:T(8,128)S(1)}, u32[]{:S(2)}, u32[]{:S(2)}) %collective-permute-start.4) | collective-permute-done | bytes 131104 | tf_op jit(solution)/shard_map/ppermute | solution.py:20
  57.5 1.9 %collective-permute-start.5 = (f32[2,16,1024]{2,1,0:T(8,128)S(1)}, f32[2,16,1024]{2,1,0:T(8,128)S(1)}, u32[]{:S(2)}, u32[]{:S(2)}) collective-permute-start(f32[2,16,1024]{2,1,0:T(8,128)S(1)} %fusion.28), channel_id=1, source_target_pairs={{0,32},{8,40},{16,48},{24,56},{32,64},{40,72},{48,80},{56,88},{64,... | collective-permute-start | bytes 393224 | tf_op jit(solution)/shard_map/ppermute | solution.py:20
  59.4 3.9 %fusion.7 = (f32[64,16,129]{2,1,0:T(8,128)S(1)}, f32[64,16,129]{2,1,0:T(8,128)S(1)}) fusion(f32[64,16]{1,0:T(8,128)S(1)} %copy.53, f32[129]{0:T(256)S(1)} %iota_convert_fusion, f32[64,16]{1,0:T(8,128)S(1)} %copy.52), kind=kLoop, calls=%fused_computation.23 | loop fusion | flops 528384 | bytes 1065476 | tf_op jit(solution)/shard_map/mul | solution.py:40
  63.2 0.6 subtract_bitcast_fusion
  63.9 5.3 %collective-permute-done.5 = f32[2,16,1024]{2,1,0:T(8,128)S(1)} collective-permute-done((f32[2,16,1024]{2,1,0:T(8,128)S(1)}, f32[2,16,1024]{2,1,0:T(8,128)S(1)}, u32[]{:S(2)}, u32[]{:S(2)}) %collective-permute-start.5) | collective-permute-done | bytes 131104 | tf_op jit(solution)/shard_map/ppermute | solution.py:20
  69.2 1.9 %collective-permute-start.6 = (f32[2,16,1024]{2,1,0:T(8,128)S(1)}, f32[2,16,1024]{2,1,0:T(8,128)S(1)}, u32[]{:S(2)}, u32[]{:S(2)}) collective-permute-start(f32[2,16,1024]{2,1,0:T(8,128)S(1)} %maximum_add_fusion.1), channel_id=1, source_target_pairs={{0,64},{8,72},{16,80},{24,88},{32,96},{40,104},{48,112},{56,120},{... | collective-permute-start | bytes 393224 | tf_op jit(solution)/shard_map/ppermute | solution.py:20
  71.2 3.3 %fusion.4 = f32[64,128,128]{2,0,1:T(8,128)S(1)} fusion(s32[128,128]{1,0:T(8,128)S(1)} %iota_subtract_fusion, f32[128,128]{1,0:T(8,128)S(1)} %compare_convert_fusion, f32[64,128]{1,0:T(8,128)S(1)} %get-tuple-element.33), kind=kOutput, calls=%fused_computation.15 | convolution fusion | flops 1613758464 | bytes 4358144 | tf_op jit(solution)/shard_map/gk,kts->gts/dot_general | solution.py:34
  74.4 2.2 %collective-permute-done.6 = f32[2,16,1024]{2,1,0:T(8,128)S(1)} collective-permute-done((f32[2,16,1024]{2,1,0:T(8,128)S(1)}, f32[2,16,1024]{2,1,0:T(8,128)S(1)}, u32[]{:S(2)}, u32[]{:S(2)}) %collective-permute-start.6) | collective-permute-done | bytes 131104 | tf_op jit(solution)/shard_map/ppermute | solution.py:20
  76.6 8.8 %collective-permute-start.7 = (f32[2,16,1024]{2,1,0:T(8,128)S(1)}, f32[2,16,1024]{2,1,0:T(8,128)S(1)}, u32[]{:S(2)}, u32[]{:S(2)}) collective-permute-start(f32[2,16,1024]{2,1,0:T(8,128)S(1)} %maximum_add_fusion.2), channel_id=1, source_target_pairs={{0,128},{8,136},{16,144},{24,152},{32,160},{40,168},{48,176},{56,1... | collective-permute-start | bytes 393224 | tf_op jit(solution)/shard_map/ppermute | solution.py:20
  85.5 5.7 %fusion.1 = f32[64,16,128]{2,1,0:T(8,128)} fusion(f32[64,16,128]{2,1,0:T(8,128)S(1)} %bitcast.219, f32[64,128,128]{2,0,1:T(8,128)S(1)} %fusion.4), kind=kOutput, calls=%fused_computation.2 | convolution fusion | flops 100663296 | bytes 5242880 | tf_op jit(solution)/shard_map/gts,gis->git/dot_general | solution.py:78
  91.2 0.4 reshape.237
  91.6 2.4 %fusion.6 = f32[64,16,128]{2,1,0:T(8,128)S(1)} fusion(f32[64,16,128]{2,1,0:T(8,128)} %fusion.1, f32[1,64,16,128]{3,2,0,1:T(8,128)S(1)} %get-tuple-element.32, f32[1,64,16,128]{3,2,0,1:T(8,128)S(1)} %get-tuple-element.31, f32[2,16,64,16]{3,2,1,0:T(8,128)S(1)} %reshape.237, pred[128]{0:T(512)(128)(4,1)S(1)} %get-tuple-element.80), kind=kOutput, calls=%fused_computation.22 | convolution fusion | flops 25690112 | bytes 2228352 | tf_op jit(solution)/shard_map/rgnt,rngi->git/dot_general | solution.py:87
  94.3 4.7 %collective-permute-start.10 = (f32[128]{0:T(128)S(1)}, f32[128]{0:T(128)S(1)}, u32[]{:S(2)}, u32[]{:S(2)}) collective-permute-start(f32[128]{0:T(128)S(1)} %get-tuple-element.23), channel_id=1, source_target_pairs={{0,3},{1,0},{2,1},{3,2},{4,7},{5,4},{6,5},{7,6},{8,11},{9,8},{10,9... | collective-permute-start | bytes 1544 | tf_op jit(solution)/shard_map/ppermute | solution.py:183
  99.0 2.7 %collective-permute-start.9 = (f32[128]{0:T(128)S(1)}, f32[128]{0:T(128)S(1)}, u32[]{:S(2)}, u32[]{:S(2)}) collective-permute-start(f32[128]{0:T(128)S(1)} %get-tuple-element.23), channel_id=1, source_target_pairs={{0,2},{1,3},{2,0},{3,1},{4,6},{5,7},{6,4},{7,5},{8,10},{9,11},{10,... | collective-permute-start | bytes 1544 | tf_op jit(solution)/shard_map/ppermute | solution.py:183
  101.7 2.8 %collective-permute-start.8 = (f32[128]{0:T(128)S(1)}, f32[128]{0:T(128)S(1)}, u32[]{:S(2)}, u32[]{:S(2)}) collective-permute-start(f32[128]{0:T(128)S(1)} %get-tuple-element.23), channel_id=1, source_target_pairs={{0,1},{1,2},{2,3},{3,0},{4,5},{5,6},{6,7},{7,4},{8,9},{9,10},{10,1... | collective-permute-start | bytes 1544 | tf_op jit(solution)/shard_map/ppermute | solution.py:183
  104.5 1.4 %collective-permute-done.9 = f32[128]{0:T(128)S(1)} collective-permute-done((f32[128]{0:T(128)S(1)}, f32[128]{0:T(128)S(1)}, u32[]{:S(2)}, u32[]{:S(2)}) %collective-permute-start.9) | collective-permute-done | bytes 544 | tf_op jit(solution)/shard_map/ppermute | solution.py:183
  105.9 2.4 %collective-permute-done.8 = f32[128]{0:T(128)S(1)} collective-permute-done((f32[128]{0:T(128)S(1)}, f32[128]{0:T(128)S(1)}, u32[]{:S(2)}, u32[]{:S(2)}) %collective-permute-start.8) | collective-permute-done | bytes 544 | tf_op jit(solution)/shard_map/ppermute | solution.py:183
  108.4 7.3 %collective-permute-start.11 = (f32[128]{0:T(128)S(1)}, f32[128]{0:T(128)S(1)}, u32[]{:S(2)}, u32[]{:S(2)}) collective-permute-start(f32[128]{0:T(128)S(1)} %fusion.40), channel_id=1, source_target_pairs={{0,4},{1,5},{2,6},{3,7},{4,0},{5,1},{6,2},{7,3},{8,12},{9,13},{10,... | collective-permute-start | bytes 1544 | tf_op jit(solution)/shard_map/ppermute | solution.py:191
  115.7 2.0 %collective-permute-done.11 = f32[128]{0:T(128)S(1)} collective-permute-done((f32[128]{0:T(128)S(1)}, f32[128]{0:T(128)S(1)}, u32[]{:S(2)}, u32[]{:S(2)}) %collective-permute-start.11) | collective-permute-done | bytes 544 | tf_op jit(solution)/shard_map/ppermute | solution.py:191
  118.0 0.8 copy.58
  (83 shorter events, 5.5 us)
Async XLA Ops:
  0.0 16.5 %copy-start = (bf16[128,3,1024]{2,0,1:T(8,128)(2,1)S(1)}, bf16[128,3,1024]{2,0,1:T(8,128)(2,1)}, u32[]{:S(2)}) copy-start(bf16[128,3,1024]{2,0,1:T(8,128)(2,1)} %param.8) | copy-start | bytes 2359300
  0.9 16.1 %collective-permute-start = (bf16[6,3,1024]{2,0,1:T(8,128)(2,1)S(1)}, bf16[6,3,1024]{2,0,1:T(8,128)(2,1)S(1)}, u32[]{:S(2)}, u32[]{:S(2)}) collective-permute-start(bf16[6,3,1024]{2,0,1:T(8,128)(2,1)S(1)} %slice.247), channel_id=1, source_target_pairs={{0,8},{8,16},{16,24},{24,32},{32,40},{40,48},{48,56},{56,64},{64,7... | collective-permute-start | bytes 110600 | tf_op jit(solution)/shard_map/ppermute | solution.py:20
  28.4 21.1 %collective-permute-start.2 = (f32[2,16,1024]{2,1,0:T(8,128)S(1)}, f32[2,16,1024]{2,1,0:T(8,128)S(1)}, u32[]{:S(2)}, u32[]{:S(2)}) collective-permute-start(f32[2,16,1024]{2,1,0:T(8,128)S(1)} %reshape.236), channel_id=1, source_target_pairs={{0,16},{8,24},{16,32},{24,40},{32,48},{40,56},{48,64},{56,72},{64,... | collective-permute-start | bytes 393224 | tf_op jit(solution)/shard_map/ppermute | solution.py:20
  37.1 19.9 %copy-start.1 = (f32[64,16]{0,1:T(8,128)S(1)}, f32[64,16]{0,1:T(8,128)}, u32[]{:S(2)}) copy-start(f32[64,16]{0,1:T(8,128)} %param.11) | copy-start | bytes 12292
  37.2 20.0 %copy-start.2 = (f32[64,16]{0,1:T(8,128)S(1)}, f32[64,16]{0,1:T(8,128)}, u32[]{:S(2)}) copy-start(f32[64,16]{0,1:T(8,128)} %param.10) | copy-start | bytes 12292
  37.2 20.1 %copy-start.3 = (f32[2,64,16]{1,2,0:T(8,128)S(1)}, f32[2,64,16]{1,2,0:T(8,128)}, u32[]{:S(2)}) copy-start(f32[2,64,16]{1,2,0:T(8,128)} %param.12) | copy-start | bytes 24580
  37.7 19.4 %collective-permute-start.1 = (f32[2,16,1024]{2,1,0:T(8,128)S(1)}, f32[2,16,1024]{2,1,0:T(8,128)S(1)}, u32[]{:S(2)}, u32[]{:S(2)}) collective-permute-start(f32[2,16,1024]{2,1,0:T(8,128)S(1)} %reshape.236), channel_id=1, source_target_pairs={{0,8},{8,16},{16,24},{24,32},{32,40},{40,48},{48,56},{56,64},{64,7... | collective-permute-start | bytes 393224 | tf_op jit(solution)/shard_map/ppermute | solution.py:20
  41.0 11.1 %collective-permute-start.3 = (f32[2,16,1024]{2,1,0:T(8,128)S(1)}, f32[2,16,1024]{2,1,0:T(8,128)S(1)}, u32[]{:S(2)}, u32[]{:S(2)}) collective-permute-start(f32[2,16,1024]{2,1,0:T(8,128)S(1)} %reshape.236), channel_id=1, source_target_pairs={{0,24},{8,32},{16,40},{24,48},{32,56},{40,64},{48,72},{56,80},{64,... | collective-permute-start | bytes 393224 | tf_op jit(solution)/shard_map/ppermute | solution.py:20
  44.4 12.6 %collective-permute-start.4 = (f32[2,16,1024]{2,1,0:T(8,128)S(1)}, f32[2,16,1024]{2,1,0:T(8,128)S(1)}, u32[]{:S(2)}, u32[]{:S(2)}) collective-permute-start(f32[2,16,1024]{2,1,0:T(8,128)S(1)} %reshape.236), channel_id=1, source_target_pairs={{0,32},{8,40},{16,48},{24,56},{32,64},{40,72},{48,80},{56,88},{64,... | collective-permute-start | bytes 393224 | tf_op jit(solution)/shard_map/ppermute | solution.py:20
  57.5 11.7 %collective-permute-start.5 = (f32[2,16,1024]{2,1,0:T(8,128)S(1)}, f32[2,16,1024]{2,1,0:T(8,128)S(1)}, u32[]{:S(2)}, u32[]{:S(2)}) collective-permute-start(f32[2,16,1024]{2,1,0:T(8,128)S(1)} %fusion.28), channel_id=1, source_target_pairs={{0,32},{8,40},{16,48},{24,56},{32,64},{40,72},{48,80},{56,88},{64,... | collective-permute-start | bytes 393224 | tf_op jit(solution)/shard_map/ppermute | solution.py:20
  69.2 7.3 %collective-permute-start.6 = (f32[2,16,1024]{2,1,0:T(8,128)S(1)}, f32[2,16,1024]{2,1,0:T(8,128)S(1)}, u32[]{:S(2)}, u32[]{:S(2)}) collective-permute-start(f32[2,16,1024]{2,1,0:T(8,128)S(1)} %maximum_add_fusion.1), channel_id=1, source_target_pairs={{0,64},{8,72},{16,80},{24,88},{32,96},{40,104},{48,112},{56,120},{... | collective-permute-start | bytes 393224 | tf_op jit(solution)/shard_map/ppermute | solution.py:20
  76.6 14.6 %collective-permute-start.7 = (f32[2,16,1024]{2,1,0:T(8,128)S(1)}, f32[2,16,1024]{2,1,0:T(8,128)S(1)}, u32[]{:S(2)}, u32[]{:S(2)}) collective-permute-start(f32[2,16,1024]{2,1,0:T(8,128)S(1)} %maximum_add_fusion.2), channel_id=1, source_target_pairs={{0,128},{8,136},{16,144},{24,152},{32,160},{40,168},{48,176},{56,1... | collective-permute-start | bytes 393224 | tf_op jit(solution)/shard_map/ppermute | solution.py:20
  91.6 2.5 %copy-start.4 = (f32[1024]{0:T(1024)S(1)}, f32[1024]{0:T(1024)}, u32[]{:S(2)}) copy-start(f32[1024]{0:T(1024)} %param.13) | copy-start | bytes 12292
  94.1 23.7 %copy-start.5 = (f32[1024]{0:T(1024)S(1)}, f32[1024]{0:T(1024)}, u32[]{:S(2)}) copy-start(f32[1024]{0:T(1024)} %param.14) | copy-start | bytes 12292
  94.3 10.2 %collective-permute-start.10 = (f32[128]{0:T(128)S(1)}, f32[128]{0:T(128)S(1)}, u32[]{:S(2)}, u32[]{:S(2)}) collective-permute-start(f32[128]{0:T(128)S(1)} %get-tuple-element.23), channel_id=1, source_target_pairs={{0,3},{1,0},{2,1},{3,2},{4,7},{5,4},{6,5},{7,6},{8,11},{9,8},{10,9... | collective-permute-start | bytes 1544 | tf_op jit(solution)/shard_map/ppermute | solution.py:183
  99.0 7.0 %collective-permute-start.9 = (f32[128]{0:T(128)S(1)}, f32[128]{0:T(128)S(1)}, u32[]{:S(2)}, u32[]{:S(2)}) collective-permute-start(f32[128]{0:T(128)S(1)} %get-tuple-element.23), channel_id=1, source_target_pairs={{0,2},{1,3},{2,0},{3,1},{4,6},{5,7},{6,4},{7,5},{8,10},{9,11},{10,... | collective-permute-start | bytes 1544 | tf_op jit(solution)/shard_map/ppermute | solution.py:183
  101.7 6.7 %collective-permute-start.8 = (f32[128]{0:T(128)S(1)}, f32[128]{0:T(128)S(1)}, u32[]{:S(2)}, u32[]{:S(2)}) collective-permute-start(f32[128]{0:T(128)S(1)} %get-tuple-element.23), channel_id=1, source_target_pairs={{0,1},{1,2},{2,3},{3,0},{4,5},{5,6},{6,7},{7,4},{8,9},{9,10},{10,1... | collective-permute-start | bytes 1544 | tf_op jit(solution)/shard_map/ppermute | solution.py:183
  108.4 9.4 %collective-permute-start.11 = (f32[128]{0:T(128)S(1)}, f32[128]{0:T(128)S(1)}, u32[]{:S(2)}, u32[]{:S(2)}) collective-permute-start(f32[128]{0:T(128)S(1)} %fusion.40), channel_id=1, source_target_pairs={{0,4},{1,5},{2,6},{3,7},{4,0},{5,1},{6,2},{7,3},{8,12},{9,13},{10,... | collective-permute-start | bytes 1544 | tf_op jit(solution)/shard_map/ppermute | solution.py:191

commit v13 on v12

--- a/solution.py
+++ b/solution.py
@@ -144,7 +144,7 @@
 
     fresh = summary.reshape(2, mode_count, channels)
     running = passed_along(fresh, "ctx", 1)
-    first_width = min(4, reach)
+    first_width = min(8, reach)
     power = stepping
     for distance in range(2, first_width + 1):
         older = passed_along(fresh, "ctx", distance)

time: 120 us -> 133 us (1.11)
  the two profiles are of different devices: /device:TPU:128 before, /device:TPU:120 now
where the time goes in v13:
time: 133 us; the launch traced here: 132 us
  starting transfers between devices  59.6 us (45%)
  other arithmetic  17.7 us (13%)
  waiting for transfers between devices  16.7 us (13%)
  local copies, waits for them, and re-layouts  16.1 us (12%)
  matrix products  15.2 us (11%)
  between operations  6.6 us (5%)
    ppermute x11, starting transfers between devices, passed_along(): return lax.ppermute(block, axis, route)  47.5 us
    ppermute x3, starting transfers between devices, on_device(): gathered.append(lax.ppermute(partial, 'tp', pairs))  10.2 us
    ppermute x1, waiting for transfers between devices, on_device(): squares = squares + lax.ppermute(squares, 'tp', pairs)  7.44 us
    dot_general x1, matrix products, inside_terms(): jnp.einsum('gts,gis->git', matrix_table * same_genome[None], columns, pre...  5.72 us
    add x1, other arithmetic, short_filter(): result = result + jnp.where(keep_tap, taps_part[offset][None] * window, 0.0)  5.62 us
    ppermute x11, waiting for transfers between devices, passed_along(): return lax.ppermute(block, axis, route)  5.41 us
    mul x1, other arithmetic, pole_tables(): power_re = magnitude * jnp.cos(angle[:, :, None] * counter)  3.86 us
    ppermute x3, waiting for transfers between devices, on_device(): gathered.append(lax.ppermute(partial, 'tp', pairs))  3.83 us
  transfers between devices with their start and end apart: 15, of which 5 were waited for; matrix products, arithmetic and copies ran while one was open for 24% of the time, Pallas kernels for 0%

profile of v13, /device:TPU:120, one launch (start us, length us, event | category | flops | bytes accessed | tf_op | source)
XLA Modules:
  0.0 131.8 jit_solution(5243751216527577490)
XLA Ops:
  0.0 0.9 slice.331
  0.9 1.9 %collective-permute-start = (bf16[6,3,1024]{2,0,1:T(8,128)(2,1)S(1)}, bf16[6,3,1024]{2,0,1:T(8,128)(2,1)S(1)}, u32[]{:S(2)}, u32[]{:S(2)}) collective-permute-start(bf16[6,3,1024]{2,0,1:T(8,128)(2,1)S(1)} %slice.331), channel_id=1, source_target_pairs={{0,8},{8,16},{16,24},{24,32},{32,40},{40,48},{48,56},{56,64},{64,7... | collective-permute-start | bytes 110600 | tf_op jit(solution)/shard_map/ppermute | solution.py:20
  2.9 0.8 reduce-window.9
  3.7 1.5 %and_reduce_fusion = (pred[]{:T(512)}, pred[]{:T(512)}, pred[]{:T(512)}, pred[]{:T(512)}, pred[]{:T(512)}, /*index=5*/pred[]{:T(512)}, pred[]{:T(512)}, pred[]{:T(512)}, pred[]{:T(512)}, s32[4]{0:T(128)S(1)}) fusion(s32[]{:T(128)S(6)} %sub.209, s32[]{:T(128)S(6)} %sub.181, s32[]{:T(128)S(6)} %sub.206, s32[]{:T(128)S(6)} %sub.199, s32[]{:T(128)S(6)} %sub.196, ...), kind=kLoop, calls=%fused_computation.180 | loop fusion | flops 107 | bytes 97 | tf_op jit(solution)/shard_map/reduce_or | solution.py:140
  5.3 0.6 slice.346
  6.0 0.8 copy.49
  6.7 0.7 neg.12
  7.4 0.8 subtract_bitcast_fusion.2
  8.2 1.5 %fusion.67 = (f32[1,3,1024]{2,0,1:T(1,128)S(1)}, f32[1,3,1024]{2,0,1:T(1,128)S(1)}, f32[1,3,1024]{2,0,1:T(1,128)S(1)}, f32[1,3,1024]{2,0,1:T(1,128)S(1)}, f32[1,...) fusion(f32[7,3,1024]{2,0,1:T(8,128)} %param.9), kind=kLoop, calls=%fused_computation.216 | loop fusion | bytes 172032 | tf_op jit(solution)/shard_map/slice | solution.py:97
  15.8 2.0 %fusion.20 = (f32[1,64,16,128]{3,2,0,1:T(8,128)S(1)}, f32[1,64,16,128]{3,2,0,1:T(8,128)S(1)}) fusion(f32[64,16]{1,0:T(8,128)S(1)} %copy.49, f32[128]{0:T(128)S(1)} %subtract_convert_fusion, f32[64,16]{1,0:T(8,128)S(1)} %copy.48), kind=kLoop, calls=%fused_computation.41 | loop fusion | flops 524288 | bytes 1057280 | tf_op jit(solution)/shard_map/mul | solution.py:59
  17.8 0.6 compare_convert_fusion.1
  18.5 0.4 copy.45
  18.9 0.4 copy.46
  19.3 5.6 %select_add_fusion = f32[128,3,1024]{0,2,1:T(8,128)S(1)} fusion(bf16[128,3,1024]{0,2,1:T(8,128)(2,1)S(1)} %copy.45, bf16[6,3,1024]{0,2,1:T(8,128)(2,1)S(1)} %copy.46, f32[3,1024]{1,0:T(4,128)S(1)} %get-tuple-element.108, f32[3,1024]{1,0:T(4,128)S(1)} %get-tuple-element.109, f32[3,1024]{1,0:T(4,128)S(1)} %get-tuple-element.110, ...), kind=kLoop, calls=%fused_computation.16 | loop fusion | flops 17694720 | bytes 2483072 | tf_op jit(solution)/shard_map/add | solution.py:97
  25.0 3.8 %convolution_bitcast_fusion = f32[2,16,64,16]{1,3,0,2:T(8,128)S(1)} fusion(f32[64,16,128,1]{2,1,3,0:T(8,128)S(1)} %bitcast.586, f32[1,64,16,128]{3,2,0,1:T(8,128)S(1)} %get-tuple-element.67, f32[1,64,16,128]{3,2,0,1:T(8,128)S(1)} %get-tuple-element.66, f32[128]{0:T(128)S(1)} %compare_convert_fusion.1), kind=kOutput, calls=%fused_computation.19 | convolution fusion | flops 25690112 | bytes 1704448 | tf_op jit(solution)/shard_map/rgns,gis->rngi/dot_general | solution.py:83
  28.8 0.9 copy.50
  29.7 0.6 reshape.257
  30.3 6.8 %collective-permute-start.2 = (f32[2,16,1024]{2,1,0:T(8,128)S(1)}, f32[2,16,1024]{2,1,0:T(8,128)S(1)}, u32[]{:S(2)}, u32[]{:S(2)}) collective-permute-start(f32[2,16,1024]{2,1,0:T(8,128)S(1)} %reshape.257), channel_id=1, source_target_pairs={{0,16},{8,24},{16,32},{24,40},{32,48},{40,56},{48,64},{56,72},{64,... | collective-permute-start | bytes 393224 | tf_op jit(solution)/shard_map/ppermute | solution.py:20
  38.3 0.3 slice.361
  40.7 0.3 slice.373
  42.1 0.3 slice.393
  43.5 0.3 slice.397
  44.5 0.3 slice.418
  45.7 2.4 %collective-permute-start.1 = (f32[2,16,1024]{2,1,0:T(8,128)S(1)}, f32[2,16,1024]{2,1,0:T(8,128)S(1)}, u32[]{:S(2)}, u32[]{:S(2)}) collective-permute-start(f32[2,16,1024]{2,1,0:T(8,128)S(1)} %reshape.257), channel_id=1, source_target_pairs={{0,8},{8,16},{16,24},{24,32},{32,40},{40,48},{48,56},{56,64},{64,7... | collective-permute-start | bytes 393224 | tf_op jit(solution)/shard_map/ppermute | solution.py:20
  48.1 2.5 %collective-permute-start.3 = (f32[2,16,1024]{2,1,0:T(8,128)S(1)}, f32[2,16,1024]{2,1,0:T(8,128)S(1)}, u32[]{:S(2)}, u32[]{:S(2)}) collective-permute-start(f32[2,16,1024]{2,1,0:T(8,128)S(1)} %reshape.257), channel_id=1, source_target_pairs={{0,24},{8,32},{16,40},{24,48},{32,56},{40,64},{48,72},{56,80},{64,... | collective-permute-start | bytes 393224 | tf_op jit(solution)/shard_map/ppermute | solution.py:20
  50.6 5.9 %collective-permute-start.4 = (f32[2,16,1024]{2,1,0:T(8,128)S(1)}, f32[2,16,1024]{2,1,0:T(8,128)S(1)}, u32[]{:S(2)}, u32[]{:S(2)}) collective-permute-start(f32[2,16,1024]{2,1,0:T(8,128)S(1)} %reshape.257), channel_id=1, source_target_pairs={{0,32},{8,40},{16,48},{24,56},{32,64},{40,72},{48,80},{56,88},{64,... | collective-permute-start | bytes 393224 | tf_op jit(solution)/shard_map/ppermute | solution.py:20
  56.5 1.9 %collective-permute-start.5 = (f32[2,16,1024]{2,1,0:T(8,128)S(1)}, f32[2,16,1024]{2,1,0:T(8,128)S(1)}, u32[]{:S(2)}, u32[]{:S(2)}) collective-permute-start(f32[2,16,1024]{2,1,0:T(8,128)S(1)} %reshape.257), channel_id=1, source_target_pairs={{0,40},{8,48},{16,56},{24,64},{32,72},{40,80},{48,88},{56,96},{64,... | collective-permute-start | bytes 393224 | tf_op jit(solution)/shard_map/ppermute | solution.py:20
  58.4 6.2 %collective-permute-start.6 = (f32[2,16,1024]{2,1,0:T(8,128)S(1)}, f32[2,16,1024]{2,1,0:T(8,128)S(1)}, u32[]{:S(2)}, u32[]{:S(2)}) collective-permute-start(f32[2,16,1024]{2,1,0:T(8,128)S(1)} %reshape.257), channel_id=1, source_target_pairs={{0,48},{8,56},{16,64},{24,72},{32,80},{40,88},{48,96},{56,104},{64... | collective-permute-start | bytes 393224 | tf_op jit(solution)/shard_map/ppermute | solution.py:20
  64.7 3.7 %collective-permute-start.7 = (f32[2,16,1024]{2,1,0:T(8,128)S(1)}, f32[2,16,1024]{2,1,0:T(8,128)S(1)}, u32[]{:S(2)}, u32[]{:S(2)}) collective-permute-start(f32[2,16,1024]{2,1,0:T(8,128)S(1)} %reshape.257), channel_id=1, source_target_pairs={{0,56},{8,64},{16,72},{24,80},{32,88},{40,96},{48,104},{56,112},{6... | collective-permute-start | bytes 393224 | tf_op jit(solution)/shard_map/ppermute | solution.py:20
  68.4 0.9 collective-permute-done.4
  69.3 2.4 %collective-permute-start.8 = (f32[2,16,1024]{2,1,0:T(8,128)S(1)}, f32[2,16,1024]{2,1,0:T(8,128)S(1)}, u32[]{:S(2)}, u32[]{:S(2)}) collective-permute-start(f32[2,16,1024]{2,1,0:T(8,128)S(1)} %reshape.257), channel_id=1, source_target_pairs={{0,64},{8,72},{16,80},{24,88},{32,96},{40,104},{48,112},{56,120},{... | collective-permute-start | bytes 393224 | tf_op jit(solution)/shard_map/ppermute | solution.py:20
  71.9 4.4 %collective-permute-done.8 = f32[2,16,1024]{2,1,0:T(8,128)S(1)} collective-permute-done((f32[2,16,1024]{2,1,0:T(8,128)S(1)}, f32[2,16,1024]{2,1,0:T(8,128)S(1)}, u32[]{:S(2)}, u32[]{:S(2)}) %collective-permute-start.8) | collective-permute-done | bytes 131104 | tf_op jit(solution)/shard_map/ppermute | solution.py:20
  76.8 7.0 %collective-permute-start.9 = (f32[2,16,1024]{2,1,0:T(8,128)S(1)}, f32[2,16,1024]{2,1,0:T(8,128)S(1)}, u32[]{:S(2)}, u32[]{:S(2)}) collective-permute-start(f32[2,16,1024]{2,1,0:T(8,128)S(1)} %fusion.32), channel_id=1, source_target_pairs={{0,64},{8,72},{16,80},{24,88},{32,96},{40,104},{48,112},{56,120},{... | collective-permute-start | bytes 393224 | tf_op jit(solution)/shard_map/ppermute | solution.py:20
  83.9 3.9 %fusion.7 = (f32[64,16,129]{2,1,0:T(8,128)S(1)}, f32[64,16,129]{2,1,0:T(8,128)S(1)}) fusion(f32[64,16]{1,0:T(8,128)S(1)} %copy.53, f32[129]{0:T(256)S(1)} %iota_convert_fusion, f32[64,16]{1,0:T(8,128)S(1)} %copy.52), kind=kLoop, calls=%fused_computation.23 | loop fusion | flops 528384 | bytes 1065476 | tf_op jit(solution)/shard_map/mul | solution.py:40
  87.7 0.6 subtract_bitcast_fusion
  88.4 3.3 %fusion.4 = f32[64,128,128]{2,0,1:T(8,128)S(1)} fusion(s32[128,128]{1,0:T(8,128)S(1)} %iota_subtract_fusion, f32[128,128]{1,0:T(8,128)S(1)} %compare_convert_fusion, f32[64,128]{1,0:T(8,128)S(1)} %get-tuple-element.36), kind=kOutput, calls=%fused_computation.15 | convolution fusion | flops 1613758464 | bytes 4358144 | tf_op jit(solution)/shard_map/gk,kts->gts/dot_general | solution.py:34
  91.7 6.8 %collective-permute-start.10 = (f32[2,16,1024]{2,1,0:T(8,128)S(1)}, f32[2,16,1024]{2,1,0:T(8,128)S(1)}, u32[]{:S(2)}, u32[]{:S(2)}) collective-permute-start(f32[2,16,1024]{2,1,0:T(8,128)S(1)} %maximum_add_fusion.1), channel_id=1, source_target_pairs={{0,128},{8,136},{16,144},{24,152},{32,160},{40,168},{48,176},{56,1... | collective-permute-start | bytes 393224 | tf_op jit(solution)/shard_map/ppermute | solution.py:20
  98.5 5.7 %fusion.1 = f32[64,16,128]{2,1,0:T(8,128)} fusion(f32[64,16,128]{2,1,0:T(8,128)S(1)} %bitcast.587, f32[64,128,128]{2,0,1:T(8,128)S(1)} %fusion.4), kind=kOutput, calls=%fused_computation.2 | convolution fusion | flops 100663296 | bytes 5242880 | tf_op jit(solution)/shard_map/gts,gis->git/dot_general | solution.py:78
  104.2 0.4 reshape.258
  104.6 2.4 %fusion.6 = f32[64,16,128]{2,1,0:T(8,128)S(1)} fusion(f32[64,16,128]{2,1,0:T(8,128)} %fusion.1, f32[1,64,16,128]{3,2,0,1:T(8,128)S(1)} %get-tuple-element.35, f32[1,64,16,128]{3,2,0,1:T(8,128)S(1)} %get-tuple-element.34, f32[2,16,64,16]{3,2,1,0:T(8,128)S(1)} %reshape.258, pred[128]{0:T(512)(128)(4,1)S(1)} %get-tuple-element.100), kind=kOutput, calls=%fused_computation.22 | convolution fusion | flops 25690112 | bytes 2228352 | tf_op jit(solution)/shard_map/rgnt,rngi->git/dot_general | solution.py:87
  107.3 4.7 %collective-permute-start.13 = (f32[128]{0:T(128)S(1)}, f32[128]{0:T(128)S(1)}, u32[]{:S(2)}, u32[]{:S(2)}) collective-permute-start(f32[128]{0:T(128)S(1)} %get-tuple-element.26), channel_id=1, source_target_pairs={{0,3},{1,0},{2,1},{3,2},{4,7},{5,4},{6,5},{7,6},{8,11},{9,8},{10,9... | collective-permute-start | bytes 1544 | tf_op jit(solution)/shard_map/ppermute | solution.py:183
  112.0 2.7 %collective-permute-start.12 = (f32[128]{0:T(128)S(1)}, f32[128]{0:T(128)S(1)}, u32[]{:S(2)}, u32[]{:S(2)}) collective-permute-start(f32[128]{0:T(128)S(1)} %get-tuple-element.26), channel_id=1, source_target_pairs={{0,2},{1,3},{2,0},{3,1},{4,6},{5,7},{6,4},{7,5},{8,10},{9,11},{10,... | collective-permute-start | bytes 1544 | tf_op jit(solution)/shard_map/ppermute | solution.py:183
  114.7 2.8 %collective-permute-start.11 = (f32[128]{0:T(128)S(1)}, f32[128]{0:T(128)S(1)}, u32[]{:S(2)}, u32[]{:S(2)}) collective-permute-start(f32[128]{0:T(128)S(1)} %get-tuple-element.26), channel_id=1, source_target_pairs={{0,1},{1,2},{2,3},{3,0},{4,5},{5,6},{6,7},{7,4},{8,9},{9,10},{10,1... | collective-permute-start | bytes 1544 | tf_op jit(solution)/shard_map/ppermute | solution.py:183
  117.5 1.4 %collective-permute-done.12 = f32[128]{0:T(128)S(1)} collective-permute-done((f32[128]{0:T(128)S(1)}, f32[128]{0:T(128)S(1)}, u32[]{:S(2)}, u32[]{:S(2)}) %collective-permute-start.12) | collective-permute-done | bytes 544 | tf_op jit(solution)/shard_map/ppermute | solution.py:183
  118.9 2.4 %collective-permute-done.11 = f32[128]{0:T(128)S(1)} collective-permute-done((f32[128]{0:T(128)S(1)}, f32[128]{0:T(128)S(1)}, u32[]{:S(2)}, u32[]{:S(2)}) %collective-permute-start.11) | collective-permute-done | bytes 544 | tf_op jit(solution)/shard_map/ppermute | solution.py:183
  121.4 1.9 %collective-permute-start.14 = (f32[128]{0:T(128)S(1)}, f32[128]{0:T(128)S(1)}, u32[]{:S(2)}, u32[]{:S(2)}) collective-permute-start(f32[128]{0:T(128)S(1)} %fusion.59), channel_id=1, source_target_pairs={{0,4},{1,5},{2,6},{3,7},{4,0},{5,1},{6,2},{7,3},{8,12},{9,13},{10,... | collective-permute-start | bytes 1544 | tf_op jit(solution)/shard_map/ppermute | solution.py:191
  123.3 7.4 %collective-permute-done.14 = f32[128]{0:T(128)S(1)} collective-permute-done((f32[128]{0:T(128)S(1)}, f32[128]{0:T(128)S(1)}, u32[]{:S(2)}, u32[]{:S(2)}) %collective-permute-start.14) | collective-permute-done | bytes 544 | tf_op jit(solution)/shard_map/ppermute | solution.py:191
  131.0 0.8 copy.58
  (109 shorter events, 8.7 us)
Async XLA Ops:
  0.0 18.4 %copy-start = (bf16[128,3,1024]{2,0,1:T(8,128)(2,1)S(1)}, bf16[128,3,1024]{2,0,1:T(8,128)(2,1)}, u32[]{:S(2)}) copy-start(bf16[128,3,1024]{2,0,1:T(8,128)(2,1)} %param.8) | copy-start | bytes 2359300
  0.9 18.0 %collective-permute-start = (bf16[6,3,1024]{2,0,1:T(8,128)(2,1)S(1)}, bf16[6,3,1024]{2,0,1:T(8,128)(2,1)S(1)}, u32[]{:S(2)}, u32[]{:S(2)}) collective-permute-start(bf16[6,3,1024]{2,0,1:T(8,128)(2,1)S(1)} %slice.331), channel_id=1, source_target_pairs={{0,8},{8,16},{16,24},{24,32},{32,40},{40,48},{48,56},{56,64},{64,7... | collective-permute-start | bytes 110600 | tf_op jit(solution)/shard_map/ppermute | solution.py:20
  30.3 28.1 %collective-permute-start.2 = (f32[2,16,1024]{2,1,0:T(8,128)S(1)}, f32[2,16,1024]{2,1,0:T(8,128)S(1)}, u32[]{:S(2)}, u32[]{:S(2)}) collective-permute-start(f32[2,16,1024]{2,1,0:T(8,128)S(1)} %reshape.257), channel_id=1, source_target_pairs={{0,16},{8,24},{16,32},{24,40},{32,48},{40,56},{48,64},{56,72},{64,... | collective-permute-start | bytes 393224 | tf_op jit(solution)/shard_map/ppermute | solution.py:20
  45.7 30.7 %collective-permute-start.1 = (f32[2,16,1024]{2,1,0:T(8,128)S(1)}, f32[2,16,1024]{2,1,0:T(8,128)S(1)}, u32[]{:S(2)}, u32[]{:S(2)}) collective-permute-start(f32[2,16,1024]{2,1,0:T(8,128)S(1)} %reshape.257), channel_id=1, source_target_pairs={{0,8},{8,16},{16,24},{24,32},{32,40},{40,48},{48,56},{56,64},{64,7... | collective-permute-start | bytes 393224 | tf_op jit(solution)/shard_map/ppermute | solution.py:20
  48.1 16.5 %collective-permute-start.3 = (f32[2,16,1024]{2,1,0:T(8,128)S(1)}, f32[2,16,1024]{2,1,0:T(8,128)S(1)}, u32[]{:S(2)}, u32[]{:S(2)}) collective-permute-start(f32[2,16,1024]{2,1,0:T(8,128)S(1)} %reshape.257), channel_id=1, source_target_pairs={{0,24},{8,32},{16,40},{24,48},{32,56},{40,64},{48,72},{56,80},{64,... | collective-permute-start | bytes 393224 | tf_op jit(solution)/shard_map/ppermute | solution.py:20
  50.6 18.7 %collective-permute-start.4 = (f32[2,16,1024]{2,1,0:T(8,128)S(1)}, f32[2,16,1024]{2,1,0:T(8,128)S(1)}, u32[]{:S(2)}, u32[]{:S(2)}) collective-permute-start(f32[2,16,1024]{2,1,0:T(8,128)S(1)} %reshape.257), channel_id=1, source_target_pairs={{0,32},{8,40},{16,48},{24,56},{32,64},{40,72},{48,80},{56,88},{64,... | collective-permute-start | bytes 393224 | tf_op jit(solution)/shard_map/ppermute | solution.py:20
  56.5 15.4 %collective-permute-start.5 = (f32[2,16,1024]{2,1,0:T(8,128)S(1)}, f32[2,16,1024]{2,1,0:T(8,128)S(1)}, u32[]{:S(2)}, u32[]{:S(2)}) collective-permute-start(f32[2,16,1024]{2,1,0:T(8,128)S(1)} %reshape.257), channel_id=1, source_target_pairs={{0,40},{8,48},{16,56},{24,64},{32,72},{40,80},{48,88},{56,96},{64,... | collective-permute-start | bytes 393224 | tf_op jit(solution)/shard_map/ppermute | solution.py:20
  58.4 13.5 %collective-permute-start.6 = (f32[2,16,1024]{2,1,0:T(8,128)S(1)}, f32[2,16,1024]{2,1,0:T(8,128)S(1)}, u32[]{:S(2)}, u32[]{:S(2)}) collective-permute-start(f32[2,16,1024]{2,1,0:T(8,128)S(1)} %reshape.257), channel_id=1, source_target_pairs={{0,48},{8,56},{16,64},{24,72},{32,80},{40,88},{48,96},{56,104},{64... | collective-permute-start | bytes 393224 | tf_op jit(solution)/shard_map/ppermute | solution.py:20
  64.7 7.2 %collective-permute-start.7 = (f32[2,16,1024]{2,1,0:T(8,128)S(1)}, f32[2,16,1024]{2,1,0:T(8,128)S(1)}, u32[]{:S(2)}, u32[]{:S(2)}) collective-permute-start(f32[2,16,1024]{2,1,0:T(8,128)S(1)} %reshape.257), channel_id=1, source_target_pairs={{0,56},{8,64},{16,72},{24,80},{32,88},{40,96},{48,104},{56,112},{6... | collective-permute-start | bytes 393224 | tf_op jit(solution)/shard_map/ppermute | solution.py:20
  68.4 8.1 %copy-start.1 = (f32[64,16]{0,1:T(8,128)S(1)}, f32[64,16]{0,1:T(8,128)}, u32[]{:S(2)}) copy-start(f32[64,16]{0,1:T(8,128)} %param.11) | copy-start | bytes 12292
  68.4 8.2 %copy-start.2 = (f32[64,16]{0,1:T(8,128)S(1)}, f32[64,16]{0,1:T(8,128)}, u32[]{:S(2)}) copy-start(f32[64,16]{0,1:T(8,128)} %param.10) | copy-start | bytes 12292
  68.4 8.3 %copy-start.3 = (f32[2,64,16]{1,2,0:T(8,128)S(1)}, f32[2,64,16]{1,2,0:T(8,128)}, u32[]{:S(2)}) copy-start(f32[2,64,16]{1,2,0:T(8,128)} %param.12) | copy-start | bytes 24580
  69.3 7.0 %collective-permute-start.8 = (f32[2,16,1024]{2,1,0:T(8,128)S(1)}, f32[2,16,1024]{2,1,0:T(8,128)S(1)}, u32[]{:S(2)}, u32[]{:S(2)}) collective-permute-start(f32[2,16,1024]{2,1,0:T(8,128)S(1)} %reshape.257), channel_id=1, source_target_pairs={{0,64},{8,72},{16,80},{24,88},{32,96},{40,104},{48,112},{56,120},{... | collective-permute-start | bytes 393224 | tf_op jit(solution)/shard_map/ppermute | solution.py:20
  76.8 14.8 %collective-permute-start.9 = (f32[2,16,1024]{2,1,0:T(8,128)S(1)}, f32[2,16,1024]{2,1,0:T(8,128)S(1)}, u32[]{:S(2)}, u32[]{:S(2)}) collective-permute-start(f32[2,16,1024]{2,1,0:T(8,128)S(1)} %fusion.32), channel_id=1, source_target_pairs={{0,64},{8,72},{16,80},{24,88},{32,96},{40,104},{48,112},{56,120},{... | collective-permute-start | bytes 393224 | tf_op jit(solution)/shard_map/ppermute | solution.py:20
  91.7 12.5 %collective-permute-start.10 = (f32[2,16,1024]{2,1,0:T(8,128)S(1)}, f32[2,16,1024]{2,1,0:T(8,128)S(1)}, u32[]{:S(2)}, u32[]{:S(2)}) collective-permute-start(f32[2,16,1024]{2,1,0:T(8,128)S(1)} %maximum_add_fusion.1), channel_id=1, source_target_pairs={{0,128},{8,136},{16,144},{24,152},{32,160},{40,168},{48,176},{56,1... | collective-permute-start | bytes 393224 | tf_op jit(solution)/shard_map/ppermute | solution.py:20
  104.6 2.5 %copy-start.4 = (f32[1024]{0:T(1024)S(1)}, f32[1024]{0:T(1024)}, u32[]{:S(2)}) copy-start(f32[1024]{0:T(1024)} %param.13) | copy-start | bytes 12292
  107.1 23.7 %copy-start.5 = (f32[1024]{0:T(1024)S(1)}, f32[1024]{0:T(1024)}, u32[]{:S(2)}) copy-start(f32[1024]{0:T(1024)} %param.14) | copy-start | bytes 12292
  107.3 10.2 %collective-permute-start.13 = (f32[128]{0:T(128)S(1)}, f32[128]{0:T(128)S(1)}, u32[]{:S(2)}, u32[]{:S(2)}) collective-permute-start(f32[128]{0:T(128)S(1)} %get-tuple-element.26), channel_id=1, source_target_pairs={{0,3},{1,0},{2,1},{3,2},{4,7},{5,4},{6,5},{7,6},{8,11},{9,8},{10,9... | collective-permute-start | bytes 1544 | tf_op jit(solution)/shard_map/ppermute | solution.py:183
  112.0 7.0 %collective-permute-start.12 = (f32[128]{0:T(128)S(1)}, f32[128]{0:T(128)S(1)}, u32[]{:S(2)}, u32[]{:S(2)}) collective-permute-start(f32[128]{0:T(128)S(1)} %get-tuple-element.26), channel_id=1, source_target_pairs={{0,2},{1,3},{2,0},{3,1},{4,6},{5,7},{6,4},{7,5},{8,10},{9,11},{10,... | collective-permute-start | bytes 1544 | tf_op jit(solution)/shard_map/ppermute | solution.py:183
  114.7 6.7 %collective-permute-start.11 = (f32[128]{0:T(128)S(1)}, f32[128]{0:T(128)S(1)}, u32[]{:S(2)}, u32[]{:S(2)}) collective-permute-start(f32[128]{0:T(128)S(1)} %get-tuple-element.26), channel_id=1, source_target_pairs={{0,1},{1,2},{2,3},{3,0},{4,5},{5,6},{6,7},{7,4},{8,9},{9,10},{10,1... | collective-permute-start | bytes 1544 | tf_op jit(solution)/shard_map/ppermute | solution.py:183
  121.4 9.4 %collective-permute-start.14 = (f32[128]{0:T(128)S(1)}, f32[128]{0:T(128)S(1)}, u32[]{:S(2)}, u32[]{:S(2)}) collective-permute-start(f32[128]{0:T(128)S(1)} %fusion.59), channel_id=1, source_target_pairs={{0,4},{1,5},{2,6},{3,7},{4,0},{5,1},{6,2},{7,3},{8,12},{9,13},{10,... | collective-permute-start | bytes 1544 | tf_op jit(solution)/shard_map/ppermute | solution.py:191

commit v14 on v12

--- a/solution.py
+++ b/solution.py
@@ -31,7 +31,7 @@
     group_count, block = response.shape
     lag = jnp.arange(block, dtype=jnp.int32)
     picks = (lag[:, None, None] == lag[None, :, None] - lag[None, None, :]).astype(jnp.float32)
-    return jnp.einsum("gk,kts->gts", response, picks, precision=HIGHEST)
+    return jnp.einsum("gk,kts->gts", response, picks, precision=HIGH)
 
 
 def pole_tables(rate, angle, residue, block):

time: 120 us -> 120 us (level)
  transfers between devices with their start and end apart: 12 -> 12, of which waited for: 7 -> 7; matrix products, arithmetic and copies ran while one was open for 25% -> 24% of each run, Pallas kernels for 0% -> 0%
where the time goes in v14:
time: 120 us; the launch traced here: 119 us
  starting transfers between devices  47.4 us (40%)
  waiting for transfers between devices  21.4 us (18%)
  other arithmetic  17.6 us (15%)
  matrix products  14.5 us (12%)
  local copies, waits for them, and re-layouts  13.4 us (11%)
  between operations  4.54 us (4%)
    ppermute x8, starting transfers between devices, passed_along(): return lax.ppermute(block, axis, route)  29.9 us
    ppermute x8, waiting for transfers between devices, passed_along(): return lax.ppermute(block, axis, route)  15.5 us
    ppermute x3, starting transfers between devices, on_device(): gathered.append(lax.ppermute(partial, 'tp', pairs))  10.2 us
    ppermute x1, starting transfers between devices, on_device(): squares = squares + lax.ppermute(squares, 'tp', pairs)  7.31 us
    dot_general x1, matrix products, inside_terms(): jnp.einsum('gts,gis->git', matrix_table * same_genome[None], columns, pre...  5.72 us
    add x1, other arithmetic, short_filter(): result = result + jnp.where(keep_tap, taps_part[offset][None] * window, 0.0)  5.62 us
    mul x1, other arithmetic, pole_tables(): power_re = magnitude * jnp.cos(angle[:, :, None] * counter)  3.86 us
    ppermute x3, waiting for transfers between devices, on_device(): gathered.append(lax.ppermute(partial, 'tp', pairs))  3.83 us
  transfers between devices with their start and end apart: 12, of which 7 were waited for; matrix products, arithmetic and copies ran while one was open for 24% of the time, Pallas kernels for 0%

profile of v14, /device:TPU:128, one launch (start us, length us, event | category | flops | bytes accessed | tf_op | source)
XLA Modules:
  0.0 118.9 jit_solution(4647354706576376752)
XLA Ops:
  0.0 0.9 slice.247
  0.9 1.9 %collective-permute-start = (bf16[6,3,1024]{2,0,1:T(8,128)(2,1)S(1)}, bf16[6,3,1024]{2,0,1:T(8,128)(2,1)S(1)}, u32[]{:S(2)}, u32[]{:S(2)}) collective-permute-start(bf16[6,3,1024]{2,0,1:T(8,128)(2,1)S(1)} %slice.247), channel_id=1, source_target_pairs={{0,8},{8,16},{16,24},{24,32},{32,40},{40,48},{48,56},{56,64},{64,7... | collective-permute-start | bytes 110600 | tf_op jit(solution)/shard_map/ppermute | solution.py:20
  2.9 0.8 reduce-window.9
  3.7 1.4 %and_reduce_fusion = (pred[]{:T(512)}, pred[]{:T(512)}, pred[]{:T(512)}, pred[]{:T(512)}, pred[]{:T(512)}, /*index=5*/pred[]{:T(512)}, s32[4]{0:T(128)S(1)}) fusion(s32[]{:T(128)S(6)} %sub.167, s32[]{:T(128)S(6)} %sub.148, s32[]{:T(128)S(6)} %sub.164, s32[]{:T(128)S(6)} %sub.161, s32[]{:T(128)S(6)} %sub.154, s32[]{:T(128)S(6)} %sub.151, s32[]{:T(128)S(6)} %sub.147, ...), kind=kLoop, calls=%fused_computation.133 | loop fusion | flops 74 | bytes 82 | tf_op jit(solution)/shard_map/reduce_or | solution.py:140
  5.3 0.7 slice.262
  6.0 0.8 copy.49
  6.8 0.7 neg.12
  7.5 0.8 subtract_bitcast_fusion.2
  8.2 1.5 %fusion.49 = (f32[1,3,1024]{2,0,1:T(1,128)S(1)}, f32[1,3,1024]{2,0,1:T(1,128)S(1)}, f32[1,3,1024]{2,0,1:T(1,128)S(1)}, f32[1,3,1024]{2,0,1:T(1,128)S(1)}, f32[1,...) fusion(f32[7,3,1024]{2,0,1:T(8,128)} %param.9), kind=kLoop, calls=%fused_computation.167 | loop fusion | bytes 172032 | tf_op jit(solution)/shard_map/slice | solution.py:97
  13.9 2.0 %fusion.20 = (f32[1,64,16,128]{3,2,0,1:T(8,128)S(1)}, f32[1,64,16,128]{3,2,0,1:T(8,128)S(1)}) fusion(f32[64,16]{1,0:T(8,128)S(1)} %copy.49, f32[128]{0:T(128)S(1)} %subtract_convert_fusion, f32[64,16]{1,0:T(8,128)S(1)} %copy.48), kind=kLoop, calls=%fused_computation.41 | loop fusion | flops 524288 | bytes 1057280 | tf_op jit(solution)/shard_map/mul | solution.py:59
  15.8 0.7 compare_convert_fusion.1
  16.6 0.4 copy.45
  17.0 0.4 copy.46
  17.4 5.6 %select_add_fusion = f32[128,3,1024]{0,2,1:T(8,128)S(1)} fusion(bf16[128,3,1024]{0,2,1:T(8,128)(2,1)S(1)} %copy.45, bf16[6,3,1024]{0,2,1:T(8,128)(2,1)S(1)} %copy.46, f32[3,1024]{1,0:T(4,128)S(1)} %get-tuple-element.88, f32[3,1024]{1,0:T(4,128)S(1)} %get-tuple-element.89, f32[3,1024]{1,0:T(4,128)S(1)} %get-tuple-element.90, ...), kind=kLoop, calls=%fused_computation.16 | loop fusion | flops 17694720 | bytes 2483072 | tf_op jit(solution)/shard_map/add | solution.py:97
  23.1 3.8 %convolution_bitcast_fusion = f32[2,16,64,16]{1,3,0,2:T(8,128)S(1)} fusion(f32[64,16,128,1]{2,1,3,0:T(8,128)S(1)} %bitcast.218, f32[1,64,16,128]{3,2,0,1:T(8,128)S(1)} %get-tuple-element.58, f32[1,64,16,128]{3,2,0,1:T(8,128)S(1)} %get-tuple-element.57, f32[128]{0:T(128)S(1)} %compare_convert_fusion.1), kind=kOutput, calls=%fused_computation.19 | convolution fusion | flops 25690112 | bytes 1704448 | tf_op jit(solution)/shard_map/rgns,gis->rngi/dot_general | solution.py:83
  26.9 0.9 copy.50
  27.8 0.6 reshape.236
  28.4 3.5 %collective-permute-start.2 = (f32[2,16,1024]{2,1,0:T(8,128)S(1)}, f32[2,16,1024]{2,1,0:T(8,128)S(1)}, u32[]{:S(2)}, u32[]{:S(2)}) collective-permute-start(f32[2,16,1024]{2,1,0:T(8,128)S(1)} %reshape.236), channel_id=1, source_target_pairs={{0,16},{8,24},{16,32},{24,40},{32,48},{40,56},{48,64},{56,72},{64,... | collective-permute-start | bytes 393224 | tf_op jit(solution)/shard_map/ppermute | solution.py:20
  32.2 0.3 slice.269
  32.6 0.3 slice.265
  33.1 0.3 slice.277
  33.6 0.3 slice.273
  35.0 0.3 slice.314
  36.4 0.3 slice.302
  37.7 3.3 %collective-permute-start.1 = (f32[2,16,1024]{2,1,0:T(8,128)S(1)}, f32[2,16,1024]{2,1,0:T(8,128)S(1)}, u32[]{:S(2)}, u32[]{:S(2)}) collective-permute-start(f32[2,16,1024]{2,1,0:T(8,128)S(1)} %reshape.236), channel_id=1, source_target_pairs={{0,8},{8,16},{16,24},{24,32},{32,40},{40,48},{48,56},{56,64},{64,7... | collective-permute-start | bytes 393224 | tf_op jit(solution)/shard_map/ppermute | solution.py:20
  41.0 3.4 %collective-permute-start.3 = (f32[2,16,1024]{2,1,0:T(8,128)S(1)}, f32[2,16,1024]{2,1,0:T(8,128)S(1)}, u32[]{:S(2)}, u32[]{:S(2)}) collective-permute-start(f32[2,16,1024]{2,1,0:T(8,128)S(1)} %reshape.236), channel_id=1, source_target_pairs={{0,24},{8,32},{16,40},{24,48},{32,56},{40,64},{48,72},{56,80},{64,... | collective-permute-start | bytes 393224 | tf_op jit(solution)/shard_map/ppermute | solution.py:20
  44.4 5.1 %collective-permute-start.4 = (f32[2,16,1024]{2,1,0:T(8,128)S(1)}, f32[2,16,1024]{2,1,0:T(8,128)S(1)}, u32[]{:S(2)}, u32[]{:S(2)}) collective-permute-start(f32[2,16,1024]{2,1,0:T(8,128)S(1)} %reshape.236), channel_id=1, source_target_pairs={{0,32},{8,40},{16,48},{24,56},{32,64},{40,72},{48,80},{56,88},{64,... | collective-permute-start | bytes 393224 | tf_op jit(solution)/shard_map/ppermute | solution.py:20
  49.5 2.6 %collective-permute-done.3 = f32[2,16,1024]{2,1,0:T(8,128)S(1)} collective-permute-done((f32[2,16,1024]{2,1,0:T(8,128)S(1)}, f32[2,16,1024]{2,1,0:T(8,128)S(1)}, u32[]{:S(2)}, u32[]{:S(2)}) %collective-permute-start.3) | collective-permute-done | bytes 131104 | tf_op jit(solution)/shard_map/ppermute | solution.py:20
  52.1 4.9 %collective-permute-done.4 = f32[2,16,1024]{2,1,0:T(8,128)S(1)} collective-permute-done((f32[2,16,1024]{2,1,0:T(8,128)S(1)}, f32[2,16,1024]{2,1,0:T(8,128)S(1)}, u32[]{:S(2)}, u32[]{:S(2)}) %collective-permute-start.4) | collective-permute-done | bytes 131104 | tf_op jit(solution)/shard_map/ppermute | solution.py:20
  57.5 1.9 %collective-permute-start.5 = (f32[2,16,1024]{2,1,0:T(8,128)S(1)}, f32[2,16,1024]{2,1,0:T(8,128)S(1)}, u32[]{:S(2)}, u32[]{:S(2)}) collective-permute-start(f32[2,16,1024]{2,1,0:T(8,128)S(1)} %fusion.28), channel_id=1, source_target_pairs={{0,32},{8,40},{16,48},{24,56},{32,64},{40,72},{48,80},{56,88},{64,... | collective-permute-start | bytes 393224 | tf_op jit(solution)/shard_map/ppermute | solution.py:20
  59.4 3.9 %fusion.7 = (f32[64,16,129]{2,1,0:T(8,128)S(1)}, f32[64,16,129]{2,1,0:T(8,128)S(1)}) fusion(f32[64,16]{1,0:T(8,128)S(1)} %copy.53, f32[129]{0:T(256)S(1)} %iota_convert_fusion, f32[64,16]{1,0:T(8,128)S(1)} %copy.52), kind=kLoop, calls=%fused_computation.23 | loop fusion | flops 528384 | bytes 1065476 | tf_op jit(solution)/shard_map/mul | solution.py:40
  63.2 0.6 subtract_bitcast_fusion
  63.9 5.3 %collective-permute-done.5 = f32[2,16,1024]{2,1,0:T(8,128)S(1)} collective-permute-done((f32[2,16,1024]{2,1,0:T(8,128)S(1)}, f32[2,16,1024]{2,1,0:T(8,128)S(1)}, u32[]{:S(2)}, u32[]{:S(2)}) %collective-permute-start.5) | collective-permute-done | bytes 131104 | tf_op jit(solution)/shard_map/ppermute | solution.py:20
  69.2 1.9 %collective-permute-start.6 = (f32[2,16,1024]{2,1,0:T(8,128)S(1)}, f32[2,16,1024]{2,1,0:T(8,128)S(1)}, u32[]{:S(2)}, u32[]{:S(2)}) collective-permute-start(f32[2,16,1024]{2,1,0:T(8,128)S(1)} %maximum_add_fusion.1), channel_id=1, source_target_pairs={{0,64},{8,72},{16,80},{24,88},{32,96},{40,104},{48,112},{56,120},{... | collective-permute-start | bytes 393224 | tf_op jit(solution)/shard_map/ppermute | solution.py:20
  71.2 2.6 %fusion.4 = f32[64,128,128]{2,0,1:T(8,128)S(1)} fusion(s32[128,128]{1,0:T(8,128)S(1)} %iota_subtract_fusion, f32[128,128]{1,0:T(8,128)S(1)} %compare_convert_fusion, f32[64,128]{1,0:T(8,128)S(1)} %get-tuple-element.33), kind=kOutput, calls=%fused_computation.15 | convolution fusion | flops 808452096 | bytes 4358144 | tf_op jit(solution)/shard_map/gk,kts->gts/dot_general | solution.py:34
  73.8 2.8 %collective-permute-done.6 = f32[2,16,1024]{2,1,0:T(8,128)S(1)} collective-permute-done((f32[2,16,1024]{2,1,0:T(8,128)S(1)}, f32[2,16,1024]{2,1,0:T(8,128)S(1)}, u32[]{:S(2)}, u32[]{:S(2)}) %collective-permute-start.6) | collective-permute-done | bytes 131104 | tf_op jit(solution)/shard_map/ppermute | solution.py:20
  76.6 8.8 %collective-permute-start.7 = (f32[2,16,1024]{2,1,0:T(8,128)S(1)}, f32[2,16,1024]{2,1,0:T(8,128)S(1)}, u32[]{:S(2)}, u32[]{:S(2)}) collective-permute-start(f32[2,16,1024]{2,1,0:T(8,128)S(1)} %maximum_add_fusion.2), channel_id=1, source_target_pairs={{0,128},{8,136},{16,144},{24,152},{32,160},{40,168},{48,176},{56,1... | collective-permute-start | bytes 393224 | tf_op jit(solution)/shard_map/ppermute | solution.py:20
  85.5 5.7 %fusion.1 = f32[64,16,128]{2,1,0:T(8,128)} fusion(f32[64,16,128]{2,1,0:T(8,128)S(1)} %bitcast.219, f32[64,128,128]{2,0,1:T(8,128)S(1)} %fusion.4), kind=kOutput, calls=%fused_computation.2 | convolution fusion | flops 100663296 | bytes 5242880 | tf_op jit(solution)/shard_map/gts,gis->git/dot_general | solution.py:78
  91.2 0.4 reshape.237
  91.6 2.4 %fusion.6 = f32[64,16,128]{2,1,0:T(8,128)S(1)} fusion(f32[64,16,128]{2,1,0:T(8,128)} %fusion.1, f32[1,64,16,128]{3,2,0,1:T(8,128)S(1)} %get-tuple-element.32, f32[1,64,16,128]{3,2,0,1:T(8,128)S(1)} %get-tuple-element.31, f32[2,16,64,16]{3,2,1,0:T(8,128)S(1)} %reshape.237, pred[128]{0:T(512)(128)(4,1)S(1)} %get-tuple-element.80), kind=kOutput, calls=%fused_computation.22 | convolution fusion | flops 25690112 | bytes 2228352 | tf_op jit(solution)/shard_map/rgnt,rngi->git/dot_general | solution.py:87
  94.3 4.7 %collective-permute-start.10 = (f32[128]{0:T(128)S(1)}, f32[128]{0:T(128)S(1)}, u32[]{:S(2)}, u32[]{:S(2)}) collective-permute-start(f32[128]{0:T(128)S(1)} %get-tuple-element.23), channel_id=1, source_target_pairs={{0,3},{1,0},{2,1},{3,2},{4,7},{5,4},{6,5},{7,6},{8,11},{9,8},{10,9... | collective-permute-start | bytes 1544 | tf_op jit(solution)/shard_map/ppermute | solution.py:183
  99.0 2.7 %collective-permute-start.9 = (f32[128]{0:T(128)S(1)}, f32[128]{0:T(128)S(1)}, u32[]{:S(2)}, u32[]{:S(2)}) collective-permute-start(f32[128]{0:T(128)S(1)} %get-tuple-element.23), channel_id=1, source_target_pairs={{0,2},{1,3},{2,0},{3,1},{4,6},{5,7},{6,4},{7,5},{8,10},{9,11},{10,... | collective-permute-start | bytes 1544 | tf_op jit(solution)/shard_map/ppermute | solution.py:183
  101.7 2.8 %collective-permute-start.8 = (f32[128]{0:T(128)S(1)}, f32[128]{0:T(128)S(1)}, u32[]{:S(2)}, u32[]{:S(2)}) collective-permute-start(f32[128]{0:T(128)S(1)} %get-tuple-element.23), channel_id=1, source_target_pairs={{0,1},{1,2},{2,3},{3,0},{4,5},{5,6},{6,7},{7,4},{8,9},{9,10},{10,1... | collective-permute-start | bytes 1544 | tf_op jit(solution)/shard_map/ppermute | solution.py:183
  104.5 1.4 %collective-permute-done.9 = f32[128]{0:T(128)S(1)} collective-permute-done((f32[128]{0:T(128)S(1)}, f32[128]{0:T(128)S(1)}, u32[]{:S(2)}, u32[]{:S(2)}) %collective-permute-start.9) | collective-permute-done | bytes 544 | tf_op jit(solution)/shard_map/ppermute | solution.py:183
  105.9 2.4 %collective-permute-done.8 = f32[128]{0:T(128)S(1)} collective-permute-done((f32[128]{0:T(128)S(1)}, f32[128]{0:T(128)S(1)}, u32[]{:S(2)}, u32[]{:S(2)}) %collective-permute-start.8) | collective-permute-done | bytes 544 | tf_op jit(solution)/shard_map/ppermute | solution.py:183
  108.4 7.3 %collective-permute-start.11 = (f32[128]{0:T(128)S(1)}, f32[128]{0:T(128)S(1)}, u32[]{:S(2)}, u32[]{:S(2)}) collective-permute-start(f32[128]{0:T(128)S(1)} %fusion.40), channel_id=1, source_target_pairs={{0,4},{1,5},{2,6},{3,7},{4,0},{5,1},{6,2},{7,3},{8,12},{9,13},{10,... | collective-permute-start | bytes 1544 | tf_op jit(solution)/shard_map/ppermute | solution.py:191
  115.7 2.0 %collective-permute-done.11 = f32[128]{0:T(128)S(1)} collective-permute-done((f32[128]{0:T(128)S(1)}, f32[128]{0:T(128)S(1)}, u32[]{:S(2)}, u32[]{:S(2)}) %collective-permute-start.11) | collective-permute-done | bytes 544 | tf_op jit(solution)/shard_map/ppermute | solution.py:191
  118.0 0.8 copy.58
  (83 shorter events, 5.5 us)
Async XLA Ops:
  0.0 16.5 %copy-start = (bf16[128,3,1024]{2,0,1:T(8,128)(2,1)S(1)}, bf16[128,3,1024]{2,0,1:T(8,128)(2,1)}, u32[]{:S(2)}) copy-start(bf16[128,3,1024]{2,0,1:T(8,128)(2,1)} %param.8) | copy-start | bytes 2359300
  0.9 16.1 %collective-permute-start = (bf16[6,3,1024]{2,0,1:T(8,128)(2,1)S(1)}, bf16[6,3,1024]{2,0,1:T(8,128)(2,1)S(1)}, u32[]{:S(2)}, u32[]{:S(2)}) collective-permute-start(bf16[6,3,1024]{2,0,1:T(8,128)(2,1)S(1)} %slice.247), channel_id=1, source_target_pairs={{0,8},{8,16},{16,24},{24,32},{32,40},{40,48},{48,56},{56,64},{64,7... | collective-permute-start | bytes 110600 | tf_op jit(solution)/shard_map/ppermute | solution.py:20
  28.4 21.1 %collective-permute-start.2 = (f32[2,16,1024]{2,1,0:T(8,128)S(1)}, f32[2,16,1024]{2,1,0:T(8,128)S(1)}, u32[]{:S(2)}, u32[]{:S(2)}) collective-permute-start(f32[2,16,1024]{2,1,0:T(8,128)S(1)} %reshape.236), channel_id=1, source_target_pairs={{0,16},{8,24},{16,32},{24,40},{32,48},{40,56},{48,64},{56,72},{64,... | collective-permute-start | bytes 393224 | tf_op jit(solution)/shard_map/ppermute | solution.py:20
  37.1 19.9 %copy-start.1 = (f32[64,16]{0,1:T(8,128)S(1)}, f32[64,16]{0,1:T(8,128)}, u32[]{:S(2)}) copy-start(f32[64,16]{0,1:T(8,128)} %param.11) | copy-start | bytes 12292
  37.2 20.0 %copy-start.2 = (f32[64,16]{0,1:T(8,128)S(1)}, f32[64,16]{0,1:T(8,128)}, u32[]{:S(2)}) copy-start(f32[64,16]{0,1:T(8,128)} %param.10) | copy-start | bytes 12292
  37.2 20.1 %copy-start.3 = (f32[2,64,16]{1,2,0:T(8,128)S(1)}, f32[2,64,16]{1,2,0:T(8,128)}, u32[]{:S(2)}) copy-start(f32[2,64,16]{1,2,0:T(8,128)} %param.12) | copy-start | bytes 24580
  37.7 19.4 %collective-permute-start.1 = (f32[2,16,1024]{2,1,0:T(8,128)S(1)}, f32[2,16,1024]{2,1,0:T(8,128)S(1)}, u32[]{:S(2)}, u32[]{:S(2)}) collective-permute-start(f32[2,16,1024]{2,1,0:T(8,128)S(1)} %reshape.236), channel_id=1, source_target_pairs={{0,8},{8,16},{16,24},{24,32},{32,40},{40,48},{48,56},{56,64},{64,7... | collective-permute-start | bytes 393224 | tf_op jit(solution)/shard_map/ppermute | solution.py:20
  41.0 11.1 %collective-permute-start.3 = (f32[2,16,1024]{2,1,0:T(8,128)S(1)}, f32[2,16,1024]{2,1,0:T(8,128)S(1)}, u32[]{:S(2)}, u32[]{:S(2)}) collective-permute-start(f32[2,16,1024]{2,1,0:T(8,128)S(1)} %reshape.236), channel_id=1, source_target_pairs={{0,24},{8,32},{16,40},{24,48},{32,56},{40,64},{48,72},{56,80},{64,... | collective-permute-start | bytes 393224 | tf_op jit(solution)/shard_map/ppermute | solution.py:20
  44.4 12.6 %collective-permute-start.4 = (f32[2,16,1024]{2,1,0:T(8,128)S(1)}, f32[2,16,1024]{2,1,0:T(8,128)S(1)}, u32[]{:S(2)}, u32[]{:S(2)}) collective-permute-start(f32[2,16,1024]{2,1,0:T(8,128)S(1)} %reshape.236), channel_id=1, source_target_pairs={{0,32},{8,40},{16,48},{24,56},{32,64},{40,72},{48,80},{56,88},{64,... | collective-permute-start | bytes 393224 | tf_op jit(solution)/shard_map/ppermute | solution.py:20
  57.5 11.7 %collective-permute-start.5 = (f32[2,16,1024]{2,1,0:T(8,128)S(1)}, f32[2,16,1024]{2,1,0:T(8,128)S(1)}, u32[]{:S(2)}, u32[]{:S(2)}) collective-permute-start(f32[2,16,1024]{2,1,0:T(8,128)S(1)} %fusion.28), channel_id=1, source_target_pairs={{0,32},{8,40},{16,48},{24,56},{32,64},{40,72},{48,80},{56,88},{64,... | collective-permute-start | bytes 393224 | tf_op jit(solution)/shard_map/ppermute | solution.py:20
  69.2 7.3 %collective-permute-start.6 = (f32[2,16,1024]{2,1,0:T(8,128)S(1)}, f32[2,16,1024]{2,1,0:T(8,128)S(1)}, u32[]{:S(2)}, u32[]{:S(2)}) collective-permute-start(f32[2,16,1024]{2,1,0:T(8,128)S(1)} %maximum_add_fusion.1), channel_id=1, source_target_pairs={{0,64},{8,72},{16,80},{24,88},{32,96},{40,104},{48,112},{56,120},{... | collective-permute-start | bytes 393224 | tf_op jit(solution)/shard_map/ppermute | solution.py:20
  76.6 14.6 %collective-permute-start.7 = (f32[2,16,1024]{2,1,0:T(8,128)S(1)}, f32[2,16,1024]{2,1,0:T(8,128)S(1)}, u32[]{:S(2)}, u32[]{:S(2)}) collective-permute-start(f32[2,16,1024]{2,1,0:T(8,128)S(1)} %maximum_add_fusion.2), channel_id=1, source_target_pairs={{0,128},{8,136},{16,144},{24,152},{32,160},{40,168},{48,176},{56,1... | collective-permute-start | bytes 393224 | tf_op jit(solution)/shard_map/ppermute | solution.py:20
  91.6 2.5 %copy-start.4 = (f32[1024]{0:T(1024)S(1)}, f32[1024]{0:T(1024)}, u32[]{:S(2)}) copy-start(f32[1024]{0:T(1024)} %param.13) | copy-start | bytes 12292
  94.1 23.7 %copy-start.5 = (f32[1024]{0:T(1024)S(1)}, f32[1024]{0:T(1024)}, u32[]{:S(2)}) copy-start(f32[1024]{0:T(1024)} %param.14) | copy-start | bytes 12292
  94.3 10.2 %collective-permute-start.10 = (f32[128]{0:T(128)S(1)}, f32[128]{0:T(128)S(1)}, u32[]{:S(2)}, u32[]{:S(2)}) collective-permute-start(f32[128]{0:T(128)S(1)} %get-tuple-element.23), channel_id=1, source_target_pairs={{0,3},{1,0},{2,1},{3,2},{4,7},{5,4},{6,5},{7,6},{8,11},{9,8},{10,9... | collective-permute-start | bytes 1544 | tf_op jit(solution)/shard_map/ppermute | solution.py:183
  99.0 7.0 %collective-permute-start.9 = (f32[128]{0:T(128)S(1)}, f32[128]{0:T(128)S(1)}, u32[]{:S(2)}, u32[]{:S(2)}) collective-permute-start(f32[128]{0:T(128)S(1)} %get-tuple-element.23), channel_id=1, source_target_pairs={{0,2},{1,3},{2,0},{3,1},{4,6},{5,7},{6,4},{7,5},{8,10},{9,11},{10,... | collective-permute-start | bytes 1544 | tf_op jit(solution)/shard_map/ppermute | solution.py:183
  101.7 6.7 %collective-permute-start.8 = (f32[128]{0:T(128)S(1)}, f32[128]{0:T(128)S(1)}, u32[]{:S(2)}, u32[]{:S(2)}) collective-permute-start(f32[128]{0:T(128)S(1)} %get-tuple-element.23), channel_id=1, source_target_pairs={{0,1},{1,2},{2,3},{3,0},{4,5},{5,6},{6,7},{7,4},{8,9},{9,10},{10,1... | collective-permute-start | bytes 1544 | tf_op jit(solution)/shard_map/ppermute | solution.py:183
  108.4 9.4 %collective-permute-start.11 = (f32[128]{0:T(128)S(1)}, f32[128]{0:T(128)S(1)}, u32[]{:S(2)}, u32[]{:S(2)}) collective-permute-start(f32[128]{0:T(128)S(1)} %fusion.40), channel_id=1, source_target_pairs={{0,4},{1,5},{2,6},{3,7},{4,0},{5,1},{6,2},{7,3},{8,12},{9,13},{10,... | collective-permute-start | bytes 1544 | tf_op jit(solution)/shard_map/ppermute | solution.py:191
